TPU v7x, 512 devices: a whole 4x4x16 slice. The times are simulated.
512 devices in a mesh: seq: 64 (over z, x_hi, core), section: 8 (over y, x_lo).
Axes of the slice: x: 4 (x_hi: 2, x_lo: 2; x = x_hi * 2 + x_lo), y: 4, z: 16, core: 2. Of those that a mesh axis runs over, the one named last changes fastest.
Arguments:
- fwd_input: bfloat16 [8, 16384, 768], P('section', 'seq'), may hold values from -6 to 6
- bwd_input: bfloat16 [8, 16384, 768], P('section', 'seq'), may hold values from -6 to 6
- bwd_cotangent: bfloat16 [8, 16384, 768], P('section', 'seq'), may hold values from -6 to 6
- conv_weight: bfloat16 [8, 2, 3, 768, 384], P('section', None, None, 'seq'), may hold values from -0.125 to 0.125
- proj_weight: bfloat16 [8, 2, 384, 768], P('section', None, 'seq'), may hold values from -0.3125 to 0.3125
Outputs:
- next_input: bfloat16 [8, 16384, 768], P('section', 'seq')
- prev_cotangent: bfloat16 [8, 16384, 768], P('section', 'seq')
All inputs are finite; a program needn't handle non-finite values.
Results may differ from a plain program's by a relative error of at most 0.012.
Values may be sent and summed in bfloat16 or wider, within the bound.
No kernel may reach another device: no remote copies, remote signals or barrier semaphores. Data moves between devices by JAX's collectives and lax.ppermute only.
A program may use at most 64 MiB of HBM per device.

v0:
```python
import jax
import jax.numpy as jnp
from jax import lax
from jax.sharding import PartitionSpec as P

BLOCKS = 2
FIRST_DILATION = 128


def padded(x, sides, width):
    for axis, dim in sides:
        size, length = (lax.axis_size(axis), x.shape[dim])
        up = [(i, (i + 1) % size) for i in range(size - 1)]
        down = [(j, i) for i, j in up]
        last = lax.slice_in_dim(x, length - width, length, axis=dim)
        initial = lax.slice_in_dim(x, 0, width, axis=dim)
        before = lax.ppermute(last, axis, up)
        after = lax.ppermute(initial, axis, down)
        x = jnp.concatenate([before, x, after], axis=dim)
    return x


def from_behind(block, axis, distance):
    devices = range(lax.axis_size(axis))
    route = [(i - distance, i) for i in devices if i - distance in devices]
    return lax.ppermute(block, axis, route)


def from_behind_2(block, axis, distance):
    devices = range(lax.axis_size(axis))
    route = [((i - distance) % len(devices), i) for i in devices]
    return lax.ppermute(block, axis, route)


def gelu_back(value, cotangent):
    return jax.vjp(jax.nn.gelu, value)[1](cotangent)[0]


def rounded(product):
    return lax.optimization_barrier(product.astype(jnp.bfloat16)).astype(jnp.float32)


def reach(values, spacing_gap):
    length = values.shape[1]
    if spacing_gap < length:
        padded_input = padded(values, (("seq", 1),), spacing_gap)
        return (padded_input[:, :length], padded_input[:, 2 * spacing_gap :])
    shard_hops = spacing_gap // length
    earlier = from_behind(values, "seq", shard_hops)
    later = from_behind(values, "seq", -shard_hops)
    return (earlier, later)


def conv_apply(values, weight):
    return jnp.einsum("krc,ch->krh", values, weight, preferred_element_type=jnp.float32)


def conv_transpose(values, weight):
    return jnp.einsum("krh,ch->krc", values, weight, preferred_element_type=jnp.float32)


def run_forward(present_state, pieces):
    stored = []
    for depth_level in range(BLOCKS):
        conv_part, proj_part = pieces[depth_level]
        spacing_gap = FIRST_DILATION * 4**depth_level
        activated = jax.nn.gelu(present_state.astype(jnp.float32)).astype(jnp.bfloat16)
        middle = conv_apply(activated, conv_part[1])
        earlier, later = reach(activated, spacing_gap)
        preact = (
            rounded(conv_apply(earlier, conv_part[0]))
            + middle
            + rounded(conv_apply(later, conv_part[2]))
        )
        hidden = jax.nn.gelu(preact).astype(jnp.bfloat16)
        stored.append((present_state, preact))
        branch = jnp.einsum("krh,hc->krc", hidden, proj_part, preferred_element_type=jnp.float32)
        present_state = (present_state.astype(jnp.float32) + branch).astype(jnp.bfloat16)
    return (present_state, stored)


def local(fwd_input, bwd_input, bwd_cotangent, conv_weight, proj_weight):
    convolution_complete, proj_full = (
        lax.all_gather(conv_weight, "seq", axis=3, tiled=True),
        lax.all_gather(proj_weight, "seq", axis=2, tiled=True),
    )
    pieces = [
        (convolution_complete[0, depth_level], proj_full[0, depth_level])
        for depth_level in range(BLOCKS)
    ]
    forward_out, unused = run_forward(fwd_input, pieces)
    unused_out, stored = run_forward(bwd_input, pieces)
    cotangent = bwd_cotangent
    for depth_level in reversed(range(BLOCKS)):
        conv_part, proj_part = pieces[depth_level]
        spacing_gap = FIRST_DILATION * 4**depth_level
        block_in, preact = stored[depth_level]
        d_hidden = jnp.einsum(
            "krc,hc->krh", cotangent, proj_part, preferred_element_type=jnp.float32
        )
        d_preact = gelu_back(preact, d_hidden).astype(jnp.bfloat16)
        earlier, later = reach(d_preact, spacing_gap)
        d_act = (
            conv_transpose(later, conv_part[0])
            + conv_transpose(d_preact, conv_part[1])
            + conv_transpose(earlier, conv_part[2])
        )
        total = cotangent.astype(jnp.float32) + gelu_back(block_in.astype(jnp.float32), d_act)
        cotangent = total.astype(jnp.bfloat16)
    next_input = from_behind_2(forward_out, "section", 1)
    prev_cotangent = from_behind_2(cotangent, "section", -1)
    return (next_input, prev_cotangent)


def solution(mesh):
    in_specs = (
        P("section", "seq", None),
        P("section", "seq", None),
        P("section", "seq", None),
        P("section", None, None, "seq", None),
        P("section", None, "seq", None),
    )
    out_specs = (P("section", "seq", None), P("section", "seq", None))
    return jax.shard_map(local, mesh=mesh, in_specs=in_specs, out_specs=out_specs, check_vma=False)
```

profile of v0, /device:TPU:103, one launch (start us, length us, event | category | flops | bytes accessed | tf_op | source)
XLA Modules:
  0.0 411.6 jit_solution(7806383991603172441)
XLA Ops:
  11.6 6.1 %collective-permute-start.5 = (bf16[1,128,768]{2,1,0:T(8,128)(2,1)}, bf16[1,128,768]{2,1,0:T(8,128)(2,1)}, u32[]{:S(2)}, u32[]{:S(2)}) collective-permute-start(bf16[1,128,768]{2,1,0:T(8,128)(2,1)} %get-tuple-element.10), channel_id=1, source_target_pairs={{0,8},{8,16},{16,24},{24,32},{32,40},{40,48},{48,56},{56,64},{64,7... | collective-permute-start | bytes 589832 | tf_op jit(solution)/shard_map/ppermute | solution.py:17
  17.7 1.9 collective-permute-start.6
  21.5 7.2 %collective-permute-start = (bf16[1,128,768]{2,1,0:T(8,128)(2,1)}, bf16[1,128,768]{2,1,0:T(8,128)(2,1)}, u32[]{:S(2)}, u32[]{:S(2)}) collective-permute-start(bf16[1,128,768]{2,1,0:T(8,128)(2,1)} %get-tuple-element.12), channel_id=1, source_target_pairs={{0,8},{8,16},{16,24},{24,32},{32,40},{40,48},{48,56},{56,64},{64,7... | collective-permute-start | bytes 589832 | tf_op jit(solution)/shard_map/ppermute | solution.py:17
  28.8 1.9 collective-permute-start.1
  30.7 123.7 %all-gather.5.cloned.1.call-done = bf16[1,2,384,768]{3,1,0,2:T(2,128)(2,1)} async-done(((bf16[1,2,6,768]{3,1,0,2:T(2,128)(2,1)}), bf16[1,2,384,768]{3,1,0,2:T(2,128)(2,1)}) %all-gather.5.cloned.1.call-update) | async-done | bytes 1179664 | tf_op jit(solution)/shard_map/all_gather | solution.py:85
  154.4 5.1 %fusion.172 = (bf16[1,1,384,768]{3,1,0,2:T(2,128)(2,1)}, bf16[1,1,384,768]{3,1,0,2:T(2,128)(2,1)}) fusion(bf16[1,2,384,768]{3,1,0,2:T(2,128)(2,1)} %all-gather.5.cloned.1.call-done), kind=kLoop, calls=%fused_computation.215 | loop fusion | bytes 2359296 | tf_op jit(solution)/shard_map/slice | solution.py:88
  159.5 141.4 %all-gather.3.cloned.1.call-done = bf16[1,2,3,768,384]{4,1,2,0,3:T(2,128)(2,1)} async-done(((bf16[1,2,3,12,384]{4,1,2,0,3:T(2,128)(2,1)}), bf16[1,2,3,768,384]{4,1,2,0,3:T(2,128)(2,1)}) %all-gather.3.cloned.1.call-update) | async-done | bytes 3538960 | tf_op jit(solution)/shard_map/all_gather | solution.py:84
  300.9 9.0 %fusion.171 = (bf16[1,1,1,768,384]{4,1,2,0,3:T(2,128)(2,1)}, bf16[1,1,1,768,384]{4,1,2,0,3:T(2,128)(2,1)}, bf16[1,1,1,768,384]{4,1,2,0,3:T(2,128)(2,1)S(1)}, bf1...) fusion(bf16[1,2,3,768,384]{4,1,2,0,3:T(2,128)(2,1)} %all-gather, ...), kind=kLoop, calls=%fused_computation.214 | loop fusion | bytes 7077888 | tf_op jit(solution)/shard_map/slice | solution.py:68
  315.6 3.8 collective-permute-start.7
  319.4 3.0 collective-permute-start.8
  322.4 2.0 fusion.15
  324.4 2.0 fusion.16
  326.4 3.5 fusion.44
  329.9 5.9 %collective-permute-start.2 = (bf16[1,256,768]{2,1,0:T(8,128)(2,1)}, bf16[1,256,768]{2,1,0:T(8,128)(2,1)S(1)}, u32[]{:S(2)}, u32[]{:S(2)}) collective-permute-start(bf16[1,256,768]{2,1,0:T(8,128)(2,1)} %get-tuple-element.16), channel_id=1, source_target_pairs={{0,16},{8,24},{16,32},{24,40},{32,48},{40,56},{48,64},{56,72},{64,... | collective-permute-start | bytes 1179656 | tf_op jit(solution)/shard_map/ppermute | solution.py:26
  340.0 6.2 %collective-permute-done.8 = bf16[1,256,768]{2,1,0:T(8,128)(2,1)} collective-permute-done((bf16[1,256,768]{2,1,0:T(8,128)(2,1)}, bf16[1,256,768]{2,1,0:T(8,128)(2,1)}, u32[]{:S(2)}, u32[]{:S(2)}) %collective-permute-start.8) | collective-permute-done | bytes 393248 | tf_op jit(solution)/shard_map/ppermute | solution.py:26
  350.1 6.9 %collective-permute-start.10 = (bf16[1,256,384]{2,1,0:T(8,128)(2,1)}, bf16[1,256,384]{2,1,0:T(8,128)(2,1)}, u32[]{:S(2)}, u32[]{:S(2)}) collective-permute-start(bf16[1,256,384]{2,1,0:T(8,128)(2,1)} %fusion.70), channel_id=1, source_target_pairs={{0,16},{8,24},{16,32},{24,40},{32,48},{40,56},{48,64},{56,72},{64,... | collective-permute-start | bytes 589832 | tf_op jit(solution)/shard_map/ppermute | solution.py:26
  357.0 2.1 collective-permute-start.9
  361.3 3.5 fusion.5
  364.8 3.4 collective-permute-start.4
  374.0 8.8 %collective-permute-start.12 = (bf16[1,128,384]{2,1,0:T(8,128)(2,1)S(1)}, bf16[1,128,384]{2,1,0:T(8,128)(2,1)S(1)}, u32[]{:S(2)}, u32[]{:S(2)}) collective-permute-start(bf16[1,128,384]{2,1,0:T(8,128)(2,1)S(1)} %get-tuple-element.15), channel_id=1, source_target_pairs={{0,8},{8,16},{16,24},{24,32},{32,40},{40,48},{48,56},{56,64},{64,7... | collective-permute-start | bytes 294920 | tf_op jit(solution)/shard_map/ppermute | solution.py:17
  383.3 2.1 collective-permute-start.11
  385.7 7.3 %collective-permute-done.11 = bf16[1,128,384]{2,1,0:T(8,128)(2,1)S(1)} collective-permute-done((bf16[1,128,384]{2,1,0:T(8,128)(2,1)S(1)}, bf16[1,128,384]{2,1,0:T(8,128)(2,1)S(1)}, u32[]{:S(2)}, u32[]{:S(2)}) %collective-permute-start.11) | collective-permute-done | bytes 98336 | tf_op jit(solution)/shard_map/ppermute | solution.py:18
  393.9 1.9 collective-permute-start.13
  395.8 7.5 %collective-permute-done.13 = bf16[1,256,768]{2,1,0:T(8,128)(2,1)S(1)} collective-permute-done((bf16[1,256,768]{2,1,0:T(8,128)(2,1)S(1)}, bf16[1,256,768]{2,1,0:T(8,128)(2,1)S(1)}, u32[]{:S(2)}, u32[]{:S(2)}) %collective-permute-start.13) | collective-permute-done | bytes 393248 | tf_op jit(solution)/shard_map/ppermute | solution.py:32
  (83 shorter events, 30.7 us)
Async XLA Ops:
  7.2 12.5 %copy-start.12 = (bf16[1,256,768]{2,1,0:T(8,128)(2,1)S(1)}, bf16[1,256,768]{2,1,0:T(8,128)(2,1)}, u32[]{:S(2)}) copy-start(bf16[1,256,768]{2,1,0:T(8,128)(2,1)} %param.5) | copy-start | bytes 1179652
  7.2 147.3 %all-gather.5.cloned.1.call-start = ((), (), s32[]{:S(2)}) async-start(), calls=%async_computation.1 | async-start | bytes 1198080 | tf_op jit(solution)/shard_map/all_gather | solution.py:85
  7.9 293.0 %all-gather.3.cloned.1.call-start = ((), (), s32[]{:S(2)}) async-start(), calls=%async_computation | async-start | bytes 3594240 | tf_op jit(solution)/shard_map/all_gather | solution.py:84
  11.6 298.4 %collective-permute-start.5 = (bf16[1,128,768]{2,1,0:T(8,128)(2,1)}, bf16[1,128,768]{2,1,0:T(8,128)(2,1)}, u32[]{:S(2)}, u32[]{:S(2)}) collective-permute-start(bf16[1,128,768]{2,1,0:T(8,128)(2,1)} %get-tuple-element.10), channel_id=1, source_target_pairs={{0,8},{8,16},{16,24},{24,32},{32,40},{40,48},{48,56},{56,64},{64,7... | collective-permute-start | bytes 589832 | tf_op jit(solution)/shard_map/ppermute | solution.py:17
  17.7 293.8 %collective-permute-start.6 = (bf16[1,128,768]{2,1,0:T(8,128)(2,1)}, bf16[1,128,768]{2,1,0:T(8,128)(2,1)}, u32[]{:S(2)}, u32[]{:S(2)}) collective-permute-start(bf16[1,128,768]{2,1,0:T(8,128)(2,1)} %get-tuple-element.11), channel_id=1, source_target_pairs={{8,0},{16,8},{24,16},{32,24},{40,32},{48,40},{56,48},{64,56},{72,6... | collective-permute-start | bytes 589832 | tf_op jit(solution)/shard_map/ppermute | solution.py:18
  21.5 300.9 %collective-permute-start = (bf16[1,128,768]{2,1,0:T(8,128)(2,1)}, bf16[1,128,768]{2,1,0:T(8,128)(2,1)}, u32[]{:S(2)}, u32[]{:S(2)}) collective-permute-start(bf16[1,128,768]{2,1,0:T(8,128)(2,1)} %get-tuple-element.12), channel_id=1, source_target_pairs={{0,8},{8,16},{16,24},{24,32},{32,40},{40,48},{48,56},{56,64},{64,7... | collective-permute-start | bytes 589832 | tf_op jit(solution)/shard_map/ppermute | solution.py:17
  28.8 295.7 %collective-permute-start.1 = (bf16[1,128,768]{2,1,0:T(8,128)(2,1)}, bf16[1,128,768]{2,1,0:T(8,128)(2,1)}, u32[]{:S(2)}, u32[]{:S(2)}) collective-permute-start(bf16[1,128,768]{2,1,0:T(8,128)(2,1)} %get-tuple-element.13), channel_id=1, source_target_pairs={{8,0},{16,8},{24,16},{32,24},{40,32},{48,40},{56,48},{64,56},{72,6... | collective-permute-start | bytes 589832 | tf_op jit(solution)/shard_map/ppermute | solution.py:18
  300.9 9.0 %copy-start.4 = (bf16[1,256,768]{2,1,0:T(8,128)(2,1)S(1)}, bf16[1,256,768]{2,1,0:T(8,128)(2,1)}, u32[]{:S(2)}) copy-start(bf16[1,256,768]{2,1,0:T(8,128)(2,1)} %copy-done.3) | copy-start | bytes 1179652
  310.0 12.5 %copy-start.5 = (bf16[1,1,1,768,384]{4,1,2,0,3:T(2,128)(2,1)}, bf16[1,1,1,768,384]{4,1,2,0,3:T(2,128)(2,1)S(1)}, u32[]{:S(2)}) copy-start(bf16[1,1,1,768,384]{4,1,2,0,3:T(2,128)(2,1)S(1)} %get-tuple-element.6) | copy-start | bytes 1769476
  315.6 22.5 %collective-permute-start.7 = (bf16[1,256,768]{2,1,0:T(8,128)(2,1)}, bf16[1,256,768]{2,1,0:T(8,128)(2,1)}, u32[]{:S(2)}, u32[]{:S(2)}) collective-permute-start(bf16[1,256,768]{2,1,0:T(8,128)(2,1)} %get-tuple-element.18), channel_id=1, source_target_pairs={{0,16},{8,24},{16,32},{24,40},{32,48},{40,56},{48,64},{56,72},{64,... | collective-permute-start | bytes 1179656 | tf_op jit(solution)/shard_map/ppermute | solution.py:26
  319.4 26.8 %collective-permute-start.8 = (bf16[1,256,768]{2,1,0:T(8,128)(2,1)}, bf16[1,256,768]{2,1,0:T(8,128)(2,1)}, u32[]{:S(2)}, u32[]{:S(2)}) collective-permute-start(bf16[1,256,768]{2,1,0:T(8,128)(2,1)} %get-tuple-element.18), channel_id=1, source_target_pairs={{16,0},{24,8},{32,16},{40,24},{48,32},{56,40},{64,48},{72,56},{80,... | collective-permute-start | bytes 1179656 | tf_op jit(solution)/shard_map/ppermute | solution.py:26
  329.9 29.2 %collective-permute-start.2 = (bf16[1,256,768]{2,1,0:T(8,128)(2,1)}, bf16[1,256,768]{2,1,0:T(8,128)(2,1)S(1)}, u32[]{:S(2)}, u32[]{:S(2)}) collective-permute-start(bf16[1,256,768]{2,1,0:T(8,128)(2,1)} %get-tuple-element.16), channel_id=1, source_target_pairs={{0,16},{8,24},{16,32},{24,40},{32,48},{40,56},{48,64},{56,72},{64,... | collective-permute-start | bytes 1179656 | tf_op jit(solution)/shard_map/ppermute | solution.py:26
  335.8 24.4 %collective-permute-start.3 = (bf16[1,256,768]{2,1,0:T(8,128)(2,1)}, bf16[1,256,768]{2,1,0:T(8,128)(2,1)S(1)}, u32[]{:S(2)}, u32[]{:S(2)}) collective-permute-start(bf16[1,256,768]{2,1,0:T(8,128)(2,1)} %get-tuple-element.16), channel_id=1, source_target_pairs={{16,0},{24,8},{32,16},{40,24},{48,32},{56,40},{64,48},{72,56},{80,... | collective-permute-start | bytes 1179656 | tf_op jit(solution)/shard_map/ppermute | solution.py:26
  338.1 9.4 %copy-start = (bf16[1,1,1,768,384]{4,1,2,0,3:T(2,128)(2,1)S(1)}, bf16[1,1,1,768,384]{4,1,2,0,3:T(2,128)(2,1)}, u32[]{:S(2)}) copy-start(bf16[1,1,1,768,384]{4,1,2,0,3:T(2,128)(2,1)} %get-tuple-element.2) | copy-start | bytes 1769476
  338.1 9.4 %copy-start.19 = (bf16[1,256,768]{2,1,0:T(8,128)(2,1)S(1)}, bf16[1,256,768]{2,1,0:T(8,128)(2,1)}, u32[]{:S(2)}) copy-start(bf16[1,256,768]{2,1,0:T(8,128)(2,1)} %get-tuple-element.19) | copy-start | bytes 1179652
  348.9 10.2 %copy-start.7 = (bf16[1,1,1,768,384]{4,1,2,0,3:T(2,128)(2,1)S(1)}, bf16[1,1,1,768,384]{4,1,2,0,3:T(2,128)(2,1)}, u32[]{:S(2)}) copy-start(bf16[1,1,1,768,384]{4,1,2,0,3:T(2,128)(2,1)} %get-tuple-element.3) | copy-start | bytes 1769476
  350.1 19.9 %collective-permute-start.10 = (bf16[1,256,384]{2,1,0:T(8,128)(2,1)}, bf16[1,256,384]{2,1,0:T(8,128)(2,1)}, u32[]{:S(2)}, u32[]{:S(2)}) collective-permute-start(bf16[1,256,384]{2,1,0:T(8,128)(2,1)} %fusion.70), channel_id=1, source_target_pairs={{0,16},{8,24},{16,32},{24,40},{32,48},{40,56},{48,64},{56,72},{64,... | collective-permute-start | bytes 589832 | tf_op jit(solution)/shard_map/ppermute | solution.py:26
  357.0 14.5 %collective-permute-start.9 = (bf16[1,256,384]{2,1,0:T(8,128)(2,1)}, bf16[1,256,384]{2,1,0:T(8,128)(2,1)}, u32[]{:S(2)}, u32[]{:S(2)}) collective-permute-start(bf16[1,256,384]{2,1,0:T(8,128)(2,1)} %fusion.70), channel_id=1, source_target_pairs={{16,0},{24,8},{32,16},{40,24},{48,32},{56,40},{64,48},{72,56},{80,... | collective-permute-start | bytes 589832 | tf_op jit(solution)/shard_map/ppermute | solution.py:26
  364.8 31.0 %collective-permute-start.4 = (bf16[1,256,768]{2,1,0:T(8,128)(2,1)}, bf16[1,256,768]{2,1,0:T(8,128)(2,1)S(1)}, u32[]{:S(2)}, u32[]{:S(2)}) collective-permute-start(bf16[1,256,768]{2,1,0:T(8,128)(2,1)} %fusion.5), channel_id=1, source_target_pairs={{7,0},{0,1},{1,2},{2,3},{3,4},{4,5},{5,6},{6,7},{15,8},{8,9},{9,10... | collective-permute-start | bytes 1179656 | tf_op jit(solution)/shard_map/ppermute | solution.py:32
  374.0 11.3 %collective-permute-start.12 = (bf16[1,128,384]{2,1,0:T(8,128)(2,1)S(1)}, bf16[1,128,384]{2,1,0:T(8,128)(2,1)S(1)}, u32[]{:S(2)}, u32[]{:S(2)}) collective-permute-start(bf16[1,128,384]{2,1,0:T(8,128)(2,1)S(1)} %get-tuple-element.15), channel_id=1, source_target_pairs={{0,8},{8,16},{16,24},{24,32},{32,40},{40,48},{48,56},{56,64},{64,7... | collective-permute-start | bytes 294920 | tf_op jit(solution)/shard_map/ppermute | solution.py:17
  383.3 9.8 %copy-start.6 = (bf16[1,1,1,768,384]{4,1,2,0,3:T(2,128)(2,1)S(1)}, bf16[1,1,1,768,384]{4,1,2,0,3:T(2,128)(2,1)}, u32[]{:S(2)}) copy-start(bf16[1,1,1,768,384]{4,1,2,0,3:T(2,128)(2,1)} %copy-done.5) | copy-start | bytes 1769476
  383.3 9.8 %copy-start.14 = (bf16[1,256,768]{2,1,0:T(8,128)(2,1)S(1)}, bf16[1,256,768]{2,1,0:T(8,128)(2,1)}, u32[]{:S(2)}) copy-start(bf16[1,256,768]{2,1,0:T(8,128)(2,1)} %param.6) | copy-start | bytes 1179652
  383.3 9.8 %collective-permute-start.11 = (bf16[1,128,384]{2,1,0:T(8,128)(2,1)S(1)}, bf16[1,128,384]{2,1,0:T(8,128)(2,1)S(1)}, u32[]{:S(2)}, u32[]{:S(2)}) collective-permute-start(bf16[1,128,384]{2,1,0:T(8,128)(2,1)S(1)} %get-tuple-element.14), channel_id=1, source_target_pairs={{8,0},{16,8},{24,16},{32,24},{40,32},{48,40},{56,48},{64,56},{72,6... | collective-permute-start | bytes 294920 | tf_op jit(solution)/shard_map/ppermute | solution.py:18
  393.9 9.4 %collective-permute-start.13 = (bf16[1,256,768]{2,1,0:T(8,128)(2,1)S(1)}, bf16[1,256,768]{2,1,0:T(8,128)(2,1)S(1)}, u32[]{:S(2)}, u32[]{:S(2)}) collective-permute-start(bf16[1,256,768]{2,1,0:T(8,128)(2,1)S(1)} %fusion.28), channel_id=1, source_target_pairs={{1,0},{2,1},{3,2},{4,3},{5,4},{6,5},{7,6},{0,7},{9,8},{10,9},{11,1... | collective-permute-start | bytes 1179656 | tf_op jit(solution)/shard_map/ppermute | solution.py:32
  (13 other events, 33.7 us)
Sparse Core Ops, SparseCore 0:
  11.2 143.1 all-gather.4
  157.7 143.1 all-gather.2
where the time goes:
time: 413 us; the launch traced here: 412 us
  waiting for transfers between devices  287 us (69%)
  starting transfers between devices  57.1 us (14%)
  matrix products  30 us (7%)
  local copies, waits for them, and re-layouts  21.2 us (5%)
  between operations  14.5 us (4%)
    all_gather x1, waiting for transfers between devices, local(): lax.all_gather(conv_weight, 'seq', axis=3, tiled=True)  141 us
    all_gather x1, waiting for transfers between devices, local(): lax.all_gather(proj_weight, 'seq', axis=2, tiled=True)  124 us
    ppermute x6, starting transfers between devices, from_behind(): return lax.ppermute(block, axis, route)  23.6 us
    ppermute x3, starting transfers between devices, padded(): before = lax.ppermute(last, axis, up)  22.2 us
    dot_general x10, matrix products, conv_apply(): jnp.einsum('krc,ch->krh', values, weight, preferred_element_type=jnp.floa...  13.1 us
    slice x1, local copies, waits for them, and re-layouts, run_forward(): middle = conv_apply(activated, conv_part[1])  9.01 us
    dot_general x3, matrix products, run_forward(): jnp.einsum('krh,hc->krc', hidden, proj_part, preferred_element_type=jnp.f...  8.49 us
  transfers between devices with their start and end apart: 16, of which 6 were waited for; matrix products, arithmetic and copies ran while one was open for 12% of the time, Pallas kernels for 0%

commit v1 on v0

--- a/solution.py
+++ b/solution.py
@@ -1,15 +1,25 @@
 import jax
 import jax.numpy as jnp
 from jax import lax
-from jax.sharding import PartitionSpec as P
+from jax.sharding import Mesh, PartitionSpec as P
 
 BLOCKS = 2
 FIRST_DILATION = 128
+SEQ = ("z", "xh", "core")
+
+
+def seq_size(axis):
+    if isinstance(axis, tuple):
+        size = 1
+        for name in axis:
+            size *= lax.axis_size(name)
+        return size
+    return lax.axis_size(axis)
 
 
 def padded(x, sides, width):
     for axis, dim in sides:
-        size, length = (lax.axis_size(axis), x.shape[dim])
+        size, length = (seq_size(axis), x.shape[dim])
         up = [(i, (i + 1) % size) for i in range(size - 1)]
         down = [(j, i) for i, j in up]
         last = lax.slice_in_dim(x, length - width, length, axis=dim)
@@ -21,13 +31,13 @@
 
 
 def from_behind(block, axis, distance):
-    devices = range(lax.axis_size(axis))
+    devices = range(seq_size(axis))
     route = [(i - distance, i) for i in devices if i - distance in devices]
     return lax.ppermute(block, axis, route)
 
 
 def from_behind_2(block, axis, distance):
-    devices = range(lax.axis_size(axis))
+    devices = range(seq_size(axis))
     route = [((i - distance) % len(devices), i) for i in devices]
     return lax.ppermute(block, axis, route)
 
@@ -43,11 +53,11 @@
 def reach(values, spacing_gap):
     length = values.shape[1]
     if spacing_gap < length:
-        padded_input = padded(values, (("seq", 1),), spacing_gap)
+        padded_input = padded(values, ((SEQ, 1),), spacing_gap)
         return (padded_input[:, :length], padded_input[:, 2 * spacing_gap :])
     shard_hops = spacing_gap // length
-    earlier = from_behind(values, "seq", shard_hops)
-    later = from_behind(values, "seq", -shard_hops)
+    earlier = from_behind(values, SEQ, shard_hops)
+    later = from_behind(values, SEQ, -shard_hops)
     return (earlier, later)
 
 
@@ -79,11 +89,20 @@
     return (present_state, stored)
 
 
+def gather_weights(conv_weight, proj_weight):
+    flat = jnp.concatenate([conv_weight.reshape(1, -1), proj_weight.reshape(1, -1)], axis=1)
+    for axis in reversed(SEQ):
+        flat = lax.all_gather(flat, axis, axis=0, tiled=True)
+    shards, split = flat.shape[0], conv_weight.size
+    conv = flat[:, :split].reshape((shards,) + conv_weight.shape[1:])
+    proj = flat[:, split:].reshape((shards,) + proj_weight.shape[1:])
+    conv = jnp.moveaxis(conv, 0, 2).reshape(conv_weight.shape[:3] + (-1, conv_weight.shape[4]))
+    proj = jnp.moveaxis(proj, 0, 1).reshape(proj_weight.shape[:2] + (-1, proj_weight.shape[3]))
+    return conv, proj
+
+
 def local(fwd_input, bwd_input, bwd_cotangent, conv_weight, proj_weight):
-    convolution_complete, proj_full = (
-        lax.all_gather(conv_weight, "seq", axis=3, tiled=True),
-        lax.all_gather(proj_weight, "seq", axis=2, tiled=True),
-    )
+    convolution_complete, proj_full = gather_weights(conv_weight, proj_weight)
     pieces = [
         (convolution_complete[0, depth_level], proj_full[0, depth_level])
         for depth_level in range(BLOCKS)
@@ -113,12 +132,14 @@
 
 
 def solution(mesh):
+    seq, section = mesh.shape["seq"], mesh.shape["section"]
+    split = Mesh(mesh.devices.reshape(seq // 4, 2, 2, section), SEQ + ("section",))
     in_specs = (
-        P("section", "seq", None),
-        P("section", "seq", None),
-        P("section", "seq", None),
-        P("section", None, None, "seq", None),
-        P("section", None, "seq", None),
+        P("section", SEQ, None),
+        P("section", SEQ, None),
+        P("section", SEQ, None),
+        P("section", None, None, SEQ, None),
+        P("section", None, SEQ, None),
     )
-    out_specs = (P("section", "seq", None), P("section", "seq", None))
-    return jax.shard_map(local, mesh=mesh, in_specs=in_specs, out_specs=out_specs, check_vma=False)
+    out_specs = (P("section", SEQ, None), P("section", SEQ, None))
+    return jax.shard_map(local, mesh=split, in_specs=in_specs, out_specs=out_specs, check_vma=False)

time: 413 us -> 234 us (0.57)
  the two profiles are of different devices: /device:TPU:103 before, /device:TPU:123 now
where the time goes in v1:
time: 234 us; the launch traced here: 233 us
  waiting for transfers between devices  73.5 us (31%)
  starting transfers between devices  62.8 us (27%)
  local copies, waits for them, and re-layouts  41 us (18%)
  matrix products  30.8 us (13%)
  between operations  14.6 us (6%)
  blocking collectives  9.66 us (4%)
    all_gather x1, waiting for transfers between devices, gather_weights(): flat = lax.all_gather(flat, axis, axis=0, tiled=True)  56.9 us
    ppermute x6, starting transfers between devices, from_behind(): return lax.ppermute(block, axis, route)  24.9 us
    ppermute x3, starting transfers between devices, padded(): before = lax.ppermute(last, axis, up)  23.5 us
    dot_general x10, matrix products, conv_apply(): jnp.einsum('krc,ch->krh', values, weight, preferred_element_type=jnp.floa...  13.8 us
    unnamed x51, local copies, waits for them, and re-layouts  11.5 us
    ppermute x2, waiting for transfers between devices, from_behind_2(): return lax.ppermute(block, axis, route)  11.5 us
    all_gather x2, blocking collectives, gather_weights(): flat = lax.all_gather(flat, axis, axis=0, tiled=True)  9.66 us
    dot_general x3, matrix products, run_forward(): jnp.einsum('krh,hc->krc', hidden, proj_part, preferred_element_type=jnp.f...  8.59 us
  transfers between devices with their start and end apart: 15, of which 3 were waited for; matrix products, arithmetic and copies ran while one was open for 29% of the time, Pallas kernels for 0%

profile of v1, /device:TPU:123, one launch (start us, length us, event | category | flops | bytes accessed | tf_op | source)
XLA Modules:
  0.0 233.1 jit_solution(14517356376269916342)
XLA Ops:
  9.0 2.5 %all-gather = bf16[2,1,36864]{2,1,0:T(2,128)(2,1)S(1)} all-gather(bf16[1,1,36864]{2,1,0:T(2,128)(2,1)S(1)} %maximum_bitcast_fusion), channel_id=1, replica_groups=mesh['z'=16,'xh'=2,'core'=2,'section'=8] {'core'}, dimensions={0}, use_global_device_ids=true | all-gather | bytes 221184 | tf_op jit(solution)/shard_map/all_gather | solution.py:95
  11.7 7.2 %all-gather.1 = bf16[2,2,36864]{2,1,0:T(2,128)(2,1)S(1)} all-gather(bf16[1,2,36864]{2,1,0:T(2,128)(2,1)S(1)} %bitcast.270), channel_id=1, replica_groups=mesh['z'=16,'xh'=2,'core'=2,'section'=8] {'xh'}, dimensions={0}, use_global_device_ids=true | all-gather | bytes 442368 | tf_op jit(solution)/shard_map/all_gather | solution.py:95
  20.9 3.1 %collective-permute-start.1 = (bf16[1,128,768]{2,1,0:T(8,128)(2,1)}, bf16[1,128,768]{2,1,0:T(8,128)(2,1)}, u32[]{:S(2)}, u32[]{:S(2)}) collective-permute-start(bf16[1,128,768]{2,1,0:T(8,128)(2,1)} %get-tuple-element.13), channel_id=1, source_target_pairs={{8,0},{16,8},{24,16},{32,24},{40,32},{48,40},{56,48},{64,56},{72,6... | collective-permute-start | bytes 589832 | tf_op jit(solution)/shard_map/ppermute | solution.py:28
  24.0 3.9 %collective-permute-start = (bf16[1,128,768]{2,1,0:T(8,128)(2,1)}, bf16[1,128,768]{2,1,0:T(8,128)(2,1)}, u32[]{:S(2)}, u32[]{:S(2)}) collective-permute-start(bf16[1,128,768]{2,1,0:T(8,128)(2,1)} %get-tuple-element.12), channel_id=1, source_target_pairs={{0,8},{8,16},{16,24},{24,32},{32,40},{40,48},{48,56},{56,64},{64,7... | collective-permute-start | bytes 589832 | tf_op jit(solution)/shard_map/ppermute | solution.py:27
  31.1 5.1 %collective-permute-start.5 = (bf16[1,128,768]{2,1,0:T(8,128)(2,1)}, bf16[1,128,768]{2,1,0:T(8,128)(2,1)}, u32[]{:S(2)}, u32[]{:S(2)}) collective-permute-start(bf16[1,128,768]{2,1,0:T(8,128)(2,1)} %get-tuple-element.10), channel_id=1, source_target_pairs={{0,8},{8,16},{16,24},{24,32},{32,40},{40,48},{48,56},{56,64},{64,7... | collective-permute-start | bytes 589832 | tf_op jit(solution)/shard_map/ppermute | solution.py:27
  36.2 56.9 %all-gather.5.cloned.1.call-done = bf16[16,4,36864]{2,1,0:T(4,128)(2,1)} async-done(((bf16[1,4,36864]{2,1,0:T(4,128)(2,1)}), bf16[16,4,36864]{2,1,0:T(4,128)(2,1)}) %all-gather.5.cloned.1.call-update) | async-done | bytes 4718608 | tf_op jit(solution)/shard_map/all_gather | solution.py:95
  93.1 7.3 %reshape.172 = bf16[64,36864]{1,0:T(8,128)(2,1)} reshape(bf16[16,4,36864]{2,1,0:T(4,128)(2,1)} %all-gather.5.cloned.1.call-done) | data formatting | bytes 9437184
  100.4 4.1 %slice.121 = bf16[64,27648]{1,0:T(8,128)(2,1)} slice(bf16[64,36864]{1,0:T(8,128)(2,1)} %reshape.172), slice={[0:64], [0:27648]} | slice | bytes 7077888 | tf_op jit(solution)/shard_map/slice | solution.py:97
  107.3 6.0 %reshape.141 = bf16[64,2,3,12,384]{4,3,2,1,0:T(8,128)(2,1)} reshape(bf16[64,27648]{1,0:T(8,128)(2,1)} %slice.121) | data formatting | bytes 7077888 | tf_op jit(solution)/shard_map/reshape | solution.py:97
  113.4 6.0 %copy.20 = bf16[2,3,64,12,384]{4,0,3,2,1:T(2,128)(2,1)S(1)} copy(bf16[2,3,64,12,384]{4,3,1,0,2:T(8,128)(2,1)} %bitcast.267) | data formatting | bytes 7077888 | tf_op jit(solution)/shard_map/transpose | solution.py:99
  119.3 6.2 %fusion.239 = (bf16[1,1,1,768,384]{4,1,3,2,0:T(2,128)(2,1)}, bf16[1,1,1,768,384]{4,1,3,2,0:T(2,128)(2,1)}, bf16[1,1,1,768,384]{4,1,3,2,0:T(2,128)(2,1)}, bf16[1,...) fusion(bf16[1,2,3,768,384]{4,1,3,2,0:T(2,128)(2,1)S(1)} %bitcas, ...), kind=kLoop, calls=%fused_computation.254 | loop fusion | bytes 7077888 | tf_op jit(solution)/shard_map/slice | solution.py:78
  125.6 2.6 %fusion.240 = (bf16[1,1,384,768]{3,1,2,0:T(2,128)(2,1)}, bf16[1,1,384,768]{3,1,2,0:T(2,128)(2,1)S(1)}) fusion(bf16[1,2,384,768]{3,1,2,0:T(2,128)(2,1)S(1)} %bitcast.268), kind=kLoop, calls=%fused_computation.255 | loop fusion | bytes 2359296 | tf_op jit(solution)/shard_map/slice | solution.py:107
  133.1 5.8 %collective-permute-start.8 = (bf16[1,256,768]{2,1,0:T(8,128)(2,1)}, bf16[1,256,768]{2,1,0:T(8,128)(2,1)}, u32[]{:S(2)}, u32[]{:S(2)}) collective-permute-start(bf16[1,256,768]{2,1,0:T(8,128)(2,1)} %get-tuple-element.18), channel_id=1, source_target_pairs={{16,0},{24,8},{32,16},{40,24},{48,32},{56,40},{64,48},{72,56},{80,... | collective-permute-start | bytes 1179656 | tf_op jit(solution)/shard_map/ppermute | solution.py:36
  144.8 3.6 %fusion.44 = (bf16[1,256,768]{2,1,0:T(8,128)(2,1)}, bf16[1,256,768]{2,1,0:T(8,128)(2,1)}) fusion(bf16[1,1,384,768]{3,1,2,0:T(2,128)(2,1)} %copy-done.10, bf16[1,256,384]{2,1,0:T(8,128)(2,1)} %fusion.16, bf16[1,256,384]{2,1,0:T(8,128)(2,1)} %fusion.15, bf16[1,1,1,768,384]{4,1,3,2,0:T(2,128)(2,1)S(1)} %get-tuple-element.6, bf16[1,256,768]{2,1,0:T(8,128)(2,1)} %param.5), kind=kOutput, calls=%fused_computation.84 | convolution fusion | flops 307789824 | bytes 2752512 | tf_op jit(solution)/shard_map/krh,hc->krc/dot_general | solution.py:87
  148.4 5.9 %collective-permute-start.3 = (bf16[1,256,768]{2,1,0:T(8,128)(2,1)}, bf16[1,256,768]{2,1,0:T(8,128)(2,1)S(1)}, u32[]{:S(2)}, u32[]{:S(2)}) collective-permute-start(bf16[1,256,768]{2,1,0:T(8,128)(2,1)} %get-tuple-element.16), channel_id=1, source_target_pairs={{16,0},{24,8},{32,16},{40,24},{48,32},{56,40},{64,48},{72,56},{80,... | collective-permute-start | bytes 1179656 | tf_op jit(solution)/shard_map/ppermute | solution.py:36
  154.3 2.4 %collective-permute-start.2 = (bf16[1,256,768]{2,1,0:T(8,128)(2,1)}, bf16[1,256,768]{2,1,0:T(8,128)(2,1)S(1)}, u32[]{:S(2)}, u32[]{:S(2)}) collective-permute-start(bf16[1,256,768]{2,1,0:T(8,128)(2,1)} %get-tuple-element.16), channel_id=1, source_target_pairs={{0,16},{8,24},{16,32},{24,40},{32,48},{40,56},{48,64},{56,72},{64,... | collective-permute-start | bytes 1179656 | tf_op jit(solution)/shard_map/ppermute | solution.py:36
  162.5 7.0 %collective-permute-start.10 = (bf16[1,256,384]{2,1,0:T(8,128)(2,1)}, bf16[1,256,384]{2,1,0:T(8,128)(2,1)}, u32[]{:S(2)}, u32[]{:S(2)}) collective-permute-start(bf16[1,256,384]{2,1,0:T(8,128)(2,1)} %fusion.97), channel_id=1, source_target_pairs={{0,16},{8,24},{16,32},{24,40},{32,48},{40,56},{48,64},{56,72},{64,... | collective-permute-start | bytes 589832 | tf_op jit(solution)/shard_map/ppermute | solution.py:36
  173.5 3.5 %fusion.5 = bf16[1,256,768]{2,1,0:T(8,128)(2,1)} fusion(bf16[1,256,768]{2,1,0:T(8,128)(2,1)} %get-tuple-element.17, bf16[1,256,384]{2,1,0:T(8,128)(2,1)} %fusion.18, bf16[1,256,384]{2,1,0:T(8,128)(2,1)} %fusion.17, bf16[1,1,384,768]{3,1,2,0:T(2,128)(2,1)} %get-tuple-element.8, bf16[1,1,1,768,384]{4,1,3,2,0:T(2,128)(2,1)} %get-tuple-element.2), kind=kOutput, calls=%fused_computation.31 | convolution fusion | flops 305823744 | bytes 2359296 | tf_op jit(solution)/shard_map/krh,hc->krc/dot_general | solution.py:87
  177.0 3.6 %collective-permute-start.4 = (bf16[1,256,768]{2,1,0:T(8,128)(2,1)}, bf16[1,256,768]{2,1,0:T(8,128)(2,1)S(1)}, u32[]{:S(2)}, u32[]{:S(2)}) collective-permute-start(bf16[1,256,768]{2,1,0:T(8,128)(2,1)} %fusion.5), channel_id=1, source_target_pairs={{7,0},{0,1},{1,2},{2,3},{3,4},{4,5},{5,6},{6,7},{15,8},{8,9},{9,10... | collective-permute-start | bytes 1179656 | tf_op jit(solution)/shard_map/ppermute | solution.py:42
  186.4 14.4 %collective-permute-start.12 = (bf16[1,128,384]{2,1,0:T(8,128)(2,1)S(1)}, bf16[1,128,384]{2,1,0:T(8,128)(2,1)S(1)}, u32[]{:S(2)}, u32[]{:S(2)}) collective-permute-start(bf16[1,128,384]{2,1,0:T(8,128)(2,1)S(1)} %get-tuple-element.15), channel_id=1, source_target_pairs={{0,8},{8,16},{16,24},{24,32},{32,40},{40,48},{48,56},{56,64},{64,7... | collective-permute-start | bytes 294920 | tf_op jit(solution)/shard_map/ppermute | solution.py:27
  201.3 2.1 collective-permute-start.11
  203.7 5.1 %collective-permute-done.11 = bf16[1,128,384]{2,1,0:T(8,128)(2,1)S(1)} collective-permute-done((bf16[1,128,384]{2,1,0:T(8,128)(2,1)S(1)}, bf16[1,128,384]{2,1,0:T(8,128)(2,1)S(1)}, u32[]{:S(2)}, u32[]{:S(2)}) %collective-permute-start.11) | collective-permute-done | bytes 98336 | tf_op jit(solution)/shard_map/ppermute | solution.py:28
  209.7 3.6 %collective-permute-start.13 = (bf16[1,256,768]{2,1,0:T(8,128)(2,1)S(1)}, bf16[1,256,768]{2,1,0:T(8,128)(2,1)S(1)}, u32[]{:S(2)}, u32[]{:S(2)}) collective-permute-start(bf16[1,256,768]{2,1,0:T(8,128)(2,1)S(1)} %fusion.28), channel_id=1, source_target_pairs={{1,0},{2,1},{3,2},{4,3},{5,4},{6,5},{7,6},{0,7},{9,8},{10,9},{11,1... | collective-permute-start | bytes 1179656 | tf_op jit(solution)/shard_map/ppermute | solution.py:42
  213.3 11.5 %collective-permute-done.13 = bf16[1,256,768]{2,1,0:T(8,128)(2,1)S(1)} collective-permute-done((bf16[1,256,768]{2,1,0:T(8,128)(2,1)S(1)}, bf16[1,256,768]{2,1,0:T(8,128)(2,1)S(1)}, u32[]{:S(2)}, u32[]{:S(2)}) %collective-permute-start.13) | collective-permute-done | bytes 393248 | tf_op jit(solution)/shard_map/ppermute | solution.py:42
  (98 shorter events, 39.1 us)
Async XLA Ops:
  7.2 86.0 %all-gather.5.cloned.1.call-start = ((), (), s32[]{:S(2)}) async-start(), calls=%async_computation | async-start | bytes 5013504 | tf_op jit(solution)/shard_map/all_gather | solution.py:95
  9.0 10.8 %copy-start.13 = (bf16[1,256,768]{2,1,0:T(8,128)(2,1)S(1)}, bf16[1,256,768]{2,1,0:T(8,128)(2,1)}, u32[]{:S(2)}) copy-start(bf16[1,256,768]{2,1,0:T(8,128)(2,1)} %param.5) | copy-start | bytes 1179652
  18.9 9.1 %copy-start.14 = (bf16[1,256,768]{2,1,0:T(8,128)(2,1)S(1)}, bf16[1,256,768]{2,1,0:T(8,128)(2,1)}, u32[]{:S(2)}) copy-start(bf16[1,256,768]{2,1,0:T(8,128)(2,1)} %param.6) | copy-start | bytes 1179652
  20.1 9.1 %copy-start.2 = (bf16[1,256,768]{2,1,0:T(8,128)(2,1)}, bf16[1,256,768]{2,1,0:T(8,128)(2,1)S(1)}, u32[]{:S(2)}) copy-start(bf16[1,256,768]{2,1,0:T(8,128)(2,1)S(1)} %fusion.38) | copy-start | bytes 1179652
  20.9 119.9 %collective-permute-start.1 = (bf16[1,128,768]{2,1,0:T(8,128)(2,1)}, bf16[1,128,768]{2,1,0:T(8,128)(2,1)}, u32[]{:S(2)}, u32[]{:S(2)}) collective-permute-start(bf16[1,128,768]{2,1,0:T(8,128)(2,1)} %get-tuple-element.13), channel_id=1, source_target_pairs={{8,0},{16,8},{24,16},{32,24},{40,32},{48,40},{56,48},{64,56},{72,6... | collective-permute-start | bytes 589832 | tf_op jit(solution)/shard_map/ppermute | solution.py:28
  24.0 118.8 %collective-permute-start = (bf16[1,128,768]{2,1,0:T(8,128)(2,1)}, bf16[1,128,768]{2,1,0:T(8,128)(2,1)}, u32[]{:S(2)}, u32[]{:S(2)}) collective-permute-start(bf16[1,128,768]{2,1,0:T(8,128)(2,1)} %get-tuple-element.12), channel_id=1, source_target_pairs={{0,8},{8,16},{16,24},{24,32},{32,40},{40,48},{48,56},{56,64},{64,7... | collective-permute-start | bytes 589832 | tf_op jit(solution)/shard_map/ppermute | solution.py:27
  29.2 99.0 %collective-permute-start.6 = (bf16[1,128,768]{2,1,0:T(8,128)(2,1)}, bf16[1,128,768]{2,1,0:T(8,128)(2,1)}, u32[]{:S(2)}, u32[]{:S(2)}) collective-permute-start(bf16[1,128,768]{2,1,0:T(8,128)(2,1)} %get-tuple-element.11), channel_id=1, source_target_pairs={{8,0},{16,8},{24,16},{32,24},{40,32},{48,40},{56,48},{64,56},{72,6... | collective-permute-start | bytes 589832 | tf_op jit(solution)/shard_map/ppermute | solution.py:28
  31.1 98.7 %collective-permute-start.5 = (bf16[1,128,768]{2,1,0:T(8,128)(2,1)}, bf16[1,128,768]{2,1,0:T(8,128)(2,1)}, u32[]{:S(2)}, u32[]{:S(2)}) collective-permute-start(bf16[1,128,768]{2,1,0:T(8,128)(2,1)} %get-tuple-element.10), channel_id=1, source_target_pairs={{0,8},{8,16},{16,24},{24,32},{32,40},{40,48},{48,56},{56,64},{64,7... | collective-permute-start | bytes 589832 | tf_op jit(solution)/shard_map/ppermute | solution.py:27
  125.6 17.3 %copy-start.6 = (bf16[1,1,1,768,384]{4,1,3,2,0:T(2,128)(2,1)}, bf16[1,1,1,768,384]{4,1,3,2,0:T(2,128)(2,1)S(1)}, u32[]{:S(2)}) copy-start(bf16[1,1,1,768,384]{4,1,3,2,0:T(2,128)(2,1)S(1)} %get-tuple-element.7) | copy-start | bytes 1769476
  131.6 9.2 %copy-start.3 = (bf16[1,256,768]{2,1,0:T(8,128)(2,1)S(1)}, bf16[1,256,768]{2,1,0:T(8,128)(2,1)}, u32[]{:S(2)}) copy-start(bf16[1,256,768]{2,1,0:T(8,128)(2,1)} %copy-done.2) | copy-start | bytes 1179652
  133.1 23.7 %collective-permute-start.8 = (bf16[1,256,768]{2,1,0:T(8,128)(2,1)}, bf16[1,256,768]{2,1,0:T(8,128)(2,1)}, u32[]{:S(2)}, u32[]{:S(2)}) collective-permute-start(bf16[1,256,768]{2,1,0:T(8,128)(2,1)} %get-tuple-element.18), channel_id=1, source_target_pairs={{16,0},{24,8},{32,16},{40,24},{48,32},{56,40},{64,48},{72,56},{80,... | collective-permute-start | bytes 1179656 | tf_op jit(solution)/shard_map/ppermute | solution.py:36
  138.9 19.4 %collective-permute-start.7 = (bf16[1,256,768]{2,1,0:T(8,128)(2,1)}, bf16[1,256,768]{2,1,0:T(8,128)(2,1)}, u32[]{:S(2)}, u32[]{:S(2)}) collective-permute-start(bf16[1,256,768]{2,1,0:T(8,128)(2,1)} %get-tuple-element.18), channel_id=1, source_target_pairs={{0,16},{8,24},{16,32},{24,40},{32,48},{40,56},{48,64},{56,72},{64,... | collective-permute-start | bytes 1179656 | tf_op jit(solution)/shard_map/ppermute | solution.py:36
  144.8 12.0 %copy-start = (bf16[1,1,1,768,384]{4,1,3,2,0:T(2,128)(2,1)S(1)}, bf16[1,1,1,768,384]{4,1,3,2,0:T(2,128)(2,1)}, u32[]{:S(2)}) copy-start(bf16[1,1,1,768,384]{4,1,3,2,0:T(2,128)(2,1)} %get-tuple-element.3) | copy-start | bytes 1769476
  148.4 9.9 %copy-start.8 = (bf16[1,1,1,768,384]{4,1,3,2,0:T(2,128)(2,1)S(1)}, bf16[1,1,1,768,384]{4,1,3,2,0:T(2,128)(2,1)}, u32[]{:S(2)}) copy-start(bf16[1,1,1,768,384]{4,1,3,2,0:T(2,128)(2,1)} %get-tuple-element.4) | copy-start | bytes 1769476
  148.4 23.0 %collective-permute-start.3 = (bf16[1,256,768]{2,1,0:T(8,128)(2,1)}, bf16[1,256,768]{2,1,0:T(8,128)(2,1)S(1)}, u32[]{:S(2)}, u32[]{:S(2)}) collective-permute-start(bf16[1,256,768]{2,1,0:T(8,128)(2,1)} %get-tuple-element.16), channel_id=1, source_target_pairs={{16,0},{24,8},{32,16},{40,24},{48,32},{56,40},{64,48},{72,56},{80,... | collective-permute-start | bytes 1179656 | tf_op jit(solution)/shard_map/ppermute | solution.py:36
  154.3 18.1 %collective-permute-start.2 = (bf16[1,256,768]{2,1,0:T(8,128)(2,1)}, bf16[1,256,768]{2,1,0:T(8,128)(2,1)S(1)}, u32[]{:S(2)}, u32[]{:S(2)}) collective-permute-start(bf16[1,256,768]{2,1,0:T(8,128)(2,1)} %get-tuple-element.16), channel_id=1, source_target_pairs={{0,16},{8,24},{16,32},{24,40},{32,48},{40,56},{48,64},{56,72},{64,... | collective-permute-start | bytes 1179656 | tf_op jit(solution)/shard_map/ppermute | solution.py:36
  162.5 20.0 %collective-permute-start.10 = (bf16[1,256,384]{2,1,0:T(8,128)(2,1)}, bf16[1,256,384]{2,1,0:T(8,128)(2,1)}, u32[]{:S(2)}, u32[]{:S(2)}) collective-permute-start(bf16[1,256,384]{2,1,0:T(8,128)(2,1)} %fusion.97), channel_id=1, source_target_pairs={{0,16},{8,24},{16,32},{24,40},{32,48},{40,56},{48,64},{56,72},{64,... | collective-permute-start | bytes 589832 | tf_op jit(solution)/shard_map/ppermute | solution.py:36
  169.4 14.5 %collective-permute-start.9 = (bf16[1,256,384]{2,1,0:T(8,128)(2,1)}, bf16[1,256,384]{2,1,0:T(8,128)(2,1)}, u32[]{:S(2)}, u32[]{:S(2)}) collective-permute-start(bf16[1,256,384]{2,1,0:T(8,128)(2,1)} %fusion.97), channel_id=1, source_target_pairs={{16,0},{24,8},{32,16},{40,24},{48,32},{56,40},{64,48},{72,56},{80,... | collective-permute-start | bytes 589832 | tf_op jit(solution)/shard_map/ppermute | solution.py:36
  177.0 36.3 %collective-permute-start.4 = (bf16[1,256,768]{2,1,0:T(8,128)(2,1)}, bf16[1,256,768]{2,1,0:T(8,128)(2,1)S(1)}, u32[]{:S(2)}, u32[]{:S(2)}) collective-permute-start(bf16[1,256,768]{2,1,0:T(8,128)(2,1)} %fusion.5), channel_id=1, source_target_pairs={{7,0},{0,1},{1,2},{2,3},{3,4},{4,5},{5,6},{6,7},{15,8},{8,9},{9,10... | collective-permute-start | bytes 1179656 | tf_op jit(solution)/shard_map/ppermute | solution.py:42
  186.4 16.9 %collective-permute-start.12 = (bf16[1,128,384]{2,1,0:T(8,128)(2,1)S(1)}, bf16[1,128,384]{2,1,0:T(8,128)(2,1)S(1)}, u32[]{:S(2)}, u32[]{:S(2)}) collective-permute-start(bf16[1,128,384]{2,1,0:T(8,128)(2,1)S(1)} %get-tuple-element.15), channel_id=1, source_target_pairs={{0,8},{8,16},{16,24},{24,32},{32,40},{40,48},{48,56},{56,64},{64,7... | collective-permute-start | bytes 294920 | tf_op jit(solution)/shard_map/ppermute | solution.py:27
  201.2 7.6 %copy-start.7 = (bf16[1,1,1,768,384]{4,1,3,2,0:T(2,128)(2,1)S(1)}, bf16[1,1,1,768,384]{4,1,3,2,0:T(2,128)(2,1)}, u32[]{:S(2)}) copy-start(bf16[1,1,1,768,384]{4,1,3,2,0:T(2,128)(2,1)} %copy-done.6) | copy-start | bytes 1769476
  201.3 7.6 %copy-start.16 = (bf16[1,256,768]{2,1,0:T(8,128)(2,1)S(1)}, bf16[1,256,768]{2,1,0:T(8,128)(2,1)}, u32[]{:S(2)}) copy-start(bf16[1,256,768]{2,1,0:T(8,128)(2,1)} %param.6) | copy-start | bytes 1179652
  201.3 7.6 %collective-permute-start.11 = (bf16[1,128,384]{2,1,0:T(8,128)(2,1)S(1)}, bf16[1,128,384]{2,1,0:T(8,128)(2,1)S(1)}, u32[]{:S(2)}, u32[]{:S(2)}) collective-permute-start(bf16[1,128,384]{2,1,0:T(8,128)(2,1)S(1)} %get-tuple-element.14), channel_id=1, source_target_pairs={{8,0},{16,8},{24,16},{32,24},{40,32},{48,40},{56,48},{64,56},{72,6... | collective-permute-start | bytes 294920 | tf_op jit(solution)/shard_map/ppermute | solution.py:28
  209.7 15.1 %collective-permute-start.13 = (bf16[1,256,768]{2,1,0:T(8,128)(2,1)S(1)}, bf16[1,256,768]{2,1,0:T(8,128)(2,1)S(1)}, u32[]{:S(2)}, u32[]{:S(2)}) collective-permute-start(bf16[1,256,768]{2,1,0:T(8,128)(2,1)S(1)} %fusion.28), channel_id=1, source_target_pairs={{1,0},{2,1},{3,2},{4,3},{5,4},{6,5},{7,6},{0,7},{9,8},{10,9},{11,1... | collective-permute-start | bytes 1179656 | tf_op jit(solution)/shard_map/ppermute | solution.py:42
  (14 other events, 30.2 us)
Sparse Core Ops, SparseCore 0:
  19.9 73.2 all-gather.4

commit v2 on v1

--- a/solution.py
+++ b/solution.py
@@ -107,8 +107,9 @@
         (convolution_complete[0, depth_level], proj_full[0, depth_level])
         for depth_level in range(BLOCKS)
     ]
-    forward_out, unused = run_forward(fwd_input, pieces)
-    unused_out, stored = run_forward(bwd_input, pieces)
+    both_out, both_stored = run_forward(jnp.concatenate([fwd_input, bwd_input], axis=0), pieces)
+    forward_out = both_out[:1]
+    stored = [(block_in[1:], preact[1:]) for block_in, preact in both_stored]
     cotangent = bwd_cotangent
     for depth_level in reversed(range(BLOCKS)):
         conv_part, proj_part = pieces[depth_level]

time: 234 us -> 228 us (0.974)
  the two profiles are of different devices: /device:TPU:123 before, /device:TPU:31 now
where the time goes in v2:
time: 228 us; the launch traced here: 227 us
  waiting for transfers between devices  114 us (50%)
  local copies, waits for them, and re-layouts  38.9 us (17%)
  starting transfers between devices  37.5 us (16%)
  between operations  14.5 us (6%)
  matrix products  12.2 us (5%)
  blocking collectives  9.53 us (4%)
    all_gather x1, waiting for transfers between devices, gather_weights(): flat = lax.all_gather(flat, axis, axis=0, tiled=True)  65.8 us
    ppermute x4, waiting for transfers between devices, from_behind(): return lax.ppermute(block, axis, route)  31.1 us
    ppermute x2, starting transfers between devices, padded(): before = lax.ppermute(last, axis, up)  14.6 us
    ppermute x4, starting transfers between devices, from_behind(): return lax.ppermute(block, axis, route)  14.6 us
    unnamed x33, local copies, waits for them, and re-layouts  13.2 us
    ppermute x2, waiting for transfers between devices, from_behind_2(): return lax.ppermute(block, axis, route)  10.9 us
    all_gather x2, blocking collectives, gather_weights(): flat = lax.all_gather(flat, axis, axis=0, tiled=True)  9.53 us
    slice x1, local copies, waits for them, and re-layouts, run_forward(): conv_part[0]  6.42 us
  transfers between devices with their start and end apart: 11, of which 6 were waited for; matrix products, arithmetic and copies ran while one was open for 16% of the time, Pallas kernels for 0%

profile of v2, /device:TPU:31, one launch (start us, length us, event | category | flops | bytes accessed | tf_op | source)
XLA Modules:
  0.0 227.4 jit_solution(8790683109421019405)
XLA Ops:
  9.1 2.3 %all-gather = bf16[2,1,36864]{2,1,0:T(2,128)(2,1)S(1)} all-gather(bf16[1,1,36864]{2,1,0:T(2,128)(2,1)S(1)} %maximum_bitcast_fusion), channel_id=1, replica_groups=mesh['z'=16,'xh'=2,'core'=2,'section'=8] {'core'}, dimensions={0}, use_global_device_ids=true | all-gather | bytes 221184 | tf_op jit(solution)/shard_map/all_gather | solution.py:95
  11.6 7.2 %all-gather.1 = bf16[2,2,36864]{2,1,0:T(2,128)(2,1)S(1)} all-gather(bf16[1,2,36864]{2,1,0:T(2,128)(2,1)S(1)} %bitcast.123), channel_id=1, replica_groups=mesh['z'=16,'xh'=2,'core'=2,'section'=8] {'xh'}, dimensions={0}, use_global_device_ids=true | all-gather | bytes 442368 | tf_op jit(solution)/shard_map/all_gather | solution.py:95
  22.1 5.5 %collective-permute-start = (bf16[2,128,768]{2,1,0:T(8,128)(2,1)}, bf16[2,128,768]{2,1,0:T(8,128)(2,1)}, u32[]{:S(2)}, u32[]{:S(2)}) collective-permute-start(bf16[2,128,768]{2,1,0:T(8,128)(2,1)} %get-tuple-element.10), channel_id=1, source_target_pairs={{0,8},{8,16},{16,24},{24,32},{32,40},{40,48},{48,56},{56,64},{64,7... | collective-permute-start | bytes 1179656 | tf_op jit(solution)/shard_map/ppermute | solution.py:27
  27.6 1.9 collective-permute-start.1
  29.5 65.8 %all-gather.5.cloned.1.call-done = bf16[16,4,36864]{2,1,0:T(4,128)(2,1)} async-done(((bf16[1,4,36864]{2,1,0:T(4,128)(2,1)}), bf16[16,4,36864]{2,1,0:T(4,128)(2,1)}) %all-gather.5.cloned.1.call-update) | async-done | bytes 4718608 | tf_op jit(solution)/shard_map/all_gather | solution.py:95
  95.3 7.3 %reshape.89 = bf16[64,36864]{1,0:T(8,128)(2,1)} reshape(bf16[16,4,36864]{2,1,0:T(4,128)(2,1)} %all-gather.5.cloned.1.call-done) | data formatting | bytes 9437184
  102.6 2.0 slice-done
  104.6 4.3 %reshape.72 = bf16[64,2,3,12,384]{4,3,2,1,0:T(8,128)(2,1)} reshape(bf16[64,27648]{1,0:T(8,128)(2,1)S(1)} %slice-done) | data formatting | bytes 7077888 | tf_op jit(solution)/shard_map/reshape | solution.py:97
  108.9 6.0 %copy.23 = bf16[2,3,64,12,384]{4,0,3,2,1:T(2,128)(2,1)S(1)} copy(bf16[2,3,64,12,384]{4,3,1,0,2:T(8,128)(2,1)} %bitcast.120) | data formatting | bytes 7077888 | tf_op jit(solution)/shard_map/transpose | solution.py:99
  114.9 6.4 %fusion.155 = (bf16[1,1,1,768,384]{4,1,3,2,0:T(2,128)(2,1)}, bf16[1,1,1,768,384]{4,1,3,2,0:T(2,128)(2,1)}, bf16[1,1,1,768,384]{4,1,3,2,0:T(2,128)(2,1)}, bf16[1,...) fusion(bf16[1,2,3,768,384]{4,1,3,2,0:T(2,128)(2,1)S(1)} %bitcast.119), kind=kLoop, calls=%fused_computation.179 | loop fusion | bytes 7077888 | tf_op jit(solution)/shard_map/slice | solution.py:81
  122.6 2.1 reshape.74
  129.4 1.7 convolution_convert_fusion.2
  133.2 3.2 %collective-permute-start.3 = (bf16[2,256,768]{2,1,0:T(8,128)(2,1)S(1)}, bf16[2,256,768]{2,1,0:T(8,128)(2,1)S(1)}, u32[]{:S(2)}, u32[]{:S(2)}) collective-permute-start(bf16[2,256,768]{2,1,0:T(8,128)(2,1)S(1)} %get-tuple-element.14), channel_id=1, source_target_pairs={{16,0},{24,8},{32,16},{40,24},{48,32},{56,40},{64,48},{72,56},{80,... | collective-permute-start | bytes 2359304 | tf_op jit(solution)/shard_map/ppermute | solution.py:36
  136.4 4.6 %collective-permute-start.2 = (bf16[2,256,768]{2,1,0:T(8,128)(2,1)S(1)}, bf16[2,256,768]{2,1,0:T(8,128)(2,1)S(1)}, u32[]{:S(2)}, u32[]{:S(2)}) collective-permute-start(bf16[2,256,768]{2,1,0:T(8,128)(2,1)S(1)} %get-tuple-element.14), channel_id=1, source_target_pairs={{0,16},{8,24},{16,32},{24,40},{32,48},{40,56},{48,64},{56,72},{64,... | collective-permute-start | bytes 2359304 | tf_op jit(solution)/shard_map/ppermute | solution.py:36
  142.0 6.5 %collective-permute-done.3 = bf16[2,256,768]{2,1,0:T(8,128)(2,1)S(1)} collective-permute-done((bf16[2,256,768]{2,1,0:T(8,128)(2,1)S(1)}, bf16[2,256,768]{2,1,0:T(8,128)(2,1)S(1)}, u32[]{:S(2)}, u32[]{:S(2)}) %collective-permute-start.3) | collective-permute-done | bytes 786464 | tf_op jit(solution)/shard_map/ppermute | solution.py:36
  149.1 23.9 %collective-permute-done.2 = bf16[2,256,768]{2,1,0:T(8,128)(2,1)S(1)} collective-permute-done((bf16[2,256,768]{2,1,0:T(8,128)(2,1)S(1)}, bf16[2,256,768]{2,1,0:T(8,128)(2,1)S(1)}, u32[]{:S(2)}, u32[]{:S(2)}) %collective-permute-start.2) | collective-permute-done | bytes 786464 | tf_op jit(solution)/shard_map/ppermute | solution.py:36
  175.2 1.9 collective-permute-start.6
  177.2 4.9 %collective-permute-start.5 = (bf16[1,256,384]{2,1,0:T(8,128)(2,1)S(1)}, bf16[1,256,384]{2,1,0:T(8,128)(2,1)S(1)}, u32[]{:S(2)}, u32[]{:S(2)}) collective-permute-start(bf16[1,256,384]{2,1,0:T(8,128)(2,1)S(1)} %fusion.87), channel_id=1, source_target_pairs={{16,0},{24,8},{32,16},{40,24},{48,32},{56,40},{64,48},{72,56},{80,... | collective-permute-start | bytes 589832 | tf_op jit(solution)/shard_map/ppermute | solution.py:36
  182.2 2.5 %collective-permute-start.4 = (bf16[1,256,768]{2,1,0:T(8,128)(2,1)S(1)}, bf16[1,256,768]{2,1,0:T(8,128)(2,1)S(1)}, u32[]{:S(2)}, u32[]{:S(2)}) collective-permute-start(bf16[1,256,768]{2,1,0:T(8,128)(2,1)S(1)} %fusion.56), channel_id=1, source_target_pairs={{7,0},{0,1},{1,2},{2,3},{3,4},{4,5},{5,6},{6,7},{15,8},{8,9},{9,10... | collective-permute-start | bytes 1179656 | tf_op jit(solution)/shard_map/ppermute | solution.py:42
  187.5 9.1 %collective-permute-start.8 = (bf16[1,128,384]{2,1,0:T(8,128)(2,1)S(1)}, bf16[1,128,384]{2,1,0:T(8,128)(2,1)S(1)}, u32[]{:S(2)}, u32[]{:S(2)}) collective-permute-start(bf16[1,128,384]{2,1,0:T(8,128)(2,1)S(1)} %get-tuple-element.13), channel_id=1, source_target_pairs={{0,8},{8,16},{16,24},{24,32},{32,40},{40,48},{48,56},{56,64},{64,7... | collective-permute-start | bytes 294920 | tf_op jit(solution)/shard_map/ppermute | solution.py:27
  197.0 1.9 collective-permute-start.7
  199.3 6.0 %collective-permute-done.7 = bf16[1,128,384]{2,1,0:T(8,128)(2,1)S(1)} collective-permute-done((bf16[1,128,384]{2,1,0:T(8,128)(2,1)S(1)}, bf16[1,128,384]{2,1,0:T(8,128)(2,1)S(1)}, u32[]{:S(2)}, u32[]{:S(2)}) %collective-permute-start.7) | collective-permute-done | bytes 98336 | tf_op jit(solution)/shard_map/ppermute | solution.py:28
  206.2 1.9 collective-permute-start.9
  208.1 10.9 %collective-permute-done.9 = bf16[1,256,768]{2,1,0:T(8,128)(2,1)S(1)} collective-permute-done((bf16[1,256,768]{2,1,0:T(8,128)(2,1)S(1)}, bf16[1,256,768]{2,1,0:T(8,128)(2,1)S(1)}, u32[]{:S(2)}, u32[]{:S(2)}) %collective-permute-start.9) | collective-permute-done | bytes 393248 | tf_op jit(solution)/shard_map/ppermute | solution.py:42
  (69 shorter events, 23.0 us)
Async XLA Ops:
  7.2 12.5 %copy-start.10 = (bf16[1,256,768]{2,1,0:T(8,128)(2,1)S(1)}, bf16[1,256,768]{2,1,0:T(8,128)(2,1)}, u32[]{:S(2)}) copy-start(bf16[1,256,768]{2,1,0:T(8,128)(2,1)} %param.6) | copy-start | bytes 1179652
  7.2 12.5 %copy-start.8 = (bf16[1,256,768]{2,1,0:T(8,128)(2,1)S(1)}, bf16[1,256,768]{2,1,0:T(8,128)(2,1)}, u32[]{:S(2)}) copy-start(bf16[1,256,768]{2,1,0:T(8,128)(2,1)} %param.5) | copy-start | bytes 1179652
  7.2 88.1 %all-gather.5.cloned.1.call-start = ((), (), s32[]{:S(2)}) async-start(), calls=%async_computation | async-start | bytes 5013504 | tf_op jit(solution)/shard_map/all_gather | solution.py:95
  22.1 103.5 %collective-permute-start = (bf16[2,128,768]{2,1,0:T(8,128)(2,1)}, bf16[2,128,768]{2,1,0:T(8,128)(2,1)}, u32[]{:S(2)}, u32[]{:S(2)}) collective-permute-start(bf16[2,128,768]{2,1,0:T(8,128)(2,1)} %get-tuple-element.10), channel_id=1, source_target_pairs={{0,8},{8,16},{16,24},{24,32},{32,40},{40,48},{48,56},{56,64},{64,7... | collective-permute-start | bytes 1179656 | tf_op jit(solution)/shard_map/ppermute | solution.py:27
  27.6 101.8 %collective-permute-start.1 = (bf16[2,128,768]{2,1,0:T(8,128)(2,1)}, bf16[2,128,768]{2,1,0:T(8,128)(2,1)}, u32[]{:S(2)}, u32[]{:S(2)}) collective-permute-start(bf16[2,128,768]{2,1,0:T(8,128)(2,1)} %get-tuple-element.11), channel_id=1, source_target_pairs={{8,0},{16,8},{24,16},{32,24},{40,32},{48,40},{56,48},{64,56},{72,6... | collective-permute-start | bytes 1179656 | tf_op jit(solution)/shard_map/ppermute | solution.py:28
  102.6 2.0 slice-start
  121.3 1.3 slice-start.1
  124.6 1.1 copy-start.1
  124.7 1.5 copy-start.6
  127.7 1.7 copy-start.2
  129.4 1.8 copy-start.3
  129.4 1.8 copy-start.9
  129.4 1.8 copy-start.11
  133.2 8.0 %copy-start.5 = (bf16[1,1,1,768,384]{4,1,3,2,0:T(2,128)(2,1)S(1)}, bf16[1,1,1,768,384]{4,1,3,2,0:T(2,128)(2,1)}, u32[]{:S(2)}) copy-start(bf16[1,1,1,768,384]{4,1,3,2,0:T(2,128)(2,1)} %get-tuple-element.3) | copy-start | bytes 1769476
  133.2 15.4 %collective-permute-start.3 = (bf16[2,256,768]{2,1,0:T(8,128)(2,1)S(1)}, bf16[2,256,768]{2,1,0:T(8,128)(2,1)S(1)}, u32[]{:S(2)}, u32[]{:S(2)}) collective-permute-start(bf16[2,256,768]{2,1,0:T(8,128)(2,1)S(1)} %get-tuple-element.14), channel_id=1, source_target_pairs={{16,0},{24,8},{32,16},{40,24},{48,32},{56,40},{64,48},{72,56},{80,... | collective-permute-start | bytes 2359304 | tf_op jit(solution)/shard_map/ppermute | solution.py:36
  136.4 36.6 %collective-permute-start.2 = (bf16[2,256,768]{2,1,0:T(8,128)(2,1)S(1)}, bf16[2,256,768]{2,1,0:T(8,128)(2,1)S(1)}, u32[]{:S(2)}, u32[]{:S(2)}) collective-permute-start(bf16[2,256,768]{2,1,0:T(8,128)(2,1)S(1)} %get-tuple-element.14), channel_id=1, source_target_pairs={{0,16},{8,24},{16,32},{24,40},{32,48},{40,56},{48,64},{56,72},{64,... | collective-permute-start | bytes 2359304 | tf_op jit(solution)/shard_map/ppermute | solution.py:36
  141.1 7.4 %copy-start.4 = (bf16[1,1,1,768,384]{4,1,3,2,0:T(2,128)(2,1)S(1)}, bf16[1,1,1,768,384]{4,1,3,2,0:T(2,128)(2,1)}, u32[]{:S(2)}) copy-start(bf16[1,1,1,768,384]{4,1,3,2,0:T(2,128)(2,1)} %get-tuple-element.7) | copy-start | bytes 1769476
  142.0 31.0 %copy-start.7 = (bf16[1,1,1,768,384]{4,1,3,2,0:T(2,128)(2,1)S(1)}, bf16[1,1,1,768,384]{4,1,3,2,0:T(2,128)(2,1)}, u32[]{:S(2)}) copy-start(bf16[1,1,1,768,384]{4,1,3,2,0:T(2,128)(2,1)} %get-tuple-element.2) | copy-start | bytes 1769476
  175.2 9.8 %collective-permute-start.6 = (bf16[1,256,384]{2,1,0:T(8,128)(2,1)S(1)}, bf16[1,256,384]{2,1,0:T(8,128)(2,1)S(1)}, u32[]{:S(2)}, u32[]{:S(2)}) collective-permute-start(bf16[1,256,384]{2,1,0:T(8,128)(2,1)S(1)} %fusion.87), channel_id=1, source_target_pairs={{0,16},{8,24},{16,32},{24,40},{32,48},{40,56},{48,64},{56,72},{64,... | collective-permute-start | bytes 589832 | tf_op jit(solution)/shard_map/ppermute | solution.py:36
  177.2 8.9 %collective-permute-start.5 = (bf16[1,256,384]{2,1,0:T(8,128)(2,1)S(1)}, bf16[1,256,384]{2,1,0:T(8,128)(2,1)S(1)}, u32[]{:S(2)}, u32[]{:S(2)}) collective-permute-start(bf16[1,256,384]{2,1,0:T(8,128)(2,1)S(1)} %fusion.87), channel_id=1, source_target_pairs={{16,0},{24,8},{32,16},{40,24},{48,32},{56,40},{64,48},{72,56},{80,... | collective-permute-start | bytes 589832 | tf_op jit(solution)/shard_map/ppermute | solution.py:36
  182.2 25.9 %collective-permute-start.4 = (bf16[1,256,768]{2,1,0:T(8,128)(2,1)S(1)}, bf16[1,256,768]{2,1,0:T(8,128)(2,1)S(1)}, u32[]{:S(2)}, u32[]{:S(2)}) collective-permute-start(bf16[1,256,768]{2,1,0:T(8,128)(2,1)S(1)} %fusion.56), channel_id=1, source_target_pairs={{7,0},{0,1},{1,2},{2,3},{3,4},{4,5},{5,6},{6,7},{15,8},{8,9},{9,10... | collective-permute-start | bytes 1179656 | tf_op jit(solution)/shard_map/ppermute | solution.py:42
  187.5 11.5 %collective-permute-start.8 = (bf16[1,128,384]{2,1,0:T(8,128)(2,1)S(1)}, bf16[1,128,384]{2,1,0:T(8,128)(2,1)S(1)}, u32[]{:S(2)}, u32[]{:S(2)}) collective-permute-start(bf16[1,128,384]{2,1,0:T(8,128)(2,1)S(1)} %get-tuple-element.13), channel_id=1, source_target_pairs={{0,8},{8,16},{16,24},{24,32},{32,40},{40,48},{48,56},{56,64},{64,7... | collective-permute-start | bytes 294920 | tf_op jit(solution)/shard_map/ppermute | solution.py:27
  197.0 8.3 %collective-permute-start.7 = (bf16[1,128,384]{2,1,0:T(8,128)(2,1)S(1)}, bf16[1,128,384]{2,1,0:T(8,128)(2,1)S(1)}, u32[]{:S(2)}, u32[]{:S(2)}) collective-permute-start(bf16[1,128,384]{2,1,0:T(8,128)(2,1)S(1)} %get-tuple-element.12), channel_id=1, source_target_pairs={{8,0},{16,8},{24,16},{32,24},{40,32},{48,40},{56,48},{64,56},{72,6... | collective-permute-start | bytes 294920 | tf_op jit(solution)/shard_map/ppermute | solution.py:28
  206.2 12.9 %collective-permute-start.9 = (bf16[1,256,768]{2,1,0:T(8,128)(2,1)S(1)}, bf16[1,256,768]{2,1,0:T(8,128)(2,1)S(1)}, u32[]{:S(2)}, u32[]{:S(2)}) collective-permute-start(bf16[1,256,768]{2,1,0:T(8,128)(2,1)S(1)} %fusion.25), channel_id=1, source_target_pairs={{1,0},{2,1},{3,2},{4,3},{5,4},{6,5},{7,6},{0,7},{9,8},{10,9},{11,1... | collective-permute-start | bytes 1179656 | tf_op jit(solution)/shard_map/ppermute | solution.py:42
  (2 other events, 1.9 us)
Sparse Core Ops, SparseCore 0:
  19.8 75.4 all-gather.4

commit v3 on v2

--- a/solution.py
+++ b/solution.py
@@ -76,11 +76,14 @@
         spacing_gap = FIRST_DILATION * 4**depth_level
         activated = jax.nn.gelu(present_state.astype(jnp.float32)).astype(jnp.bfloat16)
         middle = conv_apply(activated, conv_part[1])
-        earlier, later = reach(activated, spacing_gap)
+        first_tap = conv_apply(activated, conv_part[0]).astype(jnp.bfloat16)
+        last_tap = conv_apply(activated, conv_part[2]).astype(jnp.bfloat16)
+        earlier, unused_later = reach(first_tap, spacing_gap)
+        unused_earlier, later = reach(last_tap, spacing_gap)
         preact = (
-            rounded(conv_apply(earlier, conv_part[0]))
+            lax.optimization_barrier(earlier).astype(jnp.float32)
             + middle
-            + rounded(conv_apply(later, conv_part[2]))
+            + lax.optimization_barrier(later).astype(jnp.float32)
         )
         hidden = jax.nn.gelu(preact).astype(jnp.bfloat16)
         stored.append((present_state, preact))

time: 228 us -> 226 us (level)
  the two profiles are of different devices: /device:TPU:31 before, /device:TPU:59 now
where the time goes in v3:
time: 226 us
  waiting for transfers between devices  111 us (49%)
  starting transfers between devices  41.9 us (19%)
  local copies, waits for them, and re-layouts  37.3 us (17%)
  between operations  14.4 us (6%)
  matrix products  10.7 us (5%)
  blocking collectives  9.53 us (4%)
    all_gather x1, waiting for transfers between devices, gather_weights(): flat = lax.all_gather(flat, axis, axis=0, tiled=True)  74.5 us
    ppermute x4, waiting for transfers between devices, from_behind(): return lax.ppermute(block, axis, route)  18.1 us
    ppermute x4, starting transfers between devices, from_behind(): return lax.ppermute(block, axis, route)  15.4 us
    ppermute x2, starting transfers between devices, padded(): after = lax.ppermute(initial, axis, down)  12.8 us
    ppermute x2, waiting for transfers between devices, from_behind_2(): return lax.ppermute(block, axis, route)  11.7 us
    unnamed x13, local copies, waits for them, and re-layouts  11.7 us
    all_gather x2, blocking collectives, gather_weights(): flat = lax.all_gather(flat, axis, axis=0, tiled=True)  9.53 us
    ppermute x2, starting transfers between devices, padded(): before = lax.ppermute(last, axis, up)  7.71 us
  transfers between devices with their start and end apart: 11, of which 7 were waited for; matrix products, arithmetic and copies ran while one was open for 3% of the time, Pallas kernels for 0%

profile of v3, /device:TPU:59, one launch (start us, length us, event | category | flops | bytes accessed | tf_op | source)
XLA Modules:
  0.0 225.5 jit_solution(4950099758715491696)
XLA Ops:
  9.0 2.3 %all-gather = bf16[2,1,36864]{2,1,0:T(2,128)(2,1)S(1)} all-gather(bf16[1,1,36864]{2,1,0:T(2,128)(2,1)S(1)} %maximum_bitcast_fusion), channel_id=1, replica_groups=mesh['z'=16,'xh'=2,'core'=2,'section'=8] {'core'}, dimensions={0}, use_global_device_ids=true | all-gather | bytes 221184 | tf_op jit(solution)/shard_map/all_gather | solution.py:98
  11.6 7.2 %all-gather.1 = bf16[2,2,36864]{2,1,0:T(2,128)(2,1)S(1)} all-gather(bf16[1,2,36864]{2,1,0:T(2,128)(2,1)S(1)} %bitcast.121), channel_id=1, replica_groups=mesh['z'=16,'xh'=2,'core'=2,'section'=8] {'xh'}, dimensions={0}, use_global_device_ids=true | all-gather | bytes 442368 | tf_op jit(solution)/shard_map/all_gather | solution.py:98
  19.6 74.5 %all-gather.5.cloned.1.call-done = bf16[16,4,36864]{2,1,0:T(4,128)(2,1)} async-done(((bf16[1,4,36864]{2,1,0:T(4,128)(2,1)}), bf16[16,4,36864]{2,1,0:T(4,128)(2,1)}) %all-gather.5.cloned.1.call-update) | async-done | bytes 4718608 | tf_op jit(solution)/shard_map/all_gather | solution.py:98
  94.1 7.3 %reshape.89 = bf16[64,36864]{1,0:T(8,128)(2,1)} reshape(bf16[16,4,36864]{2,1,0:T(4,128)(2,1)} %all-gather.5.cloned.1.call-done) | data formatting | bytes 9437184
  101.4 4.1 %slice.112 = bf16[64,27648]{1,0:T(8,128)(2,1)} slice(bf16[64,36864]{1,0:T(8,128)(2,1)} %reshape.89), slice={[0:64], [0:27648]} | slice | bytes 7077888 | tf_op jit(solution)/shard_map/slice | solution.py:100
  105.5 1.9 reshape.74
  108.3 6.0 %reshape.72 = bf16[64,2,3,12,384]{4,3,2,1,0:T(8,128)(2,1)} reshape(bf16[64,27648]{1,0:T(8,128)(2,1)} %slice.112) | data formatting | bytes 7077888 | tf_op jit(solution)/shard_map/reshape | solution.py:100
  114.3 6.0 %copy.23 = bf16[2,3,64,12,384]{4,0,3,2,1:T(2,128)(2,1)S(1)} copy(bf16[2,3,64,12,384]{4,3,1,0,2:T(8,128)(2,1)} %bitcast.118) | data formatting | bytes 7077888 | tf_op jit(solution)/shard_map/transpose | solution.py:102
  122.0 5.0 %fusion.155 = (bf16[1,1,1,768,384]{4,1,3,2,0:T(2,128)(2,1)S(1)}, bf16[1,1,1,768,384]{4,1,3,2,0:T(2,128)(2,1)S(1)}, bf16[1,1,1,768,384]{4,1,3,2,0:T(2,128)(2,1)S(...) fusion(bf16[1,2,3,768,384]{4,1,3,2,0:T(2,128)(2,1)S(1)} %bitcas, ...), kind=kLoop, calls=%fused_computation.175 | loop fusion | bytes 7077888 | tf_op jit(solution)/shard_map/slice | solution.py:79
  127.8 10.9 %collective-permute-start.1 = (bf16[2,128,384]{2,1,0:T(8,128)(2,1)S(1)}, bf16[2,128,384]{2,1,0:T(8,128)(2,1)S(1)}, u32[]{:S(2)}, u32[]{:S(2)}) collective-permute-start(bf16[2,128,384]{2,1,0:T(8,128)(2,1)S(1)} %slice.117), channel_id=1, source_target_pairs={{8,0},{16,8},{24,16},{32,24},{40,32},{48,40},{56,48},{64,56},{72,6... | collective-permute-start | bytes 589832 | tf_op jit(solution)/shard_map/ppermute | solution.py:28
  139.6 3.8 %collective-permute-start = (bf16[2,128,384]{2,1,0:T(8,128)(2,1)S(1)}, bf16[2,128,384]{2,1,0:T(8,128)(2,1)S(1)}, u32[]{:S(2)}, u32[]{:S(2)}) collective-permute-start(bf16[2,128,384]{2,1,0:T(8,128)(2,1)S(1)} %slice.114), channel_id=1, source_target_pairs={{0,8},{8,16},{16,24},{24,32},{32,40},{40,48},{48,56},{56,64},{64,7... | collective-permute-start | bytes 589832 | tf_op jit(solution)/shard_map/ppermute | solution.py:27
  147.7 4.0 %collective-permute-start.2 = (bf16[2,256,384]{2,1,0:T(8,128)(2,1)S(1)}, bf16[2,256,384]{2,1,0:T(8,128)(2,1)S(1)}, u32[]{:S(2)}, u32[]{:S(2)}) collective-permute-start(bf16[2,256,384]{2,1,0:T(8,128)(2,1)S(1)} %convolution_convert_fusion.1), channel_id=1, source_target_pairs={{0,16},{8,24},{16,32},{24,40},{32,48},{40,56},{48,64},{56,72},{64,... | collective-permute-start | bytes 1179656 | tf_op jit(solution)/shard_map/ppermute | solution.py:36
  152.6 3.7 %collective-permute-start.3 = (bf16[2,256,384]{2,1,0:T(8,128)(2,1)S(1)}, bf16[2,256,384]{2,1,0:T(8,128)(2,1)S(1)}, u32[]{:S(2)}, u32[]{:S(2)}) collective-permute-start(bf16[2,256,384]{2,1,0:T(8,128)(2,1)S(1)} %convolution_convert_fusion), channel_id=1, source_target_pairs={{16,0},{24,8},{32,16},{40,24},{48,32},{56,40},{64,48},{72,56},{80,... | collective-permute-start | bytes 1179656 | tf_op jit(solution)/shard_map/ppermute | solution.py:36
  157.1 9.3 %collective-permute-done.2 = bf16[2,256,384]{2,1,0:T(8,128)(2,1)S(1)} collective-permute-done((bf16[2,256,384]{2,1,0:T(8,128)(2,1)S(1)}, bf16[2,256,384]{2,1,0:T(8,128)(2,1)S(1)}, u32[]{:S(2)}, u32[]{:S(2)}) %collective-permute-start.2) | collective-permute-done | bytes 393248 | tf_op jit(solution)/shard_map/ppermute | solution.py:36
  166.5 5.0 %collective-permute-done.3 = bf16[2,256,384]{2,1,0:T(8,128)(2,1)S(1)} collective-permute-done((bf16[2,256,384]{2,1,0:T(8,128)(2,1)S(1)}, bf16[2,256,384]{2,1,0:T(8,128)(2,1)S(1)}, u32[]{:S(2)}, u32[]{:S(2)}) %collective-permute-start.3) | collective-permute-done | bytes 393248 | tf_op jit(solution)/shard_map/ppermute | solution.py:36
  173.1 1.9 collective-permute-start.6
  175.0 5.8 %collective-permute-start.5 = (bf16[1,256,384]{2,1,0:T(8,128)(2,1)S(1)}, bf16[1,256,384]{2,1,0:T(8,128)(2,1)S(1)}, u32[]{:S(2)}, u32[]{:S(2)}) collective-permute-start(bf16[1,256,384]{2,1,0:T(8,128)(2,1)S(1)} %fusion.85), channel_id=1, source_target_pairs={{16,0},{24,8},{32,16},{40,24},{48,32},{56,40},{64,48},{72,56},{80,... | collective-permute-start | bytes 589832 | tf_op jit(solution)/shard_map/ppermute | solution.py:36
  180.9 3.0 %collective-permute-start.4 = (bf16[1,256,768]{2,1,0:T(8,128)(2,1)S(1)}, bf16[1,256,768]{2,1,0:T(8,128)(2,1)S(1)}, u32[]{:S(2)}, u32[]{:S(2)}) collective-permute-start(bf16[1,256,768]{2,1,0:T(8,128)(2,1)S(1)} %fusion.55), channel_id=1, source_target_pairs={{7,0},{0,1},{1,2},{2,3},{3,4},{4,5},{5,6},{6,7},{15,8},{8,9},{9,10... | collective-permute-start | bytes 1179656 | tf_op jit(solution)/shard_map/ppermute | solution.py:42
  184.6 3.8 %collective-permute-done.5 = bf16[1,256,384]{2,1,0:T(8,128)(2,1)S(1)} collective-permute-done((bf16[1,256,384]{2,1,0:T(8,128)(2,1)S(1)}, bf16[1,256,384]{2,1,0:T(8,128)(2,1)S(1)}, u32[]{:S(2)}, u32[]{:S(2)}) %collective-permute-start.5) | collective-permute-done | bytes 196640 | tf_op jit(solution)/shard_map/ppermute | solution.py:36
  189.8 3.9 %collective-permute-start.8 = (bf16[1,128,384]{2,1,0:T(8,128)(2,1)S(1)}, bf16[1,128,384]{2,1,0:T(8,128)(2,1)S(1)}, u32[]{:S(2)}, u32[]{:S(2)}) collective-permute-start(bf16[1,128,384]{2,1,0:T(8,128)(2,1)S(1)} %get-tuple-element.11), channel_id=1, source_target_pairs={{0,8},{8,16},{16,24},{24,32},{32,40},{40,48},{48,56},{56,64},{64,7... | collective-permute-start | bytes 294920 | tf_op jit(solution)/shard_map/ppermute | solution.py:27
  194.1 1.9 collective-permute-start.7
  196.4 5.1 %collective-permute-done.7 = bf16[1,128,384]{2,1,0:T(8,128)(2,1)S(1)} collective-permute-done((bf16[1,128,384]{2,1,0:T(8,128)(2,1)S(1)}, bf16[1,128,384]{2,1,0:T(8,128)(2,1)S(1)}, u32[]{:S(2)}, u32[]{:S(2)}) %collective-permute-start.7) | collective-permute-done | bytes 98336 | tf_op jit(solution)/shard_map/ppermute | solution.py:28
  202.4 3.1 %collective-permute-start.9 = (bf16[1,256,768]{2,1,0:T(8,128)(2,1)S(1)}, bf16[1,256,768]{2,1,0:T(8,128)(2,1)S(1)}, u32[]{:S(2)}, u32[]{:S(2)}) collective-permute-start(bf16[1,256,768]{2,1,0:T(8,128)(2,1)S(1)} %fusion.24), channel_id=1, source_target_pairs={{1,0},{2,1},{3,2},{4,3},{5,4},{6,5},{7,6},{0,7},{9,8},{10,9},{11,1... | collective-permute-start | bytes 1179656 | tf_op jit(solution)/shard_map/ppermute | solution.py:42
  205.5 11.7 %collective-permute-done.9 = bf16[1,256,768]{2,1,0:T(8,128)(2,1)S(1)} collective-permute-done((bf16[1,256,768]{2,1,0:T(8,128)(2,1)S(1)}, bf16[1,256,768]{2,1,0:T(8,128)(2,1)S(1)}, u32[]{:S(2)}, u32[]{:S(2)}) %collective-permute-start.9) | collective-permute-done | bytes 393248 | tf_op jit(solution)/shard_map/ppermute | solution.py:42
  (50 shorter events, 20.1 us)
Async XLA Ops:
  7.2 87.0 %all-gather.5.cloned.1.call-start = ((), (), s32[]{:S(2)}) async-start(), calls=%async_computation | async-start | bytes 5013504 | tf_op jit(solution)/shard_map/all_gather | solution.py:98
  101.4 4.1 %slice-start = ((bf16[64,36864]{1,0:T(8,128)(2,1)}), bf16[64,9216]{1,0:T(8,128)(2,1)S(1)}, s32[]{:S(2)}) async-start(bf16[64,36864]{1,0:T(8,128)(2,1)} %reshape.89), calls=%async_computation.1 | async-start | bytes 2359296 | tf_op jit(solution)/shard_map/slice | solution.py:101
  122.0 5.0 %copy-start = (bf16[1,256,768]{2,1,0:T(8,128)(2,1)S(1)}, bf16[1,256,768]{2,1,0:T(8,128)(2,1)}, u32[]{:S(2)}) copy-start(bf16[1,256,768]{2,1,0:T(8,128)(2,1)} %param.5) | copy-start | bytes 1179652
  122.0 5.0 %copy-start.2 = (bf16[1,256,768]{2,1,0:T(8,128)(2,1)S(1)}, bf16[1,256,768]{2,1,0:T(8,128)(2,1)}, u32[]{:S(2)}) copy-start(bf16[1,256,768]{2,1,0:T(8,128)(2,1)} %param.6) | copy-start | bytes 1179652
  127.8 16.3 %collective-permute-start.1 = (bf16[2,128,384]{2,1,0:T(8,128)(2,1)S(1)}, bf16[2,128,384]{2,1,0:T(8,128)(2,1)S(1)}, u32[]{:S(2)}, u32[]{:S(2)}) collective-permute-start(bf16[2,128,384]{2,1,0:T(8,128)(2,1)S(1)} %slice.117), channel_id=1, source_target_pairs={{8,0},{16,8},{24,16},{32,24},{40,32},{48,40},{56,48},{64,56},{72,6... | collective-permute-start | bytes 589832 | tf_op jit(solution)/shard_map/ppermute | solution.py:28
  139.6 6.4 %collective-permute-start = (bf16[2,128,384]{2,1,0:T(8,128)(2,1)S(1)}, bf16[2,128,384]{2,1,0:T(8,128)(2,1)S(1)}, u32[]{:S(2)}, u32[]{:S(2)}) collective-permute-start(bf16[2,128,384]{2,1,0:T(8,128)(2,1)S(1)} %slice.114), channel_id=1, source_target_pairs={{0,8},{8,16},{16,24},{24,32},{32,40},{40,48},{48,56},{56,64},{64,7... | collective-permute-start | bytes 589832 | tf_op jit(solution)/shard_map/ppermute | solution.py:27
  147.7 18.8 %collective-permute-start.2 = (bf16[2,256,384]{2,1,0:T(8,128)(2,1)S(1)}, bf16[2,256,384]{2,1,0:T(8,128)(2,1)S(1)}, u32[]{:S(2)}, u32[]{:S(2)}) collective-permute-start(bf16[2,256,384]{2,1,0:T(8,128)(2,1)S(1)} %convolution_convert_fusion.1), channel_id=1, source_target_pairs={{0,16},{8,24},{16,32},{24,40},{32,48},{40,56},{48,64},{56,72},{64,... | collective-permute-start | bytes 1179656 | tf_op jit(solution)/shard_map/ppermute | solution.py:36
  152.6 18.9 %collective-permute-start.3 = (bf16[2,256,384]{2,1,0:T(8,128)(2,1)S(1)}, bf16[2,256,384]{2,1,0:T(8,128)(2,1)S(1)}, u32[]{:S(2)}, u32[]{:S(2)}) collective-permute-start(bf16[2,256,384]{2,1,0:T(8,128)(2,1)S(1)} %convolution_convert_fusion), channel_id=1, source_target_pairs={{16,0},{24,8},{32,16},{40,24},{48,32},{56,40},{64,48},{72,56},{80,... | collective-permute-start | bytes 1179656 | tf_op jit(solution)/shard_map/ppermute | solution.py:36
  171.6 1.0 copy-start.1
  173.1 11.2 %collective-permute-start.6 = (bf16[1,256,384]{2,1,0:T(8,128)(2,1)S(1)}, bf16[1,256,384]{2,1,0:T(8,128)(2,1)S(1)}, u32[]{:S(2)}, u32[]{:S(2)}) collective-permute-start(bf16[1,256,384]{2,1,0:T(8,128)(2,1)S(1)} %fusion.85), channel_id=1, source_target_pairs={{0,16},{8,24},{16,32},{24,40},{32,48},{40,56},{48,64},{56,72},{64,... | collective-permute-start | bytes 589832 | tf_op jit(solution)/shard_map/ppermute | solution.py:36
  175.0 13.4 %collective-permute-start.5 = (bf16[1,256,384]{2,1,0:T(8,128)(2,1)S(1)}, bf16[1,256,384]{2,1,0:T(8,128)(2,1)S(1)}, u32[]{:S(2)}, u32[]{:S(2)}) collective-permute-start(bf16[1,256,384]{2,1,0:T(8,128)(2,1)S(1)} %fusion.85), channel_id=1, source_target_pairs={{16,0},{24,8},{32,16},{40,24},{48,32},{56,40},{64,48},{72,56},{80,... | collective-permute-start | bytes 589832 | tf_op jit(solution)/shard_map/ppermute | solution.py:36
  180.9 24.6 %collective-permute-start.4 = (bf16[1,256,768]{2,1,0:T(8,128)(2,1)S(1)}, bf16[1,256,768]{2,1,0:T(8,128)(2,1)S(1)}, u32[]{:S(2)}, u32[]{:S(2)}) collective-permute-start(bf16[1,256,768]{2,1,0:T(8,128)(2,1)S(1)} %fusion.55), channel_id=1, source_target_pairs={{7,0},{0,1},{1,2},{2,3},{3,4},{4,5},{5,6},{6,7},{15,8},{8,9},{9,10... | collective-permute-start | bytes 1179656 | tf_op jit(solution)/shard_map/ppermute | solution.py:42
  189.8 6.3 %collective-permute-start.8 = (bf16[1,128,384]{2,1,0:T(8,128)(2,1)S(1)}, bf16[1,128,384]{2,1,0:T(8,128)(2,1)S(1)}, u32[]{:S(2)}, u32[]{:S(2)}) collective-permute-start(bf16[1,128,384]{2,1,0:T(8,128)(2,1)S(1)} %get-tuple-element.11), channel_id=1, source_target_pairs={{0,8},{8,16},{16,24},{24,32},{32,40},{40,48},{48,56},{56,64},{64,7... | collective-permute-start | bytes 294920 | tf_op jit(solution)/shard_map/ppermute | solution.py:27
  194.1 7.4 %collective-permute-start.7 = (bf16[1,128,384]{2,1,0:T(8,128)(2,1)S(1)}, bf16[1,128,384]{2,1,0:T(8,128)(2,1)S(1)}, u32[]{:S(2)}, u32[]{:S(2)}) collective-permute-start(bf16[1,128,384]{2,1,0:T(8,128)(2,1)S(1)} %get-tuple-element.10), channel_id=1, source_target_pairs={{8,0},{16,8},{24,16},{32,24},{40,32},{48,40},{56,48},{64,56},{72,6... | collective-permute-start | bytes 294920 | tf_op jit(solution)/shard_map/ppermute | solution.py:28
  202.4 14.8 %collective-permute-start.9 = (bf16[1,256,768]{2,1,0:T(8,128)(2,1)S(1)}, bf16[1,256,768]{2,1,0:T(8,128)(2,1)S(1)}, u32[]{:S(2)}, u32[]{:S(2)}) collective-permute-start(bf16[1,256,768]{2,1,0:T(8,128)(2,1)S(1)} %fusion.24), channel_id=1, source_target_pairs={{1,0},{2,1},{3,2},{4,3},{5,4},{6,5},{7,6},{0,7},{9,8},{10,9},{11,1... | collective-permute-start | bytes 1179656 | tf_op jit(solution)/shard_map/ppermute | solution.py:42
Sparse Core Ops, SparseCore 0:
  19.7 74.3 all-gather.4

commit v4 on v3

--- a/solution.py
+++ b/solution.py
@@ -92,10 +92,37 @@
     return (present_state, stored)
 
 
+def ring_gather(block):
+    rows, width = block.shape
+    span, lanes, cores = lax.axis_size("z"), lax.axis_size("xh"), lax.axis_size("core")
+    here, core = lax.axis_index("z"), lax.axis_index("core")
+    sign = 2 * core - 1
+    route = []
+    for z in range(span):
+        for x in range(lanes):
+            route.append(((z * lanes + x) * cores, (((z + 1) % span) * lanes + x) * cores))
+            route.append(((z * lanes + x) * cores + 1, (((z - 1) % span) * lanes + x) * cores + 1))
+    half = span // 2
+    gathered = jnp.zeros((span, rows, width), block.dtype)
+    gathered = lax.dynamic_update_slice(gathered, block[None], (here, 0, 0))
+    current, received = block, []
+    for step in range(1, half + 1):
+        current = lax.ppermute(current, SEQ, route)
+        received.append(current)
+        source = (here + sign * step) % span
+        gathered = lax.dynamic_update_slice(gathered, current[None], (source, 0, 0))
+    shared = lax.ppermute(jnp.stack(received[: span - half - 1]), "core", [(0, 1), (1, 0)])
+    for step in range(1, span - half):
+        source = (here - sign * step) % span
+        gathered = lax.dynamic_update_slice(gathered, shared[step - 1][None], (source, 0, 0))
+    return gathered.reshape(span * rows, width)
+
+
 def gather_weights(conv_weight, proj_weight):
     flat = jnp.concatenate([conv_weight.reshape(1, -1), proj_weight.reshape(1, -1)], axis=1)
-    for axis in reversed(SEQ):
-        flat = lax.all_gather(flat, axis, axis=0, tiled=True)
+    flat = lax.all_gather(flat, "core", axis=0, tiled=True)
+    flat = lax.all_gather(flat, "xh", axis=0, tiled=True)
+    flat = ring_gather(flat)
     shards, split = flat.shape[0], conv_weight.size
     conv = flat[:, :split].reshape((shards,) + conv_weight.shape[1:])
     proj = flat[:, split:].reshape((shards,) + proj_weight.shape[1:])

time: 226 us -> 218 us (0.965)
  the two profiles are of different devices: /device:TPU:59 before, /device:TPU:255 now
where the time goes in v4:
time: 218 us; the launch traced here: 217 us
  waiting for transfers between devices  76.8 us (35%)
  starting transfers between devices  62.3 us (29%)
  local copies, waits for them, and re-layouts  53.9 us (25%)
  matrix products  10.7 us (5%)
  blocking collectives  9.53 us (4%)
  other arithmetic  2.39 us (1%)
    ppermute x8, waiting for transfers between devices, ring_gather(): current = lax.ppermute(current, SEQ, route)  37 us
    ppermute x4, waiting for transfers between devices, from_behind(): return lax.ppermute(block, axis, route)  18.8 us
    ppermute x8, starting transfers between devices, ring_gather(): current = lax.ppermute(current, SEQ, route)  15.3 us
    ppermute x1, starting transfers between devices, ring_gather(): lax.ppermute(jnp.stack(received[:span - half - 1]), 'core', [(0, 1), (1,...  14.3 us
    ppermute x4, starting transfers between devices, from_behind(): return lax.ppermute(block, axis, route)  13.9 us
    ppermute x2, starting transfers between devices, padded(): before = lax.ppermute(last, axis, up)  10.5 us
    unnamed x38, local copies, waits for them, and re-layouts  9.74 us
    ppermute x2, waiting for transfers between devices, padded(): after = lax.ppermute(initial, axis, down)  9.62 us
  transfers between devices with their start and end apart: 19, of which 13 were waited for; matrix products, arithmetic and copies ran while one was open for 12% of the time, Pallas kernels for 0%

profile of v4, /device:TPU:255, one launch (start us, length us, event | category | flops | bytes accessed | tf_op | source)
XLA Modules:
  0.0 216.8 jit_solution(18446674059529549886)
XLA Ops:
  2.4 2.3 %all-gather = bf16[2,1,36864]{2,1,0:T(2,128)(2,1)S(1)} all-gather(bf16[1,1,36864]{2,1,0:T(2,128)(2,1)S(1)} %maximum_bitcast_fusion), channel_id=1, replica_groups=mesh['z'=16,'xh'=2,'core'=2,'section'=8] {'core'}, dimensions={0}, use_global_device_ids=true | all-gather | bytes 221184 | tf_op jit(solution)/shard_map/all_gather | solution.py:123
  5.0 7.2 %all-gather.1 = bf16[2,2,36864]{2,1,0:T(2,128)(2,1)S(1)} all-gather(bf16[1,2,36864]{2,1,0:T(2,128)(2,1)S(1)} %bitcast.144), channel_id=1, replica_groups=mesh['z'=16,'xh'=2,'core'=2,'section'=8] {'xh'}, dimensions={0}, use_global_device_ids=true | all-gather | bytes 442368 | tf_op jit(solution)/shard_map/all_gather | solution.py:124
  14.4 4.0 %broadcast_in_dim.30 = bf16[16,4,36864]{2,1,0:T(4,128)(2,1)} broadcast(bf16[]{:T(256)} %constant.111.clone.1), dimensions={} | broadcast | bytes 4718594 | tf_op jit(solution)/shard_map/broadcast_in_dim | solution.py:106
  23.9 5.9 %collective-permute-done.1 = bf16[4,36864]{1,0:T(4,128)(2,1)S(1)} collective-permute-done((bf16[4,36864]{1,0:T(4,128)(2,1)S(1)}, bf16[4,36864]{1,0:T(4,128)(2,1)S(1)}, u32[]{:S(2)}, u32[]{:S(2)}) %collective-permute-start.1) | collective-permute-done | bytes 294944 | tf_op jit(solution)/shard_map/ppermute | solution.py:110
  32.7 5.8 %collective-permute-done.2 = bf16[4,36864]{1,0:T(4,128)(2,1)S(1)} collective-permute-done((bf16[4,36864]{1,0:T(4,128)(2,1)S(1)}, bf16[4,36864]{1,0:T(4,128)(2,1)S(1)}, u32[]{:S(2)}, u32[]{:S(2)}) %collective-permute-start.2) | collective-permute-done | bytes 294944 | tf_op jit(solution)/shard_map/ppermute | solution.py:110
  41.3 5.8 %collective-permute-done.3 = bf16[4,36864]{1,0:T(4,128)(2,1)S(1)} collective-permute-done((bf16[4,36864]{1,0:T(4,128)(2,1)S(1)}, bf16[4,36864]{1,0:T(4,128)(2,1)S(1)}, u32[]{:S(2)}, u32[]{:S(2)}) %collective-permute-start.3) | collective-permute-done | bytes 294944 | tf_op jit(solution)/shard_map/ppermute | solution.py:110
  50.0 5.8 %collective-permute-done.4 = bf16[4,36864]{1,0:T(4,128)(2,1)S(1)} collective-permute-done((bf16[4,36864]{1,0:T(4,128)(2,1)S(1)}, bf16[4,36864]{1,0:T(4,128)(2,1)S(1)}, u32[]{:S(2)}, u32[]{:S(2)}) %collective-permute-start.4) | collective-permute-done | bytes 294944 | tf_op jit(solution)/shard_map/ppermute | solution.py:110
  58.7 5.8 %collective-permute-done.5 = bf16[4,36864]{1,0:T(4,128)(2,1)S(1)} collective-permute-done((bf16[4,36864]{1,0:T(4,128)(2,1)S(1)}, bf16[4,36864]{1,0:T(4,128)(2,1)S(1)}, u32[]{:S(2)}, u32[]{:S(2)}) %collective-permute-start.5) | collective-permute-done | bytes 294944 | tf_op jit(solution)/shard_map/ppermute | solution.py:110
  67.3 5.8 %collective-permute-done.6 = bf16[4,36864]{1,0:T(4,128)(2,1)S(1)} collective-permute-done((bf16[4,36864]{1,0:T(4,128)(2,1)S(1)}, bf16[4,36864]{1,0:T(4,128)(2,1)S(1)}, u32[]{:S(2)}, u32[]{:S(2)}) %collective-permute-start.6) | collective-permute-done | bytes 294944 | tf_op jit(solution)/shard_map/ppermute | solution.py:110
  76.0 14.3 %collective-permute-start.8 = (bf16[7,4,36864]{2,1,0:T(4,128)(2,1)S(1)}, bf16[7,4,36864]{2,1,0:T(4,128)(2,1)S(1)}, u32[]{:S(2)}, u32[]{:S(2)}) collective-permute-start(bf16[7,4,36864]{2,1,0:T(4,128)(2,1)S(1)} %get-tuple-element.10), channel_id=1, source_target_pairs={{0,8},{8,0},{1,9},{9,1},{2,10},{10,2},{3,11},{11,3},{4,12},{12,4},... | collective-permute-start | bytes 6193160 | tf_op jit(solution)/shard_map/ppermute | solution.py:114
  91.1 2.7 %collective-permute-done.8 = bf16[7,4,36864]{2,1,0:T(4,128)(2,1)S(1)} collective-permute-done((bf16[7,4,36864]{2,1,0:T(4,128)(2,1)S(1)}, bf16[7,4,36864]{2,1,0:T(4,128)(2,1)S(1)}, u32[]{:S(2)}, u32[]{:S(2)}) %collective-permute-start.8) | collective-permute-done | bytes 2064416 | tf_op jit(solution)/shard_map/ppermute | solution.py:114
  99.6 7.3 %reshape.75 = bf16[64,36864]{1,0:T(8,128)(2,1)} reshape(bf16[16,4,36864]{2,1,0:T(4,128)(2,1)} %slice_dynamic-update-slice_fusion) | data formatting | bytes 9437184 | tf_op jit(solution)/shard_map/reshape | solution.py:118
  108.9 4.3 %reshape.76 = bf16[64,2,3,12,384]{4,3,2,1,0:T(8,128)(2,1)} reshape(bf16[64,27648]{1,0:T(8,128)(2,1)S(1)} %slice-done) | data formatting | bytes 7077888 | tf_op jit(solution)/shard_map/reshape | solution.py:127
  113.1 6.0 %copy.36 = bf16[2,3,64,12,384]{4,0,3,2,1:T(2,128)(2,1)S(1)} copy(bf16[2,3,64,12,384]{4,3,1,0,2:T(8,128)(2,1)} %bitcast.141) | data formatting | bytes 7077888 | tf_op jit(solution)/shard_map/transpose | solution.py:129
  119.1 6.3 %fusion.155 = (bf16[1,1,1,768,384]{4,1,3,2,0:T(2,128)(2,1)}, bf16[1,1,1,768,384]{4,1,3,2,0:T(2,128)(2,1)}, bf16[1,1,1,768,384]{4,1,3,2,0:T(2,128)(2,1)S(1)}, bf1...) fusion(bf16[1,2,3,768,384]{4,1,3,2,0:T(2,128)(2,1)S(1)} %bitcas, ...), kind=kLoop, calls=%fused_computation.198 | loop fusion | bytes 7077888 | tf_op jit(solution)/shard_map/slice | solution.py:79
  127.2 4.6 %collective-permute-start.9 = (bf16[2,128,384]{2,1,0:T(8,128)(2,1)}, bf16[2,128,384]{2,1,0:T(8,128)(2,1)}, u32[]{:S(2)}, u32[]{:S(2)}) collective-permute-start(bf16[2,128,384]{2,1,0:T(8,128)(2,1)} %slice.149), channel_id=1, source_target_pairs={{0,8},{8,16},{16,24},{24,32},{32,40},{40,48},{48,56},{56,64},{64,7... | collective-permute-start | bytes 589832 | tf_op jit(solution)/shard_map/ppermute | solution.py:27
  141.9 2.4 %collective-permute-done.10 = bf16[2,128,384]{2,1,0:T(8,128)(2,1)} collective-permute-done((bf16[2,128,384]{2,1,0:T(8,128)(2,1)}, bf16[2,128,384]{2,1,0:T(8,128)(2,1)}, u32[]{:S(2)}, u32[]{:S(2)}) %collective-permute-start.10) | collective-permute-done | bytes 196640 | tf_op jit(solution)/shard_map/ppermute | solution.py:28
  150.3 4.9 %collective-permute-start.12 = (bf16[2,256,384]{2,1,0:T(8,128)(2,1)S(1)}, bf16[2,256,384]{2,1,0:T(8,128)(2,1)S(1)}, u32[]{:S(2)}, u32[]{:S(2)}) collective-permute-start(bf16[2,256,384]{2,1,0:T(8,128)(2,1)S(1)} %convolution_convert_fusion), channel_id=1, source_target_pairs={{16,0},{24,8},{32,16},{40,24},{48,32},{56,40},{64,48},{72,56},{80,... | collective-permute-start | bytes 1179656 | tf_op jit(solution)/shard_map/ppermute | solution.py:36
  156.1 13.1 %collective-permute-done.11 = bf16[2,256,384]{2,1,0:T(8,128)(2,1)S(1)} collective-permute-done((bf16[2,256,384]{2,1,0:T(8,128)(2,1)S(1)}, bf16[2,256,384]{2,1,0:T(8,128)(2,1)S(1)}, u32[]{:S(2)}, u32[]{:S(2)}) %collective-permute-start.11) | collective-permute-done | bytes 393248 | tf_op jit(solution)/shard_map/ppermute | solution.py:36
  169.9 5.2 %collective-permute-start.15 = (bf16[1,256,384]{2,1,0:T(8,128)(2,1)S(1)}, bf16[1,256,384]{2,1,0:T(8,128)(2,1)S(1)}, u32[]{:S(2)}, u32[]{:S(2)}) collective-permute-start(bf16[1,256,384]{2,1,0:T(8,128)(2,1)S(1)} %fusion.85), channel_id=1, source_target_pairs={{0,16},{8,24},{16,32},{24,40},{32,48},{40,56},{48,64},{56,72},{64,... | collective-permute-start | bytes 589832 | tf_op jit(solution)/shard_map/ppermute | solution.py:36
  180.7 5.6 %collective-permute-done.14 = bf16[1,256,384]{2,1,0:T(8,128)(2,1)S(1)} collective-permute-done((bf16[1,256,384]{2,1,0:T(8,128)(2,1)S(1)}, bf16[1,256,384]{2,1,0:T(8,128)(2,1)S(1)}, u32[]{:S(2)}, u32[]{:S(2)}) %collective-permute-start.14) | collective-permute-done | bytes 196640 | tf_op jit(solution)/shard_map/ppermute | solution.py:36
  187.7 5.9 %collective-permute-start.17 = (bf16[1,128,384]{2,1,0:T(8,128)(2,1)S(1)}, bf16[1,128,384]{2,1,0:T(8,128)(2,1)S(1)}, u32[]{:S(2)}, u32[]{:S(2)}) collective-permute-start(bf16[1,128,384]{2,1,0:T(8,128)(2,1)S(1)} %get-tuple-element.25), channel_id=1, source_target_pairs={{0,8},{8,16},{16,24},{24,32},{32,40},{40,48},{48,56},{56,64},{64,7... | collective-permute-start | bytes 294920 | tf_op jit(solution)/shard_map/ppermute | solution.py:27
  196.3 7.2 %collective-permute-done.16 = bf16[1,128,384]{2,1,0:T(8,128)(2,1)S(1)} collective-permute-done((bf16[1,128,384]{2,1,0:T(8,128)(2,1)S(1)}, bf16[1,128,384]{2,1,0:T(8,128)(2,1)S(1)}, u32[]{:S(2)}, u32[]{:S(2)}) %collective-permute-start.16) | collective-permute-done | bytes 98336 | tf_op jit(solution)/shard_map/ppermute | solution.py:28
  206.6 8.7 %collective-permute-done.18 = bf16[1,256,768]{2,1,0:T(8,128)(2,1)S(1)} collective-permute-done((bf16[1,256,768]{2,1,0:T(8,128)(2,1)S(1)}, bf16[1,256,768]{2,1,0:T(8,128)(2,1)S(1)}, u32[]{:S(2)}, u32[]{:S(2)}) %collective-permute-start.18) | collective-permute-done | bytes 393248 | tf_op jit(solution)/shard_map/ppermute | solution.py:42
  (104 shorter events, 68.6 us)
Async XLA Ops:
  12.3 8.9 %collective-permute-start = (bf16[4,36864]{1,0:T(4,128)(2,1)S(1)}, bf16[4,36864]{1,0:T(4,128)(2,1)S(1)}, u32[]{:S(2)}, u32[]{:S(2)}) collective-permute-start(bf16[4,36864]{1,0:T(4,128)(2,1)S(1)} %reshape.91), channel_id=1, source_target_pairs={{0,32},{8,488},{16,48},{24,504},{32,64},{40,8},{48,80},{56,24},{64... | collective-permute-start | bytes 884744 | tf_op jit(solution)/shard_map/ppermute | solution.py:110
  21.2 8.7 %collective-permute-start.1 = (bf16[4,36864]{1,0:T(4,128)(2,1)S(1)}, bf16[4,36864]{1,0:T(4,128)(2,1)S(1)}, u32[]{:S(2)}, u32[]{:S(2)}) collective-permute-start(bf16[4,36864]{1,0:T(4,128)(2,1)S(1)} %collective-permute-done), channel_id=1, source_target_pairs={{0,32},{8,488},{16,48},{24,504},{32,64},{40,8},{48,80},{56,24},{64... | collective-permute-start | bytes 884744 | tf_op jit(solution)/shard_map/ppermute | solution.py:110
  29.8 8.7 %collective-permute-start.2 = (bf16[4,36864]{1,0:T(4,128)(2,1)S(1)}, bf16[4,36864]{1,0:T(4,128)(2,1)S(1)}, u32[]{:S(2)}, u32[]{:S(2)}) collective-permute-start(bf16[4,36864]{1,0:T(4,128)(2,1)S(1)} %collective-permute-done.1), channel_id=1, source_target_pairs={{0,32},{8,488},{16,48},{24,504},{32,64},{40,8},{48,80},{56,24},{64... | collective-permute-start | bytes 884744 | tf_op jit(solution)/shard_map/ppermute | solution.py:110
  38.5 8.7 %collective-permute-start.3 = (bf16[4,36864]{1,0:T(4,128)(2,1)S(1)}, bf16[4,36864]{1,0:T(4,128)(2,1)S(1)}, u32[]{:S(2)}, u32[]{:S(2)}) collective-permute-start(bf16[4,36864]{1,0:T(4,128)(2,1)S(1)} %collective-permute-done.2), channel_id=1, source_target_pairs={{0,32},{8,488},{16,48},{24,504},{32,64},{40,8},{48,80},{56,24},{64... | collective-permute-start | bytes 884744 | tf_op jit(solution)/shard_map/ppermute | solution.py:110
  47.2 8.7 %collective-permute-start.4 = (bf16[4,36864]{1,0:T(4,128)(2,1)S(1)}, bf16[4,36864]{1,0:T(4,128)(2,1)S(1)}, u32[]{:S(2)}, u32[]{:S(2)}) collective-permute-start(bf16[4,36864]{1,0:T(4,128)(2,1)S(1)} %collective-permute-done.3), channel_id=1, source_target_pairs={{0,32},{8,488},{16,48},{24,504},{32,64},{40,8},{48,80},{56,24},{64... | collective-permute-start | bytes 884744 | tf_op jit(solution)/shard_map/ppermute | solution.py:110
  55.8 8.7 %collective-permute-start.5 = (bf16[4,36864]{1,0:T(4,128)(2,1)S(1)}, bf16[4,36864]{1,0:T(4,128)(2,1)S(1)}, u32[]{:S(2)}, u32[]{:S(2)}) collective-permute-start(bf16[4,36864]{1,0:T(4,128)(2,1)S(1)} %collective-permute-done.4), channel_id=1, source_target_pairs={{0,32},{8,488},{16,48},{24,504},{32,64},{40,8},{48,80},{56,24},{64... | collective-permute-start | bytes 884744 | tf_op jit(solution)/shard_map/ppermute | solution.py:110
  64.5 8.7 %collective-permute-start.6 = (bf16[4,36864]{1,0:T(4,128)(2,1)S(1)}, bf16[4,36864]{1,0:T(4,128)(2,1)S(1)}, u32[]{:S(2)}, u32[]{:S(2)}) collective-permute-start(bf16[4,36864]{1,0:T(4,128)(2,1)S(1)} %collective-permute-done.5), channel_id=1, source_target_pairs={{0,32},{8,488},{16,48},{24,504},{32,64},{40,8},{48,80},{56,24},{64... | collective-permute-start | bytes 884744 | tf_op jit(solution)/shard_map/ppermute | solution.py:110
  73.2 17.1 %collective-permute-start.7 = (bf16[4,36864]{1,0:T(4,128)(2,1)S(1)}, bf16[4,36864]{1,0:T(4,128)(2,1)S(1)}, u32[]{:S(2)}, u32[]{:S(2)}) collective-permute-start(bf16[4,36864]{1,0:T(4,128)(2,1)S(1)} %collective-permute-done.6), channel_id=1, source_target_pairs={{0,32},{8,488},{16,48},{24,504},{32,64},{40,8},{48,80},{56,24},{64... | collective-permute-start | bytes 884744 | tf_op jit(solution)/shard_map/ppermute | solution.py:110
  76.0 17.8 %collective-permute-start.8 = (bf16[7,4,36864]{2,1,0:T(4,128)(2,1)S(1)}, bf16[7,4,36864]{2,1,0:T(4,128)(2,1)S(1)}, u32[]{:S(2)}, u32[]{:S(2)}) collective-permute-start(bf16[7,4,36864]{2,1,0:T(4,128)(2,1)S(1)} %get-tuple-element.10), channel_id=1, source_target_pairs={{0,8},{8,0},{1,9},{9,1},{2,10},{10,2},{3,11},{11,3},{4,12},{12,4},... | collective-permute-start | bytes 6193160 | tf_op jit(solution)/shard_map/ppermute | solution.py:114
  119.1 6.4 %copy-start.8 = (bf16[1,256,768]{2,1,0:T(8,128)(2,1)S(1)}, bf16[1,256,768]{2,1,0:T(8,128)(2,1)}, u32[]{:S(2)}) copy-start(bf16[1,256,768]{2,1,0:T(8,128)(2,1)} %param.5) | copy-start | bytes 1179652
  125.5 6.4 %copy-start = (bf16[1,1,1,768,384]{4,1,3,2,0:T(2,128)(2,1)}, bf16[1,1,1,768,384]{4,1,3,2,0:T(2,128)(2,1)S(1)}, u32[]{:S(2)}) copy-start(bf16[1,1,1,768,384]{4,1,3,2,0:T(2,128)(2,1)S(1)} %get-tuple-element.4) | copy-start | bytes 1769476
  127.2 13.7 %collective-permute-start.9 = (bf16[2,128,384]{2,1,0:T(8,128)(2,1)}, bf16[2,128,384]{2,1,0:T(8,128)(2,1)}, u32[]{:S(2)}, u32[]{:S(2)}) collective-permute-start(bf16[2,128,384]{2,1,0:T(8,128)(2,1)} %slice.149), channel_id=1, source_target_pairs={{0,8},{8,16},{16,24},{24,32},{32,40},{40,48},{48,56},{56,64},{64,7... | collective-permute-start | bytes 589832 | tf_op jit(solution)/shard_map/ppermute | solution.py:27
  133.4 10.9 %collective-permute-start.10 = (bf16[2,128,384]{2,1,0:T(8,128)(2,1)}, bf16[2,128,384]{2,1,0:T(8,128)(2,1)}, u32[]{:S(2)}, u32[]{:S(2)}) collective-permute-start(bf16[2,128,384]{2,1,0:T(8,128)(2,1)} %slice.152), channel_id=1, source_target_pairs={{8,0},{16,8},{24,16},{32,24},{40,32},{48,40},{56,48},{64,56},{72,6... | collective-permute-start | bytes 589832 | tf_op jit(solution)/shard_map/ppermute | solution.py:28
  147.5 21.7 %collective-permute-start.11 = (bf16[2,256,384]{2,1,0:T(8,128)(2,1)S(1)}, bf16[2,256,384]{2,1,0:T(8,128)(2,1)S(1)}, u32[]{:S(2)}, u32[]{:S(2)}) collective-permute-start(bf16[2,256,384]{2,1,0:T(8,128)(2,1)S(1)} %convolution_convert_fusion.1), channel_id=1, source_target_pairs={{0,16},{8,24},{16,32},{24,40},{32,48},{40,56},{48,64},{56,72},{64,... | collective-permute-start | bytes 1179656 | tf_op jit(solution)/shard_map/ppermute | solution.py:36
  150.3 18.9 %collective-permute-start.12 = (bf16[2,256,384]{2,1,0:T(8,128)(2,1)S(1)}, bf16[2,256,384]{2,1,0:T(8,128)(2,1)S(1)}, u32[]{:S(2)}, u32[]{:S(2)}) collective-permute-start(bf16[2,256,384]{2,1,0:T(8,128)(2,1)S(1)} %convolution_convert_fusion), channel_id=1, source_target_pairs={{16,0},{24,8},{32,16},{40,24},{48,32},{56,40},{64,48},{72,56},{80,... | collective-permute-start | bytes 1179656 | tf_op jit(solution)/shard_map/ppermute | solution.py:36
  156.1 13.3 %copy-start.10 = (bf16[1,256,768]{2,1,0:T(8,128)(2,1)S(1)}, bf16[1,256,768]{2,1,0:T(8,128)(2,1)}, u32[]{:S(2)}) copy-start(bf16[1,256,768]{2,1,0:T(8,128)(2,1)} %param.7) | copy-start | bytes 1179652
  169.9 10.4 %collective-permute-start.15 = (bf16[1,256,384]{2,1,0:T(8,128)(2,1)S(1)}, bf16[1,256,384]{2,1,0:T(8,128)(2,1)S(1)}, u32[]{:S(2)}, u32[]{:S(2)}) collective-permute-start(bf16[1,256,384]{2,1,0:T(8,128)(2,1)S(1)} %fusion.85), channel_id=1, source_target_pairs={{0,16},{8,24},{16,32},{24,40},{32,48},{40,56},{48,64},{56,72},{64,... | collective-permute-start | bytes 589832 | tf_op jit(solution)/shard_map/ppermute | solution.py:36
  175.1 11.2 %collective-permute-start.14 = (bf16[1,256,384]{2,1,0:T(8,128)(2,1)S(1)}, bf16[1,256,384]{2,1,0:T(8,128)(2,1)S(1)}, u32[]{:S(2)}, u32[]{:S(2)}) collective-permute-start(bf16[1,256,384]{2,1,0:T(8,128)(2,1)S(1)} %fusion.85), channel_id=1, source_target_pairs={{16,0},{24,8},{32,16},{40,24},{48,32},{56,40},{64,48},{72,56},{80,... | collective-permute-start | bytes 589832 | tf_op jit(solution)/shard_map/ppermute | solution.py:36
  177.8 28.8 %collective-permute-start.13 = (bf16[1,256,768]{2,1,0:T(8,128)(2,1)S(1)}, bf16[1,256,768]{2,1,0:T(8,128)(2,1)S(1)}, u32[]{:S(2)}, u32[]{:S(2)}) collective-permute-start(bf16[1,256,768]{2,1,0:T(8,128)(2,1)S(1)} %fusion.55), channel_id=1, source_target_pairs={{7,0},{0,1},{1,2},{2,3},{3,4},{4,5},{5,6},{6,7},{15,8},{8,9},{9,10... | collective-permute-start | bytes 1179656 | tf_op jit(solution)/shard_map/ppermute | solution.py:42
  187.6 8.3 %copy-start.1 = (bf16[1,1,1,768,384]{4,1,3,2,0:T(2,128)(2,1)S(1)}, bf16[1,1,1,768,384]{4,1,3,2,0:T(2,128)(2,1)}, u32[]{:S(2)}) copy-start(bf16[1,1,1,768,384]{4,1,3,2,0:T(2,128)(2,1)} %copy-done) | copy-start | bytes 1769476
  187.7 15.9 %copy-start.6 = (bf16[1,1,1,768,384]{4,1,3,2,0:T(2,128)(2,1)S(1)}, bf16[1,1,1,768,384]{4,1,3,2,0:T(2,128)(2,1)}, u32[]{:S(2)}) copy-start(bf16[1,1,1,768,384]{4,1,3,2,0:T(2,128)(2,1)} %copy-done.5) | copy-start | bytes 1769476
  187.7 8.2 %collective-permute-start.17 = (bf16[1,128,384]{2,1,0:T(8,128)(2,1)S(1)}, bf16[1,128,384]{2,1,0:T(8,128)(2,1)S(1)}, u32[]{:S(2)}, u32[]{:S(2)}) collective-permute-start(bf16[1,128,384]{2,1,0:T(8,128)(2,1)S(1)} %get-tuple-element.25), channel_id=1, source_target_pairs={{0,8},{8,16},{16,24},{24,32},{32,40},{40,48},{48,56},{56,64},{64,7... | collective-permute-start | bytes 294920 | tf_op jit(solution)/shard_map/ppermute | solution.py:27
  194.0 9.5 %collective-permute-start.16 = (bf16[1,128,384]{2,1,0:T(8,128)(2,1)S(1)}, bf16[1,128,384]{2,1,0:T(8,128)(2,1)S(1)}, u32[]{:S(2)}, u32[]{:S(2)}) collective-permute-start(bf16[1,128,384]{2,1,0:T(8,128)(2,1)S(1)} %get-tuple-element.24), channel_id=1, source_target_pairs={{8,0},{16,8},{24,16},{32,24},{40,32},{48,40},{56,48},{64,56},{72,6... | collective-permute-start | bytes 294920 | tf_op jit(solution)/shard_map/ppermute | solution.py:28
  204.4 10.9 %collective-permute-start.18 = (bf16[1,256,768]{2,1,0:T(8,128)(2,1)S(1)}, bf16[1,256,768]{2,1,0:T(8,128)(2,1)S(1)}, u32[]{:S(2)}, u32[]{:S(2)}) collective-permute-start(bf16[1,256,768]{2,1,0:T(8,128)(2,1)S(1)} %fusion.24), channel_id=1, source_target_pairs={{1,0},{2,1},{3,2},{4,3},{5,4},{6,5},{7,6},{0,7},{9,8},{10,9},{11,1... | collective-permute-start | bytes 1179656 | tf_op jit(solution)/shard_map/ppermute | solution.py:42
  (10 other events, 28.0 us)

commit v5 on v3

--- a/solution.py
+++ b/solution.py
@@ -92,15 +92,44 @@
     return (present_state, stored)
 
 
+def place(conv, proj, block, chip, conv_shape, proj_shape):
+    rows, split = block.shape[0], 1
+    for size in conv_shape:
+        split *= size
+    part = block[:, :split].reshape((rows,) + conv_shape[1:])
+    part = jnp.moveaxis(part, 0, 2).reshape(conv_shape[:3] + (rows * conv_shape[3], conv_shape[4]))
+    conv = lax.dynamic_update_slice(conv, part, (0, 0, 0, chip * rows * conv_shape[3], 0))
+    part = block[:, split:].reshape((rows,) + proj_shape[1:])
+    part = jnp.moveaxis(part, 0, 1).reshape(proj_shape[:2] + (rows * proj_shape[2], proj_shape[3]))
+    proj = lax.dynamic_update_slice(proj, part, (0, 0, chip * rows * proj_shape[2], 0))
+    return conv, proj
+
+
 def gather_weights(conv_weight, proj_weight):
-    flat = jnp.concatenate([conv_weight.reshape(1, -1), proj_weight.reshape(1, -1)], axis=1)
-    for axis in reversed(SEQ):
-        flat = lax.all_gather(flat, axis, axis=0, tiled=True)
-    shards, split = flat.shape[0], conv_weight.size
-    conv = flat[:, :split].reshape((shards,) + conv_weight.shape[1:])
-    proj = flat[:, split:].reshape((shards,) + proj_weight.shape[1:])
-    conv = jnp.moveaxis(conv, 0, 2).reshape(conv_weight.shape[:3] + (-1, conv_weight.shape[4]))
-    proj = jnp.moveaxis(proj, 0, 1).reshape(proj_weight.shape[:2] + (-1, proj_weight.shape[3]))
+    conv_shape, proj_shape = conv_weight.shape, proj_weight.shape
+    block = jnp.concatenate([conv_weight.reshape(1, -1), proj_weight.reshape(1, -1)], axis=1)
+    block = lax.all_gather(block, "core", axis=0, tiled=True)
+    block = lax.all_gather(block, "xh", axis=0, tiled=True)
+    span, lanes, cores = lax.axis_size("z"), lax.axis_size("xh"), lax.axis_size("core")
+    here, core = lax.axis_index("z"), lax.axis_index("core")
+    sign = 2 * core - 1
+    route = []
+    for z in range(span):
+        for x in range(lanes):
+            route.append(((z * lanes + x) * cores, (((z + 1) % span) * lanes + x) * cores))
+            route.append(((z * lanes + x) * cores + 1, (((z - 1) % span) * lanes + x) * cores + 1))
+    shards = span * lanes * cores
+    conv = jnp.zeros(conv_shape[:3] + (shards * conv_shape[3], conv_shape[4]), conv_weight.dtype)
+    proj = jnp.zeros(proj_shape[:2] + (shards * proj_shape[2], proj_shape[3]), proj_weight.dtype)
+    conv, proj = place(conv, proj, block, here, conv_shape, proj_shape)
+    half = span // 2
+    current = block
+    for step in range(1, half + 1):
+        current = lax.ppermute(current, SEQ, route)
+        conv, proj = place(conv, proj, current, (here + sign * step) % span, conv_shape, proj_shape)
+        if step < span - half:
+            peer = lax.ppermute(current, "core", [(0, 1), (1, 0)])
+            conv, proj = place(conv, proj, peer, (here - sign * step) % span, conv_shape, proj_shape)
     return conv, proj
 
 

time: 226 us -> 328 us (1.45)
  the two profiles are of different devices: /device:TPU:59 before, /device:TPU:127 now
where the time goes in v5:
time: 328 us; the launch traced here: 323 us
  local copies, waits for them, and re-layouts  174 us (53%)
  starting transfers between devices  79 us (24%)
  waiting for transfers between devices  39.6 us (12%)
  matrix products  17.6 us (5%)
  blocking collectives  9.53 us (3%)
    ppermute x7, starting transfers between devices, gather_weights(): peer = lax.ppermute(current, 'core', [(0, 1), (1, 0)])  30 us
    reshape x16, local copies, waits for them, and re-layouts, place(): part = block[:, :split].reshape((rows,) + conv_shape[1:])  27.1 us
    slice x16, local copies, waits for them, and re-layouts, place(): part = block[:, :split].reshape((rows,) + conv_shape[1:])  26.5 us
    slice x16, local copies, waits for them, and re-layouts, place(): part = block[:, split:].reshape((rows,) + proj_shape[1:])  24.1 us
    reshape x16, local copies, waits for them, and re-layouts, place(): part = block[:, split:].reshape((rows,) + proj_shape[1:])  23.7 us
    transpose x16, local copies, waits for them, and re-layouts, place(): jnp.moveaxis(part, 0, 1)  22.5 us
    dynamic_update_slice x16, local copies, waits for them, and re-layouts, place(): lax.dynamic_update_slice(proj, part, (0, 0, chip * rows * proj_shape[2], 0))  21.8 us
    transpose x16, local copies, waits for them, and re-layouts, place(): jnp.moveaxis(part, 0, 2)  18.5 us
  transfers between devices with their start and end apart: 25, of which 6 were waited for; matrix products, arithmetic and copies ran while one was open for 29% of the time, Pallas kernels for 0%

profile of v5, /device:TPU:127, one launch (start us, length us, event | category | flops | bytes accessed | tf_op | source)
XLA Modules:
  0.0 322.7 jit_solution(8147360253637598649)
XLA Ops:
  2.4 2.3 all-gather
  5.0 7.2 %all-gather.1 = bf16[2,2,36864]{2,1,0:T(2,128)(2,1)S(1)} all-gather(bf16[1,2,36864]{2,1,0:T(2,128)(2,1)S(1)} %bitcast.209), channel_id=1, replica_groups=mesh['z'=16,'xh'=2,'core'=2,'section'=8] {'xh'}, dimensions={0}, use_global_device_ids=true | all-gather | bytes 442368 | tf_op jit(solution)/shard_map/all_gather | solution.py:112
  26.2 1.9 collective-permute-start.2
  28.2 7.2 %collective-permute-start.1 = (bf16[4,36864]{1,0:T(4,128)(2,1)}, bf16[4,36864]{1,0:T(4,128)(2,1)}, u32[]{:S(2)}, u32[]{:S(2)}) collective-permute-start(bf16[4,36864]{1,0:T(4,128)(2,1)} %collective-permute-done), channel_id=1, source_target_pairs={{0,8},{8,0},{1,9},{9,1},{2,10},{10,2},{3,11},{11,3},{4,12},{12,4},... | collective-permute-start | bytes 884744 | tf_op jit(solution)/shard_map/ppermute | solution.py:131
  58.3 3.3 %collective-permute-start.3 = (bf16[4,36864]{1,0:T(4,128)(2,1)}, bf16[4,36864]{1,0:T(4,128)(2,1)}, u32[]{:S(2)}, u32[]{:S(2)}) collective-permute-start(bf16[4,36864]{1,0:T(4,128)(2,1)} %collective-permute-done.2), channel_id=1, source_target_pairs={{0,8},{8,0},{1,9},{9,1},{2,10},{10,2},{3,11},{11,3},{4,12},{12,4},... | collective-permute-start | bytes 884744 | tf_op jit(solution)/shard_map/ppermute | solution.py:131
  83.5 2.4 collective-permute-start.6
  85.9 3.4 %collective-permute-start.5 = (bf16[4,36864]{1,0:T(4,128)(2,1)}, bf16[4,36864]{1,0:T(4,128)(2,1)}, u32[]{:S(2)}, u32[]{:S(2)}) collective-permute-start(bf16[4,36864]{1,0:T(4,128)(2,1)} %collective-permute-done.4), channel_id=1, source_target_pairs={{0,8},{8,0},{1,9},{9,1},{2,10},{10,2},{3,11},{11,3},{4,12},{12,4},... | collective-permute-start | bytes 884744 | tf_op jit(solution)/shard_map/ppermute | solution.py:131
  113.1 4.9 %collective-permute-start.7 = (bf16[4,36864]{1,0:T(4,128)(2,1)}, bf16[4,36864]{1,0:T(4,128)(2,1)}, u32[]{:S(2)}, u32[]{:S(2)}) collective-permute-start(bf16[4,36864]{1,0:T(4,128)(2,1)} %collective-permute-done.6), channel_id=1, source_target_pairs={{0,8},{8,0},{1,9},{9,1},{2,10},{10,2},{3,11},{11,3},{4,12},{12,4},... | collective-permute-start | bytes 884744 | tf_op jit(solution)/shard_map/ppermute | solution.py:131
  141.8 4.3 %collective-permute-start.9 = (bf16[4,36864]{1,0:T(4,128)(2,1)}, bf16[4,36864]{1,0:T(4,128)(2,1)}, u32[]{:S(2)}, u32[]{:S(2)}) collective-permute-start(bf16[4,36864]{1,0:T(4,128)(2,1)} %collective-permute-done.8), channel_id=1, source_target_pairs={{0,8},{8,0},{1,9},{9,1},{2,10},{10,2},{3,11},{11,3},{4,12},{12,4},... | collective-permute-start | bytes 884744 | tf_op jit(solution)/shard_map/ppermute | solution.py:131
  169.9 3.1 collective-permute-start.11
  194.9 2.6 collective-permute-start.14
  197.5 3.7 %collective-permute-start.13 = (bf16[4,36864]{1,0:T(4,128)(2,1)}, bf16[4,36864]{1,0:T(4,128)(2,1)}, u32[]{:S(2)}, u32[]{:S(2)}) collective-permute-start(bf16[4,36864]{1,0:T(4,128)(2,1)} %collective-permute-done.12), channel_id=1, source_target_pairs={{0,8},{8,0},{1,9},{9,1},{2,10},{10,2},{3,11},{11,3},{4,12},{12,4},... | collective-permute-start | bytes 884744 | tf_op jit(solution)/shard_map/ppermute | solution.py:131
  218.4 2.6 convolution_convert_fusion.3
  233.9 3.4 %collective-permute-start.15 = (bf16[2,128,384]{2,1,0:T(8,128)(2,1)S(1)}, bf16[2,128,384]{2,1,0:T(8,128)(2,1)S(1)}, u32[]{:S(2)}, u32[]{:S(2)}) collective-permute-start(bf16[2,128,384]{2,1,0:T(8,128)(2,1)S(1)} %slice.249), channel_id=1, source_target_pairs={{0,8},{8,16},{16,24},{24,32},{32,40},{40,48},{48,56},{56,64},{64,7... | collective-permute-start | bytes 589832 | tf_op jit(solution)/shard_map/ppermute | solution.py:27
  243.4 5.5 %collective-permute-done.16 = bf16[2,128,384]{2,1,0:T(8,128)(2,1)S(1)} collective-permute-done((bf16[2,128,384]{2,1,0:T(8,128)(2,1)S(1)}, bf16[2,128,384]{2,1,0:T(8,128)(2,1)S(1)}, u32[]{:S(2)}, u32[]{:S(2)}) %collective-permute-start.16) | collective-permute-done | bytes 196640 | tf_op jit(solution)/shard_map/ppermute | solution.py:28
  254.2 4.9 %collective-permute-start.18 = (bf16[2,256,384]{2,1,0:T(8,128)(2,1)S(1)}, bf16[2,256,384]{2,1,0:T(8,128)(2,1)S(1)}, u32[]{:S(2)}, u32[]{:S(2)}) collective-permute-start(bf16[2,256,384]{2,1,0:T(8,128)(2,1)S(1)} %convolution_convert_fusion), channel_id=1, source_target_pairs={{16,0},{24,8},{32,16},{40,24},{48,32},{56,40},{64,48},{72,56},{80,... | collective-permute-start | bytes 1179656 | tf_op jit(solution)/shard_map/ppermute | solution.py:36
  259.8 12.1 %collective-permute-done.17 = bf16[2,256,384]{2,1,0:T(8,128)(2,1)S(1)} collective-permute-done((bf16[2,256,384]{2,1,0:T(8,128)(2,1)S(1)}, bf16[2,256,384]{2,1,0:T(8,128)(2,1)S(1)}, u32[]{:S(2)}, u32[]{:S(2)}) %collective-permute-start.17) | collective-permute-done | bytes 393248 | tf_op jit(solution)/shard_map/ppermute | solution.py:36
  273.6 6.5 %collective-permute-start.21 = (bf16[1,256,384]{2,1,0:T(8,128)(2,1)S(1)}, bf16[1,256,384]{2,1,0:T(8,128)(2,1)S(1)}, u32[]{:S(2)}, u32[]{:S(2)}) collective-permute-start(bf16[1,256,384]{2,1,0:T(8,128)(2,1)S(1)} %fusion.101), channel_id=1, source_target_pairs={{0,16},{8,24},{16,32},{24,40},{32,48},{40,56},{48,64},{56,72},{64,... | collective-permute-start | bytes 589832 | tf_op jit(solution)/shard_map/ppermute | solution.py:36
  283.9 2.1 collective-permute-start.19
  286.8 4.6 %collective-permute-done.20 = bf16[1,256,384]{2,1,0:T(8,128)(2,1)S(1)} collective-permute-done((bf16[1,256,384]{2,1,0:T(8,128)(2,1)S(1)}, bf16[1,256,384]{2,1,0:T(8,128)(2,1)S(1)}, u32[]{:S(2)}, u32[]{:S(2)}) %collective-permute-start.20) | collective-permute-done | bytes 196640 | tf_op jit(solution)/shard_map/ppermute | solution.py:36
  293.8 5.7 %collective-permute-start.23 = (bf16[1,128,384]{2,1,0:T(8,128)(2,1)S(1)}, bf16[1,128,384]{2,1,0:T(8,128)(2,1)S(1)}, u32[]{:S(2)}, u32[]{:S(2)}) collective-permute-start(bf16[1,128,384]{2,1,0:T(8,128)(2,1)S(1)} %get-tuple-element.3), channel_id=1, source_target_pairs={{0,8},{8,16},{16,24},{24,32},{32,40},{40,48},{48,56},{56,64},{64,7... | collective-permute-start | bytes 294920 | tf_op jit(solution)/shard_map/ppermute | solution.py:27
  302.2 7.2 %collective-permute-done.22 = bf16[1,128,384]{2,1,0:T(8,128)(2,1)S(1)} collective-permute-done((bf16[1,128,384]{2,1,0:T(8,128)(2,1)S(1)}, bf16[1,128,384]{2,1,0:T(8,128)(2,1)S(1)}, u32[]{:S(2)}, u32[]{:S(2)}) %collective-permute-start.22) | collective-permute-done | bytes 98336 | tf_op jit(solution)/shard_map/ppermute | solution.py:28
  310.2 2.2 collective-permute-start.24
  312.4 8.7 %collective-permute-done.24 = bf16[1,256,768]{2,1,0:T(8,128)(2,1)S(1)} collective-permute-done((bf16[1,256,768]{2,1,0:T(8,128)(2,1)S(1)}, bf16[1,256,768]{2,1,0:T(8,128)(2,1)S(1)}, u32[]{:S(2)}, u32[]{:S(2)}) %collective-permute-start.24) | collective-permute-done | bytes 393248 | tf_op jit(solution)/shard_map/ppermute | solution.py:42
  (207 shorter events, 209.3 us)
Async XLA Ops:
  13.0 9.2 %collective-permute-start = (bf16[4,36864]{1,0:T(4,128)(2,1)}, bf16[4,36864]{1,0:T(4,128)(2,1)}, u32[]{:S(2)}, u32[]{:S(2)}) collective-permute-start(bf16[4,36864]{1,0:T(4,128)(2,1)} %reshape.327), channel_id=1, source_target_pairs={{0,32},{8,488},{16,48},{24,504},{32,64},{40,8},{48,80},{56,24},{64... | collective-permute-start | bytes 884744 | tf_op jit(solution)/shard_map/ppermute | solution.py:128
  26.2 14.5 %collective-permute-start.2 = (bf16[4,36864]{1,0:T(4,128)(2,1)}, bf16[4,36864]{1,0:T(4,128)(2,1)}, u32[]{:S(2)}, u32[]{:S(2)}) collective-permute-start(bf16[4,36864]{1,0:T(4,128)(2,1)} %collective-permute-done), channel_id=1, source_target_pairs={{0,32},{8,488},{16,48},{24,504},{32,64},{40,8},{48,80},{56,24},{64... | collective-permute-start | bytes 884744 | tf_op jit(solution)/shard_map/ppermute | solution.py:128
  28.2 17.3 %collective-permute-start.1 = (bf16[4,36864]{1,0:T(4,128)(2,1)}, bf16[4,36864]{1,0:T(4,128)(2,1)}, u32[]{:S(2)}, u32[]{:S(2)}) collective-permute-start(bf16[4,36864]{1,0:T(4,128)(2,1)} %collective-permute-done), channel_id=1, source_target_pairs={{0,8},{8,0},{1,9},{9,1},{2,10},{10,2},{3,11},{11,3},{4,12},{12,4},... | collective-permute-start | bytes 884744 | tf_op jit(solution)/shard_map/ppermute | solution.py:131
  56.4 11.5 %collective-permute-start.4 = (bf16[4,36864]{1,0:T(4,128)(2,1)}, bf16[4,36864]{1,0:T(4,128)(2,1)}, u32[]{:S(2)}, u32[]{:S(2)}) collective-permute-start(bf16[4,36864]{1,0:T(4,128)(2,1)} %collective-permute-done.2), channel_id=1, source_target_pairs={{0,32},{8,488},{16,48},{24,504},{32,64},{40,8},{48,80},{56,24},{64... | collective-permute-start | bytes 884744 | tf_op jit(solution)/shard_map/ppermute | solution.py:128
  58.3 14.3 %collective-permute-start.3 = (bf16[4,36864]{1,0:T(4,128)(2,1)}, bf16[4,36864]{1,0:T(4,128)(2,1)}, u32[]{:S(2)}, u32[]{:S(2)}) collective-permute-start(bf16[4,36864]{1,0:T(4,128)(2,1)} %collective-permute-done.2), channel_id=1, source_target_pairs={{0,8},{8,0},{1,9},{9,1},{2,10},{10,2},{3,11},{11,3},{4,12},{12,4},... | collective-permute-start | bytes 884744 | tf_op jit(solution)/shard_map/ppermute | solution.py:131
  83.5 12.1 %collective-permute-start.6 = (bf16[4,36864]{1,0:T(4,128)(2,1)}, bf16[4,36864]{1,0:T(4,128)(2,1)}, u32[]{:S(2)}, u32[]{:S(2)}) collective-permute-start(bf16[4,36864]{1,0:T(4,128)(2,1)} %collective-permute-done.4), channel_id=1, source_target_pairs={{0,32},{8,488},{16,48},{24,504},{32,64},{40,8},{48,80},{56,24},{64... | collective-permute-start | bytes 884744 | tf_op jit(solution)/shard_map/ppermute | solution.py:128
  85.9 14.4 %collective-permute-start.5 = (bf16[4,36864]{1,0:T(4,128)(2,1)}, bf16[4,36864]{1,0:T(4,128)(2,1)}, u32[]{:S(2)}, u32[]{:S(2)}) collective-permute-start(bf16[4,36864]{1,0:T(4,128)(2,1)} %collective-permute-done.4), channel_id=1, source_target_pairs={{0,8},{8,0},{1,9},{9,1},{2,10},{10,2},{3,11},{11,3},{4,12},{12,4},... | collective-permute-start | bytes 884744 | tf_op jit(solution)/shard_map/ppermute | solution.py:131
  111.2 13.1 %collective-permute-start.8 = (bf16[4,36864]{1,0:T(4,128)(2,1)}, bf16[4,36864]{1,0:T(4,128)(2,1)}, u32[]{:S(2)}, u32[]{:S(2)}) collective-permute-start(bf16[4,36864]{1,0:T(4,128)(2,1)} %collective-permute-done.6), channel_id=1, source_target_pairs={{0,32},{8,488},{16,48},{24,504},{32,64},{40,8},{48,80},{56,24},{64... | collective-permute-start | bytes 884744 | tf_op jit(solution)/shard_map/ppermute | solution.py:128
  113.1 15.8 %collective-permute-start.7 = (bf16[4,36864]{1,0:T(4,128)(2,1)}, bf16[4,36864]{1,0:T(4,128)(2,1)}, u32[]{:S(2)}, u32[]{:S(2)}) collective-permute-start(bf16[4,36864]{1,0:T(4,128)(2,1)} %collective-permute-done.6), channel_id=1, source_target_pairs={{0,8},{8,0},{1,9},{9,1},{2,10},{10,2},{3,11},{11,3},{4,12},{12,4},... | collective-permute-start | bytes 884744 | tf_op jit(solution)/shard_map/ppermute | solution.py:131
  139.9 12.5 %collective-permute-start.10 = (bf16[4,36864]{1,0:T(4,128)(2,1)}, bf16[4,36864]{1,0:T(4,128)(2,1)}, u32[]{:S(2)}, u32[]{:S(2)}) collective-permute-start(bf16[4,36864]{1,0:T(4,128)(2,1)} %collective-permute-done.8), channel_id=1, source_target_pairs={{0,32},{8,488},{16,48},{24,504},{32,64},{40,8},{48,80},{56,24},{64... | collective-permute-start | bytes 884744 | tf_op jit(solution)/shard_map/ppermute | solution.py:128
  141.8 15.3 %collective-permute-start.9 = (bf16[4,36864]{1,0:T(4,128)(2,1)}, bf16[4,36864]{1,0:T(4,128)(2,1)}, u32[]{:S(2)}, u32[]{:S(2)}) collective-permute-start(bf16[4,36864]{1,0:T(4,128)(2,1)} %collective-permute-done.8), channel_id=1, source_target_pairs={{0,8},{8,0},{1,9},{9,1},{2,10},{10,2},{3,11},{11,3},{4,12},{12,4},... | collective-permute-start | bytes 884744 | tf_op jit(solution)/shard_map/ppermute | solution.py:131
  168.0 11.3 %collective-permute-start.12 = (bf16[4,36864]{1,0:T(4,128)(2,1)}, bf16[4,36864]{1,0:T(4,128)(2,1)}, u32[]{:S(2)}, u32[]{:S(2)}) collective-permute-start(bf16[4,36864]{1,0:T(4,128)(2,1)} %collective-permute-done.10), channel_id=1, source_target_pairs={{0,32},{8,488},{16,48},{24,504},{32,64},{40,8},{48,80},{56,24},{64... | collective-permute-start | bytes 884744 | tf_op jit(solution)/shard_map/ppermute | solution.py:128
  169.9 14.0 %collective-permute-start.11 = (bf16[4,36864]{1,0:T(4,128)(2,1)}, bf16[4,36864]{1,0:T(4,128)(2,1)}, u32[]{:S(2)}, u32[]{:S(2)}) collective-permute-start(bf16[4,36864]{1,0:T(4,128)(2,1)} %collective-permute-done.10), channel_id=1, source_target_pairs={{0,8},{8,0},{1,9},{9,1},{2,10},{10,2},{3,11},{11,3},{4,12},{12,4},... | collective-permute-start | bytes 884744 | tf_op jit(solution)/shard_map/ppermute | solution.py:131
  194.9 12.5 %collective-permute-start.14 = (bf16[4,36864]{1,0:T(4,128)(2,1)}, bf16[4,36864]{1,0:T(4,128)(2,1)}, u32[]{:S(2)}, u32[]{:S(2)}) collective-permute-start(bf16[4,36864]{1,0:T(4,128)(2,1)} %collective-permute-done.12), channel_id=1, source_target_pairs={{0,32},{8,488},{16,48},{24,504},{32,64},{40,8},{48,80},{56,24},{64... | collective-permute-start | bytes 884744 | tf_op jit(solution)/shard_map/ppermute | solution.py:128
  197.5 15.2 %collective-permute-start.13 = (bf16[4,36864]{1,0:T(4,128)(2,1)}, bf16[4,36864]{1,0:T(4,128)(2,1)}, u32[]{:S(2)}, u32[]{:S(2)}) collective-permute-start(bf16[4,36864]{1,0:T(4,128)(2,1)} %collective-permute-done.12), channel_id=1, source_target_pairs={{0,8},{8,0},{1,9},{9,1},{2,10},{10,2},{3,11},{11,3},{4,12},{12,4},... | collective-permute-start | bytes 884744 | tf_op jit(solution)/shard_map/ppermute | solution.py:131
  233.9 8.4 %collective-permute-start.15 = (bf16[2,128,384]{2,1,0:T(8,128)(2,1)S(1)}, bf16[2,128,384]{2,1,0:T(8,128)(2,1)S(1)}, u32[]{:S(2)}, u32[]{:S(2)}) collective-permute-start(bf16[2,128,384]{2,1,0:T(8,128)(2,1)S(1)} %slice.249), channel_id=1, source_target_pairs={{0,8},{8,16},{16,24},{24,32},{32,40},{40,48},{48,56},{56,64},{64,7... | collective-permute-start | bytes 589832 | tf_op jit(solution)/shard_map/ppermute | solution.py:27
  238.3 10.6 %collective-permute-start.16 = (bf16[2,128,384]{2,1,0:T(8,128)(2,1)S(1)}, bf16[2,128,384]{2,1,0:T(8,128)(2,1)S(1)}, u32[]{:S(2)}, u32[]{:S(2)}) collective-permute-start(bf16[2,128,384]{2,1,0:T(8,128)(2,1)S(1)} %slice.252), channel_id=1, source_target_pairs={{8,0},{16,8},{24,16},{32,24},{40,32},{48,40},{56,48},{64,56},{72,6... | collective-permute-start | bytes 589832 | tf_op jit(solution)/shard_map/ppermute | solution.py:28
  251.5 20.3 %collective-permute-start.17 = (bf16[2,256,384]{2,1,0:T(8,128)(2,1)S(1)}, bf16[2,256,384]{2,1,0:T(8,128)(2,1)S(1)}, u32[]{:S(2)}, u32[]{:S(2)}) collective-permute-start(bf16[2,256,384]{2,1,0:T(8,128)(2,1)S(1)} %convolution_convert_fusion.1), channel_id=1, source_target_pairs={{0,16},{8,24},{16,32},{24,40},{32,48},{40,56},{48,64},{56,72},{64,... | collective-permute-start | bytes 1179656 | tf_op jit(solution)/shard_map/ppermute | solution.py:36
  254.2 17.7 %collective-permute-start.18 = (bf16[2,256,384]{2,1,0:T(8,128)(2,1)S(1)}, bf16[2,256,384]{2,1,0:T(8,128)(2,1)S(1)}, u32[]{:S(2)}, u32[]{:S(2)}) collective-permute-start(bf16[2,256,384]{2,1,0:T(8,128)(2,1)S(1)} %convolution_convert_fusion), channel_id=1, source_target_pairs={{16,0},{24,8},{32,16},{40,24},{48,32},{56,40},{64,48},{72,56},{80,... | collective-permute-start | bytes 1179656 | tf_op jit(solution)/shard_map/ppermute | solution.py:36
  273.6 12.8 %collective-permute-start.21 = (bf16[1,256,384]{2,1,0:T(8,128)(2,1)S(1)}, bf16[1,256,384]{2,1,0:T(8,128)(2,1)S(1)}, u32[]{:S(2)}, u32[]{:S(2)}) collective-permute-start(bf16[1,256,384]{2,1,0:T(8,128)(2,1)S(1)} %fusion.101), channel_id=1, source_target_pairs={{0,16},{8,24},{16,32},{24,40},{32,48},{40,56},{48,64},{56,72},{64,... | collective-permute-start | bytes 589832 | tf_op jit(solution)/shard_map/ppermute | solution.py:36
  280.1 11.3 %collective-permute-start.20 = (bf16[1,256,384]{2,1,0:T(8,128)(2,1)S(1)}, bf16[1,256,384]{2,1,0:T(8,128)(2,1)S(1)}, u32[]{:S(2)}, u32[]{:S(2)}) collective-permute-start(bf16[1,256,384]{2,1,0:T(8,128)(2,1)S(1)} %fusion.101), channel_id=1, source_target_pairs={{16,0},{24,8},{32,16},{40,24},{48,32},{56,40},{64,48},{72,56},{80,... | collective-permute-start | bytes 589832 | tf_op jit(solution)/shard_map/ppermute | solution.py:36
  283.9 28.6 %collective-permute-start.19 = (bf16[1,256,768]{2,1,0:T(8,128)(2,1)S(1)}, bf16[1,256,768]{2,1,0:T(8,128)(2,1)S(1)}, u32[]{:S(2)}, u32[]{:S(2)}) collective-permute-start(bf16[1,256,768]{2,1,0:T(8,128)(2,1)S(1)} %fusion.55), channel_id=1, source_target_pairs={{7,0},{0,1},{1,2},{2,3},{3,4},{4,5},{5,6},{6,7},{15,8},{8,9},{9,10... | collective-permute-start | bytes 1179656 | tf_op jit(solution)/shard_map/ppermute | solution.py:42
  299.9 9.5 %collective-permute-start.22 = (bf16[1,128,384]{2,1,0:T(8,128)(2,1)S(1)}, bf16[1,128,384]{2,1,0:T(8,128)(2,1)S(1)}, u32[]{:S(2)}, u32[]{:S(2)}) collective-permute-start(bf16[1,128,384]{2,1,0:T(8,128)(2,1)S(1)} %get-tuple-element.2), channel_id=1, source_target_pairs={{8,0},{16,8},{24,16},{32,24},{40,32},{48,40},{56,48},{64,56},{72,6... | collective-permute-start | bytes 294920 | tf_op jit(solution)/shard_map/ppermute | solution.py:28
  310.2 10.9 %collective-permute-start.24 = (bf16[1,256,768]{2,1,0:T(8,128)(2,1)S(1)}, bf16[1,256,768]{2,1,0:T(8,128)(2,1)S(1)}, u32[]{:S(2)}, u32[]{:S(2)}) collective-permute-start(bf16[1,256,768]{2,1,0:T(8,128)(2,1)S(1)} %fusion.24), channel_id=1, source_target_pairs={{1,0},{2,1},{3,2},{4,3},{5,4},{6,5},{7,6},{0,7},{9,8},{10,9},{11,1... | collective-permute-start | bytes 1179656 | tf_op jit(solution)/shard_map/ppermute | solution.py:42
  (9 other events, 71.8 us)

commit v6 on v4

--- a/solution.py
+++ b/solution.py
@@ -115,18 +115,31 @@
     for step in range(1, span - half):
         source = (here - sign * step) % span
         gathered = lax.dynamic_update_slice(gathered, shared[step - 1][None], (source, 0, 0))
-    return gathered.reshape(span * rows, width)
+    return gathered
+
+
+def ring_gather3(block):
+    return ring_gather(block)
 
 
 def gather_weights(conv_weight, proj_weight):
-    flat = jnp.concatenate([conv_weight.reshape(1, -1), proj_weight.reshape(1, -1)], axis=1)
-    flat = lax.all_gather(flat, "core", axis=0, tiled=True)
-    flat = lax.all_gather(flat, "xh", axis=0, tiled=True)
-    flat = ring_gather(flat)
-    shards, split = flat.shape[0], conv_weight.size
-    conv = flat[:, :split].reshape((shards,) + conv_weight.shape[1:])
-    proj = flat[:, split:].reshape((shards,) + proj_weight.shape[1:])
-    conv = jnp.moveaxis(conv, 0, 2).reshape(conv_weight.shape[:3] + (-1, conv_weight.shape[4]))
+    conv, proj = conv_weight[0], proj_weight[0]
+    taps, width = conv.shape[0] * conv.shape[1], conv.shape[3]
+    both = jnp.concatenate([conv.reshape((taps,) + conv.shape[2:]), proj.reshape((-1,) + conv.shape[2:])], axis=0)
+    both = lax.all_gather(lax.all_gather(both, "core", axis=0), "xh", axis=0)
+    conv = both[:, :, :taps].reshape(both.shape[:2] + conv.shape)
+    proj = both[:, :, taps:].reshape(both.shape[:2] + proj.shape)
+    chip = conv.shape[0] * conv.shape[1]
+    conv = jnp.moveaxis(conv.reshape((chip,) + conv.shape[2:]), 0, 2)
+    conv = conv.reshape(taps * chip * conv.shape[3], width)
+    proj = jnp.moveaxis(proj.reshape((chip,) + proj.shape[2:]), 0, 1)
+    proj = proj.reshape(-1, width)
+    conv_rows = conv.shape[0]
+    gathered = ring_gather3(jnp.concatenate([conv, proj], axis=0))
+    span = gathered.shape[0]
+    conv = gathered[:, :conv_rows].reshape((span,) + conv_weight.shape[1:3] + (-1, width))
+    conv = jnp.moveaxis(conv, 0, 2).reshape(conv_weight.shape[:3] + (-1, width))
+    proj = gathered[:, conv_rows:].reshape((span, proj_weight.shape[1], -1, proj_weight.shape[3]))
     proj = jnp.moveaxis(proj, 0, 1).reshape(proj_weight.shape[:2] + (-1, proj_weight.shape[3]))
     return conv, proj
 

time: 218 us -> 199 us (0.913)
  the two profiles are of different devices: /device:TPU:255 before, /device:TPU:127 now
where the time goes in v6:
time: 199 us; the launch traced here: 198 us
  waiting for transfers between devices  80.4 us (40%)
  starting transfers between devices  62.3 us (31%)
  local copies, waits for them, and re-layouts  30.9 us (16%)
  matrix products  10.8 us (5%)
  blocking collectives  9.43 us (5%)
  other arithmetic  2.39 us (1%)
    ppermute x8, waiting for transfers between devices, ring_gather(): current = lax.ppermute(current, SEQ, route)  45.3 us
    ppermute x4, waiting for transfers between devices, from_behind(): return lax.ppermute(block, axis, route)  19.4 us
    ppermute x8, starting transfers between devices, ring_gather(): current = lax.ppermute(current, SEQ, route)  15.8 us
    ppermute x4, starting transfers between devices, from_behind(): return lax.ppermute(block, axis, route)  15.2 us
    ppermute x2, starting transfers between devices, padded(): before = lax.ppermute(last, axis, up)  12.3 us
    ppermute x1, starting transfers between devices, ring_gather(): lax.ppermute(jnp.stack(received[:span - half - 1]), 'core', [(0, 1), (1,...  10.4 us
    all_gather x2, blocking collectives, gather_weights(): both = lax.all_gather(lax.all_gather(both, 'core', axis=0), 'xh', axis=0)  9.43 us
    unnamed x32, local copies, waits for them, and re-layouts  9.18 us
  transfers between devices with their start and end apart: 19, of which 12 were waited for; matrix products, arithmetic and copies ran while one was open for 13% of the time, Pallas kernels for 0%

profile of v6, /device:TPU:127, one launch (start us, length us, event | category | flops | bytes accessed | tf_op | source)
XLA Modules:
  0.0 197.6 jit_solution(9519244608166182633)
XLA Ops:
  4.5 7.2 %all-gather.1 = bf16[4,8,12,384]{3,1,0,2:T(8,128)(2,1)S(1)} all-gather(bf16[2,8,12,384]{3,1,0,2:T(8,128)(2,1)S(1)} %bitcast.168), channel_id=3, replica_groups=mesh['z'=16,'xh'=2,'core'=2,'section'=8] {'xh'}, dimensions={0}, use_global_device_ids=true | all-gather | bytes 442368 | tf_op jit(solution)/shard_map/all_gather | solution.py:129
  14.0 6.9 %collective-permute-done = bf16[384,384]{1,0:T(8,128)(2,1)S(1)} collective-permute-done((bf16[384,384]{1,0:T(8,128)(2,1)S(1)}, bf16[384,384]{1,0:T(8,128)(2,1)S(1)}, u32[]{:S(2)}, u32[]{:S(2)}) %collective-permute-start) | collective-permute-done | bytes 294944 | tf_op jit(solution)/shard_map/ppermute | solution.py:110
  22.9 6.7 %collective-permute-done.1 = bf16[384,384]{1,0:T(8,128)(2,1)S(1)} collective-permute-done((bf16[384,384]{1,0:T(8,128)(2,1)S(1)}, bf16[384,384]{1,0:T(8,128)(2,1)S(1)}, u32[]{:S(2)}, u32[]{:S(2)}) %collective-permute-start.1) | collective-permute-done | bytes 294944 | tf_op jit(solution)/shard_map/ppermute | solution.py:110
  31.6 6.7 %collective-permute-done.2 = bf16[384,384]{1,0:T(8,128)(2,1)S(1)} collective-permute-done((bf16[384,384]{1,0:T(8,128)(2,1)S(1)}, bf16[384,384]{1,0:T(8,128)(2,1)S(1)}, u32[]{:S(2)}, u32[]{:S(2)}) %collective-permute-start.2) | collective-permute-done | bytes 294944 | tf_op jit(solution)/shard_map/ppermute | solution.py:110
  40.4 2.7 %broadcast_in_dim.30 = bf16[16,384,384]{2,1,0:T(8,128)(2,1)} broadcast(bf16[]{:T(256)} %constant.111.clone.1), dimensions={} | broadcast | bytes 4718594 | tf_op jit(solution)/shard_map/broadcast_in_dim | solution.py:106
  43.9 3.1 %collective-permute-done.3 = bf16[384,384]{1,0:T(8,128)(2,1)S(1)} collective-permute-done((bf16[384,384]{1,0:T(8,128)(2,1)S(1)}, bf16[384,384]{1,0:T(8,128)(2,1)S(1)}, u32[]{:S(2)}, u32[]{:S(2)}) %collective-permute-start.3) | collective-permute-done | bytes 294944 | tf_op jit(solution)/shard_map/ppermute | solution.py:110
  50.7 5.0 %collective-permute-done.4 = bf16[384,384]{1,0:T(8,128)(2,1)S(1)} collective-permute-done((bf16[384,384]{1,0:T(8,128)(2,1)S(1)}, bf16[384,384]{1,0:T(8,128)(2,1)S(1)}, u32[]{:S(2)}, u32[]{:S(2)}) %collective-permute-start.4) | collective-permute-done | bytes 294944 | tf_op jit(solution)/shard_map/ppermute | solution.py:110
  59.3 5.0 %collective-permute-done.5 = bf16[384,384]{1,0:T(8,128)(2,1)S(1)} collective-permute-done((bf16[384,384]{1,0:T(8,128)(2,1)S(1)}, bf16[384,384]{1,0:T(8,128)(2,1)S(1)}, u32[]{:S(2)}, u32[]{:S(2)}) %collective-permute-start.5) | collective-permute-done | bytes 294944 | tf_op jit(solution)/shard_map/ppermute | solution.py:110
  68.0 5.0 %collective-permute-done.6 = bf16[384,384]{1,0:T(8,128)(2,1)S(1)} collective-permute-done((bf16[384,384]{1,0:T(8,128)(2,1)S(1)}, bf16[384,384]{1,0:T(8,128)(2,1)S(1)}, u32[]{:S(2)}, u32[]{:S(2)}) %collective-permute-start.6) | collective-permute-done | bytes 294944 | tf_op jit(solution)/shard_map/ppermute | solution.py:110
  73.8 10.4 %collective-permute-start.8 = (bf16[7,384,384]{2,1,0:T(8,128)(2,1)}, bf16[7,384,384]{2,1,0:T(8,128)(2,1)S(1)}, u32[]{:S(2)}, u32[]{:S(2)}) collective-permute-start(bf16[7,384,384]{2,1,0:T(8,128)(2,1)} %get-tuple-element.2), channel_id=1, source_target_pairs={{0,8},{8,0},{1,9},{9,1},{2,10},{10,2},{3,11},{11,3},{4,12},{12,4},... | collective-permute-start | bytes 6193160 | tf_op jit(solution)/shard_map/ppermute | solution.py:114
  84.3 2.4 %collective-permute-start.7 = (bf16[384,384]{1,0:T(8,128)(2,1)S(1)}, bf16[384,384]{1,0:T(8,128)(2,1)S(1)}, u32[]{:S(2)}, u32[]{:S(2)}) collective-permute-start(bf16[384,384]{1,0:T(8,128)(2,1)S(1)} %collective-permute-done.6), channel_id=1, source_target_pairs={{0,32},{8,488},{16,48},{24,504},{32,64},{40,8},{48,80},{56,24},{64... | collective-permute-start | bytes 884744 | tf_op jit(solution)/shard_map/ppermute | solution.py:110
  86.8 6.9 %collective-permute-done.7 = bf16[384,384]{1,0:T(8,128)(2,1)S(1)} collective-permute-done((bf16[384,384]{1,0:T(8,128)(2,1)S(1)}, bf16[384,384]{1,0:T(8,128)(2,1)S(1)}, u32[]{:S(2)}, u32[]{:S(2)}) %collective-permute-start.7) | collective-permute-done | bytes 294944 | tf_op jit(solution)/shard_map/ppermute | solution.py:110
  105.4 6.5 %collective-permute-start.9 = (bf16[2,128,384]{2,1,0:T(8,128)(2,1)}, bf16[2,128,384]{2,1,0:T(8,128)(2,1)}, u32[]{:S(2)}, u32[]{:S(2)}) collective-permute-start(bf16[2,128,384]{2,1,0:T(8,128)(2,1)} %slice.159), channel_id=1, source_target_pairs={{0,8},{8,16},{16,24},{24,32},{32,40},{40,48},{48,56},{56,64},{64,7... | collective-permute-start | bytes 589832 | tf_op jit(solution)/shard_map/ppermute | solution.py:27
  116.1 2.4 %slice.163 = bf16[16,96,384]{2,1,0:T(8,128)(2,1)} slice(bf16[16,384,384]{2,1,0:T(8,128)(2,1)} %slice_dynamic-update-slice_fusion), slice={[0:16], [288:384], [0:384]} | slice | bytes 2359296 | tf_op jit(solution)/shard_map/slice | solution.py:142
  118.5 3.0 %reshape.74 = bf16[16,2,24,768]{3,2,1,0:T(8,128)(2,1)} reshape(bf16[16,96,384]{2,1,0:T(8,128)(2,1)} %slice.163) | data formatting | bytes 2359296 | tf_op jit(solution)/shard_map/reshape | solution.py:142
  126.7 3.8 %collective-permute-start.11 = (bf16[2,256,384]{2,1,0:T(8,128)(2,1)S(1)}, bf16[2,256,384]{2,1,0:T(8,128)(2,1)S(1)}, u32[]{:S(2)}, u32[]{:S(2)}) collective-permute-start(bf16[2,256,384]{2,1,0:T(8,128)(2,1)S(1)} %convolution_convert_fusion.1), channel_id=1, source_target_pairs={{0,16},{8,24},{16,32},{24,40},{32,48},{40,56},{48,64},{56,72},{64,... | collective-permute-start | bytes 1179656 | tf_op jit(solution)/shard_map/ppermute | solution.py:36
  131.2 3.0 %collective-permute-start.12 = (bf16[2,256,384]{2,1,0:T(8,128)(2,1)S(1)}, bf16[2,256,384]{2,1,0:T(8,128)(2,1)S(1)}, u32[]{:S(2)}, u32[]{:S(2)}) collective-permute-start(bf16[2,256,384]{2,1,0:T(8,128)(2,1)S(1)} %convolution_convert_fusion), channel_id=1, source_target_pairs={{16,0},{24,8},{32,16},{40,24},{48,32},{56,40},{64,48},{72,56},{80,... | collective-permute-start | bytes 1179656 | tf_op jit(solution)/shard_map/ppermute | solution.py:36
  134.9 14.0 %collective-permute-done.11 = bf16[2,256,384]{2,1,0:T(8,128)(2,1)S(1)} collective-permute-done((bf16[2,256,384]{2,1,0:T(8,128)(2,1)S(1)}, bf16[2,256,384]{2,1,0:T(8,128)(2,1)S(1)}, u32[]{:S(2)}, u32[]{:S(2)}) %collective-permute-start.11) | collective-permute-done | bytes 393248 | tf_op jit(solution)/shard_map/ppermute | solution.py:36
  149.6 6.5 %collective-permute-start.15 = (bf16[1,256,384]{2,1,0:T(8,128)(2,1)S(1)}, bf16[1,256,384]{2,1,0:T(8,128)(2,1)S(1)}, u32[]{:S(2)}, u32[]{:S(2)}) collective-permute-start(bf16[1,256,384]{2,1,0:T(8,128)(2,1)S(1)} %fusion.101), channel_id=1, source_target_pairs={{0,16},{8,24},{16,32},{24,40},{32,48},{40,56},{48,64},{56,72},{64,... | collective-permute-start | bytes 589832 | tf_op jit(solution)/shard_map/ppermute | solution.py:36
  161.9 5.4 %collective-permute-done.14 = bf16[1,256,384]{2,1,0:T(8,128)(2,1)S(1)} collective-permute-done((bf16[1,256,384]{2,1,0:T(8,128)(2,1)S(1)}, bf16[1,256,384]{2,1,0:T(8,128)(2,1)S(1)}, u32[]{:S(2)}, u32[]{:S(2)}) %collective-permute-start.14) | collective-permute-done | bytes 196640 | tf_op jit(solution)/shard_map/ppermute | solution.py:36
  168.6 5.8 %collective-permute-start.17 = (bf16[1,128,384]{2,1,0:T(8,128)(2,1)S(1)}, bf16[1,128,384]{2,1,0:T(8,128)(2,1)S(1)}, u32[]{:S(2)}, u32[]{:S(2)}) collective-permute-start(bf16[1,128,384]{2,1,0:T(8,128)(2,1)S(1)} %get-tuple-element.17), channel_id=1, source_target_pairs={{0,8},{8,16},{16,24},{24,32},{32,40},{40,48},{48,56},{56,64},{64,7... | collective-permute-start | bytes 294920 | tf_op jit(solution)/shard_map/ppermute | solution.py:27
  177.1 7.2 %collective-permute-done.16 = bf16[1,128,384]{2,1,0:T(8,128)(2,1)S(1)} collective-permute-done((bf16[1,128,384]{2,1,0:T(8,128)(2,1)S(1)}, bf16[1,128,384]{2,1,0:T(8,128)(2,1)S(1)}, u32[]{:S(2)}, u32[]{:S(2)}) %collective-permute-start.16) | collective-permute-done | bytes 98336 | tf_op jit(solution)/shard_map/ppermute | solution.py:28
  185.2 2.5 %collective-permute-start.18 = (bf16[1,256,768]{2,1,0:T(8,128)(2,1)S(1)}, bf16[1,256,768]{2,1,0:T(8,128)(2,1)S(1)}, u32[]{:S(2)}, u32[]{:S(2)}) collective-permute-start(bf16[1,256,768]{2,1,0:T(8,128)(2,1)S(1)} %fusion.24), channel_id=1, source_target_pairs={{1,0},{2,1},{3,2},{4,3},{5,4},{6,5},{7,6},{0,7},{9,8},{10,9},{11,1... | collective-permute-start | bytes 1179656 | tf_op jit(solution)/shard_map/ppermute | solution.py:42
  187.7 8.4 %collective-permute-done.18 = bf16[1,256,768]{2,1,0:T(8,128)(2,1)S(1)} collective-permute-done((bf16[1,256,768]{2,1,0:T(8,128)(2,1)S(1)}, bf16[1,256,768]{2,1,0:T(8,128)(2,1)S(1)}, u32[]{:S(2)}, u32[]{:S(2)}) %collective-permute-start.18) | collective-permute-done | bytes 393248 | tf_op jit(solution)/shard_map/ppermute | solution.py:42
  (98 shorter events, 59.5 us)
Async XLA Ops:
  12.1 8.9 %collective-permute-start = (bf16[384,384]{1,0:T(8,128)(2,1)S(1)}, bf16[384,384]{1,0:T(8,128)(2,1)S(1)}, u32[]{:S(2)}, u32[]{:S(2)}) collective-permute-start(bf16[384,384]{1,0:T(8,128)(2,1)S(1)} %constant_dynamic-update-slice_fusion), channel_id=1, source_target_pairs={{0,32},{8,488},{16,48},{24,504},{32,64},{40,8},{48,80},{56,24},{64... | collective-permute-start | bytes 884744 | tf_op jit(solution)/shard_map/ppermute | solution.py:110
  21.0 8.7 %collective-permute-start.1 = (bf16[384,384]{1,0:T(8,128)(2,1)S(1)}, bf16[384,384]{1,0:T(8,128)(2,1)S(1)}, u32[]{:S(2)}, u32[]{:S(2)}) collective-permute-start(bf16[384,384]{1,0:T(8,128)(2,1)S(1)} %collective-permute-done), channel_id=1, source_target_pairs={{0,32},{8,488},{16,48},{24,504},{32,64},{40,8},{48,80},{56,24},{64... | collective-permute-start | bytes 884744 | tf_op jit(solution)/shard_map/ppermute | solution.py:110
  29.6 8.7 %collective-permute-start.2 = (bf16[384,384]{1,0:T(8,128)(2,1)S(1)}, bf16[384,384]{1,0:T(8,128)(2,1)S(1)}, u32[]{:S(2)}, u32[]{:S(2)}) collective-permute-start(bf16[384,384]{1,0:T(8,128)(2,1)S(1)} %collective-permute-done.1), channel_id=1, source_target_pairs={{0,32},{8,488},{16,48},{24,504},{32,64},{40,8},{48,80},{56,24},{64... | collective-permute-start | bytes 884744 | tf_op jit(solution)/shard_map/ppermute | solution.py:110
  38.3 8.7 %collective-permute-start.3 = (bf16[384,384]{1,0:T(8,128)(2,1)S(1)}, bf16[384,384]{1,0:T(8,128)(2,1)S(1)}, u32[]{:S(2)}, u32[]{:S(2)}) collective-permute-start(bf16[384,384]{1,0:T(8,128)(2,1)S(1)} %collective-permute-done.2), channel_id=1, source_target_pairs={{0,32},{8,488},{16,48},{24,504},{32,64},{40,8},{48,80},{56,24},{64... | collective-permute-start | bytes 884744 | tf_op jit(solution)/shard_map/ppermute | solution.py:110
  47.0 8.7 %collective-permute-start.4 = (bf16[384,384]{1,0:T(8,128)(2,1)S(1)}, bf16[384,384]{1,0:T(8,128)(2,1)S(1)}, u32[]{:S(2)}, u32[]{:S(2)}) collective-permute-start(bf16[384,384]{1,0:T(8,128)(2,1)S(1)} %collective-permute-done.3), channel_id=1, source_target_pairs={{0,32},{8,488},{16,48},{24,504},{32,64},{40,8},{48,80},{56,24},{64... | collective-permute-start | bytes 884744 | tf_op jit(solution)/shard_map/ppermute | solution.py:110
  55.6 8.7 %collective-permute-start.5 = (bf16[384,384]{1,0:T(8,128)(2,1)S(1)}, bf16[384,384]{1,0:T(8,128)(2,1)S(1)}, u32[]{:S(2)}, u32[]{:S(2)}) collective-permute-start(bf16[384,384]{1,0:T(8,128)(2,1)S(1)} %collective-permute-done.4), channel_id=1, source_target_pairs={{0,32},{8,488},{16,48},{24,504},{32,64},{40,8},{48,80},{56,24},{64... | collective-permute-start | bytes 884744 | tf_op jit(solution)/shard_map/ppermute | solution.py:110
  64.3 8.7 %collective-permute-start.6 = (bf16[384,384]{1,0:T(8,128)(2,1)S(1)}, bf16[384,384]{1,0:T(8,128)(2,1)S(1)}, u32[]{:S(2)}, u32[]{:S(2)}) collective-permute-start(bf16[384,384]{1,0:T(8,128)(2,1)S(1)} %collective-permute-done.5), channel_id=1, source_target_pairs={{0,32},{8,488},{16,48},{24,504},{32,64},{40,8},{48,80},{56,24},{64... | collective-permute-start | bytes 884744 | tf_op jit(solution)/shard_map/ppermute | solution.py:110
  73.8 20.6 %collective-permute-start.8 = (bf16[7,384,384]{2,1,0:T(8,128)(2,1)}, bf16[7,384,384]{2,1,0:T(8,128)(2,1)S(1)}, u32[]{:S(2)}, u32[]{:S(2)}) collective-permute-start(bf16[7,384,384]{2,1,0:T(8,128)(2,1)} %get-tuple-element.2), channel_id=1, source_target_pairs={{0,8},{8,0},{1,9},{9,1},{2,10},{10,2},{3,11},{11,3},{4,12},{12,4},... | collective-permute-start | bytes 6193160 | tf_op jit(solution)/shard_map/ppermute | solution.py:114
  84.3 9.4 %collective-permute-start.7 = (bf16[384,384]{1,0:T(8,128)(2,1)S(1)}, bf16[384,384]{1,0:T(8,128)(2,1)S(1)}, u32[]{:S(2)}, u32[]{:S(2)}) collective-permute-start(bf16[384,384]{1,0:T(8,128)(2,1)S(1)} %collective-permute-done.6), channel_id=1, source_target_pairs={{0,32},{8,488},{16,48},{24,504},{32,64},{40,8},{48,80},{56,24},{64... | collective-permute-start | bytes 884744 | tf_op jit(solution)/shard_map/ppermute | solution.py:110
  104.6 7.2 %copy-start = (bf16[2,256,384]{2,1,0:T(8,128)(2,1)}, bf16[2,256,384]{2,1,0:T(8,128)(2,1)S(1)}, u32[]{:S(2)}) copy-start(bf16[2,256,384]{2,1,0:T(8,128)(2,1)S(1)} %convolution_convert_fusion.2) | copy-start | bytes 1179652
  105.4 17.7 %collective-permute-start.9 = (bf16[2,128,384]{2,1,0:T(8,128)(2,1)}, bf16[2,128,384]{2,1,0:T(8,128)(2,1)}, u32[]{:S(2)}, u32[]{:S(2)}) collective-permute-start(bf16[2,128,384]{2,1,0:T(8,128)(2,1)} %slice.159), channel_id=1, source_target_pairs={{0,8},{8,16},{16,24},{24,32},{32,40},{40,48},{48,56},{56,64},{64,7... | collective-permute-start | bytes 589832 | tf_op jit(solution)/shard_map/ppermute | solution.py:27
  112.6 11.5 %collective-permute-start.10 = (bf16[2,128,384]{2,1,0:T(8,128)(2,1)}, bf16[2,128,384]{2,1,0:T(8,128)(2,1)}, u32[]{:S(2)}, u32[]{:S(2)}) collective-permute-start(bf16[2,128,384]{2,1,0:T(8,128)(2,1)} %slice.162), channel_id=1, source_target_pairs={{8,0},{16,8},{24,16},{32,24},{40,32},{48,40},{56,48},{64,56},{72,6... | collective-permute-start | bytes 589832 | tf_op jit(solution)/shard_map/ppermute | solution.py:28
  121.5 2.6 %copy-start.1 = (bf16[2,256,384]{2,1,0:T(8,128)(2,1)S(1)}, bf16[2,256,384]{2,1,0:T(8,128)(2,1)}, u32[]{:S(2)}) copy-start(bf16[2,256,384]{2,1,0:T(8,128)(2,1)} %copy-done) | copy-start | bytes 1179652
  121.5 3.6 %copy-start.4 = (f32[2,256,384]{2,1,0:T(8,128)S(1)}, f32[2,256,384]{2,1,0:T(8,128)}, u32[]{:S(2)}) copy-start(f32[2,256,384]{2,1,0:T(8,128)} %fusion.64) | copy-start | bytes 2359300
  123.0 2.2 %copy-start.6 = (bf16[1,256,768]{2,1,0:T(8,128)(2,1)S(1)}, bf16[1,256,768]{2,1,0:T(8,128)(2,1)}, u32[]{:S(2)}) copy-start(bf16[1,256,768]{2,1,0:T(8,128)(2,1)} %param.5) | copy-start | bytes 1179652
  126.7 22.3 %collective-permute-start.11 = (bf16[2,256,384]{2,1,0:T(8,128)(2,1)S(1)}, bf16[2,256,384]{2,1,0:T(8,128)(2,1)S(1)}, u32[]{:S(2)}, u32[]{:S(2)}) collective-permute-start(bf16[2,256,384]{2,1,0:T(8,128)(2,1)S(1)} %convolution_convert_fusion.1), channel_id=1, source_target_pairs={{0,16},{8,24},{16,32},{24,40},{32,48},{40,56},{48,64},{56,72},{64,... | collective-permute-start | bytes 1179656 | tf_op jit(solution)/shard_map/ppermute | solution.py:36
  131.2 17.8 %collective-permute-start.12 = (bf16[2,256,384]{2,1,0:T(8,128)(2,1)S(1)}, bf16[2,256,384]{2,1,0:T(8,128)(2,1)S(1)}, u32[]{:S(2)}, u32[]{:S(2)}) collective-permute-start(bf16[2,256,384]{2,1,0:T(8,128)(2,1)S(1)} %convolution_convert_fusion), channel_id=1, source_target_pairs={{16,0},{24,8},{32,16},{40,24},{48,32},{56,40},{64,48},{72,56},{80,... | collective-permute-start | bytes 1179656 | tf_op jit(solution)/shard_map/ppermute | solution.py:36
  134.9 14.1 %copy-start.7 = (bf16[1,256,768]{2,1,0:T(8,128)(2,1)S(1)}, bf16[1,256,768]{2,1,0:T(8,128)(2,1)}, u32[]{:S(2)}) copy-start(bf16[1,256,768]{2,1,0:T(8,128)(2,1)} %param.7) | copy-start | bytes 1179652
  149.6 11.9 %collective-permute-start.15 = (bf16[1,256,384]{2,1,0:T(8,128)(2,1)S(1)}, bf16[1,256,384]{2,1,0:T(8,128)(2,1)S(1)}, u32[]{:S(2)}, u32[]{:S(2)}) collective-permute-start(bf16[1,256,384]{2,1,0:T(8,128)(2,1)S(1)} %fusion.101), channel_id=1, source_target_pairs={{0,16},{8,24},{16,32},{24,40},{32,48},{40,56},{48,64},{56,72},{64,... | collective-permute-start | bytes 589832 | tf_op jit(solution)/shard_map/ppermute | solution.py:36
  156.0 11.2 %collective-permute-start.14 = (bf16[1,256,384]{2,1,0:T(8,128)(2,1)S(1)}, bf16[1,256,384]{2,1,0:T(8,128)(2,1)S(1)}, u32[]{:S(2)}, u32[]{:S(2)}) collective-permute-start(bf16[1,256,384]{2,1,0:T(8,128)(2,1)S(1)} %fusion.101), channel_id=1, source_target_pairs={{16,0},{24,8},{32,16},{40,24},{48,32},{56,40},{64,48},{72,56},{80,... | collective-permute-start | bytes 589832 | tf_op jit(solution)/shard_map/ppermute | solution.py:36
  158.8 29.0 %collective-permute-start.13 = (bf16[1,256,768]{2,1,0:T(8,128)(2,1)S(1)}, bf16[1,256,768]{2,1,0:T(8,128)(2,1)S(1)}, u32[]{:S(2)}, u32[]{:S(2)}) collective-permute-start(bf16[1,256,768]{2,1,0:T(8,128)(2,1)S(1)} %fusion.55), channel_id=1, source_target_pairs={{7,0},{0,1},{1,2},{2,3},{3,4},{4,5},{5,6},{6,7},{15,8},{8,9},{9,10... | collective-permute-start | bytes 1179656 | tf_op jit(solution)/shard_map/ppermute | solution.py:42
  168.6 8.1 %collective-permute-start.17 = (bf16[1,128,384]{2,1,0:T(8,128)(2,1)S(1)}, bf16[1,128,384]{2,1,0:T(8,128)(2,1)S(1)}, u32[]{:S(2)}, u32[]{:S(2)}) collective-permute-start(bf16[1,128,384]{2,1,0:T(8,128)(2,1)S(1)} %get-tuple-element.17), channel_id=1, source_target_pairs={{0,8},{8,16},{16,24},{24,32},{32,40},{40,48},{48,56},{56,64},{64,7... | collective-permute-start | bytes 294920 | tf_op jit(solution)/shard_map/ppermute | solution.py:27
  174.8 9.5 %collective-permute-start.16 = (bf16[1,128,384]{2,1,0:T(8,128)(2,1)S(1)}, bf16[1,128,384]{2,1,0:T(8,128)(2,1)S(1)}, u32[]{:S(2)}, u32[]{:S(2)}) collective-permute-start(bf16[1,128,384]{2,1,0:T(8,128)(2,1)S(1)} %get-tuple-element.16), channel_id=1, source_target_pairs={{8,0},{16,8},{24,16},{32,24},{40,32},{48,40},{56,48},{64,56},{72,6... | collective-permute-start | bytes 294920 | tf_op jit(solution)/shard_map/ppermute | solution.py:28
  185.2 10.9 %collective-permute-start.18 = (bf16[1,256,768]{2,1,0:T(8,128)(2,1)S(1)}, bf16[1,256,768]{2,1,0:T(8,128)(2,1)S(1)}, u32[]{:S(2)}, u32[]{:S(2)}) collective-permute-start(bf16[1,256,768]{2,1,0:T(8,128)(2,1)S(1)} %fusion.24), channel_id=1, source_target_pairs={{1,0},{2,1},{3,2},{4,3},{5,4},{6,5},{7,6},{0,7},{9,8},{10,9},{11,1... | collective-permute-start | bytes 1179656 | tf_op jit(solution)/shard_map/ppermute | solution.py:42
  (5 other events, 6.6 us)

commit v7 on v6

--- a/solution.py
+++ b/solution.py
@@ -106,8 +106,11 @@
     gathered = jnp.zeros((span, rows, width), block.dtype)
     gathered = lax.dynamic_update_slice(gathered, block[None], (here, 0, 0))
     current, received = block, []
+    cut = rows // 2
     for step in range(1, half + 1):
-        current = lax.ppermute(current, SEQ, route)
+        current = jnp.concatenate(
+            [lax.ppermute(current[:cut], SEQ, route), lax.ppermute(current[cut:], SEQ, route)], axis=0
+        )
         received.append(current)
         source = (here + sign * step) % span
         gathered = lax.dynamic_update_slice(gathered, current[None], (source, 0, 0))

time: 199 us -> 196 us (0.985)
  waiting for transfers between devices: 80.4 us -> 44.3 us
  starting transfers between devices: 62.3 us -> 95.7 us
  other arithmetic: 2.39 us -> 9.33 us
  local copies, waits for them, and re-layouts: 30.9 us -> 24 us
    ppermute x8 -> x16, waiting for transfers between devices: 45.3 us -> 10.2 us  [the longest x8 6.19 us: ring_gather(): lax.ppermute(current[cut:], SEQ, route)]
    ppermute x8 -> x16, starting transfers between devices: 15.8 us -> 49.3 us  [the longest x8 30.7 us: ring_gather(): lax.ppermute(current[:cut], SEQ, route)]
    unnamed x0 -> x6, other arithmetic: none -> 5.31 us
    unnamed x32 -> x26, local copies, waits for them, and re-layouts: 9.18 us -> 3.87 us
  transfers between devices with their start and end apart: 19 -> 27, of which waited for: 12 -> 11; matrix products, arithmetic and copies ran while one was open for 13% -> 13% of each run, Pallas kernels for 0% -> 0%
where the time goes in v7:
time: 196 us; the launch traced here: 195 us
  starting transfers between devices  95.7 us (49%)
  waiting for transfers between devices  44.3 us (23%)
  local copies, waits for them, and re-layouts  24 us (12%)
  matrix products  10.8 us (6%)
  blocking collectives  9.43 us (5%)
  other arithmetic  9.33 us (5%)
    ppermute x8, starting transfers between devices, ring_gather(): lax.ppermute(current[:cut], SEQ, route)  30.7 us
    ppermute x8, starting transfers between devices, ring_gather(): lax.ppermute(current[cut:], SEQ, route)  18.6 us
    ppermute x4, waiting for transfers between devices, from_behind(): return lax.ppermute(block, axis, route)  18.3 us
    ppermute x4, starting transfers between devices, from_behind(): return lax.ppermute(block, axis, route)  16.2 us
    ppermute x2, starting transfers between devices, padded(): before = lax.ppermute(last, axis, up)  11.4 us
    ppermute x1, starting transfers between devices, ring_gather(): lax.ppermute(jnp.stack(received[:span - half - 1]), 'core', [(0, 1), (1,...  10.2 us
    all_gather x2, blocking collectives, gather_weights(): both = lax.all_gather(lax.all_gather(both, 'core', axis=0), 'xh', axis=0)  9.43 us
    ppermute x2, waiting for transfers between devices, from_behind_2(): return lax.ppermute(block, axis, route)  8.44 us
  transfers between devices with their start and end apart: 27, of which 11 were waited for; matrix products, arithmetic and copies ran while one was open for 13% of the time, Pallas kernels for 0%

profile of v7, /device:TPU:127, one launch (start us, length us, event | category | flops | bytes accessed | tf_op | source)
XLA Modules:
  0.0 195.1 jit_solution(7108327394260631211)
XLA Ops:
  4.5 7.2 %all-gather.1 = bf16[4,8,12,384]{3,1,0,2:T(8,128)(2,1)S(1)} all-gather(bf16[2,8,12,384]{3,1,0,2:T(8,128)(2,1)S(1)} %bitcast.191), channel_id=3, replica_groups=mesh['z'=16,'xh'=2,'core'=2,'section'=8] {'xh'}, dimensions={0}, use_global_device_ids=true | all-gather | bytes 442368 | tf_op jit(solution)/shard_map/all_gather | solution.py:132
  16.0 3.4 %collective-permute-done.1 = bf16[192,384]{1,0:T(8,128)(2,1)S(1)} collective-permute-done((bf16[192,384]{1,0:T(8,128)(2,1)S(1)}, bf16[192,384]{1,0:T(8,128)(2,1)S(1)}, u32[]{:S(2)}, u32[]{:S(2)}) %collective-permute-start.1) | collective-permute-done | bytes 147488 | tf_op jit(solution)/shard_map/ppermute | solution.py:112
  21.4 7.2 %collective-permute-start.2 = (bf16[192,384]{1,0:T(8,128)(2,1)S(1)}, bf16[192,384]{1,0:T(8,128)(2,1)S(1)}, u32[]{:S(2)}, u32[]{:S(2)}) collective-permute-start(bf16[192,384]{1,0:T(8,128)(2,1)S(1)} %collective-permute-done), channel_id=1, source_target_pairs={{0,32},{8,488},{16,48},{24,504},{32,64},{40,8},{48,80},{56,24},{64... | collective-permute-start | bytes 442376 | tf_op jit(solution)/shard_map/ppermute | solution.py:112
  28.6 2.6 %collective-permute-start.5 = (bf16[192,384]{1,0:T(8,128)(2,1)S(1)}, bf16[192,384]{1,0:T(8,128)(2,1)S(1)}, u32[]{:S(2)}, u32[]{:S(2)}) collective-permute-start(bf16[192,384]{1,0:T(8,128)(2,1)S(1)} %collective-permute-done.3), channel_id=1, source_target_pairs={{0,32},{8,488},{16,48},{24,504},{32,64},{40,8},{48,80},{56,24},{64... | collective-permute-start | bytes 442376 | tf_op jit(solution)/shard_map/ppermute | solution.py:112
  31.2 4.4 %collective-permute-start.4 = (bf16[192,384]{1,0:T(8,128)(2,1)S(1)}, bf16[192,384]{1,0:T(8,128)(2,1)S(1)}, u32[]{:S(2)}, u32[]{:S(2)}) collective-permute-start(bf16[192,384]{1,0:T(8,128)(2,1)S(1)} %collective-permute-done.2), channel_id=1, source_target_pairs={{0,32},{8,488},{16,48},{24,504},{32,64},{40,8},{48,80},{56,24},{64... | collective-permute-start | bytes 442376 | tf_op jit(solution)/shard_map/ppermute | solution.py:112
  35.8 2.6 %collective-permute-start.7 = (bf16[192,384]{1,0:T(8,128)(2,1)S(1)}, bf16[192,384]{1,0:T(8,128)(2,1)S(1)}, u32[]{:S(2)}, u32[]{:S(2)}) collective-permute-start(bf16[192,384]{1,0:T(8,128)(2,1)S(1)} %collective-permute-done.5), channel_id=1, source_target_pairs={{0,32},{8,488},{16,48},{24,504},{32,64},{40,8},{48,80},{56,24},{64... | collective-permute-start | bytes 442376 | tf_op jit(solution)/shard_map/ppermute | solution.py:112
  38.5 4.4 %collective-permute-start.6 = (bf16[192,384]{1,0:T(8,128)(2,1)S(1)}, bf16[192,384]{1,0:T(8,128)(2,1)S(1)}, u32[]{:S(2)}, u32[]{:S(2)}) collective-permute-start(bf16[192,384]{1,0:T(8,128)(2,1)S(1)} %collective-permute-done.4), channel_id=1, source_target_pairs={{0,32},{8,488},{16,48},{24,504},{32,64},{40,8},{48,80},{56,24},{64... | collective-permute-start | bytes 442376 | tf_op jit(solution)/shard_map/ppermute | solution.py:112
  42.9 2.8 %broadcast_in_dim.30 = bf16[16,384,384]{2,1,0:T(8,128)(2,1)} broadcast(bf16[]{:T(256)} %constant.111.clone.1), dimensions={} | broadcast | bytes 4718594 | tf_op jit(solution)/shard_map/broadcast_in_dim | solution.py:106
  46.4 2.7 %collective-permute-start.9 = (bf16[192,384]{1,0:T(8,128)(2,1)S(1)}, bf16[192,384]{1,0:T(8,128)(2,1)S(1)}, u32[]{:S(2)}, u32[]{:S(2)}) collective-permute-start(bf16[192,384]{1,0:T(8,128)(2,1)S(1)} %collective-permute-done.7), channel_id=1, source_target_pairs={{0,32},{8,488},{16,48},{24,504},{32,64},{40,8},{48,80},{56,24},{64... | collective-permute-start | bytes 442376 | tf_op jit(solution)/shard_map/ppermute | solution.py:112
  49.0 4.2 %collective-permute-start.8 = (bf16[192,384]{1,0:T(8,128)(2,1)S(1)}, bf16[192,384]{1,0:T(8,128)(2,1)S(1)}, u32[]{:S(2)}, u32[]{:S(2)}) collective-permute-start(bf16[192,384]{1,0:T(8,128)(2,1)S(1)} %collective-permute-done.6), channel_id=1, source_target_pairs={{0,32},{8,488},{16,48},{24,504},{32,64},{40,8},{48,80},{56,24},{64... | collective-permute-start | bytes 442376 | tf_op jit(solution)/shard_map/ppermute | solution.py:112
  55.1 2.6 %collective-permute-start.11 = (bf16[192,384]{1,0:T(8,128)(2,1)S(1)}, bf16[192,384]{1,0:T(8,128)(2,1)S(1)}, u32[]{:S(2)}, u32[]{:S(2)}) collective-permute-start(bf16[192,384]{1,0:T(8,128)(2,1)S(1)} %collective-permute-done.9), channel_id=1, source_target_pairs={{0,32},{8,488},{16,48},{24,504},{32,64},{40,8},{48,80},{56,24},{64... | collective-permute-start | bytes 442376 | tf_op jit(solution)/shard_map/ppermute | solution.py:112
  64.8 3.8 %collective-permute-start.12 = (bf16[192,384]{1,0:T(8,128)(2,1)S(1)}, bf16[192,384]{1,0:T(8,128)(2,1)S(1)}, u32[]{:S(2)}, u32[]{:S(2)}) collective-permute-start(bf16[192,384]{1,0:T(8,128)(2,1)S(1)} %collective-permute-done.10), channel_id=1, source_target_pairs={{0,32},{8,488},{16,48},{24,504},{32,64},{40,8},{48,80},{56,24},{64... | collective-permute-start | bytes 442376 | tf_op jit(solution)/shard_map/ppermute | solution.py:112
  72.8 10.2 %collective-permute-start.16 = (bf16[7,384,384]{2,1,0:T(8,128)(2,1)}, bf16[7,384,384]{2,1,0:T(8,128)(2,1)S(1)}, u32[]{:S(2)}, u32[]{:S(2)}) collective-permute-start(bf16[7,384,384]{2,1,0:T(8,128)(2,1)} %get-tuple-element.2), channel_id=1, source_target_pairs={{0,8},{8,0},{1,9},{9,1},{2,10},{10,2},{3,11},{11,3},{4,12},{12,4},... | collective-permute-start | bytes 6193160 | tf_op jit(solution)/shard_map/ppermute | solution.py:117
  103.9 5.5 %collective-permute-start.17 = (bf16[2,128,384]{2,1,0:T(8,128)(2,1)}, bf16[2,128,384]{2,1,0:T(8,128)(2,1)}, u32[]{:S(2)}, u32[]{:S(2)}) collective-permute-start(bf16[2,128,384]{2,1,0:T(8,128)(2,1)} %slice.169), channel_id=1, source_target_pairs={{0,8},{8,16},{16,24},{24,32},{32,40},{40,48},{48,56},{56,64},{64,7... | collective-permute-start | bytes 589832 | tf_op jit(solution)/shard_map/ppermute | solution.py:27
  116.1 3.0 %reshape.74 = bf16[16,2,24,768]{3,2,1,0:T(8,128)(2,1)} reshape(bf16[16,96,384]{2,1,0:T(8,128)(2,1)} %slice.173) | data formatting | bytes 2359296 | tf_op jit(solution)/shard_map/reshape | solution.py:145
  124.3 3.7 %collective-permute-start.19 = (bf16[2,256,384]{2,1,0:T(8,128)(2,1)S(1)}, bf16[2,256,384]{2,1,0:T(8,128)(2,1)S(1)}, u32[]{:S(2)}, u32[]{:S(2)}) collective-permute-start(bf16[2,256,384]{2,1,0:T(8,128)(2,1)S(1)} %convolution_convert_fusion.1), channel_id=1, source_target_pairs={{0,16},{8,24},{16,32},{24,40},{32,48},{40,56},{48,64},{56,72},{64,... | collective-permute-start | bytes 1179656 | tf_op jit(solution)/shard_map/ppermute | solution.py:36
  128.7 3.1 %collective-permute-start.20 = (bf16[2,256,384]{2,1,0:T(8,128)(2,1)S(1)}, bf16[2,256,384]{2,1,0:T(8,128)(2,1)S(1)}, u32[]{:S(2)}, u32[]{:S(2)}) collective-permute-start(bf16[2,256,384]{2,1,0:T(8,128)(2,1)S(1)} %convolution_convert_fusion), channel_id=1, source_target_pairs={{16,0},{24,8},{32,16},{40,24},{48,32},{56,40},{64,48},{72,56},{80,... | collective-permute-start | bytes 1179656 | tf_op jit(solution)/shard_map/ppermute | solution.py:36
  132.5 4.3 %collective-permute-done.19 = bf16[2,256,384]{2,1,0:T(8,128)(2,1)S(1)} collective-permute-done((bf16[2,256,384]{2,1,0:T(8,128)(2,1)S(1)}, bf16[2,256,384]{2,1,0:T(8,128)(2,1)S(1)}, u32[]{:S(2)}, u32[]{:S(2)}) %collective-permute-start.19) | collective-permute-done | bytes 393248 | tf_op jit(solution)/shard_map/ppermute | solution.py:36
  136.8 8.7 %collective-permute-done.20 = bf16[2,256,384]{2,1,0:T(8,128)(2,1)S(1)} collective-permute-done((bf16[2,256,384]{2,1,0:T(8,128)(2,1)S(1)}, bf16[2,256,384]{2,1,0:T(8,128)(2,1)S(1)}, u32[]{:S(2)}, u32[]{:S(2)}) %collective-permute-start.20) | collective-permute-done | bytes 393248 | tf_op jit(solution)/shard_map/ppermute | solution.py:36
  146.1 7.5 %collective-permute-start.23 = (bf16[1,256,384]{2,1,0:T(8,128)(2,1)S(1)}, bf16[1,256,384]{2,1,0:T(8,128)(2,1)S(1)}, u32[]{:S(2)}, u32[]{:S(2)}) collective-permute-start(bf16[1,256,384]{2,1,0:T(8,128)(2,1)S(1)} %fusion.101), channel_id=1, source_target_pairs={{0,16},{8,24},{16,32},{24,40},{32,48},{40,56},{48,64},{56,72},{64,... | collective-permute-start | bytes 589832 | tf_op jit(solution)/shard_map/ppermute | solution.py:36
  159.4 5.4 %collective-permute-done.22 = bf16[1,256,384]{2,1,0:T(8,128)(2,1)S(1)} collective-permute-done((bf16[1,256,384]{2,1,0:T(8,128)(2,1)S(1)}, bf16[1,256,384]{2,1,0:T(8,128)(2,1)S(1)}, u32[]{:S(2)}, u32[]{:S(2)}) %collective-permute-start.22) | collective-permute-done | bytes 196640 | tf_op jit(solution)/shard_map/ppermute | solution.py:36
  166.1 5.8 %collective-permute-start.25 = (bf16[1,128,384]{2,1,0:T(8,128)(2,1)S(1)}, bf16[1,128,384]{2,1,0:T(8,128)(2,1)S(1)}, u32[]{:S(2)}, u32[]{:S(2)}) collective-permute-start(bf16[1,128,384]{2,1,0:T(8,128)(2,1)S(1)} %get-tuple-element.17), channel_id=1, source_target_pairs={{0,8},{8,16},{16,24},{24,32},{32,40},{40,48},{48,56},{56,64},{64,7... | collective-permute-start | bytes 294920 | tf_op jit(solution)/shard_map/ppermute | solution.py:27
  174.7 7.2 %collective-permute-done.24 = bf16[1,128,384]{2,1,0:T(8,128)(2,1)S(1)} collective-permute-done((bf16[1,128,384]{2,1,0:T(8,128)(2,1)S(1)}, bf16[1,128,384]{2,1,0:T(8,128)(2,1)S(1)}, u32[]{:S(2)}, u32[]{:S(2)}) %collective-permute-start.24) | collective-permute-done | bytes 98336 | tf_op jit(solution)/shard_map/ppermute | solution.py:28
  185.2 8.4 %collective-permute-done.26 = bf16[1,256,768]{2,1,0:T(8,128)(2,1)S(1)} collective-permute-done((bf16[1,256,768]{2,1,0:T(8,128)(2,1)S(1)}, bf16[1,256,768]{2,1,0:T(8,128)(2,1)S(1)}, u32[]{:S(2)}, u32[]{:S(2)}) %collective-permute-start.26) | collective-permute-done | bytes 393248 | tf_op jit(solution)/shard_map/ppermute | solution.py:42
  (116 shorter events, 72.8 us)
Async XLA Ops:
  12.1 7.3 %collective-permute-start.1 = (bf16[192,384]{1,0:T(8,128)(2,1)S(1)}, bf16[192,384]{1,0:T(8,128)(2,1)S(1)}, u32[]{:S(2)}, u32[]{:S(2)}) collective-permute-start(bf16[192,384]{1,0:T(8,128)(2,1)S(1)} %slice.159), channel_id=1, source_target_pairs={{0,32},{8,488},{16,48},{24,504},{32,64},{40,8},{48,80},{56,24},{64... | collective-permute-start | bytes 442376 | tf_op jit(solution)/shard_map/ppermute | solution.py:112
  14.1 7.3 %collective-permute-start = (bf16[192,384]{1,0:T(8,128)(2,1)S(1)}, bf16[192,384]{1,0:T(8,128)(2,1)S(1)}, u32[]{:S(2)}, u32[]{:S(2)}) collective-permute-start(bf16[192,384]{1,0:T(8,128)(2,1)S(1)} %slice.158), channel_id=1, source_target_pairs={{0,32},{8,488},{16,48},{24,504},{32,64},{40,8},{48,80},{56,24},{64... | collective-permute-start | bytes 442376 | tf_op jit(solution)/shard_map/ppermute | solution.py:112
  19.4 9.1 %collective-permute-start.3 = (bf16[192,384]{1,0:T(8,128)(2,1)S(1)}, bf16[192,384]{1,0:T(8,128)(2,1)S(1)}, u32[]{:S(2)}, u32[]{:S(2)}) collective-permute-start(bf16[192,384]{1,0:T(8,128)(2,1)S(1)} %collective-permute-done.1), channel_id=1, source_target_pairs={{0,32},{8,488},{16,48},{24,504},{32,64},{40,8},{48,80},{56,24},{64... | collective-permute-start | bytes 442376 | tf_op jit(solution)/shard_map/ppermute | solution.py:112
  21.4 9.8 %collective-permute-start.2 = (bf16[192,384]{1,0:T(8,128)(2,1)S(1)}, bf16[192,384]{1,0:T(8,128)(2,1)S(1)}, u32[]{:S(2)}, u32[]{:S(2)}) collective-permute-start(bf16[192,384]{1,0:T(8,128)(2,1)S(1)} %collective-permute-done), channel_id=1, source_target_pairs={{0,32},{8,488},{16,48},{24,504},{32,64},{40,8},{48,80},{56,24},{64... | collective-permute-start | bytes 442376 | tf_op jit(solution)/shard_map/ppermute | solution.py:112
  28.6 7.2 %collective-permute-start.5 = (bf16[192,384]{1,0:T(8,128)(2,1)S(1)}, bf16[192,384]{1,0:T(8,128)(2,1)S(1)}, u32[]{:S(2)}, u32[]{:S(2)}) collective-permute-start(bf16[192,384]{1,0:T(8,128)(2,1)S(1)} %collective-permute-done.3), channel_id=1, source_target_pairs={{0,32},{8,488},{16,48},{24,504},{32,64},{40,8},{48,80},{56,24},{64... | collective-permute-start | bytes 442376 | tf_op jit(solution)/shard_map/ppermute | solution.py:112
  31.2 7.2 %collective-permute-start.4 = (bf16[192,384]{1,0:T(8,128)(2,1)S(1)}, bf16[192,384]{1,0:T(8,128)(2,1)S(1)}, u32[]{:S(2)}, u32[]{:S(2)}) collective-permute-start(bf16[192,384]{1,0:T(8,128)(2,1)S(1)} %collective-permute-done.2), channel_id=1, source_target_pairs={{0,32},{8,488},{16,48},{24,504},{32,64},{40,8},{48,80},{56,24},{64... | collective-permute-start | bytes 442376 | tf_op jit(solution)/shard_map/ppermute | solution.py:112
  35.8 10.6 %collective-permute-start.7 = (bf16[192,384]{1,0:T(8,128)(2,1)S(1)}, bf16[192,384]{1,0:T(8,128)(2,1)S(1)}, u32[]{:S(2)}, u32[]{:S(2)}) collective-permute-start(bf16[192,384]{1,0:T(8,128)(2,1)S(1)} %collective-permute-done.5), channel_id=1, source_target_pairs={{0,32},{8,488},{16,48},{24,504},{32,64},{40,8},{48,80},{56,24},{64... | collective-permute-start | bytes 442376 | tf_op jit(solution)/shard_map/ppermute | solution.py:112
  38.5 10.6 %collective-permute-start.6 = (bf16[192,384]{1,0:T(8,128)(2,1)S(1)}, bf16[192,384]{1,0:T(8,128)(2,1)S(1)}, u32[]{:S(2)}, u32[]{:S(2)}) collective-permute-start(bf16[192,384]{1,0:T(8,128)(2,1)S(1)} %collective-permute-done.4), channel_id=1, source_target_pairs={{0,32},{8,488},{16,48},{24,504},{32,64},{40,8},{48,80},{56,24},{64... | collective-permute-start | bytes 442376 | tf_op jit(solution)/shard_map/ppermute | solution.py:112
  46.4 8.7 %collective-permute-start.9 = (bf16[192,384]{1,0:T(8,128)(2,1)S(1)}, bf16[192,384]{1,0:T(8,128)(2,1)S(1)}, u32[]{:S(2)}, u32[]{:S(2)}) collective-permute-start(bf16[192,384]{1,0:T(8,128)(2,1)S(1)} %collective-permute-done.7), channel_id=1, source_target_pairs={{0,32},{8,488},{16,48},{24,504},{32,64},{40,8},{48,80},{56,24},{64... | collective-permute-start | bytes 442376 | tf_op jit(solution)/shard_map/ppermute | solution.py:112
  49.0 8.6 %collective-permute-start.8 = (bf16[192,384]{1,0:T(8,128)(2,1)S(1)}, bf16[192,384]{1,0:T(8,128)(2,1)S(1)}, u32[]{:S(2)}, u32[]{:S(2)}) collective-permute-start(bf16[192,384]{1,0:T(8,128)(2,1)S(1)} %collective-permute-done.6), channel_id=1, source_target_pairs={{0,32},{8,488},{16,48},{24,504},{32,64},{40,8},{48,80},{56,24},{64... | collective-permute-start | bytes 442376 | tf_op jit(solution)/shard_map/ppermute | solution.py:112
  57.7 7.1 %collective-permute-start.10 = (bf16[192,384]{1,0:T(8,128)(2,1)S(1)}, bf16[192,384]{1,0:T(8,128)(2,1)S(1)}, u32[]{:S(2)}, u32[]{:S(2)}) collective-permute-start(bf16[192,384]{1,0:T(8,128)(2,1)S(1)} %collective-permute-done.8), channel_id=1, source_target_pairs={{0,32},{8,488},{16,48},{24,504},{32,64},{40,8},{48,80},{56,24},{64... | collective-permute-start | bytes 442376 | tf_op jit(solution)/shard_map/ppermute | solution.py:112
  62.2 8.2 %collective-permute-start.13 = (bf16[192,384]{1,0:T(8,128)(2,1)S(1)}, bf16[192,384]{1,0:T(8,128)(2,1)S(1)}, u32[]{:S(2)}, u32[]{:S(2)}) collective-permute-start(bf16[192,384]{1,0:T(8,128)(2,1)S(1)} %collective-permute-done.11), channel_id=1, source_target_pairs={{0,32},{8,488},{16,48},{24,504},{32,64},{40,8},{48,80},{56,24},{64... | collective-permute-start | bytes 442376 | tf_op jit(solution)/shard_map/ppermute | solution.py:112
  72.8 20.1 %collective-permute-start.16 = (bf16[7,384,384]{2,1,0:T(8,128)(2,1)}, bf16[7,384,384]{2,1,0:T(8,128)(2,1)S(1)}, u32[]{:S(2)}, u32[]{:S(2)}) collective-permute-start(bf16[7,384,384]{2,1,0:T(8,128)(2,1)} %get-tuple-element.2), channel_id=1, source_target_pairs={{0,8},{8,0},{1,9},{9,1},{2,10},{10,2},{3,11},{11,3},{4,12},{12,4},... | collective-permute-start | bytes 6193160 | tf_op jit(solution)/shard_map/ppermute | solution.py:117
  83.0 7.1 %collective-permute-start.15 = (bf16[192,384]{1,0:T(8,128)(2,1)S(1)}, bf16[192,384]{1,0:T(8,128)(2,1)S(1)}, u32[]{:S(2)}, u32[]{:S(2)}) collective-permute-start(bf16[192,384]{1,0:T(8,128)(2,1)S(1)} %collective-permute-done.13), channel_id=1, source_target_pairs={{0,32},{8,488},{16,48},{24,504},{32,64},{40,8},{48,80},{56,24},{64... | collective-permute-start | bytes 442376 | tf_op jit(solution)/shard_map/ppermute | solution.py:112
  103.9 16.7 %collective-permute-start.17 = (bf16[2,128,384]{2,1,0:T(8,128)(2,1)}, bf16[2,128,384]{2,1,0:T(8,128)(2,1)}, u32[]{:S(2)}, u32[]{:S(2)}) collective-permute-start(bf16[2,128,384]{2,1,0:T(8,128)(2,1)} %slice.169), channel_id=1, source_target_pairs={{0,8},{8,16},{16,24},{24,32},{32,40},{40,48},{48,56},{56,64},{64,7... | collective-permute-start | bytes 589832 | tf_op jit(solution)/shard_map/ppermute | solution.py:27
  110.1 11.5 %collective-permute-start.18 = (bf16[2,128,384]{2,1,0:T(8,128)(2,1)}, bf16[2,128,384]{2,1,0:T(8,128)(2,1)}, u32[]{:S(2)}, u32[]{:S(2)}) collective-permute-start(bf16[2,128,384]{2,1,0:T(8,128)(2,1)} %slice.172), channel_id=1, source_target_pairs={{8,0},{16,8},{24,16},{32,24},{40,32},{48,40},{56,48},{64,56},{72,6... | collective-permute-start | bytes 589832 | tf_op jit(solution)/shard_map/ppermute | solution.py:28
  124.3 12.5 %collective-permute-start.19 = (bf16[2,256,384]{2,1,0:T(8,128)(2,1)S(1)}, bf16[2,256,384]{2,1,0:T(8,128)(2,1)S(1)}, u32[]{:S(2)}, u32[]{:S(2)}) collective-permute-start(bf16[2,256,384]{2,1,0:T(8,128)(2,1)S(1)} %convolution_convert_fusion.1), channel_id=1, source_target_pairs={{0,16},{8,24},{16,32},{24,40},{32,48},{40,56},{48,64},{56,72},{64,... | collective-permute-start | bytes 1179656 | tf_op jit(solution)/shard_map/ppermute | solution.py:36
  128.7 16.8 %collective-permute-start.20 = (bf16[2,256,384]{2,1,0:T(8,128)(2,1)S(1)}, bf16[2,256,384]{2,1,0:T(8,128)(2,1)S(1)}, u32[]{:S(2)}, u32[]{:S(2)}) collective-permute-start(bf16[2,256,384]{2,1,0:T(8,128)(2,1)S(1)} %convolution_convert_fusion), channel_id=1, source_target_pairs={{16,0},{24,8},{32,16},{40,24},{48,32},{56,40},{64,48},{72,56},{80,... | collective-permute-start | bytes 1179656 | tf_op jit(solution)/shard_map/ppermute | solution.py:36
  146.1 12.9 %collective-permute-start.23 = (bf16[1,256,384]{2,1,0:T(8,128)(2,1)S(1)}, bf16[1,256,384]{2,1,0:T(8,128)(2,1)S(1)}, u32[]{:S(2)}, u32[]{:S(2)}) collective-permute-start(bf16[1,256,384]{2,1,0:T(8,128)(2,1)S(1)} %fusion.101), channel_id=1, source_target_pairs={{0,16},{8,24},{16,32},{24,40},{32,48},{40,56},{48,64},{56,72},{64,... | collective-permute-start | bytes 589832 | tf_op jit(solution)/shard_map/ppermute | solution.py:36
  153.6 11.2 %collective-permute-start.22 = (bf16[1,256,384]{2,1,0:T(8,128)(2,1)S(1)}, bf16[1,256,384]{2,1,0:T(8,128)(2,1)S(1)}, u32[]{:S(2)}, u32[]{:S(2)}) collective-permute-start(bf16[1,256,384]{2,1,0:T(8,128)(2,1)S(1)} %fusion.101), channel_id=1, source_target_pairs={{16,0},{24,8},{32,16},{40,24},{48,32},{56,40},{64,48},{72,56},{80,... | collective-permute-start | bytes 589832 | tf_op jit(solution)/shard_map/ppermute | solution.py:36
  156.3 28.9 %collective-permute-start.21 = (bf16[1,256,768]{2,1,0:T(8,128)(2,1)S(1)}, bf16[1,256,768]{2,1,0:T(8,128)(2,1)S(1)}, u32[]{:S(2)}, u32[]{:S(2)}) collective-permute-start(bf16[1,256,768]{2,1,0:T(8,128)(2,1)S(1)} %fusion.55), channel_id=1, source_target_pairs={{7,0},{0,1},{1,2},{2,3},{3,4},{4,5},{5,6},{6,7},{15,8},{8,9},{9,10... | collective-permute-start | bytes 1179656 | tf_op jit(solution)/shard_map/ppermute | solution.py:42
  166.1 8.2 %collective-permute-start.25 = (bf16[1,128,384]{2,1,0:T(8,128)(2,1)S(1)}, bf16[1,128,384]{2,1,0:T(8,128)(2,1)S(1)}, u32[]{:S(2)}, u32[]{:S(2)}) collective-permute-start(bf16[1,128,384]{2,1,0:T(8,128)(2,1)S(1)} %get-tuple-element.17), channel_id=1, source_target_pairs={{0,8},{8,16},{16,24},{24,32},{32,40},{40,48},{48,56},{56,64},{64,7... | collective-permute-start | bytes 294920 | tf_op jit(solution)/shard_map/ppermute | solution.py:27
  172.4 9.5 %collective-permute-start.24 = (bf16[1,128,384]{2,1,0:T(8,128)(2,1)S(1)}, bf16[1,128,384]{2,1,0:T(8,128)(2,1)S(1)}, u32[]{:S(2)}, u32[]{:S(2)}) collective-permute-start(bf16[1,128,384]{2,1,0:T(8,128)(2,1)S(1)} %get-tuple-element.16), channel_id=1, source_target_pairs={{8,0},{16,8},{24,16},{32,24},{40,32},{48,40},{56,48},{64,56},{72,6... | collective-permute-start | bytes 294920 | tf_op jit(solution)/shard_map/ppermute | solution.py:28
  182.7 10.9 %collective-permute-start.26 = (bf16[1,256,768]{2,1,0:T(8,128)(2,1)S(1)}, bf16[1,256,768]{2,1,0:T(8,128)(2,1)S(1)}, u32[]{:S(2)}, u32[]{:S(2)}) collective-permute-start(bf16[1,256,768]{2,1,0:T(8,128)(2,1)S(1)} %fusion.24), channel_id=1, source_target_pairs={{1,0},{2,1},{3,2},{4,3},{5,4},{6,5},{7,6},{0,7},{9,8},{10,9},{11,1... | collective-permute-start | bytes 1179656 | tf_op jit(solution)/shard_map/ppermute | solution.py:42
  (13 other events, 55.6 us)

commit v8 on v7

--- a/solution.py
+++ b/solution.py
@@ -125,11 +125,17 @@
     return ring_gather(block)
 
 
+def swap_gather(value, axis):
+    other = lax.ppermute(value, axis, [(0, 1), (1, 0)])
+    first = lax.axis_index(axis) == 0
+    return jnp.stack([jnp.where(first, value, other), jnp.where(first, other, value)])
+
+
 def gather_weights(conv_weight, proj_weight):
     conv, proj = conv_weight[0], proj_weight[0]
     taps, width = conv.shape[0] * conv.shape[1], conv.shape[3]
     both = jnp.concatenate([conv.reshape((taps,) + conv.shape[2:]), proj.reshape((-1,) + conv.shape[2:])], axis=0)
-    both = lax.all_gather(lax.all_gather(both, "core", axis=0), "xh", axis=0)
+    both = swap_gather(swap_gather(both, "core"), "xh")
     conv = both[:, :, :taps].reshape(both.shape[:2] + conv.shape)
     proj = both[:, :, taps:].reshape(both.shape[:2] + proj.shape)
     chip = conv.shape[0] * conv.shape[1]

time: 196 us -> 200 us (1.020)
  blocking collectives: 9.43 us -> 0 us
  waiting for transfers between devices: 44.3 us -> 51.7 us
  starting transfers between devices: 95.7 us -> 101 us
    all_gather x2 -> x0, blocking collectives: 9.43 us -> none  [gather_weights(): both = lax.all_gather(lax.all_gather(both, 'core', axis=0), 'xh', axis=0)]
    ppermute x0 -> x2, waiting for transfers between devices: none -> 7.37 us  [swap_gather(): other = lax.ppermute(value, axis, [(0, 1), (1, 0)])]
    ppermute x0 -> x2, starting transfers between devices: none -> 5.62 us  [swap_gather(): other = lax.ppermute(value, axis, [(0, 1), (1, 0)])]
  transfers between devices with their start and end apart: 27 -> 29, of which waited for: 11 -> 13; matrix products, arithmetic and copies ran while one was open for 13% -> 13% of each run, Pallas kernels for 0% -> 0%
where the time goes in v8:
time: 200 us; the launch traced here: 199 us
  starting transfers between devices  101 us (50%)
  waiting for transfers between devices  51.7 us (26%)
  local copies, waits for them, and re-layouts  23.8 us (12%)
  matrix products  10.8 us (5%)
  other arithmetic  9.54 us (5%)
    ppermute x8, starting transfers between devices, ring_gather(): lax.ppermute(current[:cut], SEQ, route)  30.7 us
    ppermute x8, starting transfers between devices, ring_gather(): lax.ppermute(current[cut:], SEQ, route)  18.7 us
    ppermute x4, waiting for transfers between devices, from_behind(): return lax.ppermute(block, axis, route)  18.4 us
    ppermute x4, starting transfers between devices, from_behind(): return lax.ppermute(block, axis, route)  16.4 us
    ppermute x2, starting transfers between devices, padded(): before = lax.ppermute(last, axis, up)  11.4 us
    ppermute x1, starting transfers between devices, ring_gather(): lax.ppermute(jnp.stack(received[:span - half - 1]), 'core', [(0, 1), (1,...  10.2 us
    ppermute x2, waiting for transfers between devices, from_behind_2(): return lax.ppermute(block, axis, route)  8.47 us
    ppermute x2, waiting for transfers between devices, swap_gather(): other = lax.ppermute(value, axis, [(0, 1), (1, 0)])  7.37 us
  transfers between devices with their start and end apart: 29, of which 13 were waited for; matrix products, arithmetic and copies ran while one was open for 13% of the time, Pallas kernels for 0%

profile of v8, /device:TPU:127, one launch (start us, length us, event | category | flops | bytes accessed | tf_op | source)
XLA Modules:
  0.0 198.8 jit_solution(6553023141214310039)
XLA Ops:
  5.8 3.0 %collective-permute-start.1 = (bf16[2,8,12,384]{3,2,1,0:T(8,128)(2,1)S(1)}, bf16[2,8,12,384]{3,2,1,0:T(8,128)(2,1)S(1)}, u32[]{:S(2)}, u32[]{:S(2)}) collective-permute-start(bf16[2,8,12,384]{3,2,1,0:T(8,128)(2,1)S(1)} %pad_maximum_fusion.5), channel_id=1, source_target_pairs={{0,16},{16,0},{1,17},{17,1},{2,18},{18,2},{3,19},{19,3},{4,20},{20... | collective-permute-start | bytes 442376 | tf_op jit(solution)/shard_map/ppermute | solution.py:129
  8.9 6.5 %collective-permute-done.1 = bf16[2,8,12,384]{3,2,1,0:T(8,128)(2,1)S(1)} collective-permute-done((bf16[2,8,12,384]{3,2,1,0:T(8,128)(2,1)S(1)}, bf16[2,8,12,384]{3,2,1,0:T(8,128)(2,1)S(1)}, u32[]{:S(2)}, u32[]{:S(2)}) %collective-permute-start.1) | collective-permute-done | bytes 147488 | tf_op jit(solution)/shard_map/ppermute | solution.py:129
  19.7 3.4 %collective-permute-done.3 = bf16[192,384]{1,0:T(8,128)(2,1)S(1)} collective-permute-done((bf16[192,384]{1,0:T(8,128)(2,1)S(1)}, bf16[192,384]{1,0:T(8,128)(2,1)S(1)}, u32[]{:S(2)}, u32[]{:S(2)}) %collective-permute-start.3) | collective-permute-done | bytes 147488 | tf_op jit(solution)/shard_map/ppermute | solution.py:112
  25.0 7.2 %collective-permute-start.4 = (bf16[192,384]{1,0:T(8,128)(2,1)S(1)}, bf16[192,384]{1,0:T(8,128)(2,1)S(1)}, u32[]{:S(2)}, u32[]{:S(2)}) collective-permute-start(bf16[192,384]{1,0:T(8,128)(2,1)S(1)} %collective-permute-done.2), channel_id=1, source_target_pairs={{0,32},{8,488},{16,48},{24,504},{32,64},{40,8},{48,80},{56,24},{64... | collective-permute-start | bytes 442376 | tf_op jit(solution)/shard_map/ppermute | solution.py:112
  32.2 2.6 %collective-permute-start.7 = (bf16[192,384]{1,0:T(8,128)(2,1)S(1)}, bf16[192,384]{1,0:T(8,128)(2,1)S(1)}, u32[]{:S(2)}, u32[]{:S(2)}) collective-permute-start(bf16[192,384]{1,0:T(8,128)(2,1)S(1)} %collective-permute-done.5), channel_id=1, source_target_pairs={{0,32},{8,488},{16,48},{24,504},{32,64},{40,8},{48,80},{56,24},{64... | collective-permute-start | bytes 442376 | tf_op jit(solution)/shard_map/ppermute | solution.py:112
  34.9 4.4 %collective-permute-start.6 = (bf16[192,384]{1,0:T(8,128)(2,1)S(1)}, bf16[192,384]{1,0:T(8,128)(2,1)S(1)}, u32[]{:S(2)}, u32[]{:S(2)}) collective-permute-start(bf16[192,384]{1,0:T(8,128)(2,1)S(1)} %collective-permute-done.4), channel_id=1, source_target_pairs={{0,32},{8,488},{16,48},{24,504},{32,64},{40,8},{48,80},{56,24},{64... | collective-permute-start | bytes 442376 | tf_op jit(solution)/shard_map/ppermute | solution.py:112
  39.5 2.6 %collective-permute-start.9 = (bf16[192,384]{1,0:T(8,128)(2,1)S(1)}, bf16[192,384]{1,0:T(8,128)(2,1)S(1)}, u32[]{:S(2)}, u32[]{:S(2)}) collective-permute-start(bf16[192,384]{1,0:T(8,128)(2,1)S(1)} %collective-permute-done.7), channel_id=1, source_target_pairs={{0,32},{8,488},{16,48},{24,504},{32,64},{40,8},{48,80},{56,24},{64... | collective-permute-start | bytes 442376 | tf_op jit(solution)/shard_map/ppermute | solution.py:112
  42.1 4.4 %collective-permute-start.8 = (bf16[192,384]{1,0:T(8,128)(2,1)S(1)}, bf16[192,384]{1,0:T(8,128)(2,1)S(1)}, u32[]{:S(2)}, u32[]{:S(2)}) collective-permute-start(bf16[192,384]{1,0:T(8,128)(2,1)S(1)} %collective-permute-done.6), channel_id=1, source_target_pairs={{0,32},{8,488},{16,48},{24,504},{32,64},{40,8},{48,80},{56,24},{64... | collective-permute-start | bytes 442376 | tf_op jit(solution)/shard_map/ppermute | solution.py:112
  46.5 2.8 %broadcast_in_dim.30 = bf16[16,384,384]{2,1,0:T(8,128)(2,1)} broadcast(bf16[]{:T(256)} %constant.113.clone.1), dimensions={} | broadcast | bytes 4718594 | tf_op jit(solution)/shard_map/broadcast_in_dim | solution.py:106
  50.0 2.6 %collective-permute-start.11 = (bf16[192,384]{1,0:T(8,128)(2,1)S(1)}, bf16[192,384]{1,0:T(8,128)(2,1)S(1)}, u32[]{:S(2)}, u32[]{:S(2)}) collective-permute-start(bf16[192,384]{1,0:T(8,128)(2,1)S(1)} %collective-permute-done.9), channel_id=1, source_target_pairs={{0,32},{8,488},{16,48},{24,504},{32,64},{40,8},{48,80},{56,24},{64... | collective-permute-start | bytes 442376 | tf_op jit(solution)/shard_map/ppermute | solution.py:112
  52.7 4.2 %collective-permute-start.10 = (bf16[192,384]{1,0:T(8,128)(2,1)S(1)}, bf16[192,384]{1,0:T(8,128)(2,1)S(1)}, u32[]{:S(2)}, u32[]{:S(2)}) collective-permute-start(bf16[192,384]{1,0:T(8,128)(2,1)S(1)} %collective-permute-done.8), channel_id=1, source_target_pairs={{0,32},{8,488},{16,48},{24,504},{32,64},{40,8},{48,80},{56,24},{64... | collective-permute-start | bytes 442376 | tf_op jit(solution)/shard_map/ppermute | solution.py:112
  68.4 3.8 %collective-permute-start.14 = (bf16[192,384]{1,0:T(8,128)(2,1)S(1)}, bf16[192,384]{1,0:T(8,128)(2,1)S(1)}, u32[]{:S(2)}, u32[]{:S(2)}) collective-permute-start(bf16[192,384]{1,0:T(8,128)(2,1)S(1)} %collective-permute-done.12), channel_id=1, source_target_pairs={{0,32},{8,488},{16,48},{24,504},{32,64},{40,8},{48,80},{56,24},{64... | collective-permute-start | bytes 442376 | tf_op jit(solution)/shard_map/ppermute | solution.py:112
  76.4 10.2 %collective-permute-start.18 = (bf16[7,384,384]{2,1,0:T(8,128)(2,1)}, bf16[7,384,384]{2,1,0:T(8,128)(2,1)S(1)}, u32[]{:S(2)}, u32[]{:S(2)}) collective-permute-start(bf16[7,384,384]{2,1,0:T(8,128)(2,1)} %get-tuple-element.4), channel_id=1, source_target_pairs={{0,8},{8,0},{1,9},{9,1},{2,10},{10,2},{3,11},{11,3},{4,12},{12,4},... | collective-permute-start | bytes 6193160 | tf_op jit(solution)/shard_map/ppermute | solution.py:117
  107.5 5.6 %collective-permute-start.19 = (bf16[2,128,384]{2,1,0:T(8,128)(2,1)}, bf16[2,128,384]{2,1,0:T(8,128)(2,1)}, u32[]{:S(2)}, u32[]{:S(2)}) collective-permute-start(bf16[2,128,384]{2,1,0:T(8,128)(2,1)} %slice.169), channel_id=1, source_target_pairs={{0,8},{8,16},{16,24},{24,32},{32,40},{40,48},{48,56},{56,64},{64,7... | collective-permute-start | bytes 589832 | tf_op jit(solution)/shard_map/ppermute | solution.py:27
  119.8 3.0 %reshape.74 = bf16[16,2,24,768]{3,2,1,0:T(8,128)(2,1)} reshape(bf16[16,96,384]{2,1,0:T(8,128)(2,1)} %slice.173) | data formatting | bytes 2359296 | tf_op jit(solution)/shard_map/reshape | solution.py:151
  127.9 3.7 %collective-permute-start.21 = (bf16[2,256,384]{2,1,0:T(8,128)(2,1)S(1)}, bf16[2,256,384]{2,1,0:T(8,128)(2,1)S(1)}, u32[]{:S(2)}, u32[]{:S(2)}) collective-permute-start(bf16[2,256,384]{2,1,0:T(8,128)(2,1)S(1)} %convolution_convert_fusion.1), channel_id=1, source_target_pairs={{0,16},{8,24},{16,32},{24,40},{32,48},{40,56},{48,64},{56,72},{64,... | collective-permute-start | bytes 1179656 | tf_op jit(solution)/shard_map/ppermute | solution.py:36
  132.4 3.0 %collective-permute-start.22 = (bf16[2,256,384]{2,1,0:T(8,128)(2,1)S(1)}, bf16[2,256,384]{2,1,0:T(8,128)(2,1)S(1)}, u32[]{:S(2)}, u32[]{:S(2)}) collective-permute-start(bf16[2,256,384]{2,1,0:T(8,128)(2,1)S(1)} %convolution_convert_fusion), channel_id=1, source_target_pairs={{16,0},{24,8},{32,16},{40,24},{48,32},{56,40},{64,48},{72,56},{80,... | collective-permute-start | bytes 1179656 | tf_op jit(solution)/shard_map/ppermute | solution.py:36
  136.2 4.3 %collective-permute-done.21 = bf16[2,256,384]{2,1,0:T(8,128)(2,1)S(1)} collective-permute-done((bf16[2,256,384]{2,1,0:T(8,128)(2,1)S(1)}, bf16[2,256,384]{2,1,0:T(8,128)(2,1)S(1)}, u32[]{:S(2)}, u32[]{:S(2)}) %collective-permute-start.21) | collective-permute-done | bytes 393248 | tf_op jit(solution)/shard_map/ppermute | solution.py:36
  140.4 8.7 %collective-permute-done.22 = bf16[2,256,384]{2,1,0:T(8,128)(2,1)S(1)} collective-permute-done((bf16[2,256,384]{2,1,0:T(8,128)(2,1)S(1)}, bf16[2,256,384]{2,1,0:T(8,128)(2,1)S(1)}, u32[]{:S(2)}, u32[]{:S(2)}) %collective-permute-start.22) | collective-permute-done | bytes 393248 | tf_op jit(solution)/shard_map/ppermute | solution.py:36
  149.8 7.5 %collective-permute-start.25 = (bf16[1,256,384]{2,1,0:T(8,128)(2,1)S(1)}, bf16[1,256,384]{2,1,0:T(8,128)(2,1)S(1)}, u32[]{:S(2)}, u32[]{:S(2)}) collective-permute-start(bf16[1,256,384]{2,1,0:T(8,128)(2,1)S(1)} %fusion.101), channel_id=1, source_target_pairs={{0,16},{8,24},{16,32},{24,40},{32,48},{40,56},{48,64},{56,72},{64,... | collective-permute-start | bytes 589832 | tf_op jit(solution)/shard_map/ppermute | solution.py:36
  163.1 5.4 %collective-permute-done.24 = bf16[1,256,384]{2,1,0:T(8,128)(2,1)S(1)} collective-permute-done((bf16[1,256,384]{2,1,0:T(8,128)(2,1)S(1)}, bf16[1,256,384]{2,1,0:T(8,128)(2,1)S(1)}, u32[]{:S(2)}, u32[]{:S(2)}) %collective-permute-start.24) | collective-permute-done | bytes 196640 | tf_op jit(solution)/shard_map/ppermute | solution.py:36
  169.8 5.8 %collective-permute-start.27 = (bf16[1,128,384]{2,1,0:T(8,128)(2,1)S(1)}, bf16[1,128,384]{2,1,0:T(8,128)(2,1)S(1)}, u32[]{:S(2)}, u32[]{:S(2)}) collective-permute-start(bf16[1,128,384]{2,1,0:T(8,128)(2,1)S(1)} %get-tuple-element.19), channel_id=1, source_target_pairs={{0,8},{8,16},{16,24},{24,32},{32,40},{40,48},{48,56},{56,64},{64,7... | collective-permute-start | bytes 294920 | tf_op jit(solution)/shard_map/ppermute | solution.py:27
  178.4 7.2 %collective-permute-done.26 = bf16[1,128,384]{2,1,0:T(8,128)(2,1)S(1)} collective-permute-done((bf16[1,128,384]{2,1,0:T(8,128)(2,1)S(1)}, bf16[1,128,384]{2,1,0:T(8,128)(2,1)S(1)}, u32[]{:S(2)}, u32[]{:S(2)}) %collective-permute-start.26) | collective-permute-done | bytes 98336 | tf_op jit(solution)/shard_map/ppermute | solution.py:28
  188.9 8.5 %collective-permute-done.28 = bf16[1,256,768]{2,1,0:T(8,128)(2,1)S(1)} collective-permute-done((bf16[1,256,768]{2,1,0:T(8,128)(2,1)S(1)}, bf16[1,256,768]{2,1,0:T(8,128)(2,1)S(1)}, u32[]{:S(2)}, u32[]{:S(2)}) %collective-permute-start.28) | collective-permute-done | bytes 393248 | tf_op jit(solution)/shard_map/ppermute | solution.py:42
  (120 shorter events, 76.7 us)
Async XLA Ops:
  5.8 9.5 %collective-permute-start.1 = (bf16[2,8,12,384]{3,2,1,0:T(8,128)(2,1)S(1)}, bf16[2,8,12,384]{3,2,1,0:T(8,128)(2,1)S(1)}, u32[]{:S(2)}, u32[]{:S(2)}) collective-permute-start(bf16[2,8,12,384]{3,2,1,0:T(8,128)(2,1)S(1)} %pad_maximum_fusion.5), channel_id=1, source_target_pairs={{0,16},{16,0},{1,17},{17,1},{2,18},{18,2},{3,19},{19,3},{4,20},{20... | collective-permute-start | bytes 442376 | tf_op jit(solution)/shard_map/ppermute | solution.py:129
  15.8 7.3 %collective-permute-start.3 = (bf16[192,384]{1,0:T(8,128)(2,1)S(1)}, bf16[192,384]{1,0:T(8,128)(2,1)S(1)}, u32[]{:S(2)}, u32[]{:S(2)}) collective-permute-start(bf16[192,384]{1,0:T(8,128)(2,1)S(1)} %slice.159), channel_id=1, source_target_pairs={{0,32},{8,488},{16,48},{24,504},{32,64},{40,8},{48,80},{56,24},{64... | collective-permute-start | bytes 442376 | tf_op jit(solution)/shard_map/ppermute | solution.py:112
  17.8 7.3 %collective-permute-start.2 = (bf16[192,384]{1,0:T(8,128)(2,1)S(1)}, bf16[192,384]{1,0:T(8,128)(2,1)S(1)}, u32[]{:S(2)}, u32[]{:S(2)}) collective-permute-start(bf16[192,384]{1,0:T(8,128)(2,1)S(1)} %slice.158), channel_id=1, source_target_pairs={{0,32},{8,488},{16,48},{24,504},{32,64},{40,8},{48,80},{56,24},{64... | collective-permute-start | bytes 442376 | tf_op jit(solution)/shard_map/ppermute | solution.py:112
  23.1 9.1 %collective-permute-start.5 = (bf16[192,384]{1,0:T(8,128)(2,1)S(1)}, bf16[192,384]{1,0:T(8,128)(2,1)S(1)}, u32[]{:S(2)}, u32[]{:S(2)}) collective-permute-start(bf16[192,384]{1,0:T(8,128)(2,1)S(1)} %collective-permute-done.3), channel_id=1, source_target_pairs={{0,32},{8,488},{16,48},{24,504},{32,64},{40,8},{48,80},{56,24},{64... | collective-permute-start | bytes 442376 | tf_op jit(solution)/shard_map/ppermute | solution.py:112
  25.0 9.8 %collective-permute-start.4 = (bf16[192,384]{1,0:T(8,128)(2,1)S(1)}, bf16[192,384]{1,0:T(8,128)(2,1)S(1)}, u32[]{:S(2)}, u32[]{:S(2)}) collective-permute-start(bf16[192,384]{1,0:T(8,128)(2,1)S(1)} %collective-permute-done.2), channel_id=1, source_target_pairs={{0,32},{8,488},{16,48},{24,504},{32,64},{40,8},{48,80},{56,24},{64... | collective-permute-start | bytes 442376 | tf_op jit(solution)/shard_map/ppermute | solution.py:112
  32.2 7.2 %collective-permute-start.7 = (bf16[192,384]{1,0:T(8,128)(2,1)S(1)}, bf16[192,384]{1,0:T(8,128)(2,1)S(1)}, u32[]{:S(2)}, u32[]{:S(2)}) collective-permute-start(bf16[192,384]{1,0:T(8,128)(2,1)S(1)} %collective-permute-done.5), channel_id=1, source_target_pairs={{0,32},{8,488},{16,48},{24,504},{32,64},{40,8},{48,80},{56,24},{64... | collective-permute-start | bytes 442376 | tf_op jit(solution)/shard_map/ppermute | solution.py:112
  34.9 7.2 %collective-permute-start.6 = (bf16[192,384]{1,0:T(8,128)(2,1)S(1)}, bf16[192,384]{1,0:T(8,128)(2,1)S(1)}, u32[]{:S(2)}, u32[]{:S(2)}) collective-permute-start(bf16[192,384]{1,0:T(8,128)(2,1)S(1)} %collective-permute-done.4), channel_id=1, source_target_pairs={{0,32},{8,488},{16,48},{24,504},{32,64},{40,8},{48,80},{56,24},{64... | collective-permute-start | bytes 442376 | tf_op jit(solution)/shard_map/ppermute | solution.py:112
  39.5 10.6 %collective-permute-start.9 = (bf16[192,384]{1,0:T(8,128)(2,1)S(1)}, bf16[192,384]{1,0:T(8,128)(2,1)S(1)}, u32[]{:S(2)}, u32[]{:S(2)}) collective-permute-start(bf16[192,384]{1,0:T(8,128)(2,1)S(1)} %collective-permute-done.7), channel_id=1, source_target_pairs={{0,32},{8,488},{16,48},{24,504},{32,64},{40,8},{48,80},{56,24},{64... | collective-permute-start | bytes 442376 | tf_op jit(solution)/shard_map/ppermute | solution.py:112
  42.1 10.5 %collective-permute-start.8 = (bf16[192,384]{1,0:T(8,128)(2,1)S(1)}, bf16[192,384]{1,0:T(8,128)(2,1)S(1)}, u32[]{:S(2)}, u32[]{:S(2)}) collective-permute-start(bf16[192,384]{1,0:T(8,128)(2,1)S(1)} %collective-permute-done.6), channel_id=1, source_target_pairs={{0,32},{8,488},{16,48},{24,504},{32,64},{40,8},{48,80},{56,24},{64... | collective-permute-start | bytes 442376 | tf_op jit(solution)/shard_map/ppermute | solution.py:112
  50.0 8.7 %collective-permute-start.11 = (bf16[192,384]{1,0:T(8,128)(2,1)S(1)}, bf16[192,384]{1,0:T(8,128)(2,1)S(1)}, u32[]{:S(2)}, u32[]{:S(2)}) collective-permute-start(bf16[192,384]{1,0:T(8,128)(2,1)S(1)} %collective-permute-done.9), channel_id=1, source_target_pairs={{0,32},{8,488},{16,48},{24,504},{32,64},{40,8},{48,80},{56,24},{64... | collective-permute-start | bytes 442376 | tf_op jit(solution)/shard_map/ppermute | solution.py:112
  52.7 8.7 %collective-permute-start.10 = (bf16[192,384]{1,0:T(8,128)(2,1)S(1)}, bf16[192,384]{1,0:T(8,128)(2,1)S(1)}, u32[]{:S(2)}, u32[]{:S(2)}) collective-permute-start(bf16[192,384]{1,0:T(8,128)(2,1)S(1)} %collective-permute-done.8), channel_id=1, source_target_pairs={{0,32},{8,488},{16,48},{24,504},{32,64},{40,8},{48,80},{56,24},{64... | collective-permute-start | bytes 442376 | tf_op jit(solution)/shard_map/ppermute | solution.py:112
  65.8 8.2 %collective-permute-start.15 = (bf16[192,384]{1,0:T(8,128)(2,1)S(1)}, bf16[192,384]{1,0:T(8,128)(2,1)S(1)}, u32[]{:S(2)}, u32[]{:S(2)}) collective-permute-start(bf16[192,384]{1,0:T(8,128)(2,1)S(1)} %collective-permute-done.13), channel_id=1, source_target_pairs={{0,32},{8,488},{16,48},{24,504},{32,64},{40,8},{48,80},{56,24},{64... | collective-permute-start | bytes 442376 | tf_op jit(solution)/shard_map/ppermute | solution.py:112
  76.4 20.1 %collective-permute-start.18 = (bf16[7,384,384]{2,1,0:T(8,128)(2,1)}, bf16[7,384,384]{2,1,0:T(8,128)(2,1)S(1)}, u32[]{:S(2)}, u32[]{:S(2)}) collective-permute-start(bf16[7,384,384]{2,1,0:T(8,128)(2,1)} %get-tuple-element.4), channel_id=1, source_target_pairs={{0,8},{8,0},{1,9},{9,1},{2,10},{10,2},{3,11},{11,3},{4,12},{12,4},... | collective-permute-start | bytes 6193160 | tf_op jit(solution)/shard_map/ppermute | solution.py:117
  86.6 7.1 %collective-permute-start.17 = (bf16[192,384]{1,0:T(8,128)(2,1)S(1)}, bf16[192,384]{1,0:T(8,128)(2,1)S(1)}, u32[]{:S(2)}, u32[]{:S(2)}) collective-permute-start(bf16[192,384]{1,0:T(8,128)(2,1)S(1)} %collective-permute-done.15), channel_id=1, source_target_pairs={{0,32},{8,488},{16,48},{24,504},{32,64},{40,8},{48,80},{56,24},{64... | collective-permute-start | bytes 442376 | tf_op jit(solution)/shard_map/ppermute | solution.py:112
  107.5 16.8 %collective-permute-start.19 = (bf16[2,128,384]{2,1,0:T(8,128)(2,1)}, bf16[2,128,384]{2,1,0:T(8,128)(2,1)}, u32[]{:S(2)}, u32[]{:S(2)}) collective-permute-start(bf16[2,128,384]{2,1,0:T(8,128)(2,1)} %slice.169), channel_id=1, source_target_pairs={{0,8},{8,16},{16,24},{24,32},{32,40},{40,48},{48,56},{56,64},{64,7... | collective-permute-start | bytes 589832 | tf_op jit(solution)/shard_map/ppermute | solution.py:27
  113.8 11.5 %collective-permute-start.20 = (bf16[2,128,384]{2,1,0:T(8,128)(2,1)}, bf16[2,128,384]{2,1,0:T(8,128)(2,1)}, u32[]{:S(2)}, u32[]{:S(2)}) collective-permute-start(bf16[2,128,384]{2,1,0:T(8,128)(2,1)} %slice.172), channel_id=1, source_target_pairs={{8,0},{16,8},{24,16},{32,24},{40,32},{48,40},{56,48},{64,56},{72,6... | collective-permute-start | bytes 589832 | tf_op jit(solution)/shard_map/ppermute | solution.py:28
  127.9 12.5 %collective-permute-start.21 = (bf16[2,256,384]{2,1,0:T(8,128)(2,1)S(1)}, bf16[2,256,384]{2,1,0:T(8,128)(2,1)S(1)}, u32[]{:S(2)}, u32[]{:S(2)}) collective-permute-start(bf16[2,256,384]{2,1,0:T(8,128)(2,1)S(1)} %convolution_convert_fusion.1), channel_id=1, source_target_pairs={{0,16},{8,24},{16,32},{24,40},{32,48},{40,56},{48,64},{56,72},{64,... | collective-permute-start | bytes 1179656 | tf_op jit(solution)/shard_map/ppermute | solution.py:36
  132.4 16.8 %collective-permute-start.22 = (bf16[2,256,384]{2,1,0:T(8,128)(2,1)S(1)}, bf16[2,256,384]{2,1,0:T(8,128)(2,1)S(1)}, u32[]{:S(2)}, u32[]{:S(2)}) collective-permute-start(bf16[2,256,384]{2,1,0:T(8,128)(2,1)S(1)} %convolution_convert_fusion), channel_id=1, source_target_pairs={{16,0},{24,8},{32,16},{40,24},{48,32},{56,40},{64,48},{72,56},{80,... | collective-permute-start | bytes 1179656 | tf_op jit(solution)/shard_map/ppermute | solution.py:36
  149.8 12.9 %collective-permute-start.25 = (bf16[1,256,384]{2,1,0:T(8,128)(2,1)S(1)}, bf16[1,256,384]{2,1,0:T(8,128)(2,1)S(1)}, u32[]{:S(2)}, u32[]{:S(2)}) collective-permute-start(bf16[1,256,384]{2,1,0:T(8,128)(2,1)S(1)} %fusion.101), channel_id=1, source_target_pairs={{0,16},{8,24},{16,32},{24,40},{32,48},{40,56},{48,64},{56,72},{64,... | collective-permute-start | bytes 589832 | tf_op jit(solution)/shard_map/ppermute | solution.py:36
  157.3 11.2 %collective-permute-start.24 = (bf16[1,256,384]{2,1,0:T(8,128)(2,1)S(1)}, bf16[1,256,384]{2,1,0:T(8,128)(2,1)S(1)}, u32[]{:S(2)}, u32[]{:S(2)}) collective-permute-start(bf16[1,256,384]{2,1,0:T(8,128)(2,1)S(1)} %fusion.101), channel_id=1, source_target_pairs={{16,0},{24,8},{32,16},{40,24},{48,32},{56,40},{64,48},{72,56},{80,... | collective-permute-start | bytes 589832 | tf_op jit(solution)/shard_map/ppermute | solution.py:36
  160.2 28.7 %collective-permute-start.23 = (bf16[1,256,768]{2,1,0:T(8,128)(2,1)S(1)}, bf16[1,256,768]{2,1,0:T(8,128)(2,1)S(1)}, u32[]{:S(2)}, u32[]{:S(2)}) collective-permute-start(bf16[1,256,768]{2,1,0:T(8,128)(2,1)S(1)} %fusion.55), channel_id=1, source_target_pairs={{7,0},{0,1},{1,2},{2,3},{3,4},{4,5},{5,6},{6,7},{15,8},{8,9},{9,10... | collective-permute-start | bytes 1179656 | tf_op jit(solution)/shard_map/ppermute | solution.py:42
  169.8 8.1 %collective-permute-start.27 = (bf16[1,128,384]{2,1,0:T(8,128)(2,1)S(1)}, bf16[1,128,384]{2,1,0:T(8,128)(2,1)S(1)}, u32[]{:S(2)}, u32[]{:S(2)}) collective-permute-start(bf16[1,128,384]{2,1,0:T(8,128)(2,1)S(1)} %get-tuple-element.19), channel_id=1, source_target_pairs={{0,8},{8,16},{16,24},{24,32},{32,40},{40,48},{48,56},{56,64},{64,7... | collective-permute-start | bytes 294920 | tf_op jit(solution)/shard_map/ppermute | solution.py:27
  176.0 9.5 %collective-permute-start.26 = (bf16[1,128,384]{2,1,0:T(8,128)(2,1)S(1)}, bf16[1,128,384]{2,1,0:T(8,128)(2,1)S(1)}, u32[]{:S(2)}, u32[]{:S(2)}) collective-permute-start(bf16[1,128,384]{2,1,0:T(8,128)(2,1)S(1)} %get-tuple-element.18), channel_id=1, source_target_pairs={{8,0},{16,8},{24,16},{32,24},{40,32},{48,40},{56,48},{64,56},{72,6... | collective-permute-start | bytes 294920 | tf_op jit(solution)/shard_map/ppermute | solution.py:28
  186.4 10.9 %collective-permute-start.28 = (bf16[1,256,768]{2,1,0:T(8,128)(2,1)S(1)}, bf16[1,256,768]{2,1,0:T(8,128)(2,1)S(1)}, u32[]{:S(2)}, u32[]{:S(2)}) collective-permute-start(bf16[1,256,768]{2,1,0:T(8,128)(2,1)S(1)} %fusion.24), channel_id=1, source_target_pairs={{1,0},{2,1},{3,2},{4,3},{5,4},{6,5},{7,6},{0,7},{9,8},{10,9},{11,1... | collective-permute-start | bytes 1179656 | tf_op jit(solution)/shard_map/ppermute | solution.py:42
  (15 other events, 66.3 us)

commit v9 on v7

--- a/solution.py
+++ b/solution.py
@@ -69,10 +69,10 @@
     return jnp.einsum("krh,ch->krc", values, weight, preferred_element_type=jnp.float32)
 
 
-def run_forward(present_state, pieces):
+def run_forward(present_state, pieces, first=0):
     stored = []
-    for depth_level in range(BLOCKS):
-        conv_part, proj_part = pieces[depth_level]
+    for depth_level in range(first, first + len(pieces)):
+        conv_part, proj_part = pieces[depth_level - first]
         spacing_gap = FIRST_DILATION * 4**depth_level
         activated = jax.nn.gelu(present_state.astype(jnp.float32)).astype(jnp.bfloat16)
         middle = conv_apply(activated, conv_part[1])
@@ -153,9 +153,11 @@
         (convolution_complete[0, depth_level], proj_full[0, depth_level])
         for depth_level in range(BLOCKS)
     ]
-    both_out, both_stored = run_forward(jnp.concatenate([fwd_input, bwd_input], axis=0), pieces)
-    forward_out = both_out[:1]
+    both_mid, both_stored = run_forward(jnp.concatenate([fwd_input, bwd_input], axis=0), pieces[:1])
     stored = [(block_in[1:], preact[1:]) for block_in, preact in both_stored]
+    unused_out, later_stored = run_forward(both_mid[1:], pieces[1:], first=1)
+    stored = stored + later_stored
+    forward_out, unused = run_forward(both_mid[:1], pieces[1:], first=1)
     cotangent = bwd_cotangent
     for depth_level in reversed(range(BLOCKS)):
         conv_part, proj_part = pieces[depth_level]

time: 196 us -> 199 us (1.015)
  waiting for transfers between devices: 44.3 us -> 25.3 us
  starting transfers between devices: 95.7 us -> 110 us
  matrix products: 10.8 us -> 16.7 us
    ppermute x4 -> x6, waiting for transfers between devices: 18.3 us -> 0.02 us  [from_behind(): return lax.ppermute(block, axis, route)]
    ppermute x4 -> x6, starting transfers between devices: 16.2 us -> 23.8 us  [from_behind(): return lax.ppermute(block, axis, route)]
    ppermute x2, starting transfers between devices: 11.4 us -> 17.9 us  [padded(): before = lax.ppermute(last, axis, up)]
    dot_general x6, matrix products: 3.14 us -> 6.04 us  [conv_transpose(): jnp.einsum('krh,ch->krc', values, weight, preferred_element_type=jnp.floa...]
    dot_general x2, matrix products: 1.35 us -> 3.68 us  [run_forward(): jnp.einsum('krh,hc->krc', hidden, proj_part, preferred_element_type=jnp.f...]
    unnamed x26 -> x44, local copies, waits for them, and re-layouts: 3.87 us -> 4.77 us
    dot_general x6 -> x8, matrix products: 5.26 us -> 5.26 us  [conv_apply(): jnp.einsum('krc,ch->krh', values, weight, preferred_element_type=jnp.floa...]
  transfers between devices with their start and end apart: 27 -> 29, of which waited for: 11 -> 8; matrix products, arithmetic and copies ran while one was open for 13% -> 16% of each run, Pallas kernels for 0% -> 0%
where the time goes in v9:
time: 199 us; the launch traced here: 198 us
  starting transfers between devices  110 us (55%)
  waiting for transfers between devices  25.3 us (13%)
  local copies, waits for them, and re-layouts  25 us (13%)
  matrix products  16.7 us (8%)
  other arithmetic  9.45 us (5%)
  blocking collectives  9.43 us (5%)
    ppermute x8, starting transfers between devices, ring_gather(): lax.ppermute(current[:cut], SEQ, route)  30.7 us
    ppermute x6, starting transfers between devices, from_behind(): return lax.ppermute(block, axis, route)  23.8 us
    ppermute x8, starting transfers between devices, ring_gather(): lax.ppermute(current[cut:], SEQ, route)  18.6 us
    ppermute x2, starting transfers between devices, padded(): before = lax.ppermute(last, axis, up)  17.9 us
    ppermute x1, starting transfers between devices, ring_gather(): lax.ppermute(jnp.stack(received[:span - half - 1]), 'core', [(0, 1), (1,...  10.2 us
    all_gather x2, blocking collectives, gather_weights(): both = lax.all_gather(lax.all_gather(both, 'core', axis=0), 'xh', axis=0)  9.43 us
    ppermute x2, waiting for transfers between devices, from_behind_2(): return lax.ppermute(block, axis, route)  7.75 us
    ppermute x2, waiting for transfers between devices, padded(): after = lax.ppermute(initial, axis, down)  7.22 us
  transfers between devices with their start and end apart: 29, of which 8 were waited for; matrix products, arithmetic and copies ran while one was open for 16% of the time, Pallas kernels for 0%

profile of v9, /device:TPU:127, one launch (start us, length us, event | category | flops | bytes accessed | tf_op | source)
XLA Modules:
  0.0 197.7 jit_solution(15896253411099665097)
XLA Ops:
  4.5 7.2 %all-gather.1 = bf16[4,8,12,384]{3,1,0,2:T(8,128)(2,1)S(1)} all-gather(bf16[2,8,12,384]{3,1,0,2:T(8,128)(2,1)S(1)} %bitcast.223), channel_id=3, replica_groups=mesh['z'=16,'xh'=2,'core'=2,'section'=8] {'xh'}, dimensions={0}, use_global_device_ids=true | all-gather | bytes 442368 | tf_op jit(solution)/shard_map/all_gather | solution.py:132
  16.0 3.4 %collective-permute-done.1 = bf16[192,384]{1,0:T(8,128)(2,1)S(1)} collective-permute-done((bf16[192,384]{1,0:T(8,128)(2,1)S(1)}, bf16[192,384]{1,0:T(8,128)(2,1)S(1)}, u32[]{:S(2)}, u32[]{:S(2)}) %collective-permute-start.1) | collective-permute-done | bytes 147488 | tf_op jit(solution)/shard_map/ppermute | solution.py:112
  21.4 7.2 %collective-permute-start.2 = (bf16[192,384]{1,0:T(8,128)(2,1)S(1)}, bf16[192,384]{1,0:T(8,128)(2,1)S(1)}, u32[]{:S(2)}, u32[]{:S(2)}) collective-permute-start(bf16[192,384]{1,0:T(8,128)(2,1)S(1)} %collective-permute-done), channel_id=1, source_target_pairs={{0,32},{8,488},{16,48},{24,504},{32,64},{40,8},{48,80},{56,24},{64... | collective-permute-start | bytes 442376 | tf_op jit(solution)/shard_map/ppermute | solution.py:112
  28.6 2.6 %collective-permute-start.5 = (bf16[192,384]{1,0:T(8,128)(2,1)S(1)}, bf16[192,384]{1,0:T(8,128)(2,1)S(1)}, u32[]{:S(2)}, u32[]{:S(2)}) collective-permute-start(bf16[192,384]{1,0:T(8,128)(2,1)S(1)} %collective-permute-done.3), channel_id=1, source_target_pairs={{0,32},{8,488},{16,48},{24,504},{32,64},{40,8},{48,80},{56,24},{64... | collective-permute-start | bytes 442376 | tf_op jit(solution)/shard_map/ppermute | solution.py:112
  31.2 4.4 %collective-permute-start.4 = (bf16[192,384]{1,0:T(8,128)(2,1)S(1)}, bf16[192,384]{1,0:T(8,128)(2,1)S(1)}, u32[]{:S(2)}, u32[]{:S(2)}) collective-permute-start(bf16[192,384]{1,0:T(8,128)(2,1)S(1)} %collective-permute-done.2), channel_id=1, source_target_pairs={{0,32},{8,488},{16,48},{24,504},{32,64},{40,8},{48,80},{56,24},{64... | collective-permute-start | bytes 442376 | tf_op jit(solution)/shard_map/ppermute | solution.py:112
  35.8 2.6 %collective-permute-start.7 = (bf16[192,384]{1,0:T(8,128)(2,1)S(1)}, bf16[192,384]{1,0:T(8,128)(2,1)S(1)}, u32[]{:S(2)}, u32[]{:S(2)}) collective-permute-start(bf16[192,384]{1,0:T(8,128)(2,1)S(1)} %collective-permute-done.5), channel_id=1, source_target_pairs={{0,32},{8,488},{16,48},{24,504},{32,64},{40,8},{48,80},{56,24},{64... | collective-permute-start | bytes 442376 | tf_op jit(solution)/shard_map/ppermute | solution.py:112
  38.5 4.4 %collective-permute-start.6 = (bf16[192,384]{1,0:T(8,128)(2,1)S(1)}, bf16[192,384]{1,0:T(8,128)(2,1)S(1)}, u32[]{:S(2)}, u32[]{:S(2)}) collective-permute-start(bf16[192,384]{1,0:T(8,128)(2,1)S(1)} %collective-permute-done.4), channel_id=1, source_target_pairs={{0,32},{8,488},{16,48},{24,504},{32,64},{40,8},{48,80},{56,24},{64... | collective-permute-start | bytes 442376 | tf_op jit(solution)/shard_map/ppermute | solution.py:112
  42.9 2.8 %broadcast_in_dim.30 = bf16[16,384,384]{2,1,0:T(8,128)(2,1)} broadcast(bf16[]{:T(256)} %constant.111.clone.1), dimensions={} | broadcast | bytes 4718594 | tf_op jit(solution)/shard_map/broadcast_in_dim | solution.py:106
  49.0 4.3 %collective-permute-start.8 = (bf16[192,384]{1,0:T(8,128)(2,1)S(1)}, bf16[192,384]{1,0:T(8,128)(2,1)S(1)}, u32[]{:S(2)}, u32[]{:S(2)}) collective-permute-start(bf16[192,384]{1,0:T(8,128)(2,1)S(1)} %collective-permute-done.6), channel_id=1, source_target_pairs={{0,32},{8,488},{16,48},{24,504},{32,64},{40,8},{48,80},{56,24},{64... | collective-permute-start | bytes 442376 | tf_op jit(solution)/shard_map/ppermute | solution.py:112
  55.1 2.6 %collective-permute-start.11 = (bf16[192,384]{1,0:T(8,128)(2,1)S(1)}, bf16[192,384]{1,0:T(8,128)(2,1)S(1)}, u32[]{:S(2)}, u32[]{:S(2)}) collective-permute-start(bf16[192,384]{1,0:T(8,128)(2,1)S(1)} %collective-permute-done.9), channel_id=1, source_target_pairs={{0,32},{8,488},{16,48},{24,504},{32,64},{40,8},{48,80},{56,24},{64... | collective-permute-start | bytes 442376 | tf_op jit(solution)/shard_map/ppermute | solution.py:112
  64.8 3.7 %collective-permute-start.12 = (bf16[192,384]{1,0:T(8,128)(2,1)S(1)}, bf16[192,384]{1,0:T(8,128)(2,1)S(1)}, u32[]{:S(2)}, u32[]{:S(2)}) collective-permute-start(bf16[192,384]{1,0:T(8,128)(2,1)S(1)} %collective-permute-done.10), channel_id=1, source_target_pairs={{0,32},{8,488},{16,48},{24,504},{32,64},{40,8},{48,80},{56,24},{64... | collective-permute-start | bytes 442376 | tf_op jit(solution)/shard_map/ppermute | solution.py:112
  72.8 10.2 %collective-permute-start.16 = (bf16[7,384,384]{2,1,0:T(8,128)(2,1)}, bf16[7,384,384]{2,1,0:T(8,128)(2,1)S(1)}, u32[]{:S(2)}, u32[]{:S(2)}) collective-permute-start(bf16[7,384,384]{2,1,0:T(8,128)(2,1)} %get-tuple-element.2), channel_id=1, source_target_pairs={{0,8},{8,0},{1,9},{9,1},{2,10},{10,2},{3,11},{11,3},{4,12},{12,4},... | collective-permute-start | bytes 6193160 | tf_op jit(solution)/shard_map/ppermute | solution.py:117
  85.0 2.6 %collective-permute-start.14 = (bf16[192,384]{1,0:T(8,128)(2,1)S(1)}, bf16[192,384]{1,0:T(8,128)(2,1)S(1)}, u32[]{:S(2)}, u32[]{:S(2)}) collective-permute-start(bf16[192,384]{1,0:T(8,128)(2,1)S(1)} %collective-permute-done.12), channel_id=1, source_target_pairs={{0,32},{8,488},{16,48},{24,504},{32,64},{40,8},{48,80},{56,24},{64... | collective-permute-start | bytes 442376 | tf_op jit(solution)/shard_map/ppermute | solution.py:112
  103.8 5.7 %collective-permute-start.17 = (bf16[2,128,384]{2,1,0:T(8,128)(2,1)}, bf16[2,128,384]{2,1,0:T(8,128)(2,1)}, u32[]{:S(2)}, u32[]{:S(2)}) collective-permute-start(bf16[2,128,384]{2,1,0:T(8,128)(2,1)} %slice.168), channel_id=1, source_target_pairs={{0,8},{8,16},{16,24},{24,32},{32,40},{40,48},{48,56},{56,64},{64,7... | collective-permute-start | bytes 589832 | tf_op jit(solution)/shard_map/ppermute | solution.py:27
  116.2 3.0 %reshape.98 = bf16[16,2,24,768]{3,2,1,0:T(8,128)(2,1)} reshape(bf16[16,96,384]{2,1,0:T(8,128)(2,1)} %slice.172) | data formatting | bytes 2359296 | tf_op jit(solution)/shard_map/reshape | solution.py:145
  125.9 3.9 %collective-permute-start.22 = (bf16[1,256,384]{2,1,0:T(8,128)(2,1)S(1)}, bf16[1,256,384]{2,1,0:T(8,128)(2,1)S(1)}, u32[]{:S(2)}, u32[]{:S(2)}) collective-permute-start(bf16[1,256,384]{2,1,0:T(8,128)(2,1)S(1)} %fusion.14), channel_id=1, source_target_pairs={{0,16},{8,24},{16,32},{24,40},{32,48},{40,56},{48,64},{56,72},{64,... | collective-permute-start | bytes 589832 | tf_op jit(solution)/shard_map/ppermute | solution.py:36
  129.8 3.0 %collective-permute-start.23 = (bf16[1,256,384]{2,1,0:T(8,128)(2,1)S(1)}, bf16[1,256,384]{2,1,0:T(8,128)(2,1)S(1)}, u32[]{:S(2)}, u32[]{:S(2)}) collective-permute-start(bf16[1,256,384]{2,1,0:T(8,128)(2,1)S(1)} %fusion.15), channel_id=1, source_target_pairs={{16,0},{24,8},{32,16},{40,24},{48,32},{56,40},{64,48},{72,56},{80,... | collective-permute-start | bytes 589832 | tf_op jit(solution)/shard_map/ppermute | solution.py:36
  132.9 5.9 %collective-permute-start.19 = (bf16[1,256,384]{2,1,0:T(8,128)(2,1)S(1)}, bf16[1,256,384]{2,1,0:T(8,128)(2,1)S(1)}, u32[]{:S(2)}, u32[]{:S(2)}) collective-permute-start(bf16[1,256,384]{2,1,0:T(8,128)(2,1)S(1)} %fusion.12), channel_id=1, source_target_pairs={{0,16},{8,24},{16,32},{24,40},{32,48},{40,56},{48,64},{56,72},{64,... | collective-permute-start | bytes 589832 | tf_op jit(solution)/shard_map/ppermute | solution.py:36
  142.4 7.0 %collective-permute-start.25 = (bf16[1,256,384]{2,1,0:T(8,128)(2,1)}, bf16[1,256,384]{2,1,0:T(8,128)(2,1)}, u32[]{:S(2)}, u32[]{:S(2)}) collective-permute-start(bf16[1,256,384]{2,1,0:T(8,128)(2,1)} %fusion.78), channel_id=1, source_target_pairs={{0,16},{8,24},{16,32},{24,40},{32,48},{40,56},{48,64},{56,72},{64,... | collective-permute-start | bytes 589832 | tf_op jit(solution)/shard_map/ppermute | solution.py:36
  152.2 3.0 %fusion.11 = bf16[1,256,768]{2,1,0:T(8,128)(2,1)} fusion(bf16[1,2,384,768]{3,2,1,0:T(8,128)(2,1)} %bitcast.220, bf16[2,256,768]{2,1,0:T(8,128)(2,1)} %copy-done.17, bf16[1,256,384]{2,1,0:T(8,128)(2,1)} %collective-permute-done.20, bf16[1,256,384]{2,1,0:T(8,128)(2,1)} %copy-done.16, bf16[1,2,3,768,384]{4,3,2,1,0:T(8,128)(2,1)S(1)} %bitcast.208), kind=kOutput, calls=%fused_computation.33 | convolution fusion | flops 305823744 | bytes 2752512 | tf_op jit(solution)/shard_map/krh,hc->krc/dot_general | solution.py:90
  162.5 12.3 %collective-permute-start.27 = (bf16[1,128,384]{2,1,0:T(8,128)(2,1)S(1)}, bf16[1,128,384]{2,1,0:T(8,128)(2,1)S(1)}, u32[]{:S(2)}, u32[]{:S(2)}) collective-permute-start(bf16[1,128,384]{2,1,0:T(8,128)(2,1)S(1)} %get-tuple-element.17), channel_id=1, source_target_pairs={{0,8},{8,16},{16,24},{24,32},{32,40},{40,48},{48,56},{56,64},{64,7... | collective-permute-start | bytes 294920 | tf_op jit(solution)/shard_map/ppermute | solution.py:27
  177.5 7.2 %collective-permute-done.26 = bf16[1,128,384]{2,1,0:T(8,128)(2,1)S(1)} collective-permute-done((bf16[1,128,384]{2,1,0:T(8,128)(2,1)S(1)}, bf16[1,128,384]{2,1,0:T(8,128)(2,1)S(1)}, u32[]{:S(2)}, u32[]{:S(2)}) %collective-permute-start.26) | collective-permute-done | bytes 98336 | tf_op jit(solution)/shard_map/ppermute | solution.py:28
  185.6 2.9 %collective-permute-start.28 = (bf16[1,256,768]{2,1,0:T(8,128)(2,1)S(1)}, bf16[1,256,768]{2,1,0:T(8,128)(2,1)S(1)}, u32[]{:S(2)}, u32[]{:S(2)}) collective-permute-start(bf16[1,256,768]{2,1,0:T(8,128)(2,1)S(1)} %fusion.25), channel_id=1, source_target_pairs={{1,0},{2,1},{3,2},{4,3},{5,4},{6,5},{7,6},{0,7},{9,8},{10,9},{11,1... | collective-permute-start | bytes 1179656 | tf_op jit(solution)/shard_map/ppermute | solution.py:42
  188.4 7.7 %collective-permute-done.28 = bf16[1,256,768]{2,1,0:T(8,128)(2,1)S(1)} collective-permute-done((bf16[1,256,768]{2,1,0:T(8,128)(2,1)S(1)}, bf16[1,256,768]{2,1,0:T(8,128)(2,1)S(1)}, u32[]{:S(2)}, u32[]{:S(2)}) %collective-permute-start.28) | collective-permute-done | bytes 393248 | tf_op jit(solution)/shard_map/ppermute | solution.py:42
  (138 shorter events, 76.3 us)
Async XLA Ops:
  12.1 7.3 %collective-permute-start.1 = (bf16[192,384]{1,0:T(8,128)(2,1)S(1)}, bf16[192,384]{1,0:T(8,128)(2,1)S(1)}, u32[]{:S(2)}, u32[]{:S(2)}) collective-permute-start(bf16[192,384]{1,0:T(8,128)(2,1)S(1)} %slice.158), channel_id=1, source_target_pairs={{0,32},{8,488},{16,48},{24,504},{32,64},{40,8},{48,80},{56,24},{64... | collective-permute-start | bytes 442376 | tf_op jit(solution)/shard_map/ppermute | solution.py:112
  14.1 7.3 %collective-permute-start = (bf16[192,384]{1,0:T(8,128)(2,1)S(1)}, bf16[192,384]{1,0:T(8,128)(2,1)S(1)}, u32[]{:S(2)}, u32[]{:S(2)}) collective-permute-start(bf16[192,384]{1,0:T(8,128)(2,1)S(1)} %slice.157), channel_id=1, source_target_pairs={{0,32},{8,488},{16,48},{24,504},{32,64},{40,8},{48,80},{56,24},{64... | collective-permute-start | bytes 442376 | tf_op jit(solution)/shard_map/ppermute | solution.py:112
  19.4 9.1 %collective-permute-start.3 = (bf16[192,384]{1,0:T(8,128)(2,1)S(1)}, bf16[192,384]{1,0:T(8,128)(2,1)S(1)}, u32[]{:S(2)}, u32[]{:S(2)}) collective-permute-start(bf16[192,384]{1,0:T(8,128)(2,1)S(1)} %collective-permute-done.1), channel_id=1, source_target_pairs={{0,32},{8,488},{16,48},{24,504},{32,64},{40,8},{48,80},{56,24},{64... | collective-permute-start | bytes 442376 | tf_op jit(solution)/shard_map/ppermute | solution.py:112
  21.4 9.8 %collective-permute-start.2 = (bf16[192,384]{1,0:T(8,128)(2,1)S(1)}, bf16[192,384]{1,0:T(8,128)(2,1)S(1)}, u32[]{:S(2)}, u32[]{:S(2)}) collective-permute-start(bf16[192,384]{1,0:T(8,128)(2,1)S(1)} %collective-permute-done), channel_id=1, source_target_pairs={{0,32},{8,488},{16,48},{24,504},{32,64},{40,8},{48,80},{56,24},{64... | collective-permute-start | bytes 442376 | tf_op jit(solution)/shard_map/ppermute | solution.py:112
  28.6 7.2 %collective-permute-start.5 = (bf16[192,384]{1,0:T(8,128)(2,1)S(1)}, bf16[192,384]{1,0:T(8,128)(2,1)S(1)}, u32[]{:S(2)}, u32[]{:S(2)}) collective-permute-start(bf16[192,384]{1,0:T(8,128)(2,1)S(1)} %collective-permute-done.3), channel_id=1, source_target_pairs={{0,32},{8,488},{16,48},{24,504},{32,64},{40,8},{48,80},{56,24},{64... | collective-permute-start | bytes 442376 | tf_op jit(solution)/shard_map/ppermute | solution.py:112
  31.2 7.2 %collective-permute-start.4 = (bf16[192,384]{1,0:T(8,128)(2,1)S(1)}, bf16[192,384]{1,0:T(8,128)(2,1)S(1)}, u32[]{:S(2)}, u32[]{:S(2)}) collective-permute-start(bf16[192,384]{1,0:T(8,128)(2,1)S(1)} %collective-permute-done.2), channel_id=1, source_target_pairs={{0,32},{8,488},{16,48},{24,504},{32,64},{40,8},{48,80},{56,24},{64... | collective-permute-start | bytes 442376 | tf_op jit(solution)/shard_map/ppermute | solution.py:112
  35.8 10.6 %collective-permute-start.7 = (bf16[192,384]{1,0:T(8,128)(2,1)S(1)}, bf16[192,384]{1,0:T(8,128)(2,1)S(1)}, u32[]{:S(2)}, u32[]{:S(2)}) collective-permute-start(bf16[192,384]{1,0:T(8,128)(2,1)S(1)} %collective-permute-done.5), channel_id=1, source_target_pairs={{0,32},{8,488},{16,48},{24,504},{32,64},{40,8},{48,80},{56,24},{64... | collective-permute-start | bytes 442376 | tf_op jit(solution)/shard_map/ppermute | solution.py:112
  38.5 10.6 %collective-permute-start.6 = (bf16[192,384]{1,0:T(8,128)(2,1)S(1)}, bf16[192,384]{1,0:T(8,128)(2,1)S(1)}, u32[]{:S(2)}, u32[]{:S(2)}) collective-permute-start(bf16[192,384]{1,0:T(8,128)(2,1)S(1)} %collective-permute-done.4), channel_id=1, source_target_pairs={{0,32},{8,488},{16,48},{24,504},{32,64},{40,8},{48,80},{56,24},{64... | collective-permute-start | bytes 442376 | tf_op jit(solution)/shard_map/ppermute | solution.py:112
  46.4 8.7 %collective-permute-start.9 = (bf16[192,384]{1,0:T(8,128)(2,1)S(1)}, bf16[192,384]{1,0:T(8,128)(2,1)S(1)}, u32[]{:S(2)}, u32[]{:S(2)}) collective-permute-start(bf16[192,384]{1,0:T(8,128)(2,1)S(1)} %collective-permute-done.7), channel_id=1, source_target_pairs={{0,32},{8,488},{16,48},{24,504},{32,64},{40,8},{48,80},{56,24},{64... | collective-permute-start | bytes 442376 | tf_op jit(solution)/shard_map/ppermute | solution.py:112
  49.0 8.7 %collective-permute-start.8 = (bf16[192,384]{1,0:T(8,128)(2,1)S(1)}, bf16[192,384]{1,0:T(8,128)(2,1)S(1)}, u32[]{:S(2)}, u32[]{:S(2)}) collective-permute-start(bf16[192,384]{1,0:T(8,128)(2,1)S(1)} %collective-permute-done.6), channel_id=1, source_target_pairs={{0,32},{8,488},{16,48},{24,504},{32,64},{40,8},{48,80},{56,24},{64... | collective-permute-start | bytes 442376 | tf_op jit(solution)/shard_map/ppermute | solution.py:112
  62.2 8.1 %collective-permute-start.13 = (bf16[192,384]{1,0:T(8,128)(2,1)S(1)}, bf16[192,384]{1,0:T(8,128)(2,1)S(1)}, u32[]{:S(2)}, u32[]{:S(2)}) collective-permute-start(bf16[192,384]{1,0:T(8,128)(2,1)S(1)} %collective-permute-done.11), channel_id=1, source_target_pairs={{0,32},{8,488},{16,48},{24,504},{32,64},{40,8},{48,80},{56,24},{64... | collective-permute-start | bytes 442376 | tf_op jit(solution)/shard_map/ppermute | solution.py:112
  72.8 20.1 %collective-permute-start.16 = (bf16[7,384,384]{2,1,0:T(8,128)(2,1)}, bf16[7,384,384]{2,1,0:T(8,128)(2,1)S(1)}, u32[]{:S(2)}, u32[]{:S(2)}) collective-permute-start(bf16[7,384,384]{2,1,0:T(8,128)(2,1)} %get-tuple-element.2), channel_id=1, source_target_pairs={{0,8},{8,0},{1,9},{9,1},{2,10},{10,2},{3,11},{11,3},{4,12},{12,4},... | collective-permute-start | bytes 6193160 | tf_op jit(solution)/shard_map/ppermute | solution.py:117
  103.8 16.8 %collective-permute-start.17 = (bf16[2,128,384]{2,1,0:T(8,128)(2,1)}, bf16[2,128,384]{2,1,0:T(8,128)(2,1)}, u32[]{:S(2)}, u32[]{:S(2)}) collective-permute-start(bf16[2,128,384]{2,1,0:T(8,128)(2,1)} %slice.168), channel_id=1, source_target_pairs={{0,8},{8,16},{16,24},{24,32},{32,40},{40,48},{48,56},{56,64},{64,7... | collective-permute-start | bytes 589832 | tf_op jit(solution)/shard_map/ppermute | solution.py:27
  110.2 11.9 %collective-permute-start.18 = (bf16[2,128,384]{2,1,0:T(8,128)(2,1)}, bf16[2,128,384]{2,1,0:T(8,128)(2,1)}, u32[]{:S(2)}, u32[]{:S(2)}) collective-permute-start(bf16[2,128,384]{2,1,0:T(8,128)(2,1)} %slice.171), channel_id=1, source_target_pairs={{8,0},{16,8},{24,16},{32,24},{40,32},{48,40},{56,48},{64,56},{72,6... | collective-permute-start | bytes 589832 | tf_op jit(solution)/shard_map/ppermute | solution.py:28
  125.9 15.2 %collective-permute-start.22 = (bf16[1,256,384]{2,1,0:T(8,128)(2,1)S(1)}, bf16[1,256,384]{2,1,0:T(8,128)(2,1)S(1)}, u32[]{:S(2)}, u32[]{:S(2)}) collective-permute-start(bf16[1,256,384]{2,1,0:T(8,128)(2,1)S(1)} %fusion.14), channel_id=1, source_target_pairs={{0,16},{8,24},{16,32},{24,40},{32,48},{40,56},{48,64},{56,72},{64,... | collective-permute-start | bytes 589832 | tf_op jit(solution)/shard_map/ppermute | solution.py:36
  129.8 11.3 %collective-permute-start.23 = (bf16[1,256,384]{2,1,0:T(8,128)(2,1)S(1)}, bf16[1,256,384]{2,1,0:T(8,128)(2,1)S(1)}, u32[]{:S(2)}, u32[]{:S(2)}) collective-permute-start(bf16[1,256,384]{2,1,0:T(8,128)(2,1)S(1)} %fusion.15), channel_id=1, source_target_pairs={{16,0},{24,8},{32,16},{40,24},{48,32},{56,40},{64,48},{72,56},{80,... | collective-permute-start | bytes 589832 | tf_op jit(solution)/shard_map/ppermute | solution.py:36
  132.9 18.6 %collective-permute-start.19 = (bf16[1,256,384]{2,1,0:T(8,128)(2,1)S(1)}, bf16[1,256,384]{2,1,0:T(8,128)(2,1)S(1)}, u32[]{:S(2)}, u32[]{:S(2)}) collective-permute-start(bf16[1,256,384]{2,1,0:T(8,128)(2,1)S(1)} %fusion.12), channel_id=1, source_target_pairs={{0,16},{8,24},{16,32},{24,40},{32,48},{40,56},{48,64},{56,72},{64,... | collective-permute-start | bytes 589832 | tf_op jit(solution)/shard_map/ppermute | solution.py:36
  138.8 13.4 %collective-permute-start.20 = (bf16[1,256,384]{2,1,0:T(8,128)(2,1)S(1)}, bf16[1,256,384]{2,1,0:T(8,128)(2,1)}, u32[]{:S(2)}, u32[]{:S(2)}) collective-permute-start(bf16[1,256,384]{2,1,0:T(8,128)(2,1)S(1)} %fusion.13), channel_id=1, source_target_pairs={{16,0},{24,8},{32,16},{40,24},{48,32},{56,40},{64,48},{72,56},{80,... | collective-permute-start | bytes 589832 | tf_op jit(solution)/shard_map/ppermute | solution.py:36
  142.4 16.3 %collective-permute-start.25 = (bf16[1,256,384]{2,1,0:T(8,128)(2,1)}, bf16[1,256,384]{2,1,0:T(8,128)(2,1)}, u32[]{:S(2)}, u32[]{:S(2)}) collective-permute-start(bf16[1,256,384]{2,1,0:T(8,128)(2,1)} %fusion.78), channel_id=1, source_target_pairs={{0,16},{8,24},{16,32},{24,40},{32,48},{40,56},{48,64},{56,72},{64,... | collective-permute-start | bytes 589832 | tf_op jit(solution)/shard_map/ppermute | solution.py:36
  149.4 10.7 %collective-permute-start.24 = (bf16[1,256,384]{2,1,0:T(8,128)(2,1)}, bf16[1,256,384]{2,1,0:T(8,128)(2,1)}, u32[]{:S(2)}, u32[]{:S(2)}) collective-permute-start(bf16[1,256,384]{2,1,0:T(8,128)(2,1)} %fusion.78), channel_id=1, source_target_pairs={{16,0},{24,8},{32,16},{40,24},{48,32},{56,40},{64,48},{72,56},{80,... | collective-permute-start | bytes 589832 | tf_op jit(solution)/shard_map/ppermute | solution.py:36
  155.2 33.2 %collective-permute-start.21 = (bf16[1,256,768]{2,1,0:T(8,128)(2,1)}, bf16[1,256,768]{2,1,0:T(8,128)(2,1)S(1)}, u32[]{:S(2)}, u32[]{:S(2)}) collective-permute-start(bf16[1,256,768]{2,1,0:T(8,128)(2,1)} %fusion.11), channel_id=1, source_target_pairs={{7,0},{0,1},{1,2},{2,3},{3,4},{4,5},{5,6},{6,7},{15,8},{8,9},{9,10... | collective-permute-start | bytes 1179656 | tf_op jit(solution)/shard_map/ppermute | solution.py:42
  162.5 14.6 %collective-permute-start.27 = (bf16[1,128,384]{2,1,0:T(8,128)(2,1)S(1)}, bf16[1,128,384]{2,1,0:T(8,128)(2,1)S(1)}, u32[]{:S(2)}, u32[]{:S(2)}) collective-permute-start(bf16[1,128,384]{2,1,0:T(8,128)(2,1)S(1)} %get-tuple-element.17), channel_id=1, source_target_pairs={{0,8},{8,16},{16,24},{24,32},{32,40},{40,48},{48,56},{56,64},{64,7... | collective-permute-start | bytes 294920 | tf_op jit(solution)/shard_map/ppermute | solution.py:27
  175.2 9.5 %collective-permute-start.26 = (bf16[1,128,384]{2,1,0:T(8,128)(2,1)S(1)}, bf16[1,128,384]{2,1,0:T(8,128)(2,1)S(1)}, u32[]{:S(2)}, u32[]{:S(2)}) collective-permute-start(bf16[1,128,384]{2,1,0:T(8,128)(2,1)S(1)} %get-tuple-element.16), channel_id=1, source_target_pairs={{8,0},{16,8},{24,16},{32,24},{40,32},{48,40},{56,48},{64,56},{72,6... | collective-permute-start | bytes 294920 | tf_op jit(solution)/shard_map/ppermute | solution.py:28
  185.6 10.6 %collective-permute-start.28 = (bf16[1,256,768]{2,1,0:T(8,128)(2,1)S(1)}, bf16[1,256,768]{2,1,0:T(8,128)(2,1)S(1)}, u32[]{:S(2)}, u32[]{:S(2)}) collective-permute-start(bf16[1,256,768]{2,1,0:T(8,128)(2,1)S(1)} %fusion.25), channel_id=1, source_target_pairs={{1,0},{2,1},{3,2},{4,3},{5,4},{6,5},{7,6},{0,7},{9,8},{10,9},{11,1... | collective-permute-start | bytes 1179656 | tf_op jit(solution)/shard_map/ppermute | solution.py:42
  (24 other events, 148.2 us)

commit v10 on v7

--- a/solution.py
+++ b/solution.py
@@ -33,7 +33,10 @@
 def from_behind(block, axis, distance):
     devices = range(seq_size(axis))
     route = [(i - distance, i) for i in devices if i - distance in devices]
-    return lax.ppermute(block, axis, route)
+    cut = block.shape[1] // 2
+    return jnp.concatenate(
+        [lax.ppermute(block[:, :cut], axis, route), lax.ppermute(block[:, cut:], axis, route)], axis=1
+    )
 
 
 def from_behind_2(block, axis, distance):

time: 196 us -> 205 us (1.046)
  starting transfers between devices: 95.7 us -> 111 us
  waiting for transfers between devices: 44.3 us -> 37.8 us
    ppermute x4 -> x8, starting transfers between devices: 16.2 us -> 31.3 us  [the longest x4 16.2 us: from_behind(): lax.ppermute(block[:, :cut], axis, route)]
    ppermute x4 -> x8, waiting for transfers between devices: 18.3 us -> 10.5 us  [the longest x4 9.88 us: from_behind(): lax.ppermute(block[:, cut:], axis, route)]
  transfers between devices with their start and end apart: 27 -> 31, of which waited for: 11 -> 11; matrix products, arithmetic and copies ran while one was open for 13% -> 12% of each run, Pallas kernels for 0% -> 0%
where the time goes in v10:
time: 205 us; the launch traced here: 204 us
  starting transfers between devices  111 us (54%)
  waiting for transfers between devices  37.8 us (18%)
  local copies, waits for them, and re-layouts  24.2 us (12%)
  matrix products  10.7 us (5%)
  other arithmetic  9.45 us (5%)
  blocking collectives  9.43 us (5%)
    ppermute x8, starting transfers between devices, ring_gather(): lax.ppermute(current[:cut], SEQ, route)  30.7 us
    ppermute x8, starting transfers between devices, ring_gather(): lax.ppermute(current[cut:], SEQ, route)  18.6 us
    ppermute x4, starting transfers between devices, from_behind(): lax.ppermute(block[:, :cut], axis, route)  16.2 us
    ppermute x4, starting transfers between devices, from_behind(): lax.ppermute(block[:, cut:], axis, route)  15 us
    ppermute x2, starting transfers between devices, padded(): before = lax.ppermute(last, axis, up)  12.1 us
    ppermute x1, starting transfers between devices, ring_gather(): lax.ppermute(jnp.stack(received[:span - half - 1]), 'core', [(0, 1), (1,...  10.2 us
    ppermute x4, waiting for transfers between devices, from_behind(): lax.ppermute(block[:, cut:], axis, route)  9.88 us
    ppermute x2, waiting for transfers between devices, from_behind_2(): return lax.ppermute(block, axis, route)  9.78 us
  transfers between devices with their start and end apart: 31, of which 11 were waited for; matrix products, arithmetic and copies ran while one was open for 12% of the time, Pallas kernels for 0%

profile of v10, /device:TPU:127, one launch (start us, length us, event | category | flops | bytes accessed | tf_op | source)
XLA Modules:
  0.0 204.1 jit_solution(420132671025879389)
XLA Ops:
  4.5 7.2 %all-gather.1 = bf16[4,8,12,384]{3,1,0,2:T(8,128)(2,1)S(1)} all-gather(bf16[2,8,12,384]{3,1,0,2:T(8,128)(2,1)S(1)} %bitcast.191), channel_id=3, replica_groups=mesh['z'=16,'xh'=2,'core'=2,'section'=8] {'xh'}, dimensions={0}, use_global_device_ids=true | all-gather | bytes 442368 | tf_op jit(solution)/shard_map/all_gather | solution.py:135
  16.0 3.4 %collective-permute-done.1 = bf16[192,384]{1,0:T(8,128)(2,1)S(1)} collective-permute-done((bf16[192,384]{1,0:T(8,128)(2,1)S(1)}, bf16[192,384]{1,0:T(8,128)(2,1)S(1)}, u32[]{:S(2)}, u32[]{:S(2)}) %collective-permute-start.1) | collective-permute-done | bytes 147488 | tf_op jit(solution)/shard_map/ppermute | solution.py:115
  21.4 7.2 %collective-permute-start.2 = (bf16[192,384]{1,0:T(8,128)(2,1)S(1)}, bf16[192,384]{1,0:T(8,128)(2,1)S(1)}, u32[]{:S(2)}, u32[]{:S(2)}) collective-permute-start(bf16[192,384]{1,0:T(8,128)(2,1)S(1)} %collective-permute-done), channel_id=1, source_target_pairs={{0,32},{8,488},{16,48},{24,504},{32,64},{40,8},{48,80},{56,24},{64... | collective-permute-start | bytes 442376 | tf_op jit(solution)/shard_map/ppermute | solution.py:115
  28.6 2.6 %collective-permute-start.5 = (bf16[192,384]{1,0:T(8,128)(2,1)S(1)}, bf16[192,384]{1,0:T(8,128)(2,1)S(1)}, u32[]{:S(2)}, u32[]{:S(2)}) collective-permute-start(bf16[192,384]{1,0:T(8,128)(2,1)S(1)} %collective-permute-done.3), channel_id=1, source_target_pairs={{0,32},{8,488},{16,48},{24,504},{32,64},{40,8},{48,80},{56,24},{64... | collective-permute-start | bytes 442376 | tf_op jit(solution)/shard_map/ppermute | solution.py:115
  31.2 4.4 %collective-permute-start.4 = (bf16[192,384]{1,0:T(8,128)(2,1)S(1)}, bf16[192,384]{1,0:T(8,128)(2,1)S(1)}, u32[]{:S(2)}, u32[]{:S(2)}) collective-permute-start(bf16[192,384]{1,0:T(8,128)(2,1)S(1)} %collective-permute-done.2), channel_id=1, source_target_pairs={{0,32},{8,488},{16,48},{24,504},{32,64},{40,8},{48,80},{56,24},{64... | collective-permute-start | bytes 442376 | tf_op jit(solution)/shard_map/ppermute | solution.py:115
  35.8 2.6 %collective-permute-start.7 = (bf16[192,384]{1,0:T(8,128)(2,1)S(1)}, bf16[192,384]{1,0:T(8,128)(2,1)S(1)}, u32[]{:S(2)}, u32[]{:S(2)}) collective-permute-start(bf16[192,384]{1,0:T(8,128)(2,1)S(1)} %collective-permute-done.5), channel_id=1, source_target_pairs={{0,32},{8,488},{16,48},{24,504},{32,64},{40,8},{48,80},{56,24},{64... | collective-permute-start | bytes 442376 | tf_op jit(solution)/shard_map/ppermute | solution.py:115
  38.5 4.4 %collective-permute-start.6 = (bf16[192,384]{1,0:T(8,128)(2,1)S(1)}, bf16[192,384]{1,0:T(8,128)(2,1)S(1)}, u32[]{:S(2)}, u32[]{:S(2)}) collective-permute-start(bf16[192,384]{1,0:T(8,128)(2,1)S(1)} %collective-permute-done.4), channel_id=1, source_target_pairs={{0,32},{8,488},{16,48},{24,504},{32,64},{40,8},{48,80},{56,24},{64... | collective-permute-start | bytes 442376 | tf_op jit(solution)/shard_map/ppermute | solution.py:115
  42.9 2.8 %broadcast_in_dim.30 = bf16[16,384,384]{2,1,0:T(8,128)(2,1)} broadcast(bf16[]{:T(256)} %constant.111.clone.1), dimensions={} | broadcast | bytes 4718594 | tf_op jit(solution)/shard_map/broadcast_in_dim | solution.py:109
  46.4 2.6 %collective-permute-start.9 = (bf16[192,384]{1,0:T(8,128)(2,1)S(1)}, bf16[192,384]{1,0:T(8,128)(2,1)S(1)}, u32[]{:S(2)}, u32[]{:S(2)}) collective-permute-start(bf16[192,384]{1,0:T(8,128)(2,1)S(1)} %collective-permute-done.7), channel_id=1, source_target_pairs={{0,32},{8,488},{16,48},{24,504},{32,64},{40,8},{48,80},{56,24},{64... | collective-permute-start | bytes 442376 | tf_op jit(solution)/shard_map/ppermute | solution.py:115
  49.0 4.3 %collective-permute-start.8 = (bf16[192,384]{1,0:T(8,128)(2,1)S(1)}, bf16[192,384]{1,0:T(8,128)(2,1)S(1)}, u32[]{:S(2)}, u32[]{:S(2)}) collective-permute-start(bf16[192,384]{1,0:T(8,128)(2,1)S(1)} %collective-permute-done.6), channel_id=1, source_target_pairs={{0,32},{8,488},{16,48},{24,504},{32,64},{40,8},{48,80},{56,24},{64... | collective-permute-start | bytes 442376 | tf_op jit(solution)/shard_map/ppermute | solution.py:115
  64.8 3.8 %collective-permute-start.12 = (bf16[192,384]{1,0:T(8,128)(2,1)S(1)}, bf16[192,384]{1,0:T(8,128)(2,1)S(1)}, u32[]{:S(2)}, u32[]{:S(2)}) collective-permute-start(bf16[192,384]{1,0:T(8,128)(2,1)S(1)} %collective-permute-done.10), channel_id=1, source_target_pairs={{0,32},{8,488},{16,48},{24,504},{32,64},{40,8},{48,80},{56,24},{64... | collective-permute-start | bytes 442376 | tf_op jit(solution)/shard_map/ppermute | solution.py:115
  72.8 10.2 %collective-permute-start.16 = (bf16[7,384,384]{2,1,0:T(8,128)(2,1)}, bf16[7,384,384]{2,1,0:T(8,128)(2,1)S(1)}, u32[]{:S(2)}, u32[]{:S(2)}) collective-permute-start(bf16[7,384,384]{2,1,0:T(8,128)(2,1)} %get-tuple-element.6), channel_id=1, source_target_pairs={{0,8},{8,0},{1,9},{9,1},{2,10},{10,2},{3,11},{11,3},{4,12},{12,4},... | collective-permute-start | bytes 6193160 | tf_op jit(solution)/shard_map/ppermute | solution.py:120
  103.9 5.7 %collective-permute-start.17 = (bf16[2,128,384]{2,1,0:T(8,128)(2,1)}, bf16[2,128,384]{2,1,0:T(8,128)(2,1)}, u32[]{:S(2)}, u32[]{:S(2)}) collective-permute-start(bf16[2,128,384]{2,1,0:T(8,128)(2,1)} %slice.195), channel_id=1, source_target_pairs={{0,8},{8,16},{16,24},{24,32},{32,40},{40,48},{48,56},{56,64},{64,7... | collective-permute-start | bytes 589832 | tf_op jit(solution)/shard_map/ppermute | solution.py:27
  116.2 3.0 %reshape.74 = bf16[16,2,24,768]{3,2,1,0:T(8,128)(2,1)} reshape(bf16[16,96,384]{2,1,0:T(8,128)(2,1)} %slice.199) | data formatting | bytes 2359296 | tf_op jit(solution)/shard_map/reshape | solution.py:148
  125.1 3.7 %collective-permute-start.19 = (bf16[2,128,384]{2,1,0:T(8,128)(2,1)S(1)}, bf16[2,128,384]{2,1,0:T(8,128)(2,1)S(1)}, u32[]{:S(2)}, u32[]{:S(2)}) collective-permute-start(bf16[2,128,384]{2,1,0:T(8,128)(2,1)S(1)} %get-tuple-element.2), channel_id=1, source_target_pairs={{0,16},{8,24},{16,32},{24,40},{32,48},{40,56},{48,64},{56,72},{64,... | collective-permute-start | bytes 589832 | tf_op jit(solution)/shard_map/ppermute | solution.py:38
  131.0 4.8 %collective-permute-start.21 = (bf16[2,128,384]{2,1,0:T(8,128)(2,1)S(1)}, bf16[2,128,384]{2,1,0:T(8,128)(2,1)S(1)}, u32[]{:S(2)}, u32[]{:S(2)}) collective-permute-start(bf16[2,128,384]{2,1,0:T(8,128)(2,1)S(1)} %get-tuple-element.4), channel_id=1, source_target_pairs={{16,0},{24,8},{32,16},{40,24},{48,32},{56,40},{64,48},{72,56},{80,... | collective-permute-start | bytes 589832 | tf_op jit(solution)/shard_map/ppermute | solution.py:38
  135.8 3.9 %collective-permute-start.22 = (bf16[2,128,384]{2,1,0:T(8,128)(2,1)S(1)}, bf16[2,128,384]{2,1,0:T(8,128)(2,1)S(1)}, u32[]{:S(2)}, u32[]{:S(2)}) collective-permute-start(bf16[2,128,384]{2,1,0:T(8,128)(2,1)S(1)} %get-tuple-element.5), channel_id=1, source_target_pairs={{16,0},{24,8},{32,16},{40,24},{48,32},{56,40},{64,48},{72,56},{80,... | collective-permute-start | bytes 589832 | tf_op jit(solution)/shard_map/ppermute | solution.py:38
  141.1 6.3 %collective-permute-done.22 = bf16[2,128,384]{2,1,0:T(8,128)(2,1)S(1)} collective-permute-done((bf16[2,128,384]{2,1,0:T(8,128)(2,1)S(1)}, bf16[2,128,384]{2,1,0:T(8,128)(2,1)S(1)}, u32[]{:S(2)}, u32[]{:S(2)}) %collective-permute-start.22) | collective-permute-done | bytes 196640 | tf_op jit(solution)/shard_map/ppermute | solution.py:38
  148.5 5.8 %collective-permute-start.26 = (bf16[1,128,384]{2,1,0:T(8,128)(2,1)S(1)}, bf16[1,128,384]{2,1,0:T(8,128)(2,1)S(1)}, u32[]{:S(2)}, u32[]{:S(2)}) collective-permute-start(bf16[1,128,384]{2,1,0:T(8,128)(2,1)S(1)} %get-tuple-element.22), channel_id=1, source_target_pairs={{0,16},{8,24},{16,32},{24,40},{32,48},{40,56},{48,64},{56,72},{64,... | collective-permute-start | bytes 294920 | tf_op jit(solution)/shard_map/ppermute | solution.py:38
  156.2 7.0 %collective-permute-start.27 = (bf16[1,128,384]{2,1,0:T(8,128)(2,1)S(1)}, bf16[1,128,384]{2,1,0:T(8,128)(2,1)S(1)}, u32[]{:S(2)}, u32[]{:S(2)}) collective-permute-start(bf16[1,128,384]{2,1,0:T(8,128)(2,1)S(1)} %get-tuple-element.23), channel_id=1, source_target_pairs={{0,16},{8,24},{16,32},{24,40},{32,48},{40,56},{48,64},{56,72},{64,... | collective-permute-start | bytes 294920 | tf_op jit(solution)/shard_map/ppermute | solution.py:38
  168.7 3.6 %collective-permute-done.25 = bf16[1,128,384]{2,1,0:T(8,128)(2,1)S(1)} collective-permute-done((bf16[1,128,384]{2,1,0:T(8,128)(2,1)S(1)}, bf16[1,128,384]{2,1,0:T(8,128)(2,1)S(1)}, u32[]{:S(2)}, u32[]{:S(2)}) %collective-permute-start.25) | collective-permute-done | bytes 98336 | tf_op jit(solution)/shard_map/ppermute | solution.py:38
  173.6 6.5 %collective-permute-start.29 = (bf16[1,128,384]{2,1,0:T(8,128)(2,1)S(1)}, bf16[1,128,384]{2,1,0:T(8,128)(2,1)S(1)}, u32[]{:S(2)}, u32[]{:S(2)}) collective-permute-start(bf16[1,128,384]{2,1,0:T(8,128)(2,1)S(1)} %get-tuple-element.21), channel_id=1, source_target_pairs={{0,8},{8,16},{16,24},{24,32},{32,40},{40,48},{48,56},{56,64},{64,7... | collective-permute-start | bytes 294920 | tf_op jit(solution)/shard_map/ppermute | solution.py:27
  182.8 7.2 %collective-permute-done.28 = bf16[1,128,384]{2,1,0:T(8,128)(2,1)S(1)} collective-permute-done((bf16[1,128,384]{2,1,0:T(8,128)(2,1)S(1)}, bf16[1,128,384]{2,1,0:T(8,128)(2,1)S(1)}, u32[]{:S(2)}, u32[]{:S(2)}) %collective-permute-start.28) | collective-permute-done | bytes 98336 | tf_op jit(solution)/shard_map/ppermute | solution.py:28
  192.8 9.8 %collective-permute-done.30 = bf16[1,256,768]{2,1,0:T(8,128)(2,1)S(1)} collective-permute-done((bf16[1,256,768]{2,1,0:T(8,128)(2,1)S(1)}, bf16[1,256,768]{2,1,0:T(8,128)(2,1)S(1)}, u32[]{:S(2)}, u32[]{:S(2)}) %collective-permute-start.30) | collective-permute-done | bytes 393248 | tf_op jit(solution)/shard_map/ppermute | solution.py:45
  (129 shorter events, 79.7 us)
Async XLA Ops:
  12.1 7.3 %collective-permute-start.1 = (bf16[192,384]{1,0:T(8,128)(2,1)S(1)}, bf16[192,384]{1,0:T(8,128)(2,1)S(1)}, u32[]{:S(2)}, u32[]{:S(2)}) collective-permute-start(bf16[192,384]{1,0:T(8,128)(2,1)S(1)} %slice.185), channel_id=1, source_target_pairs={{0,32},{8,488},{16,48},{24,504},{32,64},{40,8},{48,80},{56,24},{64... | collective-permute-start | bytes 442376 | tf_op jit(solution)/shard_map/ppermute | solution.py:115
  14.1 7.3 %collective-permute-start = (bf16[192,384]{1,0:T(8,128)(2,1)S(1)}, bf16[192,384]{1,0:T(8,128)(2,1)S(1)}, u32[]{:S(2)}, u32[]{:S(2)}) collective-permute-start(bf16[192,384]{1,0:T(8,128)(2,1)S(1)} %slice.184), channel_id=1, source_target_pairs={{0,32},{8,488},{16,48},{24,504},{32,64},{40,8},{48,80},{56,24},{64... | collective-permute-start | bytes 442376 | tf_op jit(solution)/shard_map/ppermute | solution.py:115
  19.4 9.1 %collective-permute-start.3 = (bf16[192,384]{1,0:T(8,128)(2,1)S(1)}, bf16[192,384]{1,0:T(8,128)(2,1)S(1)}, u32[]{:S(2)}, u32[]{:S(2)}) collective-permute-start(bf16[192,384]{1,0:T(8,128)(2,1)S(1)} %collective-permute-done.1), channel_id=1, source_target_pairs={{0,32},{8,488},{16,48},{24,504},{32,64},{40,8},{48,80},{56,24},{64... | collective-permute-start | bytes 442376 | tf_op jit(solution)/shard_map/ppermute | solution.py:115
  21.4 9.8 %collective-permute-start.2 = (bf16[192,384]{1,0:T(8,128)(2,1)S(1)}, bf16[192,384]{1,0:T(8,128)(2,1)S(1)}, u32[]{:S(2)}, u32[]{:S(2)}) collective-permute-start(bf16[192,384]{1,0:T(8,128)(2,1)S(1)} %collective-permute-done), channel_id=1, source_target_pairs={{0,32},{8,488},{16,48},{24,504},{32,64},{40,8},{48,80},{56,24},{64... | collective-permute-start | bytes 442376 | tf_op jit(solution)/shard_map/ppermute | solution.py:115
  35.8 10.6 %collective-permute-start.7 = (bf16[192,384]{1,0:T(8,128)(2,1)S(1)}, bf16[192,384]{1,0:T(8,128)(2,1)S(1)}, u32[]{:S(2)}, u32[]{:S(2)}) collective-permute-start(bf16[192,384]{1,0:T(8,128)(2,1)S(1)} %collective-permute-done.5), channel_id=1, source_target_pairs={{0,32},{8,488},{16,48},{24,504},{32,64},{40,8},{48,80},{56,24},{64... | collective-permute-start | bytes 442376 | tf_op jit(solution)/shard_map/ppermute | solution.py:115
  38.5 10.6 %collective-permute-start.6 = (bf16[192,384]{1,0:T(8,128)(2,1)S(1)}, bf16[192,384]{1,0:T(8,128)(2,1)S(1)}, u32[]{:S(2)}, u32[]{:S(2)}) collective-permute-start(bf16[192,384]{1,0:T(8,128)(2,1)S(1)} %collective-permute-done.4), channel_id=1, source_target_pairs={{0,32},{8,488},{16,48},{24,504},{32,64},{40,8},{48,80},{56,24},{64... | collective-permute-start | bytes 442376 | tf_op jit(solution)/shard_map/ppermute | solution.py:115
  46.4 8.7 %collective-permute-start.9 = (bf16[192,384]{1,0:T(8,128)(2,1)S(1)}, bf16[192,384]{1,0:T(8,128)(2,1)S(1)}, u32[]{:S(2)}, u32[]{:S(2)}) collective-permute-start(bf16[192,384]{1,0:T(8,128)(2,1)S(1)} %collective-permute-done.7), channel_id=1, source_target_pairs={{0,32},{8,488},{16,48},{24,504},{32,64},{40,8},{48,80},{56,24},{64... | collective-permute-start | bytes 442376 | tf_op jit(solution)/shard_map/ppermute | solution.py:115
  49.0 8.7 %collective-permute-start.8 = (bf16[192,384]{1,0:T(8,128)(2,1)S(1)}, bf16[192,384]{1,0:T(8,128)(2,1)S(1)}, u32[]{:S(2)}, u32[]{:S(2)}) collective-permute-start(bf16[192,384]{1,0:T(8,128)(2,1)S(1)} %collective-permute-done.6), channel_id=1, source_target_pairs={{0,32},{8,488},{16,48},{24,504},{32,64},{40,8},{48,80},{56,24},{64... | collective-permute-start | bytes 442376 | tf_op jit(solution)/shard_map/ppermute | solution.py:115
  62.2 8.2 %collective-permute-start.13 = (bf16[192,384]{1,0:T(8,128)(2,1)S(1)}, bf16[192,384]{1,0:T(8,128)(2,1)S(1)}, u32[]{:S(2)}, u32[]{:S(2)}) collective-permute-start(bf16[192,384]{1,0:T(8,128)(2,1)S(1)} %collective-permute-done.11), channel_id=1, source_target_pairs={{0,32},{8,488},{16,48},{24,504},{32,64},{40,8},{48,80},{56,24},{64... | collective-permute-start | bytes 442376 | tf_op jit(solution)/shard_map/ppermute | solution.py:115
  72.8 20.1 %collective-permute-start.16 = (bf16[7,384,384]{2,1,0:T(8,128)(2,1)}, bf16[7,384,384]{2,1,0:T(8,128)(2,1)S(1)}, u32[]{:S(2)}, u32[]{:S(2)}) collective-permute-start(bf16[7,384,384]{2,1,0:T(8,128)(2,1)} %get-tuple-element.6), channel_id=1, source_target_pairs={{0,8},{8,0},{1,9},{9,1},{2,10},{10,2},{3,11},{11,3},{4,12},{12,4},... | collective-permute-start | bytes 6193160 | tf_op jit(solution)/shard_map/ppermute | solution.py:120
  103.9 16.8 %collective-permute-start.17 = (bf16[2,128,384]{2,1,0:T(8,128)(2,1)}, bf16[2,128,384]{2,1,0:T(8,128)(2,1)}, u32[]{:S(2)}, u32[]{:S(2)}) collective-permute-start(bf16[2,128,384]{2,1,0:T(8,128)(2,1)} %slice.195), channel_id=1, source_target_pairs={{0,8},{8,16},{16,24},{24,32},{32,40},{40,48},{48,56},{56,64},{64,7... | collective-permute-start | bytes 589832 | tf_op jit(solution)/shard_map/ppermute | solution.py:27
  110.3 11.5 %collective-permute-start.18 = (bf16[2,128,384]{2,1,0:T(8,128)(2,1)}, bf16[2,128,384]{2,1,0:T(8,128)(2,1)}, u32[]{:S(2)}, u32[]{:S(2)}) collective-permute-start(bf16[2,128,384]{2,1,0:T(8,128)(2,1)} %slice.198), channel_id=1, source_target_pairs={{8,0},{16,8},{24,16},{32,24},{40,32},{48,40},{56,48},{64,56},{72,6... | collective-permute-start | bytes 589832 | tf_op jit(solution)/shard_map/ppermute | solution.py:28
  125.1 15.3 %collective-permute-start.19 = (bf16[2,128,384]{2,1,0:T(8,128)(2,1)S(1)}, bf16[2,128,384]{2,1,0:T(8,128)(2,1)S(1)}, u32[]{:S(2)}, u32[]{:S(2)}) collective-permute-start(bf16[2,128,384]{2,1,0:T(8,128)(2,1)S(1)} %get-tuple-element.2), channel_id=1, source_target_pairs={{0,16},{8,24},{16,32},{24,40},{32,48},{40,56},{48,64},{56,72},{64,... | collective-permute-start | bytes 589832 | tf_op jit(solution)/shard_map/ppermute | solution.py:38
  128.9 11.5 %collective-permute-start.20 = (bf16[2,128,384]{2,1,0:T(8,128)(2,1)S(1)}, bf16[2,128,384]{2,1,0:T(8,128)(2,1)S(1)}, u32[]{:S(2)}, u32[]{:S(2)}) collective-permute-start(bf16[2,128,384]{2,1,0:T(8,128)(2,1)S(1)} %get-tuple-element.3), channel_id=1, source_target_pairs={{0,16},{8,24},{16,32},{24,40},{32,48},{40,56},{48,64},{56,72},{64,... | collective-permute-start | bytes 589832 | tf_op jit(solution)/shard_map/ppermute | solution.py:38
  131.0 10.1 %collective-permute-start.21 = (bf16[2,128,384]{2,1,0:T(8,128)(2,1)S(1)}, bf16[2,128,384]{2,1,0:T(8,128)(2,1)S(1)}, u32[]{:S(2)}, u32[]{:S(2)}) collective-permute-start(bf16[2,128,384]{2,1,0:T(8,128)(2,1)S(1)} %get-tuple-element.4), channel_id=1, source_target_pairs={{16,0},{24,8},{32,16},{40,24},{48,32},{56,40},{64,48},{72,56},{80,... | collective-permute-start | bytes 589832 | tf_op jit(solution)/shard_map/ppermute | solution.py:38
  135.8 11.6 %collective-permute-start.22 = (bf16[2,128,384]{2,1,0:T(8,128)(2,1)S(1)}, bf16[2,128,384]{2,1,0:T(8,128)(2,1)S(1)}, u32[]{:S(2)}, u32[]{:S(2)}) collective-permute-start(bf16[2,128,384]{2,1,0:T(8,128)(2,1)S(1)} %get-tuple-element.5), channel_id=1, source_target_pairs={{16,0},{24,8},{32,16},{40,24},{48,32},{56,40},{64,48},{72,56},{80,... | collective-permute-start | bytes 589832 | tf_op jit(solution)/shard_map/ppermute | solution.py:38
  148.5 19.8 %collective-permute-start.26 = (bf16[1,128,384]{2,1,0:T(8,128)(2,1)S(1)}, bf16[1,128,384]{2,1,0:T(8,128)(2,1)S(1)}, u32[]{:S(2)}, u32[]{:S(2)}) collective-permute-start(bf16[1,128,384]{2,1,0:T(8,128)(2,1)S(1)} %get-tuple-element.22), channel_id=1, source_target_pairs={{0,16},{8,24},{16,32},{24,40},{32,48},{40,56},{48,64},{56,72},{64,... | collective-permute-start | bytes 294920 | tf_op jit(solution)/shard_map/ppermute | solution.py:38
  154.3 14.4 %collective-permute-start.24 = (bf16[1,128,384]{2,1,0:T(8,128)(2,1)S(1)}, bf16[1,128,384]{2,1,0:T(8,128)(2,1)S(1)}, u32[]{:S(2)}, u32[]{:S(2)}) collective-permute-start(bf16[1,128,384]{2,1,0:T(8,128)(2,1)S(1)} %get-tuple-element.22), channel_id=1, source_target_pairs={{16,0},{24,8},{32,16},{40,24},{48,32},{56,40},{64,48},{72,56},{80,... | collective-permute-start | bytes 294920 | tf_op jit(solution)/shard_map/ppermute | solution.py:38
  156.2 12.0 %collective-permute-start.27 = (bf16[1,128,384]{2,1,0:T(8,128)(2,1)S(1)}, bf16[1,128,384]{2,1,0:T(8,128)(2,1)S(1)}, u32[]{:S(2)}, u32[]{:S(2)}) collective-permute-start(bf16[1,128,384]{2,1,0:T(8,128)(2,1)S(1)} %get-tuple-element.23), channel_id=1, source_target_pairs={{0,16},{8,24},{16,32},{24,40},{32,48},{40,56},{48,64},{56,72},{64,... | collective-permute-start | bytes 294920 | tf_op jit(solution)/shard_map/ppermute | solution.py:38
  163.2 9.1 %collective-permute-start.25 = (bf16[1,128,384]{2,1,0:T(8,128)(2,1)S(1)}, bf16[1,128,384]{2,1,0:T(8,128)(2,1)S(1)}, u32[]{:S(2)}, u32[]{:S(2)}) collective-permute-start(bf16[1,128,384]{2,1,0:T(8,128)(2,1)S(1)} %get-tuple-element.23), channel_id=1, source_target_pairs={{16,0},{24,8},{32,16},{40,24},{48,32},{56,40},{64,48},{72,56},{80,... | collective-permute-start | bytes 294920 | tf_op jit(solution)/shard_map/ppermute | solution.py:38
  166.1 26.7 %collective-permute-start.23 = (bf16[1,256,768]{2,1,0:T(8,128)(2,1)S(1)}, bf16[1,256,768]{2,1,0:T(8,128)(2,1)S(1)}, u32[]{:S(2)}, u32[]{:S(2)}) collective-permute-start(bf16[1,256,768]{2,1,0:T(8,128)(2,1)S(1)} %fusion.55), channel_id=1, source_target_pairs={{7,0},{0,1},{1,2},{2,3},{3,4},{4,5},{5,6},{6,7},{15,8},{8,9},{9,10... | collective-permute-start | bytes 1179656 | tf_op jit(solution)/shard_map/ppermute | solution.py:45
  173.6 8.8 %collective-permute-start.29 = (bf16[1,128,384]{2,1,0:T(8,128)(2,1)S(1)}, bf16[1,128,384]{2,1,0:T(8,128)(2,1)S(1)}, u32[]{:S(2)}, u32[]{:S(2)}) collective-permute-start(bf16[1,128,384]{2,1,0:T(8,128)(2,1)S(1)} %get-tuple-element.21), channel_id=1, source_target_pairs={{0,8},{8,16},{16,24},{24,32},{32,40},{40,48},{48,56},{56,64},{64,7... | collective-permute-start | bytes 294920 | tf_op jit(solution)/shard_map/ppermute | solution.py:27
  180.5 9.5 %collective-permute-start.28 = (bf16[1,128,384]{2,1,0:T(8,128)(2,1)S(1)}, bf16[1,128,384]{2,1,0:T(8,128)(2,1)S(1)}, u32[]{:S(2)}, u32[]{:S(2)}) collective-permute-start(bf16[1,128,384]{2,1,0:T(8,128)(2,1)S(1)} %get-tuple-element.20), channel_id=1, source_target_pairs={{8,0},{16,8},{24,16},{32,24},{40,32},{48,40},{56,48},{64,56},{72,6... | collective-permute-start | bytes 294920 | tf_op jit(solution)/shard_map/ppermute | solution.py:28
  190.8 11.7 %collective-permute-start.30 = (bf16[1,256,768]{2,1,0:T(8,128)(2,1)S(1)}, bf16[1,256,768]{2,1,0:T(8,128)(2,1)S(1)}, u32[]{:S(2)}, u32[]{:S(2)}) collective-permute-start(bf16[1,256,768]{2,1,0:T(8,128)(2,1)S(1)} %fusion.24), channel_id=1, source_target_pairs={{1,0},{2,1},{3,2},{4,3},{5,4},{6,5},{7,6},{0,7},{9,8},{10,9},{11,1... | collective-permute-start | bytes 1179656 | tf_op jit(solution)/shard_map/ppermute | solution.py:45
  (17 other events, 78.5 us)

commit v11 on v7

--- a/solution.py
+++ b/solution.py
@@ -114,10 +114,13 @@
         received.append(current)
         source = (here + sign * step) % span
         gathered = lax.dynamic_update_slice(gathered, current[None], (source, 0, 0))
-    shared = lax.ppermute(jnp.stack(received[: span - half - 1]), "core", [(0, 1), (1, 0)])
-    for step in range(1, span - half):
-        source = (here - sign * step) % span
-        gathered = lax.dynamic_update_slice(gathered, shared[step - 1][None], (source, 0, 0))
+    needed = span - half - 1
+    early = needed // 2 + needed % 2
+    for begin, end in ((0, early), (early, needed)):
+        shared = lax.ppermute(jnp.stack(received[begin:end]), "core", [(0, 1), (1, 0)])
+        for step in range(begin + 1, end + 1):
+            source = (here - sign * step) % span
+            gathered = lax.dynamic_update_slice(gathered, shared[step - 1 - begin][None], (source, 0, 0))
     return gathered
 
 

time: 196 us -> 195 us (level)
  starting transfers between devices: 95.7 us -> 91.7 us
  waiting for transfers between devices: 44.3 us -> 47.6 us
    ppermute x8, starting transfers between devices: 30.7 us -> 23.8 us  [ring_gather(): lax.ppermute(current[:cut], SEQ, route)]
    dynamic_update_slice x1 -> x8, other arithmetic: 0.74 us -> 6.08 us  [ring_gather(): gathered = lax.dynamic_update_slice(gathered, current[None], (source, 0, 0))]
    unnamed x6 -> x0, other arithmetic: 5.31 us -> none
    ppermute x8, waiting for transfers between devices: 6.19 us -> 10.9 us  [ring_gather(): lax.ppermute(current[cut:], SEQ, route)]
    ppermute x1 -> x2, starting transfers between devices: 10.2 us -> 14.5 us  [ring_gather(): lax.ppermute(jnp.stack(received[begin:end]), 'core', [(0, 1), (1, 0)])]
  transfers between devices with their start and end apart: 27 -> 28, of which waited for: 11 -> 11; matrix products, arithmetic and copies ran while one was open for 13% -> 15% of each run, Pallas kernels for 0% -> 0%
where the time goes in v11:
time: 195 us; the launch traced here: 194 us
  starting transfers between devices  91.7 us (47%)
  waiting for transfers between devices  47.6 us (24%)
  local copies, waits for them, and re-layouts  24 us (12%)
  matrix products  10.8 us (6%)
  blocking collectives  9.43 us (5%)
  other arithmetic  8.99 us (5%)
    ppermute x8, starting transfers between devices, ring_gather(): lax.ppermute(current[:cut], SEQ, route)  23.8 us
    ppermute x4, waiting for transfers between devices, from_behind(): return lax.ppermute(block, axis, route)  18.2 us
    ppermute x8, starting transfers between devices, ring_gather(): lax.ppermute(current[cut:], SEQ, route)  16.8 us
    ppermute x4, starting transfers between devices, from_behind(): return lax.ppermute(block, axis, route)  16.5 us
    ppermute x2, starting transfers between devices, ring_gather(): lax.ppermute(jnp.stack(received[begin:end]), 'core', [(0, 1), (1, 0)])  14.5 us
    ppermute x2, starting transfers between devices, padded(): before = lax.ppermute(last, axis, up)  11.7 us
    ppermute x8, waiting for transfers between devices, ring_gather(): lax.ppermute(current[cut:], SEQ, route)  10.9 us
    all_gather x2, blocking collectives, gather_weights(): both = lax.all_gather(lax.all_gather(both, 'core', axis=0), 'xh', axis=0)  9.43 us
  transfers between devices with their start and end apart: 28, of which 11 were waited for; matrix products, arithmetic and copies ran while one was open for 15% of the time, Pallas kernels for 0%

profile of v11, /device:TPU:127, one launch (start us, length us, event | category | flops | bytes accessed | tf_op | source)
XLA Modules:
  0.0 193.8 jit_solution(16212846125032013432)
XLA Ops:
  4.5 7.2 %all-gather.1 = bf16[4,8,12,384]{3,1,0,2:T(8,128)(2,1)S(1)} all-gather(bf16[2,8,12,384]{3,1,0,2:T(8,128)(2,1)S(1)} %bitcast.177), channel_id=3, replica_groups=mesh['z'=16,'xh'=2,'core'=2,'section'=8] {'xh'}, dimensions={0}, use_global_device_ids=true | all-gather | bytes 442368 | tf_op jit(solution)/shard_map/all_gather | solution.py:135
  16.0 3.4 %collective-permute-done.1 = bf16[192,384]{1,0:T(8,128)(2,1)S(1)} collective-permute-done((bf16[192,384]{1,0:T(8,128)(2,1)S(1)}, bf16[192,384]{1,0:T(8,128)(2,1)S(1)}, u32[]{:S(2)}, u32[]{:S(2)}) %collective-permute-start.1) | collective-permute-done | bytes 147488 | tf_op jit(solution)/shard_map/ppermute | solution.py:112
  21.4 7.2 %collective-permute-start.2 = (bf16[192,384]{1,0:T(8,128)(2,1)S(1)}, bf16[192,384]{1,0:T(8,128)(2,1)S(1)}, u32[]{:S(2)}, u32[]{:S(2)}) collective-permute-start(bf16[192,384]{1,0:T(8,128)(2,1)S(1)} %collective-permute-done), channel_id=1, source_target_pairs={{0,32},{8,488},{16,48},{24,504},{32,64},{40,8},{48,80},{56,24},{64... | collective-permute-start | bytes 442376 | tf_op jit(solution)/shard_map/ppermute | solution.py:112
  28.6 2.8 %broadcast_in_dim.30 = bf16[16,384,384]{2,1,0:T(8,128)(2,1)} broadcast(bf16[]{:T(256)} %constant.111.clone.1), dimensions={} | broadcast | bytes 4718594 | tf_op jit(solution)/shard_map/broadcast_in_dim | solution.py:106
  32.1 2.6 %collective-permute-start.5 = (bf16[192,384]{1,0:T(8,128)(2,1)S(1)}, bf16[192,384]{1,0:T(8,128)(2,1)S(1)}, u32[]{:S(2)}, u32[]{:S(2)}) collective-permute-start(bf16[192,384]{1,0:T(8,128)(2,1)S(1)} %collective-permute-done.3), channel_id=1, source_target_pairs={{0,32},{8,488},{16,48},{24,504},{32,64},{40,8},{48,80},{56,24},{64... | collective-permute-start | bytes 442376 | tf_op jit(solution)/shard_map/ppermute | solution.py:112
  34.8 4.4 %collective-permute-start.4 = (bf16[192,384]{1,0:T(8,128)(2,1)S(1)}, bf16[192,384]{1,0:T(8,128)(2,1)S(1)}, u32[]{:S(2)}, u32[]{:S(2)}) collective-permute-start(bf16[192,384]{1,0:T(8,128)(2,1)S(1)} %collective-permute-done.2), channel_id=1, source_target_pairs={{0,32},{8,488},{16,48},{24,504},{32,64},{40,8},{48,80},{56,24},{64... | collective-permute-start | bytes 442376 | tf_op jit(solution)/shard_map/ppermute | solution.py:112
  39.9 2.7 %collective-permute-start.7 = (bf16[192,384]{1,0:T(8,128)(2,1)S(1)}, bf16[192,384]{1,0:T(8,128)(2,1)S(1)}, u32[]{:S(2)}, u32[]{:S(2)}) collective-permute-start(bf16[192,384]{1,0:T(8,128)(2,1)S(1)} %collective-permute-done.5), channel_id=1, source_target_pairs={{0,32},{8,488},{16,48},{24,504},{32,64},{40,8},{48,80},{56,24},{64... | collective-permute-start | bytes 442376 | tf_op jit(solution)/shard_map/ppermute | solution.py:112
  42.6 2.7 %collective-permute-start.6 = (bf16[192,384]{1,0:T(8,128)(2,1)S(1)}, bf16[192,384]{1,0:T(8,128)(2,1)S(1)}, u32[]{:S(2)}, u32[]{:S(2)}) collective-permute-start(bf16[192,384]{1,0:T(8,128)(2,1)S(1)} %collective-permute-done.4), channel_id=1, source_target_pairs={{0,32},{8,488},{16,48},{24,504},{32,64},{40,8},{48,80},{56,24},{64... | collective-permute-start | bytes 442376 | tf_op jit(solution)/shard_map/ppermute | solution.py:112
  47.0 2.7 %collective-permute-done.6 = bf16[192,384]{1,0:T(8,128)(2,1)S(1)} collective-permute-done((bf16[192,384]{1,0:T(8,128)(2,1)S(1)}, bf16[192,384]{1,0:T(8,128)(2,1)S(1)}, u32[]{:S(2)}, u32[]{:S(2)}) %collective-permute-start.6) | collective-permute-done | bytes 147488 | tf_op jit(solution)/shard_map/ppermute | solution.py:112
  49.9 6.8 %collective-permute-start.16 = (bf16[4,384,384]{2,1,0:T(8,128)(2,1)S(1)}, bf16[4,384,384]{2,1,0:T(8,128)(2,1)S(1)}, u32[]{:S(2)}, u32[]{:S(2)}) collective-permute-start(bf16[4,384,384]{2,1,0:T(8,128)(2,1)S(1)} %pad_maximum_fusion), channel_id=1, source_target_pairs={{0,8},{8,0},{1,9},{9,1},{2,10},{10,2},{3,11},{11,3},{4,12},{12,4},... | collective-permute-start | bytes 3538952 | tf_op jit(solution)/shard_map/ppermute | solution.py:120
  82.0 7.7 %collective-permute-start.17 = (bf16[3,384,384]{2,1,0:T(8,128)(2,1)S(1)}, bf16[3,384,384]{2,1,0:T(8,128)(2,1)S(1)}, u32[]{:S(2)}, u32[]{:S(2)}) collective-permute-start(bf16[3,384,384]{2,1,0:T(8,128)(2,1)S(1)} %pad_maximum_fusion.1), channel_id=1, source_target_pairs={{0,8},{8,0},{1,9},{9,1},{2,10},{10,2},{3,11},{11,3},{4,12},{12,4},... | collective-permute-start | bytes 2654216 | tf_op jit(solution)/shard_map/ppermute | solution.py:120
  102.2 5.9 %collective-permute-start.18 = (bf16[2,128,384]{2,1,0:T(8,128)(2,1)}, bf16[2,128,384]{2,1,0:T(8,128)(2,1)}, u32[]{:S(2)}, u32[]{:S(2)}) collective-permute-start(bf16[2,128,384]{2,1,0:T(8,128)(2,1)} %slice.169), channel_id=1, source_target_pairs={{0,8},{8,16},{16,24},{24,32},{32,40},{40,48},{48,56},{56,64},{64,7... | collective-permute-start | bytes 589832 | tf_op jit(solution)/shard_map/ppermute | solution.py:27
  112.4 2.4 %slice.173 = bf16[16,96,384]{2,1,0:T(8,128)(2,1)} slice(bf16[16,384,384]{2,1,0:T(8,128)(2,1)} %slice_dynamic-update-slice_fusion), slice={[0:16], [288:384], [0:384]} | slice | bytes 2359296 | tf_op jit(solution)/shard_map/slice | solution.py:148
  114.8 3.0 %reshape.74 = bf16[16,2,24,768]{3,2,1,0:T(8,128)(2,1)} reshape(bf16[16,96,384]{2,1,0:T(8,128)(2,1)} %slice.173) | data formatting | bytes 2359296 | tf_op jit(solution)/shard_map/reshape | solution.py:148
  122.9 3.7 %collective-permute-start.20 = (bf16[2,256,384]{2,1,0:T(8,128)(2,1)S(1)}, bf16[2,256,384]{2,1,0:T(8,128)(2,1)S(1)}, u32[]{:S(2)}, u32[]{:S(2)}) collective-permute-start(bf16[2,256,384]{2,1,0:T(8,128)(2,1)S(1)} %convolution_convert_fusion.1), channel_id=1, source_target_pairs={{0,16},{8,24},{16,32},{24,40},{32,48},{40,56},{48,64},{56,72},{64,... | collective-permute-start | bytes 1179656 | tf_op jit(solution)/shard_map/ppermute | solution.py:36
  127.4 3.0 %collective-permute-start.21 = (bf16[2,256,384]{2,1,0:T(8,128)(2,1)S(1)}, bf16[2,256,384]{2,1,0:T(8,128)(2,1)S(1)}, u32[]{:S(2)}, u32[]{:S(2)}) collective-permute-start(bf16[2,256,384]{2,1,0:T(8,128)(2,1)S(1)} %convolution_convert_fusion), channel_id=1, source_target_pairs={{16,0},{24,8},{32,16},{40,24},{48,32},{56,40},{64,48},{72,56},{80,... | collective-permute-start | bytes 1179656 | tf_op jit(solution)/shard_map/ppermute | solution.py:36
  131.2 4.4 %collective-permute-done.20 = bf16[2,256,384]{2,1,0:T(8,128)(2,1)S(1)} collective-permute-done((bf16[2,256,384]{2,1,0:T(8,128)(2,1)S(1)}, bf16[2,256,384]{2,1,0:T(8,128)(2,1)S(1)}, u32[]{:S(2)}, u32[]{:S(2)}) %collective-permute-start.20) | collective-permute-done | bytes 393248 | tf_op jit(solution)/shard_map/ppermute | solution.py:36
  135.6 8.5 %collective-permute-done.21 = bf16[2,256,384]{2,1,0:T(8,128)(2,1)S(1)} collective-permute-done((bf16[2,256,384]{2,1,0:T(8,128)(2,1)S(1)}, bf16[2,256,384]{2,1,0:T(8,128)(2,1)S(1)}, u32[]{:S(2)}, u32[]{:S(2)}) %collective-permute-start.21) | collective-permute-done | bytes 393248 | tf_op jit(solution)/shard_map/ppermute | solution.py:36
  144.7 7.6 %collective-permute-start.24 = (bf16[1,256,384]{2,1,0:T(8,128)(2,1)S(1)}, bf16[1,256,384]{2,1,0:T(8,128)(2,1)S(1)}, u32[]{:S(2)}, u32[]{:S(2)}) collective-permute-start(bf16[1,256,384]{2,1,0:T(8,128)(2,1)S(1)} %fusion.101), channel_id=1, source_target_pairs={{0,16},{8,24},{16,32},{24,40},{32,48},{40,56},{48,64},{56,72},{64,... | collective-permute-start | bytes 589832 | tf_op jit(solution)/shard_map/ppermute | solution.py:36
  158.1 5.4 %collective-permute-done.23 = bf16[1,256,384]{2,1,0:T(8,128)(2,1)S(1)} collective-permute-done((bf16[1,256,384]{2,1,0:T(8,128)(2,1)S(1)}, bf16[1,256,384]{2,1,0:T(8,128)(2,1)S(1)}, u32[]{:S(2)}, u32[]{:S(2)}) %collective-permute-start.23) | collective-permute-done | bytes 196640 | tf_op jit(solution)/shard_map/ppermute | solution.py:36
  164.8 5.8 %collective-permute-start.26 = (bf16[1,128,384]{2,1,0:T(8,128)(2,1)S(1)}, bf16[1,128,384]{2,1,0:T(8,128)(2,1)S(1)}, u32[]{:S(2)}, u32[]{:S(2)}) collective-permute-start(bf16[1,128,384]{2,1,0:T(8,128)(2,1)S(1)} %get-tuple-element.3), channel_id=1, source_target_pairs={{0,8},{8,16},{16,24},{24,32},{32,40},{40,48},{48,56},{56,64},{64,7... | collective-permute-start | bytes 294920 | tf_op jit(solution)/shard_map/ppermute | solution.py:27
  173.4 7.2 %collective-permute-done.25 = bf16[1,128,384]{2,1,0:T(8,128)(2,1)S(1)} collective-permute-done((bf16[1,128,384]{2,1,0:T(8,128)(2,1)S(1)}, bf16[1,128,384]{2,1,0:T(8,128)(2,1)S(1)}, u32[]{:S(2)}, u32[]{:S(2)}) %collective-permute-start.25) | collective-permute-done | bytes 98336 | tf_op jit(solution)/shard_map/ppermute | solution.py:28
  181.4 2.5 %collective-permute-start.27 = (bf16[1,256,768]{2,1,0:T(8,128)(2,1)S(1)}, bf16[1,256,768]{2,1,0:T(8,128)(2,1)S(1)}, u32[]{:S(2)}, u32[]{:S(2)}) collective-permute-start(bf16[1,256,768]{2,1,0:T(8,128)(2,1)S(1)} %fusion.24), channel_id=1, source_target_pairs={{1,0},{2,1},{3,2},{4,3},{5,4},{6,5},{7,6},{0,7},{9,8},{10,9},{11,1... | collective-permute-start | bytes 1179656 | tf_op jit(solution)/shard_map/ppermute | solution.py:42
  183.9 8.5 %collective-permute-done.27 = bf16[1,256,768]{2,1,0:T(8,128)(2,1)S(1)} collective-permute-done((bf16[1,256,768]{2,1,0:T(8,128)(2,1)S(1)}, bf16[1,256,768]{2,1,0:T(8,128)(2,1)S(1)}, u32[]{:S(2)}, u32[]{:S(2)}) %collective-permute-start.27) | collective-permute-done | bytes 393248 | tf_op jit(solution)/shard_map/ppermute | solution.py:42
  (127 shorter events, 74.6 us)
Async XLA Ops:
  12.1 7.3 %collective-permute-start.1 = (bf16[192,384]{1,0:T(8,128)(2,1)S(1)}, bf16[192,384]{1,0:T(8,128)(2,1)S(1)}, u32[]{:S(2)}, u32[]{:S(2)}) collective-permute-start(bf16[192,384]{1,0:T(8,128)(2,1)S(1)} %slice.159), channel_id=1, source_target_pairs={{0,32},{8,488},{16,48},{24,504},{32,64},{40,8},{48,80},{56,24},{64... | collective-permute-start | bytes 442376 | tf_op jit(solution)/shard_map/ppermute | solution.py:112
  14.1 7.3 %collective-permute-start = (bf16[192,384]{1,0:T(8,128)(2,1)S(1)}, bf16[192,384]{1,0:T(8,128)(2,1)S(1)}, u32[]{:S(2)}, u32[]{:S(2)}) collective-permute-start(bf16[192,384]{1,0:T(8,128)(2,1)S(1)} %slice.158), channel_id=1, source_target_pairs={{0,32},{8,488},{16,48},{24,504},{32,64},{40,8},{48,80},{56,24},{64... | collective-permute-start | bytes 442376 | tf_op jit(solution)/shard_map/ppermute | solution.py:112
  19.4 12.7 %collective-permute-start.3 = (bf16[192,384]{1,0:T(8,128)(2,1)S(1)}, bf16[192,384]{1,0:T(8,128)(2,1)S(1)}, u32[]{:S(2)}, u32[]{:S(2)}) collective-permute-start(bf16[192,384]{1,0:T(8,128)(2,1)S(1)} %collective-permute-done.1), channel_id=1, source_target_pairs={{0,32},{8,488},{16,48},{24,504},{32,64},{40,8},{48,80},{56,24},{64... | collective-permute-start | bytes 442376 | tf_op jit(solution)/shard_map/ppermute | solution.py:112
  21.4 13.4 %collective-permute-start.2 = (bf16[192,384]{1,0:T(8,128)(2,1)S(1)}, bf16[192,384]{1,0:T(8,128)(2,1)S(1)}, u32[]{:S(2)}, u32[]{:S(2)}) collective-permute-start(bf16[192,384]{1,0:T(8,128)(2,1)S(1)} %collective-permute-done), channel_id=1, source_target_pairs={{0,32},{8,488},{16,48},{24,504},{32,64},{40,8},{48,80},{56,24},{64... | collective-permute-start | bytes 442376 | tf_op jit(solution)/shard_map/ppermute | solution.py:112
  32.1 7.8 %collective-permute-start.5 = (bf16[192,384]{1,0:T(8,128)(2,1)S(1)}, bf16[192,384]{1,0:T(8,128)(2,1)S(1)}, u32[]{:S(2)}, u32[]{:S(2)}) collective-permute-start(bf16[192,384]{1,0:T(8,128)(2,1)S(1)} %collective-permute-done.3), channel_id=1, source_target_pairs={{0,32},{8,488},{16,48},{24,504},{32,64},{40,8},{48,80},{56,24},{64... | collective-permute-start | bytes 442376 | tf_op jit(solution)/shard_map/ppermute | solution.py:112
  34.8 7.8 %collective-permute-start.4 = (bf16[192,384]{1,0:T(8,128)(2,1)S(1)}, bf16[192,384]{1,0:T(8,128)(2,1)S(1)}, u32[]{:S(2)}, u32[]{:S(2)}) collective-permute-start(bf16[192,384]{1,0:T(8,128)(2,1)S(1)} %collective-permute-done.2), channel_id=1, source_target_pairs={{0,32},{8,488},{16,48},{24,504},{32,64},{40,8},{48,80},{56,24},{64... | collective-permute-start | bytes 442376 | tf_op jit(solution)/shard_map/ppermute | solution.py:112
  39.9 7.1 %collective-permute-start.7 = (bf16[192,384]{1,0:T(8,128)(2,1)S(1)}, bf16[192,384]{1,0:T(8,128)(2,1)S(1)}, u32[]{:S(2)}, u32[]{:S(2)}) collective-permute-start(bf16[192,384]{1,0:T(8,128)(2,1)S(1)} %collective-permute-done.5), channel_id=1, source_target_pairs={{0,32},{8,488},{16,48},{24,504},{32,64},{40,8},{48,80},{56,24},{64... | collective-permute-start | bytes 442376 | tf_op jit(solution)/shard_map/ppermute | solution.py:112
  42.6 7.1 %collective-permute-start.6 = (bf16[192,384]{1,0:T(8,128)(2,1)S(1)}, bf16[192,384]{1,0:T(8,128)(2,1)S(1)}, u32[]{:S(2)}, u32[]{:S(2)}) collective-permute-start(bf16[192,384]{1,0:T(8,128)(2,1)S(1)} %collective-permute-done.4), channel_id=1, source_target_pairs={{0,32},{8,488},{16,48},{24,504},{32,64},{40,8},{48,80},{56,24},{64... | collective-permute-start | bytes 442376 | tf_op jit(solution)/shard_map/ppermute | solution.py:112
  49.9 41.4 %collective-permute-start.16 = (bf16[4,384,384]{2,1,0:T(8,128)(2,1)S(1)}, bf16[4,384,384]{2,1,0:T(8,128)(2,1)S(1)}, u32[]{:S(2)}, u32[]{:S(2)}) collective-permute-start(bf16[4,384,384]{2,1,0:T(8,128)(2,1)S(1)} %pad_maximum_fusion), channel_id=1, source_target_pairs={{0,8},{8,0},{1,9},{9,1},{2,10},{10,2},{3,11},{11,3},{4,12},{12,4},... | collective-permute-start | bytes 3538952 | tf_op jit(solution)/shard_map/ppermute | solution.py:120
  56.7 7.1 %collective-permute-start.9 = (bf16[192,384]{1,0:T(8,128)(2,1)S(1)}, bf16[192,384]{1,0:T(8,128)(2,1)S(1)}, u32[]{:S(2)}, u32[]{:S(2)}) collective-permute-start(bf16[192,384]{1,0:T(8,128)(2,1)S(1)} %collective-permute-done.7), channel_id=1, source_target_pairs={{0,32},{8,488},{16,48},{24,504},{32,64},{40,8},{48,80},{56,24},{64... | collective-permute-start | bytes 442376 | tf_op jit(solution)/shard_map/ppermute | solution.py:112
  58.7 7.1 %collective-permute-start.8 = (bf16[192,384]{1,0:T(8,128)(2,1)S(1)}, bf16[192,384]{1,0:T(8,128)(2,1)S(1)}, u32[]{:S(2)}, u32[]{:S(2)}) collective-permute-start(bf16[192,384]{1,0:T(8,128)(2,1)S(1)} %collective-permute-done.6), channel_id=1, source_target_pairs={{0,32},{8,488},{16,48},{24,504},{32,64},{40,8},{48,80},{56,24},{64... | collective-permute-start | bytes 442376 | tf_op jit(solution)/shard_map/ppermute | solution.py:112
  78.0 12.5 %collective-permute-start.15 = (bf16[192,384]{1,0:T(8,128)(2,1)S(1)}, bf16[192,384]{1,0:T(8,128)(2,1)S(1)}, u32[]{:S(2)}, u32[]{:S(2)}) collective-permute-start(bf16[192,384]{1,0:T(8,128)(2,1)S(1)} %collective-permute-done.13), channel_id=1, source_target_pairs={{0,32},{8,488},{16,48},{24,504},{32,64},{40,8},{48,80},{56,24},{64... | collective-permute-start | bytes 442376 | tf_op jit(solution)/shard_map/ppermute | solution.py:112
  79.9 10.6 %collective-permute-start.14 = (bf16[192,384]{1,0:T(8,128)(2,1)S(1)}, bf16[192,384]{1,0:T(8,128)(2,1)S(1)}, u32[]{:S(2)}, u32[]{:S(2)}) collective-permute-start(bf16[192,384]{1,0:T(8,128)(2,1)S(1)} %collective-permute-done.12), channel_id=1, source_target_pairs={{0,32},{8,488},{16,48},{24,504},{32,64},{40,8},{48,80},{56,24},{64... | collective-permute-start | bytes 442376 | tf_op jit(solution)/shard_map/ppermute | solution.py:112
  82.0 12.2 %collective-permute-start.17 = (bf16[3,384,384]{2,1,0:T(8,128)(2,1)S(1)}, bf16[3,384,384]{2,1,0:T(8,128)(2,1)S(1)}, u32[]{:S(2)}, u32[]{:S(2)}) collective-permute-start(bf16[3,384,384]{2,1,0:T(8,128)(2,1)S(1)} %pad_maximum_fusion.1), channel_id=1, source_target_pairs={{0,8},{8,0},{1,9},{9,1},{2,10},{10,2},{3,11},{11,3},{4,12},{12,4},... | collective-permute-start | bytes 2654216 | tf_op jit(solution)/shard_map/ppermute | solution.py:120
  102.2 17.0 %collective-permute-start.18 = (bf16[2,128,384]{2,1,0:T(8,128)(2,1)}, bf16[2,128,384]{2,1,0:T(8,128)(2,1)}, u32[]{:S(2)}, u32[]{:S(2)}) collective-permute-start(bf16[2,128,384]{2,1,0:T(8,128)(2,1)} %slice.169), channel_id=1, source_target_pairs={{0,8},{8,16},{16,24},{24,32},{32,40},{40,48},{48,56},{56,64},{64,7... | collective-permute-start | bytes 589832 | tf_op jit(solution)/shard_map/ppermute | solution.py:27
  108.8 11.5 %collective-permute-start.19 = (bf16[2,128,384]{2,1,0:T(8,128)(2,1)}, bf16[2,128,384]{2,1,0:T(8,128)(2,1)}, u32[]{:S(2)}, u32[]{:S(2)}) collective-permute-start(bf16[2,128,384]{2,1,0:T(8,128)(2,1)} %slice.172), channel_id=1, source_target_pairs={{8,0},{16,8},{24,16},{32,24},{40,32},{48,40},{56,48},{64,56},{72,6... | collective-permute-start | bytes 589832 | tf_op jit(solution)/shard_map/ppermute | solution.py:28
  122.9 12.6 %collective-permute-start.20 = (bf16[2,256,384]{2,1,0:T(8,128)(2,1)S(1)}, bf16[2,256,384]{2,1,0:T(8,128)(2,1)S(1)}, u32[]{:S(2)}, u32[]{:S(2)}) collective-permute-start(bf16[2,256,384]{2,1,0:T(8,128)(2,1)S(1)} %convolution_convert_fusion.1), channel_id=1, source_target_pairs={{0,16},{8,24},{16,32},{24,40},{32,48},{40,56},{48,64},{56,72},{64,... | collective-permute-start | bytes 1179656 | tf_op jit(solution)/shard_map/ppermute | solution.py:36
  127.4 16.7 %collective-permute-start.21 = (bf16[2,256,384]{2,1,0:T(8,128)(2,1)S(1)}, bf16[2,256,384]{2,1,0:T(8,128)(2,1)S(1)}, u32[]{:S(2)}, u32[]{:S(2)}) collective-permute-start(bf16[2,256,384]{2,1,0:T(8,128)(2,1)S(1)} %convolution_convert_fusion), channel_id=1, source_target_pairs={{16,0},{24,8},{32,16},{40,24},{48,32},{56,40},{64,48},{72,56},{80,... | collective-permute-start | bytes 1179656 | tf_op jit(solution)/shard_map/ppermute | solution.py:36
  144.7 13.0 %collective-permute-start.24 = (bf16[1,256,384]{2,1,0:T(8,128)(2,1)S(1)}, bf16[1,256,384]{2,1,0:T(8,128)(2,1)S(1)}, u32[]{:S(2)}, u32[]{:S(2)}) collective-permute-start(bf16[1,256,384]{2,1,0:T(8,128)(2,1)S(1)} %fusion.101), channel_id=1, source_target_pairs={{0,16},{8,24},{16,32},{24,40},{32,48},{40,56},{48,64},{56,72},{64,... | collective-permute-start | bytes 589832 | tf_op jit(solution)/shard_map/ppermute | solution.py:36
  152.3 11.2 %collective-permute-start.23 = (bf16[1,256,384]{2,1,0:T(8,128)(2,1)S(1)}, bf16[1,256,384]{2,1,0:T(8,128)(2,1)S(1)}, u32[]{:S(2)}, u32[]{:S(2)}) collective-permute-start(bf16[1,256,384]{2,1,0:T(8,128)(2,1)S(1)} %fusion.101), channel_id=1, source_target_pairs={{16,0},{24,8},{32,16},{40,24},{48,32},{56,40},{64,48},{72,56},{80,... | collective-permute-start | bytes 589832 | tf_op jit(solution)/shard_map/ppermute | solution.py:36
  155.2 28.7 %collective-permute-start.22 = (bf16[1,256,768]{2,1,0:T(8,128)(2,1)S(1)}, bf16[1,256,768]{2,1,0:T(8,128)(2,1)S(1)}, u32[]{:S(2)}, u32[]{:S(2)}) collective-permute-start(bf16[1,256,768]{2,1,0:T(8,128)(2,1)S(1)} %fusion.55), channel_id=1, source_target_pairs={{7,0},{0,1},{1,2},{2,3},{3,4},{4,5},{5,6},{6,7},{15,8},{8,9},{9,10... | collective-permute-start | bytes 1179656 | tf_op jit(solution)/shard_map/ppermute | solution.py:42
  164.8 8.1 %collective-permute-start.26 = (bf16[1,128,384]{2,1,0:T(8,128)(2,1)S(1)}, bf16[1,128,384]{2,1,0:T(8,128)(2,1)S(1)}, u32[]{:S(2)}, u32[]{:S(2)}) collective-permute-start(bf16[1,128,384]{2,1,0:T(8,128)(2,1)S(1)} %get-tuple-element.3), channel_id=1, source_target_pairs={{0,8},{8,16},{16,24},{24,32},{32,40},{40,48},{48,56},{56,64},{64,7... | collective-permute-start | bytes 294920 | tf_op jit(solution)/shard_map/ppermute | solution.py:27
  171.0 9.5 %collective-permute-start.25 = (bf16[1,128,384]{2,1,0:T(8,128)(2,1)S(1)}, bf16[1,128,384]{2,1,0:T(8,128)(2,1)S(1)}, u32[]{:S(2)}, u32[]{:S(2)}) collective-permute-start(bf16[1,128,384]{2,1,0:T(8,128)(2,1)S(1)} %get-tuple-element.2), channel_id=1, source_target_pairs={{8,0},{16,8},{24,16},{32,24},{40,32},{48,40},{56,48},{64,56},{72,6... | collective-permute-start | bytes 294920 | tf_op jit(solution)/shard_map/ppermute | solution.py:28
  181.4 10.9 %collective-permute-start.27 = (bf16[1,256,768]{2,1,0:T(8,128)(2,1)S(1)}, bf16[1,256,768]{2,1,0:T(8,128)(2,1)S(1)}, u32[]{:S(2)}, u32[]{:S(2)}) collective-permute-start(bf16[1,256,768]{2,1,0:T(8,128)(2,1)S(1)} %fusion.24), channel_id=1, source_target_pairs={{1,0},{2,1},{3,2},{4,3},{5,4},{6,5},{7,6},{0,7},{9,8},{10,9},{11,1... | collective-permute-start | bytes 1179656 | tf_op jit(solution)/shard_map/ppermute | solution.py:42
  (14 other events, 60.9 us)

commit v12 on v11

--- a/solution.py
+++ b/solution.py
@@ -108,8 +108,9 @@
     current, received = block, []
     cut = rows // 2
     for step in range(1, half + 1):
+        third = rows // 3
         current = jnp.concatenate(
-            [lax.ppermute(current[:cut], SEQ, route), lax.ppermute(current[cut:], SEQ, route)], axis=0
+            [lax.ppermute(current[i * third : (i + 1) * third], SEQ, route) for i in range(3)], axis=0
         )
         received.append(current)
         source = (here + sign * step) % span

time: 195 us -> 219 us (1.12)
  starting transfers between devices: 91.7 us -> 118 us
  waiting for transfers between devices: 47.6 us -> 44.6 us
    ppermute x16 -> x24, starting transfers between devices: 40.6 us -> 68.6 us  [ring_gather(): lax.ppermute(current[i * third:(i + 1) * third], SEQ, route)]
    ppermute x16 -> x24, waiting for transfers between devices: 13.7 us -> 9.76 us  [ring_gather(): lax.ppermute(current[i * third:(i + 1) * third], SEQ, route)]
    ppermute x2, starting transfers between devices: 14.5 us -> 11.7 us  [ring_gather(): lax.ppermute(jnp.stack(received[begin:end]), 'core', [(0, 1), (1, 0)])]
    ppermute x2, starting transfers between devices: 11.7 us -> 14 us  [padded(): before = lax.ppermute(last, axis, up)]
  transfers between devices with their start and end apart: 28 -> 36, of which waited for: 11 -> 10; matrix products, arithmetic and copies ran while one was open for 15% -> 13% of each run, Pallas kernels for 0% -> 0%
where the time goes in v12:
time: 219 us; the launch traced here: 217 us
  starting transfers between devices  118 us (54%)
  waiting for transfers between devices  44.6 us (20%)
  local copies, waits for them, and re-layouts  24.1 us (11%)
  matrix products  10.8 us (5%)
  blocking collectives  9.43 us (4%)
  other arithmetic  8.94 us (4%)
    ppermute x24, starting transfers between devices, ring_gather(): lax.ppermute(current[i * third:(i + 1) * third], SEQ, route)  68.6 us
    ppermute x4, waiting for transfers between devices, from_behind(): return lax.ppermute(block, axis, route)  19.2 us
    ppermute x4, starting transfers between devices, from_behind(): return lax.ppermute(block, axis, route)  15.6 us
    ppermute x2, starting transfers between devices, padded(): before = lax.ppermute(last, axis, up)  14 us
    ppermute x2, starting transfers between devices, ring_gather(): lax.ppermute(jnp.stack(received[begin:end]), 'core', [(0, 1), (1, 0)])  11.7 us
    ppermute x24, waiting for transfers between devices, ring_gather(): lax.ppermute(current[i * third:(i + 1) * third], SEQ, route)  9.76 us
    all_gather x2, blocking collectives, gather_weights(): both = lax.all_gather(lax.all_gather(both, 'core', axis=0), 'xh', axis=0)  9.43 us
    ppermute x2, waiting for transfers between devices, from_behind_2(): return lax.ppermute(block, axis, route)  8.43 us
  transfers between devices with their start and end apart: 36, of which 10 were waited for; matrix products, arithmetic and copies ran while one was open for 13% of the time, Pallas kernels for 0%

profile of v12, /device:TPU:127, one launch (start us, length us, event | category | flops | bytes accessed | tf_op | source)
XLA Modules:
  0.0 217.5 jit_solution(9080755371495019611)
XLA Ops:
  4.5 7.2 %all-gather.1 = bf16[4,8,12,384]{3,1,0,2:T(8,128)(2,1)S(1)} all-gather(bf16[2,8,12,384]{3,1,0,2:T(8,128)(2,1)S(1)} %bitcast.177), channel_id=3, replica_groups=mesh['z'=16,'xh'=2,'core'=2,'section'=8] {'xh'}, dimensions={0}, use_global_device_ids=true | all-gather | bytes 442368 | tf_op jit(solution)/shard_map/all_gather | solution.py:136
  18.0 2.8 %broadcast_in_dim.30 = bf16[16,384,384]{2,1,0:T(8,128)(2,1)} broadcast(bf16[]{:T(256)} %constant.111.clone.1), dimensions={} | broadcast | bytes 4718594 | tf_op jit(solution)/shard_map/broadcast_in_dim | solution.py:106
  21.4 10.6 %collective-permute-start.5 = (bf16[128,384]{1,0:T(8,128)(2,1)S(1)}, bf16[128,384]{1,0:T(8,128)(2,1)S(1)}, u32[]{:S(2)}, u32[]{:S(2)}) collective-permute-start(bf16[128,384]{1,0:T(8,128)(2,1)S(1)} %collective-permute-done.2), channel_id=1, source_target_pairs={{0,32},{8,488},{16,48},{24,504},{32,64},{40,8},{48,80},{56,24},{64... | collective-permute-start | bytes 294920 | tf_op jit(solution)/shard_map/ppermute | solution.py:113
  32.0 2.6 %collective-permute-start.3 = (bf16[128,384]{1,0:T(8,128)(2,1)S(1)}, bf16[128,384]{1,0:T(8,128)(2,1)S(1)}, u32[]{:S(2)}, u32[]{:S(2)}) collective-permute-start(bf16[128,384]{1,0:T(8,128)(2,1)S(1)} %collective-permute-done), channel_id=1, source_target_pairs={{0,32},{8,488},{16,48},{24,504},{32,64},{40,8},{48,80},{56,24},{64... | collective-permute-start | bytes 294920 | tf_op jit(solution)/shard_map/ppermute | solution.py:113
  34.7 2.6 %collective-permute-start.4 = (bf16[128,384]{1,0:T(8,128)(2,1)S(1)}, bf16[128,384]{1,0:T(8,128)(2,1)S(1)}, u32[]{:S(2)}, u32[]{:S(2)}) collective-permute-start(bf16[128,384]{1,0:T(8,128)(2,1)S(1)} %collective-permute-done.1), channel_id=1, source_target_pairs={{0,32},{8,488},{16,48},{24,504},{32,64},{40,8},{48,80},{56,24},{64... | collective-permute-start | bytes 294920 | tf_op jit(solution)/shard_map/ppermute | solution.py:113
  38.1 2.6 %collective-permute-start.8 = (bf16[128,384]{1,0:T(8,128)(2,1)S(1)}, bf16[128,384]{1,0:T(8,128)(2,1)S(1)}, u32[]{:S(2)}, u32[]{:S(2)}) collective-permute-start(bf16[128,384]{1,0:T(8,128)(2,1)S(1)} %collective-permute-done.5), channel_id=1, source_target_pairs={{0,32},{8,488},{16,48},{24,504},{32,64},{40,8},{48,80},{56,24},{64... | collective-permute-start | bytes 294920 | tf_op jit(solution)/shard_map/ppermute | solution.py:113
  40.8 3.9 %collective-permute-start.6 = (bf16[128,384]{1,0:T(8,128)(2,1)S(1)}, bf16[128,384]{1,0:T(8,128)(2,1)S(1)}, u32[]{:S(2)}, u32[]{:S(2)}) collective-permute-start(bf16[128,384]{1,0:T(8,128)(2,1)S(1)} %collective-permute-done.3), channel_id=1, source_target_pairs={{0,32},{8,488},{16,48},{24,504},{32,64},{40,8},{48,80},{56,24},{64... | collective-permute-start | bytes 294920 | tf_op jit(solution)/shard_map/ppermute | solution.py:113
  44.7 2.6 %collective-permute-start.7 = (bf16[128,384]{1,0:T(8,128)(2,1)S(1)}, bf16[128,384]{1,0:T(8,128)(2,1)S(1)}, u32[]{:S(2)}, u32[]{:S(2)}) collective-permute-start(bf16[128,384]{1,0:T(8,128)(2,1)S(1)} %collective-permute-done.4), channel_id=1, source_target_pairs={{0,32},{8,488},{16,48},{24,504},{32,64},{40,8},{48,80},{56,24},{64... | collective-permute-start | bytes 294920 | tf_op jit(solution)/shard_map/ppermute | solution.py:113
  48.1 2.6 %collective-permute-start.11 = (bf16[128,384]{1,0:T(8,128)(2,1)S(1)}, bf16[128,384]{1,0:T(8,128)(2,1)S(1)}, u32[]{:S(2)}, u32[]{:S(2)}) collective-permute-start(bf16[128,384]{1,0:T(8,128)(2,1)S(1)} %collective-permute-done.8), channel_id=1, source_target_pairs={{0,32},{8,488},{16,48},{24,504},{32,64},{40,8},{48,80},{56,24},{64... | collective-permute-start | bytes 294920 | tf_op jit(solution)/shard_map/ppermute | solution.py:113
  60.2 7.2 %collective-permute-start.24 = (bf16[4,384,384]{2,1,0:T(8,128)(2,1)S(1)}, bf16[4,384,384]{2,1,0:T(8,128)(2,1)S(1)}, u32[]{:S(2)}, u32[]{:S(2)}) collective-permute-start(bf16[4,384,384]{2,1,0:T(8,128)(2,1)S(1)} %pad_maximum_fusion), channel_id=1, source_target_pairs={{0,8},{8,0},{1,9},{9,1},{2,10},{10,2},{3,11},{11,3},{4,12},{12,4},... | collective-permute-start | bytes 3538952 | tf_op jit(solution)/shard_map/ppermute | solution.py:121
  72.4 3.9 %collective-permute-start.13 = (bf16[128,384]{1,0:T(8,128)(2,1)S(1)}, bf16[128,384]{1,0:T(8,128)(2,1)S(1)}, u32[]{:S(2)}, u32[]{:S(2)}) collective-permute-start(bf16[128,384]{1,0:T(8,128)(2,1)S(1)} %collective-permute-done.10), channel_id=1, source_target_pairs={{0,32},{8,488},{16,48},{24,504},{32,64},{40,8},{48,80},{56,24},{64... | collective-permute-start | bytes 294920 | tf_op jit(solution)/shard_map/ppermute | solution.py:113
  77.0 3.6 %collective-permute-start.17 = (bf16[128,384]{1,0:T(8,128)(2,1)S(1)}, bf16[128,384]{1,0:T(8,128)(2,1)S(1)}, u32[]{:S(2)}, u32[]{:S(2)}) collective-permute-start(bf16[128,384]{1,0:T(8,128)(2,1)S(1)} %collective-permute-done.14), channel_id=1, source_target_pairs={{0,32},{8,488},{16,48},{24,504},{32,64},{40,8},{48,80},{56,24},{64... | collective-permute-start | bytes 294920 | tf_op jit(solution)/shard_map/ppermute | solution.py:113
  96.3 4.4 %collective-permute-start.25 = (bf16[3,384,384]{2,1,0:T(8,128)(2,1)S(1)}, bf16[3,384,384]{2,1,0:T(8,128)(2,1)S(1)}, u32[]{:S(2)}, u32[]{:S(2)}) collective-permute-start(bf16[3,384,384]{2,1,0:T(8,128)(2,1)S(1)} %pad_maximum_fusion.1), channel_id=1, source_target_pairs={{0,8},{8,0},{1,9},{9,1},{2,10},{10,2},{3,11},{11,3},{4,12},{12,4},... | collective-permute-start | bytes 2654216 | tf_op jit(solution)/shard_map/ppermute | solution.py:121
  105.3 4.8 %collective-permute-start.22 = (bf16[128,384]{1,0:T(8,128)(2,1)S(1)}, bf16[128,384]{1,0:T(8,128)(2,1)S(1)}, u32[]{:S(2)}, u32[]{:S(2)}) collective-permute-start(bf16[128,384]{1,0:T(8,128)(2,1)S(1)} %collective-permute-done.19), channel_id=1, source_target_pairs={{0,32},{8,488},{16,48},{24,504},{32,64},{40,8},{48,80},{56,24},{64... | collective-permute-start | bytes 294920 | tf_op jit(solution)/shard_map/ppermute | solution.py:113
  123.6 8.2 %collective-permute-start.26 = (bf16[2,128,384]{2,1,0:T(8,128)(2,1)}, bf16[2,128,384]{2,1,0:T(8,128)(2,1)}, u32[]{:S(2)}, u32[]{:S(2)}) collective-permute-start(bf16[2,128,384]{2,1,0:T(8,128)(2,1)} %slice.174), channel_id=1, source_target_pairs={{0,8},{8,16},{16,24},{24,32},{32,40},{40,48},{48,56},{56,64},{64,7... | collective-permute-start | bytes 589832 | tf_op jit(solution)/shard_map/ppermute | solution.py:27
  138.5 3.0 %reshape.74 = bf16[16,2,24,768]{3,2,1,0:T(8,128)(2,1)} reshape(bf16[16,96,384]{2,1,0:T(8,128)(2,1)} %slice.178) | data formatting | bytes 2359296 | tf_op jit(solution)/shard_map/reshape | solution.py:149
  146.6 3.7 %collective-permute-start.28 = (bf16[2,256,384]{2,1,0:T(8,128)(2,1)S(1)}, bf16[2,256,384]{2,1,0:T(8,128)(2,1)S(1)}, u32[]{:S(2)}, u32[]{:S(2)}) collective-permute-start(bf16[2,256,384]{2,1,0:T(8,128)(2,1)S(1)} %convolution_convert_fusion.1), channel_id=1, source_target_pairs={{0,16},{8,24},{16,32},{24,40},{32,48},{40,56},{48,64},{56,72},{64,... | collective-permute-start | bytes 1179656 | tf_op jit(solution)/shard_map/ppermute | solution.py:36
  151.1 3.2 %collective-permute-start.29 = (bf16[2,256,384]{2,1,0:T(8,128)(2,1)S(1)}, bf16[2,256,384]{2,1,0:T(8,128)(2,1)S(1)}, u32[]{:S(2)}, u32[]{:S(2)}) collective-permute-start(bf16[2,256,384]{2,1,0:T(8,128)(2,1)S(1)} %convolution_convert_fusion), channel_id=1, source_target_pairs={{16,0},{24,8},{32,16},{40,24},{48,32},{56,40},{64,48},{72,56},{80,... | collective-permute-start | bytes 1179656 | tf_op jit(solution)/shard_map/ppermute | solution.py:36
  155.0 13.5 %collective-permute-done.28 = bf16[2,256,384]{2,1,0:T(8,128)(2,1)S(1)} collective-permute-done((bf16[2,256,384]{2,1,0:T(8,128)(2,1)S(1)}, bf16[2,256,384]{2,1,0:T(8,128)(2,1)S(1)}, u32[]{:S(2)}, u32[]{:S(2)}) %collective-permute-start.28) | collective-permute-done | bytes 393248 | tf_op jit(solution)/shard_map/ppermute | solution.py:36
  169.2 6.7 %collective-permute-start.32 = (bf16[1,256,384]{2,1,0:T(8,128)(2,1)S(1)}, bf16[1,256,384]{2,1,0:T(8,128)(2,1)S(1)}, u32[]{:S(2)}, u32[]{:S(2)}) collective-permute-start(bf16[1,256,384]{2,1,0:T(8,128)(2,1)S(1)} %fusion.101), channel_id=1, source_target_pairs={{0,16},{8,24},{16,32},{24,40},{32,48},{40,56},{48,64},{56,72},{64,... | collective-permute-start | bytes 589832 | tf_op jit(solution)/shard_map/ppermute | solution.py:36
  181.6 5.6 %collective-permute-done.31 = bf16[1,256,384]{2,1,0:T(8,128)(2,1)S(1)} collective-permute-done((bf16[1,256,384]{2,1,0:T(8,128)(2,1)S(1)}, bf16[1,256,384]{2,1,0:T(8,128)(2,1)S(1)}, u32[]{:S(2)}, u32[]{:S(2)}) %collective-permute-start.31) | collective-permute-done | bytes 196640 | tf_op jit(solution)/shard_map/ppermute | solution.py:36
  188.5 5.8 %collective-permute-start.34 = (bf16[1,128,384]{2,1,0:T(8,128)(2,1)S(1)}, bf16[1,128,384]{2,1,0:T(8,128)(2,1)S(1)}, u32[]{:S(2)}, u32[]{:S(2)}) collective-permute-start(bf16[1,128,384]{2,1,0:T(8,128)(2,1)S(1)} %get-tuple-element.5), channel_id=1, source_target_pairs={{0,8},{8,16},{16,24},{24,32},{32,40},{40,48},{48,56},{56,64},{64,7... | collective-permute-start | bytes 294920 | tf_op jit(solution)/shard_map/ppermute | solution.py:27
  197.0 7.2 %collective-permute-done.33 = bf16[1,128,384]{2,1,0:T(8,128)(2,1)S(1)} collective-permute-done((bf16[1,128,384]{2,1,0:T(8,128)(2,1)S(1)}, bf16[1,128,384]{2,1,0:T(8,128)(2,1)S(1)}, u32[]{:S(2)}, u32[]{:S(2)}) %collective-permute-start.33) | collective-permute-done | bytes 98336 | tf_op jit(solution)/shard_map/ppermute | solution.py:28
  207.6 8.4 %collective-permute-done.35 = bf16[1,256,768]{2,1,0:T(8,128)(2,1)S(1)} collective-permute-done((bf16[1,256,768]{2,1,0:T(8,128)(2,1)S(1)}, bf16[1,256,768]{2,1,0:T(8,128)(2,1)S(1)}, u32[]{:S(2)}, u32[]{:S(2)}) %collective-permute-start.35) | collective-permute-done | bytes 393248 | tf_op jit(solution)/shard_map/ppermute | solution.py:42
  (143 shorter events, 89.1 us)
Async XLA Ops:
  12.1 9.3 %collective-permute-start.2 = (bf16[128,384]{1,0:T(8,128)(2,1)S(1)}, bf16[128,384]{1,0:T(8,128)(2,1)S(1)}, u32[]{:S(2)}, u32[]{:S(2)}) collective-permute-start(bf16[128,384]{1,0:T(8,128)(2,1)S(1)} %slice.164), channel_id=1, source_target_pairs={{0,32},{8,488},{16,48},{24,504},{32,64},{40,8},{48,80},{56,24},{64... | collective-permute-start | bytes 294920 | tf_op jit(solution)/shard_map/ppermute | solution.py:113
  14.1 17.9 %collective-permute-start = (bf16[128,384]{1,0:T(8,128)(2,1)S(1)}, bf16[128,384]{1,0:T(8,128)(2,1)S(1)}, u32[]{:S(2)}, u32[]{:S(2)}) collective-permute-start(bf16[128,384]{1,0:T(8,128)(2,1)S(1)} %get-tuple-element.2), channel_id=1, source_target_pairs={{0,32},{8,488},{16,48},{24,504},{32,64},{40,8},{48,80},{56,24},{64... | collective-permute-start | bytes 294920 | tf_op jit(solution)/shard_map/ppermute | solution.py:113
  16.0 18.7 %collective-permute-start.1 = (bf16[128,384]{1,0:T(8,128)(2,1)S(1)}, bf16[128,384]{1,0:T(8,128)(2,1)S(1)}, u32[]{:S(2)}, u32[]{:S(2)}) collective-permute-start(bf16[128,384]{1,0:T(8,128)(2,1)S(1)} %get-tuple-element.3), channel_id=1, source_target_pairs={{0,32},{8,488},{16,48},{24,504},{32,64},{40,8},{48,80},{56,24},{64... | collective-permute-start | bytes 294920 | tf_op jit(solution)/shard_map/ppermute | solution.py:113
  21.4 16.7 %collective-permute-start.5 = (bf16[128,384]{1,0:T(8,128)(2,1)S(1)}, bf16[128,384]{1,0:T(8,128)(2,1)S(1)}, u32[]{:S(2)}, u32[]{:S(2)}) collective-permute-start(bf16[128,384]{1,0:T(8,128)(2,1)S(1)} %collective-permute-done.2), channel_id=1, source_target_pairs={{0,32},{8,488},{16,48},{24,504},{32,64},{40,8},{48,80},{56,24},{64... | collective-permute-start | bytes 294920 | tf_op jit(solution)/shard_map/ppermute | solution.py:113
  32.0 8.7 %collective-permute-start.3 = (bf16[128,384]{1,0:T(8,128)(2,1)S(1)}, bf16[128,384]{1,0:T(8,128)(2,1)S(1)}, u32[]{:S(2)}, u32[]{:S(2)}) collective-permute-start(bf16[128,384]{1,0:T(8,128)(2,1)S(1)} %collective-permute-done), channel_id=1, source_target_pairs={{0,32},{8,488},{16,48},{24,504},{32,64},{40,8},{48,80},{56,24},{64... | collective-permute-start | bytes 294920 | tf_op jit(solution)/shard_map/ppermute | solution.py:113
  34.7 10.0 %collective-permute-start.4 = (bf16[128,384]{1,0:T(8,128)(2,1)S(1)}, bf16[128,384]{1,0:T(8,128)(2,1)S(1)}, u32[]{:S(2)}, u32[]{:S(2)}) collective-permute-start(bf16[128,384]{1,0:T(8,128)(2,1)S(1)} %collective-permute-done.1), channel_id=1, source_target_pairs={{0,32},{8,488},{16,48},{24,504},{32,64},{40,8},{48,80},{56,24},{64... | collective-permute-start | bytes 294920 | tf_op jit(solution)/shard_map/ppermute | solution.py:113
  38.1 9.9 %collective-permute-start.8 = (bf16[128,384]{1,0:T(8,128)(2,1)S(1)}, bf16[128,384]{1,0:T(8,128)(2,1)S(1)}, u32[]{:S(2)}, u32[]{:S(2)}) collective-permute-start(bf16[128,384]{1,0:T(8,128)(2,1)S(1)} %collective-permute-done.5), channel_id=1, source_target_pairs={{0,32},{8,488},{16,48},{24,504},{32,64},{40,8},{48,80},{56,24},{64... | collective-permute-start | bytes 294920 | tf_op jit(solution)/shard_map/ppermute | solution.py:113
  40.8 12.6 %collective-permute-start.6 = (bf16[128,384]{1,0:T(8,128)(2,1)S(1)}, bf16[128,384]{1,0:T(8,128)(2,1)S(1)}, u32[]{:S(2)}, u32[]{:S(2)}) collective-permute-start(bf16[128,384]{1,0:T(8,128)(2,1)S(1)} %collective-permute-done.3), channel_id=1, source_target_pairs={{0,32},{8,488},{16,48},{24,504},{32,64},{40,8},{48,80},{56,24},{64... | collective-permute-start | bytes 294920 | tf_op jit(solution)/shard_map/ppermute | solution.py:113
  60.2 52.5 %collective-permute-start.24 = (bf16[4,384,384]{2,1,0:T(8,128)(2,1)S(1)}, bf16[4,384,384]{2,1,0:T(8,128)(2,1)S(1)}, u32[]{:S(2)}, u32[]{:S(2)}) collective-permute-start(bf16[4,384,384]{2,1,0:T(8,128)(2,1)S(1)} %pad_maximum_fusion), channel_id=1, source_target_pairs={{0,8},{8,0},{1,9},{9,1},{2,10},{10,2},{3,11},{11,3},{4,12},{12,4},... | collective-permute-start | bytes 3538952 | tf_op jit(solution)/shard_map/ppermute | solution.py:121
  68.2 8.9 %collective-permute-start.14 = (bf16[128,384]{1,0:T(8,128)(2,1)S(1)}, bf16[128,384]{1,0:T(8,128)(2,1)S(1)}, u32[]{:S(2)}, u32[]{:S(2)}) collective-permute-start(bf16[128,384]{1,0:T(8,128)(2,1)S(1)} %collective-permute-done.11), channel_id=1, source_target_pairs={{0,32},{8,488},{16,48},{24,504},{32,64},{40,8},{48,80},{56,24},{64... | collective-permute-start | bytes 294920 | tf_op jit(solution)/shard_map/ppermute | solution.py:113
  70.1 10.6 %collective-permute-start.12 = (bf16[128,384]{1,0:T(8,128)(2,1)S(1)}, bf16[128,384]{1,0:T(8,128)(2,1)S(1)}, u32[]{:S(2)}, u32[]{:S(2)}) collective-permute-start(bf16[128,384]{1,0:T(8,128)(2,1)S(1)} %collective-permute-done.9), channel_id=1, source_target_pairs={{0,32},{8,488},{16,48},{24,504},{32,64},{40,8},{48,80},{56,24},{64... | collective-permute-start | bytes 294920 | tf_op jit(solution)/shard_map/ppermute | solution.py:113
  72.4 10.2 %collective-permute-start.13 = (bf16[128,384]{1,0:T(8,128)(2,1)S(1)}, bf16[128,384]{1,0:T(8,128)(2,1)S(1)}, u32[]{:S(2)}, u32[]{:S(2)}) collective-permute-start(bf16[128,384]{1,0:T(8,128)(2,1)S(1)} %collective-permute-done.10), channel_id=1, source_target_pairs={{0,32},{8,488},{16,48},{24,504},{32,64},{40,8},{48,80},{56,24},{64... | collective-permute-start | bytes 294920 | tf_op jit(solution)/shard_map/ppermute | solution.py:113
  77.0 8.7 %collective-permute-start.17 = (bf16[128,384]{1,0:T(8,128)(2,1)S(1)}, bf16[128,384]{1,0:T(8,128)(2,1)S(1)}, u32[]{:S(2)}, u32[]{:S(2)}) collective-permute-start(bf16[128,384]{1,0:T(8,128)(2,1)S(1)} %collective-permute-done.14), channel_id=1, source_target_pairs={{0,32},{8,488},{16,48},{24,504},{32,64},{40,8},{48,80},{56,24},{64... | collective-permute-start | bytes 294920 | tf_op jit(solution)/shard_map/ppermute | solution.py:113
  96.3 19.3 %collective-permute-start.25 = (bf16[3,384,384]{2,1,0:T(8,128)(2,1)S(1)}, bf16[3,384,384]{2,1,0:T(8,128)(2,1)S(1)}, u32[]{:S(2)}, u32[]{:S(2)}) collective-permute-start(bf16[3,384,384]{2,1,0:T(8,128)(2,1)S(1)} %pad_maximum_fusion.1), channel_id=1, source_target_pairs={{0,8},{8,0},{1,9},{9,1},{2,10},{10,2},{3,11},{11,3},{4,12},{12,4},... | collective-permute-start | bytes 2654216 | tf_op jit(solution)/shard_map/ppermute | solution.py:121
  100.8 10.1 %collective-permute-start.23 = (bf16[128,384]{1,0:T(8,128)(2,1)S(1)}, bf16[128,384]{1,0:T(8,128)(2,1)S(1)}, u32[]{:S(2)}, u32[]{:S(2)}) collective-permute-start(bf16[128,384]{1,0:T(8,128)(2,1)S(1)} %collective-permute-done.20), channel_id=1, source_target_pairs={{0,32},{8,488},{16,48},{24,504},{32,64},{40,8},{48,80},{56,24},{64... | collective-permute-start | bytes 294920 | tf_op jit(solution)/shard_map/ppermute | solution.py:113
  123.6 19.3 %collective-permute-start.26 = (bf16[2,128,384]{2,1,0:T(8,128)(2,1)}, bf16[2,128,384]{2,1,0:T(8,128)(2,1)}, u32[]{:S(2)}, u32[]{:S(2)}) collective-permute-start(bf16[2,128,384]{2,1,0:T(8,128)(2,1)} %slice.174), channel_id=1, source_target_pairs={{0,8},{8,16},{16,24},{24,32},{32,40},{40,48},{48,56},{56,64},{64,7... | collective-permute-start | bytes 589832 | tf_op jit(solution)/shard_map/ppermute | solution.py:27
  132.5 11.4 %collective-permute-start.27 = (bf16[2,128,384]{2,1,0:T(8,128)(2,1)}, bf16[2,128,384]{2,1,0:T(8,128)(2,1)}, u32[]{:S(2)}, u32[]{:S(2)}) collective-permute-start(bf16[2,128,384]{2,1,0:T(8,128)(2,1)} %slice.177), channel_id=1, source_target_pairs={{8,0},{16,8},{24,16},{32,24},{40,32},{48,40},{56,48},{64,56},{72,6... | collective-permute-start | bytes 589832 | tf_op jit(solution)/shard_map/ppermute | solution.py:28
  146.6 22.0 %collective-permute-start.28 = (bf16[2,256,384]{2,1,0:T(8,128)(2,1)S(1)}, bf16[2,256,384]{2,1,0:T(8,128)(2,1)S(1)}, u32[]{:S(2)}, u32[]{:S(2)}) collective-permute-start(bf16[2,256,384]{2,1,0:T(8,128)(2,1)S(1)} %convolution_convert_fusion.1), channel_id=1, source_target_pairs={{0,16},{8,24},{16,32},{24,40},{32,48},{40,56},{48,64},{56,72},{64,... | collective-permute-start | bytes 1179656 | tf_op jit(solution)/shard_map/ppermute | solution.py:36
  151.1 17.5 %collective-permute-start.29 = (bf16[2,256,384]{2,1,0:T(8,128)(2,1)S(1)}, bf16[2,256,384]{2,1,0:T(8,128)(2,1)S(1)}, u32[]{:S(2)}, u32[]{:S(2)}) collective-permute-start(bf16[2,256,384]{2,1,0:T(8,128)(2,1)S(1)} %convolution_convert_fusion), channel_id=1, source_target_pairs={{16,0},{24,8},{32,16},{40,24},{48,32},{56,40},{64,48},{72,56},{80,... | collective-permute-start | bytes 1179656 | tf_op jit(solution)/shard_map/ppermute | solution.py:36
  169.2 12.0 %collective-permute-start.32 = (bf16[1,256,384]{2,1,0:T(8,128)(2,1)S(1)}, bf16[1,256,384]{2,1,0:T(8,128)(2,1)S(1)}, u32[]{:S(2)}, u32[]{:S(2)}) collective-permute-start(bf16[1,256,384]{2,1,0:T(8,128)(2,1)S(1)} %fusion.101), channel_id=1, source_target_pairs={{0,16},{8,24},{16,32},{24,40},{32,48},{40,56},{48,64},{56,72},{64,... | collective-permute-start | bytes 589832 | tf_op jit(solution)/shard_map/ppermute | solution.py:36
  175.9 11.2 %collective-permute-start.31 = (bf16[1,256,384]{2,1,0:T(8,128)(2,1)S(1)}, bf16[1,256,384]{2,1,0:T(8,128)(2,1)S(1)}, u32[]{:S(2)}, u32[]{:S(2)}) collective-permute-start(bf16[1,256,384]{2,1,0:T(8,128)(2,1)S(1)} %fusion.101), channel_id=1, source_target_pairs={{16,0},{24,8},{32,16},{40,24},{48,32},{56,40},{64,48},{72,56},{80,... | collective-permute-start | bytes 589832 | tf_op jit(solution)/shard_map/ppermute | solution.py:36
  178.7 28.9 %collective-permute-start.30 = (bf16[1,256,768]{2,1,0:T(8,128)(2,1)S(1)}, bf16[1,256,768]{2,1,0:T(8,128)(2,1)S(1)}, u32[]{:S(2)}, u32[]{:S(2)}) collective-permute-start(bf16[1,256,768]{2,1,0:T(8,128)(2,1)S(1)} %fusion.55), channel_id=1, source_target_pairs={{7,0},{0,1},{1,2},{2,3},{3,4},{4,5},{5,6},{6,7},{15,8},{8,9},{9,10... | collective-permute-start | bytes 1179656 | tf_op jit(solution)/shard_map/ppermute | solution.py:42
  194.7 9.5 %collective-permute-start.33 = (bf16[1,128,384]{2,1,0:T(8,128)(2,1)S(1)}, bf16[1,128,384]{2,1,0:T(8,128)(2,1)S(1)}, u32[]{:S(2)}, u32[]{:S(2)}) collective-permute-start(bf16[1,128,384]{2,1,0:T(8,128)(2,1)S(1)} %get-tuple-element.4), channel_id=1, source_target_pairs={{8,0},{16,8},{24,16},{32,24},{40,32},{48,40},{56,48},{64,56},{72,6... | collective-permute-start | bytes 294920 | tf_op jit(solution)/shard_map/ppermute | solution.py:28
  205.1 10.9 %collective-permute-start.35 = (bf16[1,256,768]{2,1,0:T(8,128)(2,1)S(1)}, bf16[1,256,768]{2,1,0:T(8,128)(2,1)S(1)}, u32[]{:S(2)}, u32[]{:S(2)}) collective-permute-start(bf16[1,256,768]{2,1,0:T(8,128)(2,1)S(1)} %fusion.24), channel_id=1, source_target_pairs={{1,0},{2,1},{3,2},{4,3},{5,4},{6,5},{7,6},{0,7},{9,8},{10,9},{11,1... | collective-permute-start | bytes 1179656 | tf_op jit(solution)/shard_map/ppermute | solution.py:42
  (22 other events, 119.4 us)

commit v13 on v11

--- a/solution.py
+++ b/solution.py
@@ -115,7 +115,7 @@
         source = (here + sign * step) % span
         gathered = lax.dynamic_update_slice(gathered, current[None], (source, 0, 0))
     needed = span - half - 1
-    early = needed // 2 + needed % 2
+    early = needed - 2
     for begin, end in ((0, early), (early, needed)):
         shared = lax.ppermute(jnp.stack(received[begin:end]), "core", [(0, 1), (1, 0)])
         for step in range(begin + 1, end + 1):

time: 195 us -> 196 us (level)
  starting transfers between devices: 91.7 us -> 93.9 us
    dynamic_update_slice x8 -> x3, other arithmetic: 6.08 us -> 2.24 us  [ring_gather(): gathered = lax.dynamic_update_slice(gathered, current[None], (source, 0, 0))]
    unnamed x0 -> x4, other arithmetic: none -> 3.17 us
  transfers between devices with their start and end apart: 28 -> 28, of which waited for: 11 -> 10; matrix products, arithmetic and copies ran while one was open for 15% -> 15% of each run, Pallas kernels for 0% -> 0%
where the time goes in v13:
time: 196 us; the launch traced here: 195 us
  starting transfers between devices  93.9 us (48%)
  waiting for transfers between devices  46.4 us (24%)
  local copies, waits for them, and re-layouts  24.1 us (12%)
  matrix products  10.8 us (6%)
  blocking collectives  9.43 us (5%)
  other arithmetic  8.73 us (4%)
    ppermute x8, starting transfers between devices, ring_gather(): lax.ppermute(current[:cut], SEQ, route)  25.7 us
    ppermute x4, waiting for transfers between devices, from_behind(): return lax.ppermute(block, axis, route)  18.4 us
    ppermute x8, starting transfers between devices, ring_gather(): lax.ppermute(current[cut:], SEQ, route)  17.5 us
    ppermute x4, starting transfers between devices, from_behind(): return lax.ppermute(block, axis, route)  16.4 us
    ppermute x2, starting transfers between devices, ring_gather(): lax.ppermute(jnp.stack(received[begin:end]), 'core', [(0, 1), (1, 0)])  14.3 us
    ppermute x2, starting transfers between devices, padded(): before = lax.ppermute(last, axis, up)  11.7 us
    ppermute x8, waiting for transfers between devices, ring_gather(): lax.ppermute(current[cut:], SEQ, route)  9.55 us
    all_gather x2, blocking collectives, gather_weights(): both = lax.all_gather(lax.all_gather(both, 'core', axis=0), 'xh', axis=0)  9.43 us
  transfers between devices with their start and end apart: 28, of which 10 were waited for; matrix products, arithmetic and copies ran while one was open for 15% of the time, Pallas kernels for 0%

profile of v13, /device:TPU:127, one launch (start us, length us, event | category | flops | bytes accessed | tf_op | source)
XLA Modules:
  0.0 194.9 jit_solution(8487147937582982203)
XLA Ops:
  4.5 7.2 %all-gather.1 = bf16[4,8,12,384]{3,1,0,2:T(8,128)(2,1)S(1)} all-gather(bf16[2,8,12,384]{3,1,0,2:T(8,128)(2,1)S(1)} %bitcast.187), channel_id=3, replica_groups=mesh['z'=16,'xh'=2,'core'=2,'section'=8] {'xh'}, dimensions={0}, use_global_device_ids=true | all-gather | bytes 442368 | tf_op jit(solution)/shard_map/all_gather | solution.py:135
  16.0 3.4 %collective-permute-done.1 = bf16[192,384]{1,0:T(8,128)(2,1)S(1)} collective-permute-done((bf16[192,384]{1,0:T(8,128)(2,1)S(1)}, bf16[192,384]{1,0:T(8,128)(2,1)S(1)}, u32[]{:S(2)}, u32[]{:S(2)}) %collective-permute-start.1) | collective-permute-done | bytes 147488 | tf_op jit(solution)/shard_map/ppermute | solution.py:112
  21.4 7.2 %collective-permute-start.2 = (bf16[192,384]{1,0:T(8,128)(2,1)S(1)}, bf16[192,384]{1,0:T(8,128)(2,1)S(1)}, u32[]{:S(2)}, u32[]{:S(2)}) collective-permute-start(bf16[192,384]{1,0:T(8,128)(2,1)S(1)} %collective-permute-done), channel_id=1, source_target_pairs={{0,32},{8,488},{16,48},{24,504},{32,64},{40,8},{48,80},{56,24},{64... | collective-permute-start | bytes 442376 | tf_op jit(solution)/shard_map/ppermute | solution.py:112
  28.7 2.6 %collective-permute-start.5 = (bf16[192,384]{1,0:T(8,128)(2,1)S(1)}, bf16[192,384]{1,0:T(8,128)(2,1)S(1)}, u32[]{:S(2)}, u32[]{:S(2)}) collective-permute-start(bf16[192,384]{1,0:T(8,128)(2,1)S(1)} %collective-permute-done.3), channel_id=1, source_target_pairs={{0,32},{8,488},{16,48},{24,504},{32,64},{40,8},{48,80},{56,24},{64... | collective-permute-start | bytes 442376 | tf_op jit(solution)/shard_map/ppermute | solution.py:112
  31.3 4.4 %collective-permute-start.4 = (bf16[192,384]{1,0:T(8,128)(2,1)S(1)}, bf16[192,384]{1,0:T(8,128)(2,1)S(1)}, u32[]{:S(2)}, u32[]{:S(2)}) collective-permute-start(bf16[192,384]{1,0:T(8,128)(2,1)S(1)} %collective-permute-done.2), channel_id=1, source_target_pairs={{0,32},{8,488},{16,48},{24,504},{32,64},{40,8},{48,80},{56,24},{64... | collective-permute-start | bytes 442376 | tf_op jit(solution)/shard_map/ppermute | solution.py:112
  35.7 2.8 %broadcast_in_dim.30 = bf16[16,384,384]{2,1,0:T(8,128)(2,1)} broadcast(bf16[]{:T(256)} %constant.111.clone.1), dimensions={} | broadcast | bytes 4718594 | tf_op jit(solution)/shard_map/broadcast_in_dim | solution.py:106
  39.2 2.7 %collective-permute-start.7 = (bf16[192,384]{1,0:T(8,128)(2,1)S(1)}, bf16[192,384]{1,0:T(8,128)(2,1)S(1)}, u32[]{:S(2)}, u32[]{:S(2)}) collective-permute-start(bf16[192,384]{1,0:T(8,128)(2,1)S(1)} %collective-permute-done.5), channel_id=1, source_target_pairs={{0,32},{8,488},{16,48},{24,504},{32,64},{40,8},{48,80},{56,24},{64... | collective-permute-start | bytes 442376 | tf_op jit(solution)/shard_map/ppermute | solution.py:112
  41.9 4.3 %collective-permute-start.6 = (bf16[192,384]{1,0:T(8,128)(2,1)S(1)}, bf16[192,384]{1,0:T(8,128)(2,1)S(1)}, u32[]{:S(2)}, u32[]{:S(2)}) collective-permute-start(bf16[192,384]{1,0:T(8,128)(2,1)S(1)} %collective-permute-done.4), channel_id=1, source_target_pairs={{0,32},{8,488},{16,48},{24,504},{32,64},{40,8},{48,80},{56,24},{64... | collective-permute-start | bytes 442376 | tf_op jit(solution)/shard_map/ppermute | solution.py:112
  47.8 2.6 %collective-permute-start.9 = (bf16[192,384]{1,0:T(8,128)(2,1)S(1)}, bf16[192,384]{1,0:T(8,128)(2,1)S(1)}, u32[]{:S(2)}, u32[]{:S(2)}) collective-permute-start(bf16[192,384]{1,0:T(8,128)(2,1)S(1)} %collective-permute-done.7), channel_id=1, source_target_pairs={{0,32},{8,488},{16,48},{24,504},{32,64},{40,8},{48,80},{56,24},{64... | collective-permute-start | bytes 442376 | tf_op jit(solution)/shard_map/ppermute | solution.py:112
  54.9 2.7 %collective-permute-done.8 = bf16[192,384]{1,0:T(8,128)(2,1)S(1)} collective-permute-done((bf16[192,384]{1,0:T(8,128)(2,1)S(1)}, bf16[192,384]{1,0:T(8,128)(2,1)S(1)}, u32[]{:S(2)}, u32[]{:S(2)}) %collective-permute-start.8) | collective-permute-done | bytes 147488 | tf_op jit(solution)/shard_map/ppermute | solution.py:112
  58.3 7.9 %collective-permute-start.16 = (bf16[5,384,384]{2,1,0:T(8,128)(2,1)S(1)}, bf16[5,384,384]{2,1,0:T(8,128)(2,1)S(1)}, u32[]{:S(2)}, u32[]{:S(2)}) collective-permute-start(bf16[5,384,384]{2,1,0:T(8,128)(2,1)S(1)} %get-tuple-element.2), channel_id=1, source_target_pairs={{0,8},{8,0},{1,9},{9,1},{2,10},{10,2},{3,11},{11,3},{4,12},{12,4},... | collective-permute-start | bytes 4423688 | tf_op jit(solution)/shard_map/ppermute | solution.py:120
  70.3 3.0 %collective-permute-done.11 = bf16[192,384]{1,0:T(8,128)(2,1)S(1)} collective-permute-done((bf16[192,384]{1,0:T(8,128)(2,1)S(1)}, bf16[192,384]{1,0:T(8,128)(2,1)S(1)}, u32[]{:S(2)}, u32[]{:S(2)}) %collective-permute-start.11) | collective-permute-done | bytes 147488 | tf_op jit(solution)/shard_map/ppermute | solution.py:112
  84.4 6.4 %collective-permute-start.17 = (bf16[2,384,384]{2,1,0:T(8,128)(2,1)S(1)}, bf16[2,384,384]{2,1,0:T(8,128)(2,1)S(1)}, u32[]{:S(2)}, u32[]{:S(2)}) collective-permute-start(bf16[2,384,384]{2,1,0:T(8,128)(2,1)S(1)} %pad_maximum_fusion.1), channel_id=1, source_target_pairs={{0,8},{8,0},{1,9},{9,1},{2,10},{10,2},{3,11},{11,3},{4,12},{12,4},... | collective-permute-start | bytes 1769480 | tf_op jit(solution)/shard_map/ppermute | solution.py:120
  103.3 5.9 %collective-permute-start.18 = (bf16[2,128,384]{2,1,0:T(8,128)(2,1)}, bf16[2,128,384]{2,1,0:T(8,128)(2,1)}, u32[]{:S(2)}, u32[]{:S(2)}) collective-permute-start(bf16[2,128,384]{2,1,0:T(8,128)(2,1)} %slice.169), channel_id=1, source_target_pairs={{0,8},{8,16},{16,24},{24,32},{32,40},{40,48},{48,56},{56,64},{64,7... | collective-permute-start | bytes 589832 | tf_op jit(solution)/shard_map/ppermute | solution.py:27
  115.9 3.0 %reshape.74 = bf16[16,2,24,768]{3,2,1,0:T(8,128)(2,1)} reshape(bf16[16,96,384]{2,1,0:T(8,128)(2,1)} %slice.173) | data formatting | bytes 2359296 | tf_op jit(solution)/shard_map/reshape | solution.py:148
  124.0 3.8 %collective-permute-start.20 = (bf16[2,256,384]{2,1,0:T(8,128)(2,1)S(1)}, bf16[2,256,384]{2,1,0:T(8,128)(2,1)S(1)}, u32[]{:S(2)}, u32[]{:S(2)}) collective-permute-start(bf16[2,256,384]{2,1,0:T(8,128)(2,1)S(1)} %convolution_convert_fusion.1), channel_id=1, source_target_pairs={{0,16},{8,24},{16,32},{24,40},{32,48},{40,56},{48,64},{56,72},{64,... | collective-permute-start | bytes 1179656 | tf_op jit(solution)/shard_map/ppermute | solution.py:36
  128.5 3.0 %collective-permute-start.21 = (bf16[2,256,384]{2,1,0:T(8,128)(2,1)S(1)}, bf16[2,256,384]{2,1,0:T(8,128)(2,1)S(1)}, u32[]{:S(2)}, u32[]{:S(2)}) collective-permute-start(bf16[2,256,384]{2,1,0:T(8,128)(2,1)S(1)} %convolution_convert_fusion), channel_id=1, source_target_pairs={{16,0},{24,8},{32,16},{40,24},{48,32},{56,40},{64,48},{72,56},{80,... | collective-permute-start | bytes 1179656 | tf_op jit(solution)/shard_map/ppermute | solution.py:36
  132.3 4.2 %collective-permute-done.20 = bf16[2,256,384]{2,1,0:T(8,128)(2,1)S(1)} collective-permute-done((bf16[2,256,384]{2,1,0:T(8,128)(2,1)S(1)}, bf16[2,256,384]{2,1,0:T(8,128)(2,1)S(1)}, u32[]{:S(2)}, u32[]{:S(2)}) %collective-permute-start.20) | collective-permute-done | bytes 393248 | tf_op jit(solution)/shard_map/ppermute | solution.py:36
  136.5 8.8 %collective-permute-done.21 = bf16[2,256,384]{2,1,0:T(8,128)(2,1)S(1)} collective-permute-done((bf16[2,256,384]{2,1,0:T(8,128)(2,1)S(1)}, bf16[2,256,384]{2,1,0:T(8,128)(2,1)S(1)}, u32[]{:S(2)}, u32[]{:S(2)}) %collective-permute-start.21) | collective-permute-done | bytes 393248 | tf_op jit(solution)/shard_map/ppermute | solution.py:36
  145.9 7.5 %collective-permute-start.24 = (bf16[1,256,384]{2,1,0:T(8,128)(2,1)S(1)}, bf16[1,256,384]{2,1,0:T(8,128)(2,1)S(1)}, u32[]{:S(2)}, u32[]{:S(2)}) collective-permute-start(bf16[1,256,384]{2,1,0:T(8,128)(2,1)S(1)} %fusion.101), channel_id=1, source_target_pairs={{0,16},{8,24},{16,32},{24,40},{32,48},{40,56},{48,64},{56,72},{64,... | collective-permute-start | bytes 589832 | tf_op jit(solution)/shard_map/ppermute | solution.py:36
  159.2 5.4 %collective-permute-done.23 = bf16[1,256,384]{2,1,0:T(8,128)(2,1)S(1)} collective-permute-done((bf16[1,256,384]{2,1,0:T(8,128)(2,1)S(1)}, bf16[1,256,384]{2,1,0:T(8,128)(2,1)S(1)}, u32[]{:S(2)}, u32[]{:S(2)}) %collective-permute-start.23) | collective-permute-done | bytes 196640 | tf_op jit(solution)/shard_map/ppermute | solution.py:36
  165.9 5.8 %collective-permute-start.26 = (bf16[1,128,384]{2,1,0:T(8,128)(2,1)S(1)}, bf16[1,128,384]{2,1,0:T(8,128)(2,1)S(1)}, u32[]{:S(2)}, u32[]{:S(2)}) collective-permute-start(bf16[1,128,384]{2,1,0:T(8,128)(2,1)S(1)} %get-tuple-element.13), channel_id=1, source_target_pairs={{0,8},{8,16},{16,24},{24,32},{32,40},{40,48},{48,56},{56,64},{64,7... | collective-permute-start | bytes 294920 | tf_op jit(solution)/shard_map/ppermute | solution.py:27
  174.5 7.2 %collective-permute-done.25 = bf16[1,128,384]{2,1,0:T(8,128)(2,1)S(1)} collective-permute-done((bf16[1,128,384]{2,1,0:T(8,128)(2,1)S(1)}, bf16[1,128,384]{2,1,0:T(8,128)(2,1)S(1)}, u32[]{:S(2)}, u32[]{:S(2)}) %collective-permute-start.25) | collective-permute-done | bytes 98336 | tf_op jit(solution)/shard_map/ppermute | solution.py:28
  185.0 8.5 %collective-permute-done.27 = bf16[1,256,768]{2,1,0:T(8,128)(2,1)S(1)} collective-permute-done((bf16[1,256,768]{2,1,0:T(8,128)(2,1)S(1)}, bf16[1,256,768]{2,1,0:T(8,128)(2,1)S(1)}, u32[]{:S(2)}, u32[]{:S(2)}) %collective-permute-start.27) | collective-permute-done | bytes 393248 | tf_op jit(solution)/shard_map/ppermute | solution.py:42
  (121 shorter events, 73.1 us)
Async XLA Ops:
  12.1 7.3 %collective-permute-start.1 = (bf16[192,384]{1,0:T(8,128)(2,1)S(1)}, bf16[192,384]{1,0:T(8,128)(2,1)S(1)}, u32[]{:S(2)}, u32[]{:S(2)}) collective-permute-start(bf16[192,384]{1,0:T(8,128)(2,1)S(1)} %slice.159), channel_id=1, source_target_pairs={{0,32},{8,488},{16,48},{24,504},{32,64},{40,8},{48,80},{56,24},{64... | collective-permute-start | bytes 442376 | tf_op jit(solution)/shard_map/ppermute | solution.py:112
  14.1 7.3 %collective-permute-start = (bf16[192,384]{1,0:T(8,128)(2,1)S(1)}, bf16[192,384]{1,0:T(8,128)(2,1)S(1)}, u32[]{:S(2)}, u32[]{:S(2)}) collective-permute-start(bf16[192,384]{1,0:T(8,128)(2,1)S(1)} %slice.158), channel_id=1, source_target_pairs={{0,32},{8,488},{16,48},{24,504},{32,64},{40,8},{48,80},{56,24},{64... | collective-permute-start | bytes 442376 | tf_op jit(solution)/shard_map/ppermute | solution.py:112
  19.4 9.2 %collective-permute-start.3 = (bf16[192,384]{1,0:T(8,128)(2,1)S(1)}, bf16[192,384]{1,0:T(8,128)(2,1)S(1)}, u32[]{:S(2)}, u32[]{:S(2)}) collective-permute-start(bf16[192,384]{1,0:T(8,128)(2,1)S(1)} %collective-permute-done.1), channel_id=1, source_target_pairs={{0,32},{8,488},{16,48},{24,504},{32,64},{40,8},{48,80},{56,24},{64... | collective-permute-start | bytes 442376 | tf_op jit(solution)/shard_map/ppermute | solution.py:112
  21.4 9.9 %collective-permute-start.2 = (bf16[192,384]{1,0:T(8,128)(2,1)S(1)}, bf16[192,384]{1,0:T(8,128)(2,1)S(1)}, u32[]{:S(2)}, u32[]{:S(2)}) collective-permute-start(bf16[192,384]{1,0:T(8,128)(2,1)S(1)} %collective-permute-done), channel_id=1, source_target_pairs={{0,32},{8,488},{16,48},{24,504},{32,64},{40,8},{48,80},{56,24},{64... | collective-permute-start | bytes 442376 | tf_op jit(solution)/shard_map/ppermute | solution.py:112
  28.7 10.6 %collective-permute-start.5 = (bf16[192,384]{1,0:T(8,128)(2,1)S(1)}, bf16[192,384]{1,0:T(8,128)(2,1)S(1)}, u32[]{:S(2)}, u32[]{:S(2)}) collective-permute-start(bf16[192,384]{1,0:T(8,128)(2,1)S(1)} %collective-permute-done.3), channel_id=1, source_target_pairs={{0,32},{8,488},{16,48},{24,504},{32,64},{40,8},{48,80},{56,24},{64... | collective-permute-start | bytes 442376 | tf_op jit(solution)/shard_map/ppermute | solution.py:112
  31.3 10.6 %collective-permute-start.4 = (bf16[192,384]{1,0:T(8,128)(2,1)S(1)}, bf16[192,384]{1,0:T(8,128)(2,1)S(1)}, u32[]{:S(2)}, u32[]{:S(2)}) collective-permute-start(bf16[192,384]{1,0:T(8,128)(2,1)S(1)} %collective-permute-done.2), channel_id=1, source_target_pairs={{0,32},{8,488},{16,48},{24,504},{32,64},{40,8},{48,80},{56,24},{64... | collective-permute-start | bytes 442376 | tf_op jit(solution)/shard_map/ppermute | solution.py:112
  39.2 8.5 %collective-permute-start.7 = (bf16[192,384]{1,0:T(8,128)(2,1)S(1)}, bf16[192,384]{1,0:T(8,128)(2,1)S(1)}, u32[]{:S(2)}, u32[]{:S(2)}) collective-permute-start(bf16[192,384]{1,0:T(8,128)(2,1)S(1)} %collective-permute-done.5), channel_id=1, source_target_pairs={{0,32},{8,488},{16,48},{24,504},{32,64},{40,8},{48,80},{56,24},{64... | collective-permute-start | bytes 442376 | tf_op jit(solution)/shard_map/ppermute | solution.py:112
  41.9 8.5 %collective-permute-start.6 = (bf16[192,384]{1,0:T(8,128)(2,1)S(1)}, bf16[192,384]{1,0:T(8,128)(2,1)S(1)}, u32[]{:S(2)}, u32[]{:S(2)}) collective-permute-start(bf16[192,384]{1,0:T(8,128)(2,1)S(1)} %collective-permute-done.4), channel_id=1, source_target_pairs={{0,32},{8,488},{16,48},{24,504},{32,64},{40,8},{48,80},{56,24},{64... | collective-permute-start | bytes 442376 | tf_op jit(solution)/shard_map/ppermute | solution.py:112
  50.4 7.1 %collective-permute-start.8 = (bf16[192,384]{1,0:T(8,128)(2,1)S(1)}, bf16[192,384]{1,0:T(8,128)(2,1)S(1)}, u32[]{:S(2)}, u32[]{:S(2)}) collective-permute-start(bf16[192,384]{1,0:T(8,128)(2,1)S(1)} %collective-permute-done.6), channel_id=1, source_target_pairs={{0,32},{8,488},{16,48},{24,504},{32,64},{40,8},{48,80},{56,24},{64... | collective-permute-start | bytes 442376 | tf_op jit(solution)/shard_map/ppermute | solution.py:112
  58.3 34.0 %collective-permute-start.16 = (bf16[5,384,384]{2,1,0:T(8,128)(2,1)S(1)}, bf16[5,384,384]{2,1,0:T(8,128)(2,1)S(1)}, u32[]{:S(2)}, u32[]{:S(2)}) collective-permute-start(bf16[5,384,384]{2,1,0:T(8,128)(2,1)S(1)} %get-tuple-element.2), channel_id=1, source_target_pairs={{0,8},{8,0},{1,9},{9,1},{2,10},{10,2},{3,11},{11,3},{4,12},{12,4},... | collective-permute-start | bytes 4423688 | tf_op jit(solution)/shard_map/ppermute | solution.py:120
  66.3 7.1 %collective-permute-start.11 = (bf16[192,384]{1,0:T(8,128)(2,1)S(1)}, bf16[192,384]{1,0:T(8,128)(2,1)S(1)}, u32[]{:S(2)}, u32[]{:S(2)}) collective-permute-start(bf16[192,384]{1,0:T(8,128)(2,1)S(1)} %collective-permute-done.9), channel_id=1, source_target_pairs={{0,32},{8,488},{16,48},{24,504},{32,64},{40,8},{48,80},{56,24},{64... | collective-permute-start | bytes 442376 | tf_op jit(solution)/shard_map/ppermute | solution.py:112
  80.4 11.2 %collective-permute-start.15 = (bf16[192,384]{1,0:T(8,128)(2,1)S(1)}, bf16[192,384]{1,0:T(8,128)(2,1)S(1)}, u32[]{:S(2)}, u32[]{:S(2)}) collective-permute-start(bf16[192,384]{1,0:T(8,128)(2,1)S(1)} %collective-permute-done.13), channel_id=1, source_target_pairs={{0,32},{8,488},{16,48},{24,504},{32,64},{40,8},{48,80},{56,24},{64... | collective-permute-start | bytes 442376 | tf_op jit(solution)/shard_map/ppermute | solution.py:112
  82.4 9.2 %collective-permute-start.14 = (bf16[192,384]{1,0:T(8,128)(2,1)S(1)}, bf16[192,384]{1,0:T(8,128)(2,1)S(1)}, u32[]{:S(2)}, u32[]{:S(2)}) collective-permute-start(bf16[192,384]{1,0:T(8,128)(2,1)S(1)} %collective-permute-done.12), channel_id=1, source_target_pairs={{0,32},{8,488},{16,48},{24,504},{32,64},{40,8},{48,80},{56,24},{64... | collective-permute-start | bytes 442376 | tf_op jit(solution)/shard_map/ppermute | solution.py:112
  84.4 11.7 %collective-permute-start.17 = (bf16[2,384,384]{2,1,0:T(8,128)(2,1)S(1)}, bf16[2,384,384]{2,1,0:T(8,128)(2,1)S(1)}, u32[]{:S(2)}, u32[]{:S(2)}) collective-permute-start(bf16[2,384,384]{2,1,0:T(8,128)(2,1)S(1)} %pad_maximum_fusion.1), channel_id=1, source_target_pairs={{0,8},{8,0},{1,9},{9,1},{2,10},{10,2},{3,11},{11,3},{4,12},{12,4},... | collective-permute-start | bytes 1769480 | tf_op jit(solution)/shard_map/ppermute | solution.py:120
  103.3 17.0 %collective-permute-start.18 = (bf16[2,128,384]{2,1,0:T(8,128)(2,1)}, bf16[2,128,384]{2,1,0:T(8,128)(2,1)}, u32[]{:S(2)}, u32[]{:S(2)}) collective-permute-start(bf16[2,128,384]{2,1,0:T(8,128)(2,1)} %slice.169), channel_id=1, source_target_pairs={{0,8},{8,16},{16,24},{24,32},{32,40},{40,48},{48,56},{56,64},{64,7... | collective-permute-start | bytes 589832 | tf_op jit(solution)/shard_map/ppermute | solution.py:27
  109.9 11.5 %collective-permute-start.19 = (bf16[2,128,384]{2,1,0:T(8,128)(2,1)}, bf16[2,128,384]{2,1,0:T(8,128)(2,1)}, u32[]{:S(2)}, u32[]{:S(2)}) collective-permute-start(bf16[2,128,384]{2,1,0:T(8,128)(2,1)} %slice.172), channel_id=1, source_target_pairs={{8,0},{16,8},{24,16},{32,24},{40,32},{48,40},{56,48},{64,56},{72,6... | collective-permute-start | bytes 589832 | tf_op jit(solution)/shard_map/ppermute | solution.py:28
  124.0 12.5 %collective-permute-start.20 = (bf16[2,256,384]{2,1,0:T(8,128)(2,1)S(1)}, bf16[2,256,384]{2,1,0:T(8,128)(2,1)S(1)}, u32[]{:S(2)}, u32[]{:S(2)}) collective-permute-start(bf16[2,256,384]{2,1,0:T(8,128)(2,1)S(1)} %convolution_convert_fusion.1), channel_id=1, source_target_pairs={{0,16},{8,24},{16,32},{24,40},{32,48},{40,56},{48,64},{56,72},{64,... | collective-permute-start | bytes 1179656 | tf_op jit(solution)/shard_map/ppermute | solution.py:36
  128.5 16.8 %collective-permute-start.21 = (bf16[2,256,384]{2,1,0:T(8,128)(2,1)S(1)}, bf16[2,256,384]{2,1,0:T(8,128)(2,1)S(1)}, u32[]{:S(2)}, u32[]{:S(2)}) collective-permute-start(bf16[2,256,384]{2,1,0:T(8,128)(2,1)S(1)} %convolution_convert_fusion), channel_id=1, source_target_pairs={{16,0},{24,8},{32,16},{40,24},{48,32},{56,40},{64,48},{72,56},{80,... | collective-permute-start | bytes 1179656 | tf_op jit(solution)/shard_map/ppermute | solution.py:36
  145.9 12.9 %collective-permute-start.24 = (bf16[1,256,384]{2,1,0:T(8,128)(2,1)S(1)}, bf16[1,256,384]{2,1,0:T(8,128)(2,1)S(1)}, u32[]{:S(2)}, u32[]{:S(2)}) collective-permute-start(bf16[1,256,384]{2,1,0:T(8,128)(2,1)S(1)} %fusion.101), channel_id=1, source_target_pairs={{0,16},{8,24},{16,32},{24,40},{32,48},{40,56},{48,64},{56,72},{64,... | collective-permute-start | bytes 589832 | tf_op jit(solution)/shard_map/ppermute | solution.py:36
  153.4 11.2 %collective-permute-start.23 = (bf16[1,256,384]{2,1,0:T(8,128)(2,1)S(1)}, bf16[1,256,384]{2,1,0:T(8,128)(2,1)S(1)}, u32[]{:S(2)}, u32[]{:S(2)}) collective-permute-start(bf16[1,256,384]{2,1,0:T(8,128)(2,1)S(1)} %fusion.101), channel_id=1, source_target_pairs={{16,0},{24,8},{32,16},{40,24},{48,32},{56,40},{64,48},{72,56},{80,... | collective-permute-start | bytes 589832 | tf_op jit(solution)/shard_map/ppermute | solution.py:36
  156.3 28.7 %collective-permute-start.22 = (bf16[1,256,768]{2,1,0:T(8,128)(2,1)S(1)}, bf16[1,256,768]{2,1,0:T(8,128)(2,1)S(1)}, u32[]{:S(2)}, u32[]{:S(2)}) collective-permute-start(bf16[1,256,768]{2,1,0:T(8,128)(2,1)S(1)} %fusion.55), channel_id=1, source_target_pairs={{7,0},{0,1},{1,2},{2,3},{3,4},{4,5},{5,6},{6,7},{15,8},{8,9},{9,10... | collective-permute-start | bytes 1179656 | tf_op jit(solution)/shard_map/ppermute | solution.py:42
  165.9 8.1 %collective-permute-start.26 = (bf16[1,128,384]{2,1,0:T(8,128)(2,1)S(1)}, bf16[1,128,384]{2,1,0:T(8,128)(2,1)S(1)}, u32[]{:S(2)}, u32[]{:S(2)}) collective-permute-start(bf16[1,128,384]{2,1,0:T(8,128)(2,1)S(1)} %get-tuple-element.13), channel_id=1, source_target_pairs={{0,8},{8,16},{16,24},{24,32},{32,40},{40,48},{48,56},{56,64},{64,7... | collective-permute-start | bytes 294920 | tf_op jit(solution)/shard_map/ppermute | solution.py:27
  172.2 9.5 %collective-permute-start.25 = (bf16[1,128,384]{2,1,0:T(8,128)(2,1)S(1)}, bf16[1,128,384]{2,1,0:T(8,128)(2,1)S(1)}, u32[]{:S(2)}, u32[]{:S(2)}) collective-permute-start(bf16[1,128,384]{2,1,0:T(8,128)(2,1)S(1)} %get-tuple-element.12), channel_id=1, source_target_pairs={{8,0},{16,8},{24,16},{32,24},{40,32},{48,40},{56,48},{64,56},{72,6... | collective-permute-start | bytes 294920 | tf_op jit(solution)/shard_map/ppermute | solution.py:28
  182.5 10.9 %collective-permute-start.27 = (bf16[1,256,768]{2,1,0:T(8,128)(2,1)S(1)}, bf16[1,256,768]{2,1,0:T(8,128)(2,1)S(1)}, u32[]{:S(2)}, u32[]{:S(2)}) collective-permute-start(bf16[1,256,768]{2,1,0:T(8,128)(2,1)S(1)} %fusion.24), channel_id=1, source_target_pairs={{1,0},{2,1},{3,2},{4,3},{5,4},{6,5},{7,6},{0,7},{9,8},{10,9},{11,1... | collective-permute-start | bytes 1179656 | tf_op jit(solution)/shard_map/ppermute | solution.py:42
  (14 other events, 61.0 us)
